TPU v7x, 32 devices: a whole 2x2x4 slice. The times are simulated.
32 devices in a mesh: req: 8 (over z, y), tp: 4 (over x, core).
Axes of the slice: x: 2, y: 2, z: 4, core: 2. Of those that a mesh axis runs over, the one named last changes fastest.
Arguments:
- hidden: bfloat16 [4096, 2048], P('req', 'tp'), may hold values from -6 to 6
- queries: bfloat16 [4096, 2048], P('req', 'tp'), may hold values from -4 to 4
- new_keys: bfloat16 [4096, 512], P('req'), may hold values from -4 to 4
- new_values: bfloat16 [4096, 512], P('req'), may hold values from -6 to 6
- cache_keys: bfloat16 [384, 64, 512], P('req'), may hold values from -6 to 6
- cache_values: bfloat16 [384, 64, 512], P('req'), may hold values from -6 to 6
- out_weight: bfloat16 [2048, 2048], P('tp'), may hold values from -0.125 to 0.125
- attn_gain: bfloat16 [2048], P('tp'), may hold values from 0.099609375 to 1.8984375
- ple_input: bfloat16 [4096, 256], P('req'), may hold values from -6 to 6
- ple_gate_weight: bfloat16 [2048, 256], P('tp'), may hold values from -0.125 to 0.125
- ple_proj_weight: bfloat16 [256, 2048], P(None, 'tp'), may hold values from -0.375 to 0.375
- ple_gain: bfloat16 [2048], P('tp'), may hold values from 0.099609375 to 1.8984375
- page_holder: int32 [384, 1], P('req'), may hold values from 0 to 7; in each aligned block of 48 rows (0 to 47, 48 to 95, ...) at most 6 rows name the same one
- page_slot: int32 [384, 1], P('req'), may hold values from 0 to 47
- page_counts: int32 [8, 8], P('req'), may hold values from 1 to 12, 48 in all within a row
- last_fill: int32 [8, 8], P('req'), may hold values from 1 to 64
- row_counts: int32 [8, 8], P('req'), may hold values from 1 to 256, 512 in all within a row
Outputs:
- layer_out: bfloat16 [4096, 2048], P('req', 'tp')
Inputs may be any that keep to these rules, and one draw needn't show every extreme that they name: `page_holder`: within the 48 page references of one device's requests (aligned blocks), no req index is named more than 6 times; in some block one is named exactly 6 times. `page_counts`: the 8 counts of one device sum to 48; some count equals 12. `row_counts`: the 8 counts of one device sum to 512; some count equals 256.
All inputs are finite; a program needn't handle non-finite values.
Results may differ from a plain program's by a relative error of at most 0.0061.
Values may be sent and summed in bfloat16 or wider, within the bound.
No kernel may reach another device: no remote copies, remote signals or barrier semaphores. Data moves between devices by JAX's collectives and lax.ppermute only.
A program may use at most 128 MiB of HBM per device.

v0:
```python
import math

import jax
import jax.numpy as jnp
from jax import lax
from jax.sharding import PartitionSpec as P

D = 2048
HD = 256


def slot_lookup(positions, counts):
    starts = jnp.cumsum(counts) - counts
    owning = jnp.sum((positions[:, None] >= starts[None, :]).astype(jnp.int32), axis=1) - 1
    return (owning, starts)


def table_pick(table, owning):
    onehot = owning[:, None] == jnp.arange(table.shape[0], dtype=jnp.int32)[None, :]
    return jnp.sum(jnp.where(onehot, table[None, :], 0), axis=1)


def attend_masks(counts_of_pages, fill_row, counts_of_rows, page_len, page_total, row_total):
    key_index = jnp.arange(page_total * page_len, dtype=jnp.int32)
    page_ref = key_index // page_len
    within = key_index % page_len
    page_owner, page_starts = slot_lookup(page_ref, counts_of_pages)
    context_len = (counts_of_pages - 1) * page_len + fill_row
    position = (page_ref - table_pick(page_starts, page_owner)) * page_len + within
    valid = position < table_pick(context_len, page_owner)
    row_index = jnp.arange(row_total, dtype=jnp.int32)
    row_owner = slot_lookup(row_index, counts_of_rows)[0]
    context_mask = (row_owner[:, None] == page_owner[None, :]) & valid[None, :]
    causal = (row_owner[:, None] == row_owner[None, :]) & (row_index[None, :] <= row_index[:, None])
    return jnp.concatenate([context_mask, causal], axis=1)


def shards(
    hidden,
    queries,
    new_keys,
    new_values,
    cache_keys,
    cache_values,
    out_weight,
    attn_gain,
    ple_input,
    ple_gate_weight,
    ple_proj_weight,
    ple_gain,
    page_holder,
    page_slot,
    page_counts,
    last_fill,
    row_counts,
):
    row_total = hidden.shape[0]
    page_total = cache_keys.shape[0]
    page_len = cache_keys.shape[1]
    req_count = lax.axis_size("req")
    tp_index = lax.axis_index("tp")
    local_heads = queries.shape[1] // HD
    kv_head = tp_index // 2
    capacity = max(2, page_total // req_count)
    holders = page_holder[:, 0]
    places = page_slot[:, 0]
    ref_index = jnp.arange(page_total, dtype=jnp.int32)
    earlier = (holders[:, None] == holders[None, :]) & (ref_index[:, None] > ref_index[None, :])
    ranking = jnp.sum(earlier.astype(jnp.int32), axis=1)
    matched = (holders[:, None, None] == jnp.arange(req_count, dtype=jnp.int32)[None, :, None]) & (
        ranking[:, None, None] == jnp.arange(capacity, dtype=jnp.int32)[None, None, :]
    )
    request_table = jnp.sum(jnp.where(matched, places[:, None, None] + 1, 0), axis=0) - 1
    asked = lax.all_to_all(request_table, "req", split_axis=0, concat_axis=0, tiled=True)
    wanted = jnp.maximum(asked, 0)
    head_keys = lax.dynamic_slice_in_dim(cache_keys, kv_head * HD, HD, 2)
    head_values = lax.dynamic_slice_in_dim(cache_values, kv_head * HD, HD, 2)
    stacked = jnp.concatenate([head_keys, head_values], axis=2)
    arrival_index = holders * capacity + ranking
    outgoing = stacked[wanted]
    arrived = lax.all_to_all(outgoing, "req", split_axis=0, concat_axis=0, tiled=True)
    context = arrived.reshape(req_count * capacity, page_len, 2 * HD)[arrival_index]
    context_keys = context[:, :, :HD].reshape(page_total * page_len, HD)
    context_values = context[:, :, HD:].reshape(page_total * page_len, HD)
    fresh_keys = lax.dynamic_slice_in_dim(new_keys, kv_head * HD, HD, 1)
    fresh_values = lax.dynamic_slice_in_dim(new_values, kv_head * HD, HD, 1)
    all_keys = jnp.concatenate([context_keys, fresh_keys], axis=0)
    all_values = jnp.concatenate([context_values, fresh_values], axis=0)
    masking = attend_masks(
        page_counts[0], last_fill[0], row_counts[0], page_len, page_total, row_total
    )
    query_rows = queries.reshape(row_total, local_heads, HD)
    scores = jnp.einsum("rhd,kd->hrk", query_rows, all_keys, preferred_element_type=jnp.float32) * (
        1.0 / math.sqrt(HD)
    )
    scores = jnp.where(masking[None], scores, -1e30)
    highest = jnp.max(scores, axis=-1, keepdims=True)
    expo = jnp.exp(scores - highest)
    weights = (expo / jnp.sum(expo, axis=-1, keepdims=True)).astype(jnp.bfloat16)
    attention = jnp.einsum("hrk,kd->rhd", weights, all_values, preferred_element_type=jnp.float32)
    attention = attention.astype(jnp.bfloat16).reshape(row_total, local_heads * HD)
    partial_sum = jnp.dot(attention, out_weight, preferred_element_type=jnp.float32)
    columns = hidden.shape[1]
    summed = lax.psum(partial_sum, "tp")
    squares = jnp.sum(summed * summed, axis=1)
    local_part = lax.dynamic_slice_in_dim(summed, tp_index * columns, columns, 1)
    normed = (
        local_part
        * lax.rsqrt(squares / D + 1e-06)[:, None]
        * attn_gain.astype(jnp.float32)[None, :]
    )
    mixed_state = (hidden.astype(jnp.float32) + normed).astype(jnp.bfloat16)
    gate = lax.psum(jnp.dot(mixed_state, ple_gate_weight, preferred_element_type=jnp.float32), "tp")
    activated = (jax.nn.gelu(gate, approximate=True) * ple_input.astype(jnp.float32)).astype(
        jnp.bfloat16
    )
    lifted = jnp.dot(activated, ple_proj_weight, preferred_element_type=jnp.float32)
    lift_squares = lax.psum(jnp.sum(lifted * lifted, axis=1), "tp")
    lift_normed = (
        lifted
        * lax.rsqrt(lift_squares / D + 1e-06)[:, None]
        * ple_gain.astype(jnp.float32)[None, :]
    )
    return (mixed_state.astype(jnp.float32) + lift_normed).astype(jnp.bfloat16)


def solution(mesh):
    return jax.shard_map(
        shards,
        mesh=mesh,
        in_specs=(
            P("req", "tp"),
            P("req", "tp"),
            P("req", None),
            P("req", None),
            P("req", None, None),
            P("req", None, None),
            P("tp", None),
            P("tp"),
            P("req", None),
            P("tp", None),
            P(None, "tp"),
            P("tp"),
            P("req", None),
            P("req", None),
            P("req", None),
            P("req", None),
            P("req", None),
        ),
        out_specs=P("req", "tp"),
        check_vma=False,
    )
```

profile of v0, /device:TPU:1, one launch (start us, length us, event | category | flops | bytes accessed | tf_op | source)
XLA Modules:
  0.0 292.8 jit_solution(17418125813564555138)
XLA Ops:
  6.5 0.0 copy-start
  6.5 1.0 convert_reduce_fusion.1
  7.5 0.7 iota_compare_fusion.5
  8.2 0.7 add_bitcast_fusion.2
  8.9 0.2 select_reduce_fusion.2
  9.1 0.7 copy.35
  9.7 6.4 %all-to-all-start = ((s32[8,1,6]{2,1,0:T(1,128)}), s32[8,1,6]{2,1,0:T(1,128)S(1)}, u32[]{:S(2)}, u32[]{:S(2)}) async-start(s32[8,1,6]{2,1,0:T(1,128)} %copy.35), calls=%async_computation | async-start | bytes 8192 | tf_op jit(solution)/shard_map/all_to_all | solution.py:74
  16.1 2.2 constant_dynamic-slice_fusion.2
  18.4 2.0 pad_maximum_fusion
  20.3 1.0 all-to-all-done
  21.4 0.1 reshape.180
  21.5 4.4 %gather_fusion = bf16[48,64,512]{2,1,0:T(8,128)(2,1)} fusion(bf16[48,64,512]{2,1,0:T(8,128)(2,1)} %pad_maximum_fusion, s32[1024]{0:T(1024)S(1)} %pad_clamp_fusion.1), kind=kCustom, calls=%fused_computation | custom fusion | bytes 6291648 | tf_op jit(solution)/shard_map/gather | solution.py:80
  25.9 0.0 copy-start.8
  25.9 0.0 copy-start.10
  25.9 0.0 copy-start.4
  25.9 0.0 copy-start.9
  25.9 0.0 copy-start.7
  25.9 4.6 %all-to-all-start.1 = ((bf16[8,6,64,512]{3,2,1,0:T(8,128)(2,1)}), bf16[8,6,64,512]{3,2,1,0:T(8,128)(2,1)}, u32[]{:S(2)}, u32[]{:S(2)}) async-start(bf16[8,6,64,512]{3,2,1,0:T(8,128)(2,1)} %bitcast.52), calls=%async_computation.1 | async-start | bytes 6291456 | tf_op jit(solution)/shard_map/all_to_all | solution.py:81
  30.5 0.0 all-reduce.3.cloned.1.call-start
  30.6 0.0 copy-done.8
  30.6 0.2 reduce-window_1_clone.1
  30.8 0.0 copy-done.10
  30.8 0.2 reduce-window_clone.1
  31.0 0.0 copy-done.4
  31.0 1.0 constant_dynamic-slice_fusion
  31.9 0.1 copy.44
  32.1 0.0 copy-done.9
  32.2 0.1 convert_reduce_fusion.2
  32.2 0.0 copy-done.7
  32.3 0.1 convert_reduce_fusion
  32.4 0.1 select_reduce_fusion.1
  32.5 0.2 fusion.12
  32.7 2.4 compare_and_fusion
  35.1 1.7 pad_add_fusion
  36.8 62.6 %all-to-all-done.1 = bf16[8,6,64,512]{3,2,1,0:T(8,128)(2,1)} async-done(((bf16[8,6,64,512]{3,2,1,0:T(8,128)(2,1)}), bf16[8,6,64,512]{3,2,1,0:T(8,128)(2,1)}, u32[]{:S(2)}, u32[]{:S(2)}) %all-to-all-start.1) | async-done | bytes 3145760 | tf_op jit(solution)/shard_map/all_to_all | solution.py:81
  99.4 4.4 %gather_fusion.1 = bf16[48,64,512]{2,1,0:T(8,128)(2,1)} fusion(bf16[48,64,512]{2,1,0:T(8,128)(2,1)} %bitcast.4, s32[1024]{0:T(1024)S(1)} %pad_clamp_fusion), kind=kCustom, calls=%fused_computation.1 | custom fusion | bytes 6291648 | tf_op jit(solution)/shard_map/gather | solution.py:82
  103.8 4.0 %fusion.49 = (bf16[48,64,256]{2,1,0:T(8,128)(2,1)}, bf16[48,64,256]{2,1,0:T(8,128)(2,1)}) fusion(bf16[48,64,512]{2,1,0:T(8,128)(2,1)} %gather_fusion.1), kind=kLoop, calls=%fused_computation.97 | loop fusion | bytes 6291456 | tf_op jit(solution)/shard_map/slice | solution.py:84
  107.8 0.0 copy-start.1
  107.8 2.7 copy.37
  110.4 0.0 copy-done.1
  110.4 8.7 %fusion.8 = f32[3584,512,2]{1,0,2:T(8,128)} fusion(bf16[512,256]{1,0:T(8,128)(2,1)S(1)} %get-tuple-element.15, bf16[3072,256]{1,0:T(8,128)(2,1)} %bitcast.53, bf16[64,2,8,256]{3,2,1,0:T(8,128)(2,1)S(1)} %bitcast.55), kind=kOutput, calls=%fused_computation.19 | convolution fusion | flops 1882718208 | bytes 17039360 | tf_op jit(solution)/shard_map/rhd,kd->hrk/dot_general | solution.py:93
  119.2 17.1 %fusion.50 = (f32[2,512]{1,0:T(2,128)S(1)}, f32[2,512,3584]{1,2,0:T(8,128)}) fusion(f32[3584,512,2]{1,0,2:T(8,128)} %fusion.8, pred[512,3584]{0,1:T(8,128)(4,1)} %pad_add_fusion), kind=kOutput, calls=%fused_computation.98 | output fusion | flops 22023680 | bytes 31199232 | tf_op jit(solution)/shard_map/sub | solution.py:98
  136.3 7.7 %fusion.11 = bf16[256,2,512]{2,0,1:T(8,128)(2,1)S(1)} fusion(f32[2,512,3584]{1,2,0:T(8,128)} %get-tuple-element.12, f32[2,512]{1,0:T(2,128)S(1)} %get-tuple-element.11, bf16[512,256]{0,1:T(8,128)(2,1)S(1)} %copy.44, bf16[3072,256]{0,1:T(8,128)(2,1)} %copy.37), kind=kOutput, calls=%fused_computation.22 | convolution fusion | flops 1890320384 | bytes 17043456 | tf_op jit(solution)/shard_map/hrk,kd->rhd/dot_general | solution.py:100
  144.0 0.0 copy-done
  144.0 3.2 %fusion.51 = f32[512,2048]{1,0:T(8,128)} fusion(bf16[512,512]{0,1:T(8,128)(2,1)S(1)} %bitcast.56, bf16[512,2048]{1,0:T(8,128)(2,1)S(1)} %copy-done), kind=kOutput, calls=%fused_computation.99 | convolution fusion | flops 1073741824 | bytes 6815744 | tf_op jit(solution)/shard_map/dot_general | solution.py:102
  147.3 0.0 copy-start.5
  147.3 0.0 all-reduce.3.cloned.1.call-update
  147.3 0.0 copy-start.2
  147.3 0.0 all-reduce.5.cloned.1.call-start
  147.3 0.6 copy-done.5
  147.9 0.0 copy-start.3
  147.9 86.1 %all-reduce.3.cloned.1.call-done = f32[512,2048]{1,0:T(8,128)} async-done(((f32[512,2048]{1,0:T(8,128)}), f32[512,2048]{1,0:T(8,128)}) %all-reduce.3.cloned.1.call-update) | async-done | bytes 4194320 | tf_op jit(solution)/shard_map/psum | solution.py:104
  234.0 2.5 multiply_reduce_fusion
  236.6 0.0 copy-done.2
  236.6 1.5 add_convert_fusion.1
  238.1 0.0 copy-done.3
  238.1 1.1 fusion.52
  239.2 0.0 all-reduce.5.cloned.1.call-update
  239.2 0.0 copy-done.6
  239.2 32.1 %all-reduce.5.cloned.1.call-done = f32[512,256]{1,0:T(8,128)} async-done(((f32[512,256]{1,0:T(8,128)}), f32[512,256]{1,0:T(8,128)}) %all-reduce.5.cloned.1.call-update) | async-done | bytes 524304 | tf_op jit(solution)/shard_map/psum | solution.py:113
  271.3 2.7 multiply_reduce_fusion.1
  274.0 2.6 copy.40
  276.6 7.1 %psum.23 = f32[512]{0:T(512)S(1)} all-reduce(f32[512]{0:T(512)S(1)} %get-tuple-element.13), channel_id=1, replica_groups=mesh['req'=8,'tp'=4] {'tp'}, use_global_device_ids=true, to_apply=%region_14.15 | all-reduce | flops 512 | bytes 4096 | tf_op jit(solution)/shard_map/psum | solution.py:118
  283.8 2.2 add_convert_fusion
  (17 shorter events, 0.1 us)
Async XLA Ops:
  6.5 137.5 %copy-start = (bf16[512,2048]{1,0:T(8,128)(2,1)S(1)}, bf16[512,2048]{1,0:T(8,128)(2,1)}, u32[]{:S(2)}) copy-start(bf16[512,2048]{1,0:T(8,128)(2,1)} %param.23) | copy-start | bytes 6291460
  9.7 11.6 %all-to-all-start = ((s32[8,1,6]{2,1,0:T(1,128)}), s32[8,1,6]{2,1,0:T(1,128)S(1)}, u32[]{:S(2)}, u32[]{:S(2)}) async-start(s32[8,1,6]{2,1,0:T(1,128)} %copy.35), calls=%async_computation | async-start | bytes 8192 | tf_op jit(solution)/shard_map/all_to_all | solution.py:74
  25.9 4.7 %copy-start.8 = (s32[1,8]{1,0:T(1,128)S(1)}, s32[1,8]{1,0:T(1,128)}, u32[]{:S(2)}) copy-start(s32[1,8]{1,0:T(1,128)} %param.31) | copy-start | bytes 100
  25.9 4.9 %copy-start.10 = (s32[1,8]{1,0:T(1,128)S(1)}, s32[1,8]{1,0:T(1,128)}, u32[]{:S(2)}) copy-start(s32[1,8]{1,0:T(1,128)} %param.33) | copy-start | bytes 100
  25.9 5.0 %copy-start.4 = (bf16[512,512]{1,0:T(8,128)(2,1)S(1)}, bf16[512,512]{1,0:T(8,128)(2,1)}, u32[]{:S(2)}) copy-start(bf16[512,512]{1,0:T(8,128)(2,1)} %param.19) | copy-start | bytes 1572868
  25.9 6.2 %copy-start.9 = (s32[48,1]{0,1:T(1,128)S(1)}, s32[48,1]{0,1:T(1,128)}, u32[]{:S(2)}) copy-start(s32[48,1]{0,1:T(1,128)} %param.29) | copy-start | bytes 580
  25.9 6.3 %copy-start.7 = (s32[1,8]{1,0:T(1,128)S(1)}, s32[1,8]{1,0:T(1,128)}, u32[]{:S(2)}) copy-start(s32[1,8]{1,0:T(1,128)} %param.32) | copy-start | bytes 100
  25.9 73.4 %all-to-all-start.1 = ((bf16[8,6,64,512]{3,2,1,0:T(8,128)(2,1)}), bf16[8,6,64,512]{3,2,1,0:T(8,128)(2,1)}, u32[]{:S(2)}, u32[]{:S(2)}) async-start(bf16[8,6,64,512]{3,2,1,0:T(8,128)(2,1)} %bitcast.52), calls=%async_computation.1 | async-start | bytes 6291456 | tf_op jit(solution)/shard_map/all_to_all | solution.py:81
  30.5 203.5 %all-reduce.3.cloned.1.call-start = ((), (), s32[]{:S(2)}) async-start(), calls=%async_computation.2 | async-start | bytes 8388608 | tf_op jit(solution)/shard_map/psum | solution.py:104
  107.8 2.7 copy-start.1
  147.3 0.7 copy-start.5
  147.3 89.3 %copy-start.2 = (bf16[512,512]{1,0:T(8,128)(2,1)S(1)}, bf16[512,512]{1,0:T(8,128)(2,1)}, u32[]{:S(2)}) copy-start(bf16[512,512]{1,0:T(8,128)(2,1)} %param.17) | copy-start | bytes 1572868
  147.3 124.0 %all-reduce.5.cloned.1.call-start = ((), (), s32[]{:S(2)}) async-start(), calls=%async_computation.3 | async-start | bytes 1048576 | tf_op jit(solution)/shard_map/psum | solution.py:113
  147.9 90.1 %copy-start.3 = (bf16[512,256]{1,0:T(8,128)(2,1)S(1)}, bf16[512,256]{1,0:T(8,128)(2,1)}, u32[]{:S(2)}) copy-start(bf16[512,256]{1,0:T(8,128)(2,1)} %param.26) | copy-start | bytes 786436
  147.9 91.2 %copy-start.6 = (bf16[512]{0:T(512)(128)(2,1)S(1)}, bf16[512]{0:T(512)(128)(2,1)}, u32[]{:S(2)}) copy-start(bf16[512]{0:T(512)(128)(2,1)} %param.28) | copy-start | bytes 3076
Sparse Core Ops, SparseCore 0:
  147.4 86.5 all-reduce.2
  239.3 31.9 all-reduce.4
where the time goes:
time: 294 us; the launch traced here: 293 us
  waiting for transfers between devices  182 us (62%)
  other arithmetic  32.8 us (11%)
  matrix products  23.5 us (8%)
  local copies, waits for them, and re-layouts  22.9 us (8%)
  between operations  13.6 us (5%)
  starting transfers between devices  11 us (4%)
  blocking collectives  7.15 us (2%)
    psum x1, waiting for transfers between devices, shards(): summed = lax.psum(partial_sum, 'tp')  86.1 us
    all_to_all x1, waiting for transfers between devices, shards(): lax.all_to_all(outgoing, 'req', split_axis=0, concat_axis=0, tiled=True)  62.6 us
    psum x1, waiting for transfers between devices, shards(): lax.psum(jnp.dot(mixed_state, ple_gate_weight, preferred_element_type=jnp...  32.1 us
    sub x1, other arithmetic, shards(): expo = jnp.exp(scores - highest)  17.1 us
    dot_general x1, matrix products, shards(): jnp.einsum('rhd,kd->hrk', query_rows, all_keys, preferred_element_type=jn...  8.73 us
    dot_general x1, matrix products, shards(): jnp.einsum('hrk,kd->rhd', weights, all_values, preferred_element_type=jnp...  7.72 us
    psum x1, blocking collectives, shards(): lift_squares = lax.psum(jnp.sum(lifted * lifted, axis=1), 'tp')  7.15 us
    all_to_all x1, starting transfers between devices, shards(): lax.all_to_all(request_table, 'req', split_axis=0, concat_axis=0, tiled=T...  6.38 us
  transfers between devices with their start and end apart: 4, of which 4 were waited for; matrix products, arithmetic and copies ran while one was open for 4% of the time, Pallas kernels for 0%

commit v1 on v0

--- a/solution.py
+++ b/solution.py
@@ -99,29 +99,37 @@
     weights = (expo / jnp.sum(expo, axis=-1, keepdims=True)).astype(jnp.bfloat16)
     attention = jnp.einsum("hrk,kd->rhd", weights, all_values, preferred_element_type=jnp.float32)
     attention = attention.astype(jnp.bfloat16).reshape(row_total, local_heads * HD)
-    partial_sum = jnp.dot(attention, out_weight, preferred_element_type=jnp.float32)
-    columns = hidden.shape[1]
-    summed = lax.psum(partial_sum, "tp")
-    squares = jnp.sum(summed * summed, axis=1)
-    local_part = lax.dynamic_slice_in_dim(summed, tp_index * columns, columns, 1)
+    tp_size = lax.axis_size("tp")
+    full_weight = lax.all_gather(out_weight, "tp", axis=0, tiled=True)
+    full_gate_weight = lax.all_gather(ple_gate_weight, "tp", axis=0, tiled=True)
+    full_proj_weight = lax.all_gather(ple_proj_weight, "tp", axis=1, tiled=True)
+    full_attn_gain = lax.all_gather(attn_gain, "tp", axis=0, tiled=True)
+    full_ple_gain = lax.all_gather(ple_gain, "tp", axis=0, tiled=True)
+    row_hidden = lax.all_to_all(hidden, "tp", split_axis=0, concat_axis=1, tiled=True)
+    row_attention = lax.all_to_all(attention, "tp", split_axis=0, concat_axis=1, tiled=True)
+    part_rows = row_attention.shape[0]
+    row_ple = lax.dynamic_slice_in_dim(ple_input, tp_index * part_rows, part_rows, 0)
+    projected = jnp.dot(row_attention, full_weight, preferred_element_type=jnp.float32)
+    squares = jnp.sum(projected * projected, axis=1)
     normed = (
-        local_part
+        projected
         * lax.rsqrt(squares / D + 1e-06)[:, None]
-        * attn_gain.astype(jnp.float32)[None, :]
+        * full_attn_gain.astype(jnp.float32)[None, :]
     )
-    mixed_state = (hidden.astype(jnp.float32) + normed).astype(jnp.bfloat16)
-    gate = lax.psum(jnp.dot(mixed_state, ple_gate_weight, preferred_element_type=jnp.float32), "tp")
-    activated = (jax.nn.gelu(gate, approximate=True) * ple_input.astype(jnp.float32)).astype(
+    mixed_state = (row_hidden.astype(jnp.float32) + normed).astype(jnp.bfloat16)
+    gate = jnp.dot(mixed_state, full_gate_weight, preferred_element_type=jnp.float32)
+    activated = (jax.nn.gelu(gate, approximate=True) * row_ple.astype(jnp.float32)).astype(
         jnp.bfloat16
     )
-    lifted = jnp.dot(activated, ple_proj_weight, preferred_element_type=jnp.float32)
-    lift_squares = lax.psum(jnp.sum(lifted * lifted, axis=1), "tp")
+    lifted = jnp.dot(activated, full_proj_weight, preferred_element_type=jnp.float32)
+    lift_squares = jnp.sum(lifted * lifted, axis=1)
     lift_normed = (
         lifted
         * lax.rsqrt(lift_squares / D + 1e-06)[:, None]
-        * ple_gain.astype(jnp.float32)[None, :]
+        * full_ple_gain.astype(jnp.float32)[None, :]
     )
-    return (mixed_state.astype(jnp.float32) + lift_normed).astype(jnp.bfloat16)
+    row_out = (mixed_state.astype(jnp.float32) + lift_normed).astype(jnp.bfloat16)
+    return lax.all_to_all(row_out, "tp", split_axis=1, concat_axis=0, tiled=True)
 
 
 def solution(mesh):

time: 294 us -> 190 us (0.65)
  waiting for transfers between devices: 182 us -> 64.7 us
  blocking collectives: 7.15 us -> 24.4 us
  starting transfers between devices: 11 us -> 21 us
  other arithmetic: 32.8 us -> 25.3 us
  local copies, waits for them, and re-layouts: 22.9 us -> 16.9 us
    psum x2 -> x0, waiting for transfers between devices: 118 us -> none  [the longest x1 86.1 us: shards(): summed = lax.psum(partial_sum, 'tp')]
    all_gather x0 -> x2, blocking collectives: none -> 14 us  [the longest x1 8.84 us: shards(): full_attn_gain = lax.all_gather(attn_gain, 'tp', axis=0, tiled=True)]
    all_to_all x0 -> x2, starting transfers between devices: none -> 10.8 us  [the longest x1 7.08 us: shards(): lax.all_to_all(hidden, 'tp', split_axis=0, concat_axis=1, tiled=True)]
    all_to_all x0 -> x1, blocking collectives: none -> 10.4 us  [shards(): lax.all_to_all(row_out, 'tp', split_axis=1, concat_axis=0, tiled=True)]
    psum x1 -> x0, blocking collectives: 7.15 us -> none  [shards(): lift_squares = lax.psum(jnp.sum(lifted * lifted, axis=1), 'tp')]
    convert_element_type x4, other arithmetic: 3.7 us -> 0.48 us  [the longest x1 0.23 us: shards(): mixed_state = (row_hidden.astype(jnp.float32) + normed).astype(jnp.bfloat16)]
    dot_general x3 -> x2, matrix products: 7 us -> 7.23 us  [the longest x1 4.76 us: shards(): jnp.dot(row_attention, full_weight, preferred_element_type=jnp.float32)]
  transfers between devices with their start and end apart: 4 -> 7, of which waited for: 4 -> 2; matrix products, arithmetic and copies ran while one was open for 4% -> 33% of each run, Pallas kernels for 0% -> 0%
where the time goes in v1:
time: 190 us; the launch traced here: 189 us
  waiting for transfers between devices  64.7 us (34%)
  other arithmetic  25.3 us (13%)
  blocking collectives  24.4 us (13%)
  matrix products  23.1 us (12%)
  starting transfers between devices  21 us (11%)
  local copies, waits for them, and re-layouts  16.9 us (9%)
  between operations  13.4 us (7%)
    all_to_all x1, waiting for transfers between devices, shards(): lax.all_to_all(outgoing, 'req', split_axis=0, concat_axis=0, tiled=True)  60.2 us
    sub x1, other arithmetic, shards(): expo = jnp.exp(scores - highest)  16 us
    all_to_all x1, blocking collectives, shards(): lax.all_to_all(row_out, 'tp', split_axis=1, concat_axis=0, tiled=True)  10.4 us
    all_gather x1, blocking collectives, shards(): full_attn_gain = lax.all_gather(attn_gain, 'tp', axis=0, tiled=True)  8.84 us
    dot_general x1, matrix products, shards(): jnp.einsum('rhd,kd->hrk', query_rows, all_keys, preferred_element_type=jn...  8.56 us
    dot_general x1, matrix products, shards(): jnp.einsum('hrk,kd->rhd', weights, all_values, preferred_element_type=jnp...  7.33 us
    all_to_all x1, starting transfers between devices, shards(): lax.all_to_all(hidden, 'tp', split_axis=0, concat_axis=1, tiled=True)  7.08 us
    all_to_all x1, starting transfers between devices, shards(): lax.all_to_all(request_table, 'req', split_axis=0, concat_axis=0, tiled=T...  6.38 us
  transfers between devices with their start and end apart: 7, of which 2 were waited for; matrix products, arithmetic and copies ran while one was open for 33% of the time, Pallas kernels for 0%

profile of v1, /device:TPU:1, one launch (start us, length us, event | category | flops | bytes accessed | tf_op | source)
XLA Modules:
  0.0 188.8 jit_solution(16006355638064620231)
XLA Ops:
  6.5 0.0 all-gather.6.cloned.1.call-start
  6.5 0.7 all-gather.6.cloned.1.call-update
  7.3 0.9 convert_reduce_fusion.1
  8.2 0.7 add_bitcast_fusion.2
  8.8 0.7 iota_compare_fusion.5
  9.5 0.2 select_reduce_fusion.2
  9.7 0.7 copy.41
  10.4 6.4 %all-to-all-start.1 = ((s32[8,1,6]{2,1,0:T(1,128)}), s32[8,1,6]{2,1,0:T(1,128)S(1)}, u32[]{:S(2)}, u32[]{:S(2)}) async-start(s32[8,1,6]{2,1,0:T(1,128)} %copy.41), calls=%async_computation.1 | async-start | bytes 8192 | tf_op jit(solution)/shard_map/all_to_all | solution.py:74
  16.8 2.6 %constant_dynamic-slice_fusion.2 = (bf16[48,64,256]{2,1,0:T(8,128)(2,1)S(1)}, bf16[48,64,256]{2,1,0:T(8,128)(2,1)S(1)}) fusion(bf16[48,64,512]{2,1,0:T(8,128)(2,1)} %param.22, s32[]{:T(128)S(6)} %select_n.60, bf16[48,64,512]{2,1,0:T(8,128)(2,1)} %param.21), kind=kLoop, calls=%fused_computation.83 | loop fusion | bytes 6291460 | tf_op jit(solution)/shard_map/dynamic_slice | solution.py:77
  19.4 0.3 pad_maximum_fusion
  19.7 2.3 %all-to-all-done.1 = s32[8,1,6]{2,1,0:T(1,128)S(1)} async-done(((s32[8,1,6]{2,1,0:T(1,128)}), s32[8,1,6]{2,1,0:T(1,128)S(1)}, u32[]{:S(2)}, u32[]{:S(2)}) %all-to-all-start.1) | async-done | bytes 224 | tf_op jit(solution)/shard_map/all_to_all | solution.py:74
  22.0 0.1 reshape.194
  22.1 2.5 %gather_fusion = bf16[48,64,512]{2,1,0:T(8,128)(2,1)} fusion(bf16[48,64,512]{2,1,0:T(8,128)(2,1)S(1)} %pad_maximum_fusion, s32[1024]{0:T(1024)S(1)} %pad_clamp_fusion.1), kind=kCustom, calls=%fused_computation | custom fusion | bytes 6291648 | tf_op jit(solution)/shard_map/gather | solution.py:80
  24.6 3.8 %all-to-all-start.2 = ((bf16[8,6,64,512]{3,2,1,0:T(8,128)(2,1)}), bf16[8,6,64,512]{3,2,1,0:T(8,128)(2,1)S(1)}, u32[]{:S(2)}, u32[]{:S(2)}) async-start(bf16[8,6,64,512]{3,2,1,0:T(8,128)(2,1)} %bitcast.73), calls=%async_computation.2 | async-start | bytes 6291456 | tf_op jit(solution)/shard_map/all_to_all | solution.py:81
  28.4 0.0 all-gather.10.cloned.1.call-start
  28.5 0.7 all-gather.10.cloned.1.call-update
  29.2 0.0 copy-done.5
  29.2 0.2 reduce-window_1_clone.1
  29.4 0.0 copy-done.7
  29.4 0.2 reduce-window_clone.1
  29.6 1.8 constant_dynamic-slice_fusion
  31.3 0.8 copy.51
  32.2 0.0 copy-done.6
  32.2 0.1 convert_reduce_fusion.2
  32.3 0.0 copy-done.4
  32.3 0.1 convert_reduce_fusion
  32.4 0.1 select_reduce_fusion.1
  32.6 0.2 fusion.13
  32.8 2.4 %compare_and_fusion = pred[512,3072]{0,1:T(8,128)(4,1)S(1)} fusion(s32[512]{0:T(512)S(1)} %broadcast_add_fusion.1, s32[3072]{0:T(1024)S(1)} %broadcast_add_fusion, pred[3072]{0:T(1024)(128)(4,1)S(1)} %fusion.40), kind=kLoop, calls=%fused_computation.12 | loop fusion | flops 3145728 | bytes 1590272 | tf_op jit(solution)/shard_map/and | solution.py:33
  35.1 1.7 pad_add_fusion
  36.8 60.2 %all-to-all-done.2 = bf16[8,6,64,512]{3,2,1,0:T(8,128)(2,1)S(1)} async-done(((bf16[8,6,64,512]{3,2,1,0:T(8,128)(2,1)}), bf16[8,6,64,512]{3,2,1,0:T(8,128)(2,1)S(1)}, u32[]{:S(2)}, u32[]{:S(2)}) %all-to-all-start.2) | async-done | bytes 3145760 | tf_op jit(solution)/shard_map/all_to_all | solution.py:81
  97.0 7.1 %all-to-all-start = ((bf16[4,128,512]{2,1,0:T(8,128)(2,1)}), bf16[4,128,512]{2,1,0:T(8,128)(2,1)}, u32[]{:S(2)}, u32[]{:S(2)}) async-start(bf16[4,128,512]{2,1,0:T(8,128)(2,1)} %bitcast.82), calls=%async_computation | async-start | bytes 1048576 | tf_op jit(solution)/shard_map/all_to_all | solution.py:108
  104.1 2.5 %gather_fusion.1 = bf16[48,64,512]{2,1,0:T(8,128)(2,1)} fusion(bf16[48,64,512]{2,1,0:T(8,128)(2,1)S(1)} %bitcast.72, s32[1024]{0:T(1024)S(1)} %pad_clamp_fusion), kind=kCustom, calls=%fused_computation.1 | custom fusion | bytes 6291648 | tf_op jit(solution)/shard_map/gather | solution.py:82
  106.6 2.1 %fusion.52 = (bf16[48,64,256]{2,1,0:T(8,128)(2,1)S(1)}, bf16[48,64,256]{2,1,0:T(8,128)(2,1)S(1)}) fusion(bf16[48,64,512]{2,1,0:T(8,128)(2,1)} %gather_fusion.1), kind=kLoop, calls=%fused_computation.102 | loop fusion | bytes 6291456 | tf_op jit(solution)/shard_map/slice | solution.py:84
  108.7 1.8 copy.43
  110.5 8.6 %fusion.8 = f32[3584,512,2]{1,0,2:T(8,128)} fusion(bf16[512,256]{1,0:T(8,128)(2,1)} %get-tuple-element.17, bf16[3072,256]{1,0:T(8,128)(2,1)S(1)} %bitcast.74, bf16[64,2,8,256]{3,2,1,0:T(8,128)(2,1)} %bitcast.81), kind=kOutput, calls=%fused_computation.18 | convolution fusion | flops 1882718208 | bytes 17039360 | tf_op jit(solution)/shard_map/rhd,kd->hrk/dot_general | solution.py:93
  119.1 0.0 copy-done
  119.1 16.0 %fusion.53 = (f32[2,512]{1,0:T(2,128)S(1)}, f32[2,512,3584]{1,2,0:T(8,128)}) fusion(f32[3584,512,2]{1,0,2:T(8,128)} %fusion.8, pred[512,3584]{0,1:T(8,128)(4,1)S(1)} %copy-done), kind=kOutput, calls=%fused_computation.103 | output fusion | flops 22023680 | bytes 31199232 | tf_op jit(solution)/shard_map/sub | solution.py:98
  135.0 0.0 copy-done.1
  135.0 7.3 %fusion.12 = bf16[512,2,256]{0,2,1:T(8,128)(2,1)S(1)} fusion(f32[2,512,3584]{1,2,0:T(8,128)} %get-tuple-element.12, f32[2,512]{1,0:T(2,128)S(1)} %get-tuple-element.11, bf16[512,256]{0,1:T(8,128)(2,1)} %copy.51, bf16[3072,256]{0,1:T(8,128)(2,1)S(1)} %copy-done.1), kind=kOutput, calls=%fused_computation.22 | convolution fusion | flops 1890320384 | bytes 17043456 | tf_op jit(solution)/shard_map/hrk,kd->rhd/dot_general | solution.py:100
  142.4 0.0 copy-start.2
  142.4 0.0 copy-start.3
  142.4 0.1 all_to_all.49
  142.5 0.9 copy.46
  143.4 0.0 all-to-all-done
  143.4 3.7 %all-to-all-start.3 = ((bf16[4,128,512]{1,2,0:T(8,128)(2,1)}), bf16[4,128,512]{1,2,0:T(8,128)(2,1)S(1)}, u32[]{:S(2)}, u32[]{:S(2)}) async-start(bf16[4,128,512]{1,2,0:T(8,128)(2,1)} %copy.46), calls=%async_computation.3 | async-start | bytes 1048576 | tf_op jit(solution)/shard_map/all_to_all | solution.py:109
  147.1 0.0 all-gather.8.cloned.1.call-start
  147.1 0.7 all-gather.8.cloned.1.call-update
  147.8 0.0 copy-done.2
  147.8 8.8 %all-gather = bf16[4,1,512]{2,1,0:T(2,128)(2,1)S(1)} all-gather(bf16[1,1,512]{2,1,0:T(2,128)(2,1)S(1)} %reshape.210), channel_id=1, replica_groups=mesh['req'=8,'tp'=4] {'tp'}, dimensions={0}, use_global_device_ids=true | all-gather | bytes 5120 | tf_op jit(solution)/shard_map/all_gather | solution.py:106
  156.7 0.0 copy-done.3
  156.7 5.2 %all-gather.1 = bf16[4,1,512]{2,1,0:T(2,128)(2,1)S(1)} all-gather(bf16[1,1,512]{2,1,0:T(2,128)(2,1)S(1)} %reshape.212), channel_id=1, replica_groups=mesh['req'=8,'tp'=4] {'tp'}, dimensions={0}, use_global_device_ids=true | all-gather | bytes 5120 | tf_op jit(solution)/shard_map/all_gather | solution.py:107
  161.9 1.2 convert_bitcast_fusion
  163.1 0.1 copy.54
  163.2 0.0 all-to-all-done.3
  163.2 0.0 all-gather.6.cloned.1.call-done
  163.2 4.8 %multiply_reduce_fusion.1 = (f32[128]{0:T(128)S(1)}, f32[128,2048]{1,0:T(8,128)S(1)}) fusion(bf16[128,2048]{0,1:T(8,128)(2,1)S(1)} %bitcast.77, bf16[2048,2048]{1,0:T(8,128)(2,1)} %all-gather.6.cloned.1.call-done), kind=kOutput, calls=%fused_computation.27 | convolution fusion | flops 1074265984 | bytes 9961984 | tf_op jit(solution)/shard_map/dot_general | solution.py:112
  168.0 0.2 add_convert_fusion.1
  168.2 0.0 all-gather.10.cloned.1.call-done
  168.2 0.0 all-gather.8.cloned.1.call-done
  168.3 2.5 %multiply_reduce_fusion = (f32[128]{0:T(128)S(1)}, f32[128,2048]{1,0:T(8,128)S(1)}) fusion(bf16[256,2048]{1,0:T(8,128)(2,1)} %all-gather.10.cloned.1.call-done, bf16[512,256]{1,0:T(8,128)(2,1)} %param.25, s32[]{:T(128)S(6)} %select_n.68, bf16[128,2048]{1,0:T(8,128)(2,1)S(1)} %add_convert_fusion.1, bf16[2048,256]{1,0:T(8,128)(2,1)} %all-gather.8.cloned.1.call-done), kind=kOutput, calls=%fused_computation.25 | convolution fusion | flops 269320064 | bytes 3736068 | tf_op jit(solution)/shard_map/dot_general | solution.py:124
  170.8 0.2 add_convert_fusion
  171.0 10.4 %all_to_all.62 = bf16[128,4,512]{2,0,1:T(8,128)(2,1)S(1)} all-to-all(bf16[128,4,512]{2,0,1:T(8,128)(2,1)S(1)} %bitcast.79), channel_id=1, replica_groups=mesh['req'=8,'tp'=4] {'tp'}, dimensions={1} | all-to-all | bytes 1048576 | tf_op jit(solution)/shard_map/all_to_all | solution.py:132
  181.5 0.8 copy.62
  (25 shorter events, 0.2 us)
Async XLA Ops:
  6.5 156.7 %all-gather.6.cloned.1.call-start = ((), (), s32[]{:S(2)}) async-start(), calls=%async_computation.5 | async-start | bytes 10485760 | tf_op jit(solution)/shard_map/all_gather | solution.py:103
  10.4 11.6 %all-to-all-start.1 = ((s32[8,1,6]{2,1,0:T(1,128)}), s32[8,1,6]{2,1,0:T(1,128)S(1)}, u32[]{:S(2)}, u32[]{:S(2)}) async-start(s32[8,1,6]{2,1,0:T(1,128)} %copy.41), calls=%async_computation.1 | async-start | bytes 8192 | tf_op jit(solution)/shard_map/all_to_all | solution.py:74
  24.6 4.6 %copy-start.5 = (s32[1,8]{1,0:T(1,128)S(1)}, s32[1,8]{1,0:T(1,128)}, u32[]{:S(2)}) copy-start(s32[1,8]{1,0:T(1,128)} %param.31) | copy-start | bytes 100
  24.6 4.8 %copy-start.7 = (s32[1,8]{1,0:T(1,128)S(1)}, s32[1,8]{1,0:T(1,128)}, u32[]{:S(2)}) copy-start(s32[1,8]{1,0:T(1,128)} %param.33) | copy-start | bytes 100
  24.6 7.5 %copy-start.6 = (s32[48,1]{0,1:T(1,128)S(1)}, s32[48,1]{0,1:T(1,128)}, u32[]{:S(2)}) copy-start(s32[48,1]{0,1:T(1,128)} %param.29) | copy-start | bytes 580
  24.6 7.7 %copy-start.4 = (s32[1,8]{1,0:T(1,128)S(1)}, s32[1,8]{1,0:T(1,128)}, u32[]{:S(2)}) copy-start(s32[1,8]{1,0:T(1,128)} %param.32) | copy-start | bytes 100
  24.6 72.4 %all-to-all-start.2 = ((bf16[8,6,64,512]{3,2,1,0:T(8,128)(2,1)}), bf16[8,6,64,512]{3,2,1,0:T(8,128)(2,1)S(1)}, u32[]{:S(2)}, u32[]{:S(2)}) async-start(bf16[8,6,64,512]{3,2,1,0:T(8,128)(2,1)} %bitcast.73), calls=%async_computation.2 | async-start | bytes 6291456 | tf_op jit(solution)/shard_map/all_to_all | solution.py:81
  28.4 139.8 %all-gather.10.cloned.1.call-start = ((), (), s32[]{:S(2)}) async-start(), calls=%async_computation.7 | async-start | bytes 1310720 | tf_op jit(solution)/shard_map/all_gather | solution.py:105
  97.0 46.4 %all-to-all-start = ((bf16[4,128,512]{2,1,0:T(8,128)(2,1)}), bf16[4,128,512]{2,1,0:T(8,128)(2,1)}, u32[]{:S(2)}, u32[]{:S(2)}) async-start(bf16[4,128,512]{2,1,0:T(8,128)(2,1)} %bitcast.82), calls=%async_computation | async-start | bytes 1048576 | tf_op jit(solution)/shard_map/all_to_all | solution.py:108
  110.5 8.6 %copy-start = (pred[512,3584]{0,1:T(8,128)(4,1)S(1)}, pred[512,3584]{0,1:T(8,128)(4,1)}, u32[]{:S(2)}) copy-start(pred[512,3584]{0,1:T(8,128)(4,1)} %pad_add_fusion) | copy-start | bytes 5505028
  119.1 16.0 %copy-start.1 = (bf16[3072,256]{0,1:T(8,128)(2,1)S(1)}, bf16[3072,256]{0,1:T(8,128)(2,1)}, u32[]{:S(2)}) copy-start(bf16[3072,256]{0,1:T(8,128)(2,1)} %copy.43) | copy-start | bytes 4718596
  142.4 5.4 %copy-start.2 = (bf16[512]{0:T(512)(128)(2,1)S(1)}, bf16[512]{0:T(512)(128)(2,1)}, u32[]{:S(2)}) copy-start(bf16[512]{0:T(512)(128)(2,1)} %param.24) | copy-start | bytes 3076
  142.4 14.3 %copy-start.3 = (bf16[512]{0:T(512)(128)(2,1)S(1)}, bf16[512]{0:T(512)(128)(2,1)}, u32[]{:S(2)}) copy-start(bf16[512]{0:T(512)(128)(2,1)} %param.28) | copy-start | bytes 3076
  143.4 19.8 %all-to-all-start.3 = ((bf16[4,128,512]{1,2,0:T(8,128)(2,1)}), bf16[4,128,512]{1,2,0:T(8,128)(2,1)S(1)}, u32[]{:S(2)}, u32[]{:S(2)}) async-start(bf16[4,128,512]{1,2,0:T(8,128)(2,1)} %copy.46), calls=%async_computation.3 | async-start | bytes 1048576 | tf_op jit(solution)/shard_map/all_to_all | solution.py:109
  147.1 21.2 %all-gather.8.cloned.1.call-start = ((), (), s32[]{:S(2)}) async-start(), calls=%async_computation.6 | async-start | bytes 1310720 | tf_op jit(solution)/shard_map/all_gather | solution.py:104
Sparse Core Ops, SparseCore 0:
  8.9 60.7 all-gather.5
  71.3 16.6 all-gather.9
  149.5 16.0 all-gather.7

commit v2 on v1

--- a/solution.py
+++ b/solution.py
@@ -73,15 +73,23 @@
     request_table = jnp.sum(jnp.where(matched, places[:, None, None] + 1, 0), axis=0) - 1
     asked = lax.all_to_all(request_table, "req", split_axis=0, concat_axis=0, tiled=True)
     wanted = jnp.maximum(asked, 0)
-    head_keys = lax.dynamic_slice_in_dim(cache_keys, kv_head * HD, HD, 2)
-    head_values = lax.dynamic_slice_in_dim(cache_values, kv_head * HD, HD, 2)
-    stacked = jnp.concatenate([head_keys, head_values], axis=2)
+    tp_count = lax.axis_size("tp")
+    half = tp_index % 2
+    partner = [(i, i ^ 1) for i in range(tp_count)]
+    own_cache = jnp.where(half == 0, cache_keys, cache_values)
+    head_cache = lax.dynamic_slice_in_dim(own_cache, kv_head * HD, HD, 2)
     arrival_index = holders * capacity + ranking
-    outgoing = stacked[wanted]
+    outgoing = head_cache[wanted]
     arrived = lax.all_to_all(outgoing, "req", split_axis=0, concat_axis=0, tiled=True)
-    context = arrived.reshape(req_count * capacity, page_len, 2 * HD)[arrival_index]
-    context_keys = context[:, :, :HD].reshape(page_total * page_len, HD)
-    context_values = context[:, :, HD:].reshape(page_total * page_len, HD)
+    swapped = lax.ppermute(arrived, "tp", partner)
+    key_pages = jnp.where(half == 0, arrived, swapped)
+    value_pages = jnp.where(half == 0, swapped, arrived)
+    context_keys = key_pages.reshape(req_count * capacity, page_len, HD)[arrival_index].reshape(
+        page_total * page_len, HD
+    )
+    context_values = value_pages.reshape(req_count * capacity, page_len, HD)[
+        arrival_index
+    ].reshape(page_total * page_len, HD)
     fresh_keys = lax.dynamic_slice_in_dim(new_keys, kv_head * HD, HD, 1)
     fresh_values = lax.dynamic_slice_in_dim(new_values, kv_head * HD, HD, 1)
     all_keys = jnp.concatenate([context_keys, fresh_keys], axis=0)
@@ -103,9 +111,17 @@
     full_weight = lax.all_gather(out_weight, "tp", axis=0, tiled=True)
     full_gate_weight = lax.all_gather(ple_gate_weight, "tp", axis=0, tiled=True)
     full_proj_weight = lax.all_gather(ple_proj_weight, "tp", axis=1, tiled=True)
-    full_attn_gain = lax.all_gather(attn_gain, "tp", axis=0, tiled=True)
-    full_ple_gain = lax.all_gather(ple_gain, "tp", axis=0, tiled=True)
-    row_hidden = lax.all_to_all(hidden, "tp", split_axis=0, concat_axis=1, tiled=True)
+    hidden_parts = hidden.reshape(tp_size, -1, hidden.shape[1])
+    gain_rows = jnp.zeros((8, hidden.shape[1]), hidden.dtype).at[0].set(attn_gain).at[1].set(ple_gain)
+    with_gains = jnp.concatenate(
+        [hidden_parts, jnp.broadcast_to(gain_rows[None], (tp_size, 8, hidden.shape[1]))], axis=1
+    )
+    row_hidden_gains = lax.all_to_all(
+        with_gains.reshape(-1, hidden.shape[1]), "tp", split_axis=0, concat_axis=1, tiled=True
+    )
+    row_hidden = row_hidden_gains[: hidden_parts.shape[1]]
+    full_attn_gain = row_hidden_gains[hidden_parts.shape[1]]
+    full_ple_gain = row_hidden_gains[hidden_parts.shape[1] + 1]
     row_attention = lax.all_to_all(attention, "tp", split_axis=0, concat_axis=1, tiled=True)
     part_rows = row_attention.shape[0]
     row_ple = lax.dynamic_slice_in_dim(ple_input, tp_index * part_rows, part_rows, 0)

time: 190 us -> 155 us (0.82)
  waiting for transfers between devices: 64.7 us -> 43.2 us
  blocking collectives: 24.4 us -> 11 us
  local copies, waits for them, and re-layouts: 16.9 us -> 10.8 us
  other arithmetic: 25.3 us -> 30.3 us
    all_to_all x1, waiting for transfers between devices: 60.2 us -> 32.5 us  [shards(): lax.all_to_all(outgoing, 'req', split_axis=0, concat_axis=0, tiled=True)]
    all_gather x2 -> x0, blocking collectives: 14 us -> none  [the longest x1 8.84 us: shards(): full_attn_gain = lax.all_gather(attn_gain, 'tp', axis=0, tiled=True)]
    all_to_all x1, waiting for transfers between devices: 0.01 us -> 5.93 us  [shards(): lax.all_to_all(attention, 'tp', split_axis=0, concat_axis=1, tiled=True)]
    select_n x1 -> x3, other arithmetic: 0.01 us -> 5.29 us  [the longest x1 2.76 us: shards(): value_pages = jnp.where(half == 0, swapped, arrived)]
    dynamic_slice x1 -> x0, local copies, waits for them, and re-layouts: 2.65 us -> none  [shards(): head_values = lax.dynamic_slice_in_dim(cache_values, kv_head * HD, HD, 2)]
    slice x1 -> x0, local copies, waits for them, and re-layouts: 2.1 us -> none  [shards(): context_values = context[:, :, HD:].reshape(page_total * page_len, HD)]
    gather x2 -> x3, local copies, waits for them, and re-layouts: 5.04 us -> 4.64 us  [the longest x1 2.12 us: shards(): value_pages.reshape(req_count * capacity, page_len, HD)[arrival_index]]
  transfers between devices with their start and end apart: 7 -> 8, of which waited for: 2 -> 3; matrix products, arithmetic and copies ran while one was open for 33% -> 39% of each run, Pallas kernels for 0% -> 0%
where the time goes in v2:
time: 155 us; the launch traced here: 153 us
  waiting for transfers between devices  43.2 us (28%)
  other arithmetic  30.3 us (20%)
  matrix products  23.1 us (15%)
  starting transfers between devices  21.3 us (14%)
  between operations  13.4 us (9%)
  blocking collectives  11 us (7%)
  local copies, waits for them, and re-layouts  10.8 us (7%)
    all_to_all x1, waiting for transfers between devices, shards(): lax.all_to_all(outgoing, 'req', split_axis=0, concat_axis=0, tiled=True)  32.5 us
    sub x1, other arithmetic, shards(): expo = jnp.exp(scores - highest)  16.3 us
    all_to_all x1, blocking collectives, shards(): lax.all_to_all(row_out, 'tp', split_axis=1, concat_axis=0, tiled=True)  11 us
    dot_general x1, matrix products, shards(): jnp.einsum('rhd,kd->hrk', query_rows, all_keys, preferred_element_type=jn...  8.55 us
    dot_general x1, matrix products, shards(): jnp.einsum('hrk,kd->rhd', weights, all_values, preferred_element_type=jnp...  7.33 us
    all_to_all x1, starting transfers between devices, shards(): lax.all_to_all(with_gains.reshape(-1, hidden.shape[1]), 'tp', split_axis=...  7.17 us
    all_to_all x1, starting transfers between devices, shards(): lax.all_to_all(request_table, 'req', split_axis=0, concat_axis=0, tiled=T...  6.38 us
    all_to_all x1, waiting for transfers between devices, shards(): lax.all_to_all(attention, 'tp', split_axis=0, concat_axis=1, tiled=True)  5.93 us
  transfers between devices with their start and end apart: 8, of which 3 were waited for; matrix products, arithmetic and copies ran while one was open for 39% of the time, Pallas kernels for 0%

profile of v2, /device:TPU:1, one launch (start us, length us, event | category | flops | bytes accessed | tf_op | source)
XLA Modules:
  0.0 153.2 jit_solution(3531479990960998969)
XLA Ops:
  6.5 0.0 all-gather.4.cloned.1.call-start
  6.5 0.7 all-gather.4.cloned.1.call-update
  7.3 0.0 all-gather.6.cloned.1.call-start
  7.3 0.7 all-gather.6.cloned.1.call-update
  8.0 0.0 copy-done.11
  8.0 0.2 convert_reduce_fusion.1
  8.2 0.0 copy-done.9
  8.2 0.2 select_reduce_fusion.2
  8.4 0.7 copy.40
  9.1 6.4 %all-to-all-start.1 = ((s32[8,1,6]{2,1,0:T(1,128)}), s32[8,1,6]{2,1,0:T(1,128)S(1)}, u32[]{:S(2)}, u32[]{:S(2)}) async-start(s32[8,1,6]{2,1,0:T(1,128)} %copy.40), calls=%async_computation.1 | async-start | bytes 8192 | tf_op jit(solution)/shard_map/all_to_all | solution.py:74
  15.5 2.5 %dynamic-slice_select_fusion = bf16[48,64,256]{2,1,0:T(8,128)(2,1)S(1)} fusion(bf16[48,64,512]{2,1,0:T(8,128)(2,1)} %param.26, s32[]{:T(128)S(6)} %select_n.90, bf16[48,64,512]{2,1,0:T(8,128)(2,1)} %param.25, pred[]{:T(512)S(6)} %eq.52), kind=kLoop, calls=%fused_computation.21 | loop fusion | flops 786432 | bytes 4718597 | tf_op jit(solution)/shard_map/jit(_where)/select_n | solution.py:79
  18.0 2.7 %all-to-all-done.1 = s32[8,1,6]{2,1,0:T(1,128)S(1)} async-done(((s32[8,1,6]{2,1,0:T(1,128)}), s32[8,1,6]{2,1,0:T(1,128)S(1)}, u32[]{:S(2)}, u32[]{:S(2)}) %all-to-all-start.1) | async-done | bytes 224 | tf_op jit(solution)/shard_map/all_to_all | solution.py:74
  20.8 0.1 reshape.280
  20.8 1.9 %gather_fusion = bf16[48,64,256]{2,1,0:T(8,128)(2,1)} fusion(bf16[48,64,256]{2,1,0:T(8,128)(2,1)S(1)} %dynamic-slice_select_fusion, s32[1024]{0:T(1024)S(1)} %pad_clamp_fusion.1), kind=kCustom, calls=%fused_computation | custom fusion | bytes 3145920 | tf_op jit(solution)/shard_map/gather | solution.py:82
  22.7 0.0 copy-start.7
  22.7 0.0 copy-start.2
  22.7 3.7 %all-to-all-start.2 = ((bf16[8,6,64,256]{3,2,1,0:T(8,128)(2,1)}), bf16[8,6,64,256]{3,2,1,0:T(8,128)(2,1)S(1)}, u32[]{:S(2)}, u32[]{:S(2)}) async-start(bf16[8,6,64,256]{3,2,1,0:T(8,128)(2,1)} %bitcast.5), calls=%async_computation.2 | async-start | bytes 3145728 | tf_op jit(solution)/shard_map/all_to_all | solution.py:83
  26.5 0.0 copy-start.3
  26.5 0.0 copy-start.4
  26.5 0.0 all-gather.8.cloned.1.call-start
  26.6 0.7 all-gather.8.cloned.1.call-update
  27.2 0.0 copy-done.8
  27.3 0.2 reduce-window_1_clone.1
  27.4 0.0 copy-done.10
  27.4 0.2 reduce-window_clone.1
  27.6 0.0 copy-done.5
  27.7 0.1 convert_reduce_fusion.2
  27.8 0.1 convert_reduce_fusion
  27.9 0.1 select_reduce_fusion.1
  28.1 0.0 copy-done.2
  28.1 0.9 pad_maximum_fusion
  29.0 32.5 %all-to-all-done.2 = bf16[8,6,64,256]{3,2,1,0:T(8,128)(2,1)S(1)} async-done(((bf16[8,6,64,256]{3,2,1,0:T(8,128)(2,1)}), bf16[8,6,64,256]{3,2,1,0:T(8,128)(2,1)S(1)}, u32[]{:S(2)}, u32[]{:S(2)}) %all-to-all-start.2) | async-done | bytes 1572896 | tf_op jit(solution)/shard_map/all_to_all | solution.py:83
  61.5 7.2 %all-to-all-start = ((bf16[4,136,512]{2,1,0:T(8,128)(2,1)}), bf16[4,136,512]{2,1,0:T(8,128)(2,1)}, u32[]{:S(2)}, u32[]{:S(2)}) async-start(bf16[4,136,512]{2,1,0:T(8,128)(2,1)} %pad_maximum_fusion), calls=%async_computation | async-start | bytes 1114112 | tf_op jit(solution)/shard_map/all_to_all | solution.py:119
  68.6 0.1 collective-permute-start
  68.8 0.0 copy-done.4
  68.8 0.7 constant_dynamic-slice_fusion
  69.5 0.8 copy.50
  70.3 0.2 fusion.13
  70.5 2.4 %compare_and_fusion = pred[512,3072]{0,1:T(8,128)(4,1)S(1)} fusion(s32[512]{0:T(512)S(1)} %broadcast_add_fusion.1, s32[3072]{0:T(1024)S(1)} %broadcast_add_fusion, pred[3072]{0:T(1024)(128)(4,1)S(1)} %fusion.40), kind=kLoop, calls=%fused_computation.13 | loop fusion | flops 3145728 | bytes 1590272 | tf_op jit(solution)/shard_map/and | solution.py:33
  72.9 1.7 %pad_add_fusion = pred[512,3584]{0,1:T(8,128)(4,1)} fusion(pred[512,512]{0,1:T(8,128)(4,1)S(1)} %fusion.13, pred[512,3072]{0,1:T(8,128)(4,1)S(1)} %compare_and_fusion), kind=kLoop, calls=%fused_computation.10 | loop fusion | flops 1835008 | bytes 3670016 | tf_op jit(solution)/shard_map/concatenate | solution.py:35
  74.6 0.0 collective-permute-done
  74.6 2.8 %broadcast_select_fusion.1 = (bf16[8,6,64,256]{3,2,1,0:T(8,128)(2,1)}, bf16[8,6,64,256]{3,2,1,0:T(8,128)(2,1)S(1)}) fusion(bf16[8,6,64,256]{3,2,1,0:T(8,128)(2,1)} %collective-permute-done, bf16[8,6,64,256]{3,2,1,0:T(8,128)(2,1)S(1)} %all-to-all-done.2, pred[]{:T(512)S(6)} %eq.52), kind=kLoop, calls=%fused_computation.23 | loop fusion | flops 1572864 | bytes 6291457 | tf_op jit(solution)/shard_map/jit(_where)/select_n | solution.py:86
  77.3 0.7 gather_fusion.2
  78.0 2.1 %gather_fusion.1 = bf16[48,64,256]{2,1,0:T(8,128)(2,1)S(1)} fusion(bf16[48,64,256]{2,1,0:T(8,128)(2,1)} %bitcast.75, s32[1024]{0:T(1024)S(1)} %pad_clamp_fusion), kind=kCustom, calls=%fused_computation.1 | custom fusion | bytes 3145920 | tf_op jit(solution)/shard_map/gather | solution.py:90
  80.1 1.8 %copy.42 = bf16[3072,256]{0,1:T(8,128)(2,1)} copy(bf16[3072,256]{1,0:T(8,128)(2,1)S(1)} %bitcast.74) | data formatting | bytes 3145728 | tf_op jit(solution)/shard_map/reshape | solution.py:92
  81.9 8.6 %fusion.8 = f32[3584,512,2]{1,0,2:T(8,128)} fusion(bf16[512,256]{1,0:T(8,128)(2,1)} %get-tuple-element.43, bf16[3072,256]{1,0:T(8,128)(2,1)S(1)} %bitcast.73, bf16[64,2,8,256]{3,2,1,0:T(8,128)(2,1)} %bitcast.82), kind=kOutput, calls=%fused_computation.18 | convolution fusion | flops 1882718208 | bytes 17039360 | tf_op jit(solution)/shard_map/rhd,kd->hrk/dot_general | solution.py:101
  90.5 16.3 %fusion.52 = (f32[2,512]{1,0:T(2,128)S(1)}, f32[2,512,3584]{1,2,0:T(8,128)}) fusion(f32[3584,512,2]{1,0,2:T(8,128)} %fusion.8, pred[512,3584]{0,1:T(8,128)(4,1)S(1)} %copy-done), kind=kOutput, calls=%fused_computation.106 | output fusion | flops 22023680 | bytes 31199232 | tf_op jit(solution)/shard_map/sub | solution.py:106
  106.8 7.3 %fusion.12 = bf16[512,2,256]{0,2,1:T(8,128)(2,1)S(1)} fusion(f32[2,512,3584]{1,2,0:T(8,128)} %get-tuple-element.38, f32[2,512]{1,0:T(2,128)S(1)} %get-tuple-element.37, bf16[512,256]{0,1:T(8,128)(2,1)} %copy.50, bf16[3072,256]{0,1:T(8,128)(2,1)S(1)} %copy-done.1), kind=kOutput, calls=%fused_computation.25 | convolution fusion | flops 1890320384 | bytes 17043456 | tf_op jit(solution)/shard_map/hrk,kd->rhd/dot_general | solution.py:108
  114.1 0.1 all_to_all.49
  114.3 0.9 copy.45
  115.1 0.0 all-to-all-done
  115.1 3.8 %all-to-all-start.3 = ((bf16[4,128,512]{1,2,0:T(8,128)(2,1)}), bf16[4,128,512]{1,2,0:T(8,128)(2,1)S(1)}, u32[]{:S(2)}, u32[]{:S(2)}) async-start(bf16[4,128,512]{1,2,0:T(8,128)(2,1)} %copy.45), calls=%async_computation.3 | async-start | bytes 1048576 | tf_op jit(solution)/shard_map/all_to_all | solution.py:125
  119.0 1.2 convert_bitcast_fusion
  120.2 0.1 copy.53
  120.3 0.8 slice_convert_fusion
  121.1 5.9 %all-to-all-done.3 = bf16[4,128,512]{1,2,0:T(8,128)(2,1)S(1)} async-done(((bf16[4,128,512]{1,2,0:T(8,128)(2,1)}), bf16[4,128,512]{1,2,0:T(8,128)(2,1)S(1)}, u32[]{:S(2)}, u32[]{:S(2)}) %all-to-all-start.3) | async-done | bytes 524320 | tf_op jit(solution)/shard_map/all_to_all | solution.py:125
  127.0 4.7 %multiply_reduce_fusion.1 = (f32[128]{0:T(128)S(1)}, f32[128,2048]{1,0:T(8,128)S(1)}) fusion(bf16[128,2048]{0,1:T(8,128)(2,1)S(1)} %bitcast.78, bf16[2048,2048]{1,0:T(8,128)(2,1)} %all-gather.4.cloned.1.call-done), kind=kOutput, calls=%fused_computation.30 | convolution fusion | flops 1074265984 | bytes 9961984 | tf_op jit(solution)/shard_map/dot_general | solution.py:128
  131.8 0.2 add_convert_fusion.1
  132.0 0.0 all-gather.6.cloned.1.call-done
  132.1 0.0 all-gather.8.cloned.1.call-done
  132.1 2.5 %multiply_reduce_fusion = (f32[128]{0:T(128)S(1)}, f32[128,2048]{1,0:T(8,128)S(1)}) fusion(bf16[256,2048]{1,0:T(8,128)(2,1)} %all-gather.8.cloned.1.call-done, bf16[512,256]{1,0:T(8,128)(2,1)} %param.29, s32[]{:T(128)S(6)} %select_n.100, bf16[128,2048]{1,0:T(8,128)(2,1)S(1)} %add_convert_fusion.1, bf16[2048,256]{1,0:T(8,128)(2,1)} %all-gather.6.cloned.1.call-done), kind=kOutput, calls=%fused_computation.28 | convolution fusion | flops 269320064 | bytes 3736068 | tf_op jit(solution)/shard_map/dot_general | solution.py:140
  134.6 0.2 add_convert_fusion
  134.8 11.0 %all_to_all.62 = bf16[128,4,512]{2,0,1:T(8,128)(2,1)S(1)} all-to-all(bf16[128,4,512]{2,0,1:T(8,128)(2,1)S(1)} %bitcast.80), channel_id=1, replica_groups=mesh['req'=8,'tp'=4] {'tp'}, dimensions={1} | all-to-all | bytes 1048576 | tf_op jit(solution)/shard_map/all_to_all | solution.py:148
  145.9 0.8 copy.62
  (36 shorter events, 0.2 us)
Async XLA Ops:
  6.5 1.5 copy-start.11
  6.5 1.7 %copy-start.9 = (s32[48,1]{0,1:T(1,128)S(1)}, s32[48,1]{0,1:T(1,128)}, u32[]{:S(2)}) copy-start(s32[48,1]{0,1:T(1,128)} %param.34) | copy-start | bytes 580
  6.5 120.5 %all-gather.4.cloned.1.call-start = ((), (), s32[]{:S(2)}) async-start(), calls=%async_computation.5 | async-start | bytes 10485760 | tf_op jit(solution)/shard_map/all_gather | solution.py:111
  7.3 124.8 %all-gather.6.cloned.1.call-start = ((), (), s32[]{:S(2)}) async-start(), calls=%async_computation.6 | async-start | bytes 1310720 | tf_op jit(solution)/shard_map/all_gather | solution.py:112
  9.1 11.6 %all-to-all-start.1 = ((s32[8,1,6]{2,1,0:T(1,128)}), s32[8,1,6]{2,1,0:T(1,128)S(1)}, u32[]{:S(2)}, u32[]{:S(2)}) async-start(s32[8,1,6]{2,1,0:T(1,128)} %copy.40), calls=%async_computation.1 | async-start | bytes 8192 | tf_op jit(solution)/shard_map/all_to_all | solution.py:74
  22.7 4.5 %copy-start.8 = (s32[1,8]{1,0:T(1,128)S(1)}, s32[1,8]{1,0:T(1,128)}, u32[]{:S(2)}) copy-start(s32[1,8]{1,0:T(1,128)} %param.35) | copy-start | bytes 100
  22.7 4.7 %copy-start.10 = (s32[1,8]{1,0:T(1,128)S(1)}, s32[1,8]{1,0:T(1,128)}, u32[]{:S(2)}) copy-start(s32[1,8]{1,0:T(1,128)} %param.37) | copy-start | bytes 100
  22.7 4.9 %copy-start.5 = (bf16[512]{0:T(512)(128)(2,1)S(1)}, bf16[512]{0:T(512)(128)(2,1)}, u32[]{:S(2)}) copy-start(bf16[512]{0:T(512)(128)(2,1)} %param.28) | copy-start | bytes 3076
  22.7 4.9 %copy-start.6 = (bf16[512]{0:T(512)(128)(2,1)S(1)}, bf16[512]{0:T(512)(128)(2,1)}, u32[]{:S(2)}) copy-start(bf16[512]{0:T(512)(128)(2,1)} %param.32) | copy-start | bytes 3076
  22.7 5.1 %copy-start.7 = (s32[1,8]{1,0:T(1,128)S(1)}, s32[1,8]{1,0:T(1,128)}, u32[]{:S(2)}) copy-start(s32[1,8]{1,0:T(1,128)} %param.36) | copy-start | bytes 100
  22.7 5.3 %copy-start.2 = (bf16[512,512]{1,0:T(8,128)(2,1)S(1)}, bf16[512,512]{1,0:T(8,128)(2,1)}, u32[]{:S(2)}) copy-start(bf16[512,512]{1,0:T(8,128)(2,1)} %param.21) | copy-start | bytes 1572868
  22.7 38.7 %all-to-all-start.2 = ((bf16[8,6,64,256]{3,2,1,0:T(8,128)(2,1)}), bf16[8,6,64,256]{3,2,1,0:T(8,128)(2,1)S(1)}, u32[]{:S(2)}, u32[]{:S(2)}) async-start(bf16[8,6,64,256]{3,2,1,0:T(8,128)(2,1)} %bitcast.5), calls=%async_computation.2 | async-start | bytes 3145728 | tf_op jit(solution)/shard_map/all_to_all | solution.py:83
  26.5 42.3 %copy-start.3 = (bf16[512,512]{1,0:T(8,128)(2,1)S(1)}, bf16[512,512]{1,0:T(8,128)(2,1)}, u32[]{:S(2)}) copy-start(bf16[512,512]{1,0:T(8,128)(2,1)} %param.23) | copy-start | bytes 1572868
  26.5 42.3 %copy-start.4 = (bf16[512,512]{1,0:T(8,128)(2,1)S(1)}, bf16[512,512]{1,0:T(8,128)(2,1)}, u32[]{:S(2)}) copy-start(bf16[512,512]{1,0:T(8,128)(2,1)} %param.24) | copy-start | bytes 1572868
  26.5 105.6 %all-gather.8.cloned.1.call-start = ((), (), s32[]{:S(2)}) async-start(), calls=%async_computation.7 | async-start | bytes 1310720 | tf_op jit(solution)/shard_map/all_gather | solution.py:113
  61.5 53.7 %all-to-all-start = ((bf16[4,136,512]{2,1,0:T(8,128)(2,1)}), bf16[4,136,512]{2,1,0:T(8,128)(2,1)}, u32[]{:S(2)}, u32[]{:S(2)}) async-start(bf16[4,136,512]{2,1,0:T(8,128)(2,1)} %pad_maximum_fusion), calls=%async_computation | async-start | bytes 1114112 | tf_op jit(solution)/shard_map/all_to_all | solution.py:119
  68.6 6.0 %collective-permute-start = (bf16[8,6,64,256]{3,2,1,0:T(8,128)(2,1)S(1)}, bf16[8,6,64,256]{3,2,1,0:T(8,128)(2,1)}, u32[]{:S(2)}, u32[]{:S(2)}) collective-permute-start(bf16[8,6,64,256]{3,2,1,0:T(8,128)(2,1)S(1)} %all-to-all-done.2), channel_id=1, source_target_pairs={{0,1},{1,0},{2,3},{3,2},{4,5},{5,4},{6,7},{7,6},{8,9},{9,8},{10,11... | collective-permute-start | bytes 4718600 | tf_op jit(solution)/shard_map/ppermute | solution.py:84
  81.9 8.6 %copy-start = (pred[512,3584]{0,1:T(8,128)(4,1)S(1)}, pred[512,3584]{0,1:T(8,128)(4,1)}, u32[]{:S(2)}) copy-start(pred[512,3584]{0,1:T(8,128)(4,1)} %pad_add_fusion) | copy-start | bytes 5505028
  90.5 16.3 %copy-start.1 = (bf16[3072,256]{0,1:T(8,128)(2,1)S(1)}, bf16[3072,256]{0,1:T(8,128)(2,1)}, u32[]{:S(2)}) copy-start(bf16[3072,256]{0,1:T(8,128)(2,1)} %copy.42) | copy-start | bytes 4718596
  115.1 11.9 %all-to-all-start.3 = ((bf16[4,128,512]{1,2,0:T(8,128)(2,1)}), bf16[4,128,512]{1,2,0:T(8,128)(2,1)S(1)}, u32[]{:S(2)}, u32[]{:S(2)}) async-start(bf16[4,128,512]{1,2,0:T(8,128)(2,1)} %copy.45), calls=%async_computation.3 | async-start | bytes 1048576 | tf_op jit(solution)/shard_map/all_to_all | solution.py:125
Sparse Core Ops, SparseCore 0:
  8.9 60.9 all-gather.3
  71.5 18.2 all-gather.5
  91.4 16.7 all-gather.7

commit v3 on v2

--- a/solution.py
+++ b/solution.py
@@ -3,6 +3,8 @@
 import jax
 import jax.numpy as jnp
 from jax import lax
+from jax.experimental import pallas as pl
+from jax.experimental.pallas import tpu as pltpu
 from jax.sharding import PartitionSpec as P
 
 D = 2048
@@ -33,6 +35,138 @@
     context_mask = (row_owner[:, None] == page_owner[None, :]) & valid[None, :]
     causal = (row_owner[:, None] == row_owner[None, :]) & (row_index[None, :] <= row_index[:, None])
     return jnp.concatenate([context_mask, causal], axis=1)
+
+
+ROW_BLOCK = 128
+KEY_CHUNK = 256
+
+
+def pick(table, index):
+    onehot = index[:, None] == jnp.arange(table.shape[0], dtype=jnp.int32)[None, :]
+    return jnp.sum(jnp.where(onehot, table[None, :], 0), axis=1)
+
+
+def attention_kernel(
+    ranges_ref, q_ref, k_ref, v_ref, kown_ref, kpos_ref, rown_ref, o_ref, s_scr, acc_scr
+):
+    block = pl.program_id(0)
+    ctx_lo = ranges_ref[block, 0]
+    ctx_n = ranges_ref[block, 1]
+    new_lo = ranges_ref[block, 2]
+    total = ctx_n + ranges_ref[block, 3]
+    first_new = ranges_ref[block, 4]
+    heads = q_ref.shape[1] // HD
+    q = q_ref[...]
+    stacked = jnp.concatenate([q[:, h * HD:(h + 1) * HD] for h in range(heads)], axis=0)
+    row_owner = rown_ref[...]
+    row_index = block * ROW_BLOCK + lax.broadcasted_iota(jnp.int32, (ROW_BLOCK, 1), 0)
+    scale = 1.0 / math.sqrt(HD)
+
+    def chunk_of(t):
+        return jnp.where(t < ctx_n, ctx_lo + t, first_new + new_lo + t - ctx_n)
+
+    def scores_pass(t, highest):
+        c = chunk_of(t)
+        start = pl.multiple_of(c * KEY_CHUNK, KEY_CHUNK)
+        keys = k_ref[pl.ds(start, KEY_CHUNK), :]
+        s = lax.dot_general(
+            stacked, keys, (((1,), (1,)), ((), ())), preferred_element_type=jnp.float32
+        ) * scale
+        seen = (kown_ref[c] == row_owner) & (kpos_ref[c] <= row_index)
+        seen = jnp.concatenate([seen] * heads, axis=0)
+        s = jnp.where(seen, s, -1e30)
+        s_scr[c] = s
+        return jnp.maximum(highest, jnp.max(s, axis=1, keepdims=True))
+
+    highest = lax.fori_loop(
+        0, total, scores_pass, jnp.full((heads * ROW_BLOCK, 1), -1e30, jnp.float32)
+    )
+
+    def exp_pass(t, summed):
+        c = chunk_of(t)
+        e = jnp.exp(s_scr[c] - highest)
+        s_scr[c] = e
+        return summed + jnp.sum(e, axis=1, keepdims=True)
+
+    summed = lax.fori_loop(0, total, exp_pass, jnp.zeros((heads * ROW_BLOCK, 1), jnp.float32))
+    acc_scr[...] = jnp.zeros(acc_scr.shape, jnp.float32)
+
+    def value_pass(t, carry):
+        c = chunk_of(t)
+        start = pl.multiple_of(c * KEY_CHUNK, KEY_CHUNK)
+        w = (s_scr[c] / summed).astype(jnp.bfloat16)
+        acc_scr[...] += jnp.dot(w, v_ref[pl.ds(start, KEY_CHUNK), :], preferred_element_type=jnp.float32)
+        return carry
+
+    lax.fori_loop(0, total, value_pass, 0)
+    for h in range(heads):
+        o_ref[:, h * HD:(h + 1) * HD] = acc_scr[h * ROW_BLOCK:(h + 1) * ROW_BLOCK, :].astype(
+            jnp.bfloat16
+        )
+
+
+def sparse_attention(queries, keys, values, page_counts, last_fill, row_counts, page_len):
+    row_total = queries.shape[0]
+    key_total = keys.shape[0]
+    ctx_total = key_total - row_total
+    page_total = ctx_total // page_len
+    heads = queries.shape[1] // HD
+    blocks = row_total // ROW_BLOCK
+    chunks = key_total // KEY_CHUNK
+    ctx_chunks = ctx_total // KEY_CHUNK
+    key_index = jnp.arange(ctx_total, dtype=jnp.int32)
+    page_ref = key_index // page_len
+    page_owner, page_starts = slot_lookup(page_ref, page_counts)
+    context_len = (page_counts - 1) * page_len + last_fill
+    position = (page_ref - table_pick(page_starts, page_owner)) * page_len + key_index % page_len
+    valid = position < table_pick(context_len, page_owner)
+    row_index = jnp.arange(row_total, dtype=jnp.int32)
+    row_owner, row_starts = slot_lookup(row_index, row_counts)
+    key_owner = jnp.concatenate([jnp.where(valid, page_owner, -1), row_owner])
+    key_pos = jnp.concatenate([jnp.full((ctx_total,), -1, jnp.int32), row_index])
+    first = row_owner[::ROW_BLOCK]
+    last = row_owner[ROW_BLOCK - 1::ROW_BLOCK]
+    ctx_from = pick(page_starts, first) * page_len
+    ctx_to = (pick(page_starts, last) + pick(page_counts, last)) * page_len
+    ctx_lo = ctx_from // KEY_CHUNK
+    ctx_n = (ctx_to + KEY_CHUNK - 1) // KEY_CHUNK - ctx_lo
+    new_from = pick(row_starts, first)
+    new_to = jnp.arange(1, blocks + 1, dtype=jnp.int32) * ROW_BLOCK
+    new_lo = new_from // KEY_CHUNK
+    new_n = (new_to + KEY_CHUNK - 1) // KEY_CHUNK - new_lo
+    ranges = jnp.stack(
+        [ctx_lo, ctx_n, new_lo, new_n, jnp.full((blocks,), ctx_chunks, jnp.int32)], axis=1
+    ).astype(jnp.int32)
+    full = lambda b, r: (0, 0)
+    return pl.pallas_call(
+        attention_kernel,
+        grid_spec=pltpu.PrefetchScalarGridSpec(
+            num_scalar_prefetch=1,
+            grid=(blocks,),
+            in_specs=[
+                pl.BlockSpec((ROW_BLOCK, heads * HD), lambda b, r: (b, 0)),
+                pl.BlockSpec((key_total, HD), full),
+                pl.BlockSpec((key_total, HD), full),
+                pl.BlockSpec((chunks, 1, KEY_CHUNK), lambda b, r: (0, 0, 0)),
+                pl.BlockSpec((chunks, 1, KEY_CHUNK), lambda b, r: (0, 0, 0)),
+                pl.BlockSpec((ROW_BLOCK, 1), lambda b, r: (b, 0)),
+            ],
+            out_specs=pl.BlockSpec((ROW_BLOCK, heads * HD), lambda b, r: (b, 0)),
+            scratch_shapes=[
+                pltpu.VMEM((chunks, heads * ROW_BLOCK, KEY_CHUNK), jnp.float32),
+                pltpu.VMEM((heads * ROW_BLOCK, HD), jnp.float32),
+            ],
+        ),
+        out_shape=jax.ShapeDtypeStruct((row_total, heads * HD), jnp.bfloat16),
+    )(
+        ranges,
+        queries,
+        keys,
+        values,
+        key_owner.reshape(chunks, 1, KEY_CHUNK),
+        key_pos.reshape(chunks, 1, KEY_CHUNK),
+        row_owner.reshape(row_total, 1),
+    )
 
 
 def shards(
@@ -94,19 +228,9 @@
     fresh_values = lax.dynamic_slice_in_dim(new_values, kv_head * HD, HD, 1)
     all_keys = jnp.concatenate([context_keys, fresh_keys], axis=0)
     all_values = jnp.concatenate([context_values, fresh_values], axis=0)
-    masking = attend_masks(
-        page_counts[0], last_fill[0], row_counts[0], page_len, page_total, row_total
-    )
-    query_rows = queries.reshape(row_total, local_heads, HD)
-    scores = jnp.einsum("rhd,kd->hrk", query_rows, all_keys, preferred_element_type=jnp.float32) * (
-        1.0 / math.sqrt(HD)
-    )
-    scores = jnp.where(masking[None], scores, -1e30)
-    highest = jnp.max(scores, axis=-1, keepdims=True)
-    expo = jnp.exp(scores - highest)
-    weights = (expo / jnp.sum(expo, axis=-1, keepdims=True)).astype(jnp.bfloat16)
-    attention = jnp.einsum("hrk,kd->rhd", weights, all_values, preferred_element_type=jnp.float32)
-    attention = attention.astype(jnp.bfloat16).reshape(row_total, local_heads * HD)
+    attention = sparse_attention(
+        queries, all_keys, all_values, page_counts[0], last_fill[0], row_counts[0], page_len
+    )
     tp_size = lax.axis_size("tp")
     full_weight = lax.all_gather(out_weight, "tp", axis=0, tiled=True)
     full_gate_weight = lax.all_gather(ple_gate_weight, "tp", axis=0, tiled=True)

time: 155 us -> 142 us (0.916)
  Pallas kernels: 0 us -> 18.3 us
  other arithmetic: 30.3 us -> 12.9 us
  matrix products: 23.1 us -> 7.21 us
  local copies, waits for them, and re-layouts: 10.8 us -> 14.3 us
    pallas_call x0 -> x1, Pallas kernels: none -> 18.3 us  [sparse_attention(): pl.pallas_call(attention_kernel, grid_spec=pltpu.PrefetchScalarGridSpec(n...]
    sub x1 -> x2, other arithmetic: 16.3 us -> 0.02 us  [sparse_attention(): ctx_n = (ctx_to + KEY_CHUNK - 1) // KEY_CHUNK - ctx_lo]
    dot_general x2 -> x0, matrix products: 15.9 us -> none  [the longest x1 8.55 us: shards(): jnp.einsum('rhd,kd->hrk', query_rows, all_keys, preferred_element_type=jn...]
    and x2 -> x0, other arithmetic: 2.55 us -> none  [the longest x1 2.35 us: attend_masks(): context_mask = (row_owner[:, None] == page_owner[None, :]) & valid[None, :]]
    concatenate x1 -> x3, other arithmetic: 1.68 us -> 3.74 us  [the longest x1 2.31 us: shards(): all_values = jnp.concatenate([context_values, fresh_values], axis=0)]
  transfers between devices with their start and end apart: 8 -> 8, of which waited for: 3 -> 3; matrix products, arithmetic and copies ran while one was open for 39% -> 22% of each run, Pallas kernels for 0% -> 13%
where the time goes in v3:
time: 142 us; the launch traced here: 141 us
  waiting for transfers between devices  42 us (30%)
  starting transfers between devices  21.3 us (15%)
  Pallas kernels  18.3 us (13%)
  local copies, waits for them, and re-layouts  14.3 us (10%)
  between operations  13.4 us (9%)
  other arithmetic  12.9 us (9%)
  blocking collectives  11.1 us (8%)
  matrix products  7.21 us (5%)
    all_to_all x1, waiting for transfers between devices, shards(): lax.all_to_all(outgoing, 'req', split_axis=0, concat_axis=0, tiled=True)  32.1 us
    pallas_call x1, Pallas kernels, sparse_attention(): pl.pallas_call(attention_kernel, grid_spec=pltpu.PrefetchScalarGridSpec(n...  18.3 us
    all_to_all x1, blocking collectives, shards(): lax.all_to_all(row_out, 'tp', split_axis=1, concat_axis=0, tiled=True)  11.1 us
    all_to_all x1, starting transfers between devices, shards(): lax.all_to_all(with_gains.reshape(-1, hidden.shape[1]), 'tp', split_axis=...  7.17 us
    all_to_all x1, starting transfers between devices, shards(): lax.all_to_all(request_table, 'req', split_axis=0, concat_axis=0, tiled=T...  6.38 us
    all_to_all x1, waiting for transfers between devices, shards(): lax.all_to_all(attention, 'tp', split_axis=0, concat_axis=1, tiled=True)  5.86 us
    dot_general x1, matrix products, shards(): jnp.dot(row_attention, full_weight, preferred_element_type=jnp.float32)  4.74 us
    all_to_all x1, starting transfers between devices, shards(): lax.all_to_all(attention, 'tp', split_axis=0, concat_axis=1, tiled=True)  3.83 us
  transfers between devices with their start and end apart: 8, of which 3 were waited for; matrix products, arithmetic and copies ran while one was open for 22% of the time, Pallas kernels for 13%

profile of v3, /device:TPU:1, one launch (start us, length us, event | category | flops | bytes accessed | tf_op | source)
XLA Modules:
  0.0 140.6 jit_solution(10163136356163212358)
XLA Ops:
  6.5 0.0 all-gather.4.cloned.1.call-start
  6.5 0.7 all-gather.4.cloned.1.call-update
  7.3 0.0 copy-done.7
  7.3 0.2 convert_reduce_fusion.1
  7.4 0.0 copy-done.5
  7.5 0.2 select_reduce_fusion.2
  7.7 0.7 copy.79
  8.4 6.4 %all-to-all-start.1 = ((s32[8,1,6]{2,1,0:T(1,128)}), s32[8,1,6]{2,1,0:T(1,128)S(1)}, u32[]{:S(2)}, u32[]{:S(2)}) async-start(s32[8,1,6]{2,1,0:T(1,128)} %copy.79), calls=%async_computation.1 | async-start | bytes 8192 | tf_op jit(solution)/shard_map/all_to_all | solution.py:208
  14.7 0.0 all-gather.6.cloned.1.call-start
  14.8 0.7 all-gather.6.cloned.1.call-update
  15.5 2.5 %dynamic-slice_select_fusion = bf16[48,64,256]{2,1,0:T(8,128)(2,1)S(1)} fusion(bf16[48,64,512]{2,1,0:T(8,128)(2,1)} %param.26, s32[]{:T(128)S(6)} %select_n.153, bf16[48,64,512]{2,1,0:T(8,128)(2,1)} %param.25, pred[]{:T(512)S(6)} %eq.58), kind=kLoop, calls=%fused_computation.5 | loop fusion | flops 786432 | bytes 4718597 | tf_op jit(solution)/shard_map/jit(_where)/select_n | solution.py:213
  18.1 1.9 %all-to-all-done.1 = s32[8,1,6]{2,1,0:T(1,128)S(1)} async-done(((s32[8,1,6]{2,1,0:T(1,128)}), s32[8,1,6]{2,1,0:T(1,128)S(1)}, u32[]{:S(2)}, u32[]{:S(2)}) %all-to-all-start.1) | async-done | bytes 224 | tf_op jit(solution)/shard_map/all_to_all | solution.py:208
  20.0 0.1 reshape.493
  20.1 1.9 %gather_fusion = bf16[48,64,256]{2,1,0:T(8,128)(2,1)} fusion(bf16[48,64,256]{2,1,0:T(8,128)(2,1)S(1)} %dynamic-slice_select_fusion, s32[1024]{0:T(1024)S(1)} %pad_clamp_fusion.1), kind=kCustom, calls=%fused_computation | custom fusion | bytes 3145920 | tf_op jit(solution)/shard_map/gather | solution.py:216
  22.1 0.0 copy-start.3
  22.1 0.0 copy-start
  22.1 3.7 %all-to-all-start.2 = ((bf16[8,6,64,256]{3,2,1,0:T(8,128)(2,1)}), bf16[8,6,64,256]{3,2,1,0:T(8,128)(2,1)S(1)}, u32[]{:S(2)}, u32[]{:S(2)}) async-start(bf16[8,6,64,256]{3,2,1,0:T(8,128)(2,1)} %bitcast.11), calls=%async_computation.2 | async-start | bytes 3145728 | tf_op jit(solution)/shard_map/all_to_all | solution.py:217
  25.8 0.0 all-gather.8.cloned.1.call-start
  25.9 0.7 all-gather.8.cloned.1.call-update
  26.6 0.0 copy-done.6
  26.6 0.2 reduce-window_clone.1
  26.8 0.1 convert_reduce_fusion.2
  26.9 0.1 slice.48
  27.0 0.1 slice.49
  27.1 0.0 copy-done.1
  27.1 0.2 reduce-window_1_clone.1
  27.2 0.0 copy-done.4
  27.3 0.2 select_reduce_fusion.3
  27.5 0.1 copy.70
  27.6 0.1 copy.66
  27.7 0.1 copy.74
  27.8 0.0 copy-done.2
  27.9 0.8 pad_maximum_fusion.2
  28.7 32.1 %all-to-all-done.2 = bf16[8,6,64,256]{3,2,1,0:T(8,128)(2,1)S(1)} async-done(((bf16[8,6,64,256]{3,2,1,0:T(8,128)(2,1)}), bf16[8,6,64,256]{3,2,1,0:T(8,128)(2,1)S(1)}, u32[]{:S(2)}, u32[]{:S(2)}) %all-to-all-start.2) | async-done | bytes 1572896 | tf_op jit(solution)/shard_map/all_to_all | solution.py:217
  60.8 7.2 %all-to-all-start = ((bf16[4,136,512]{2,1,0:T(8,128)(2,1)}), bf16[4,136,512]{2,1,0:T(8,128)(2,1)}, u32[]{:S(2)}, u32[]{:S(2)}) async-start(bf16[4,136,512]{2,1,0:T(8,128)(2,1)} %pad_maximum_fusion.2), calls=%async_computation | async-start | bytes 1114112 | tf_op jit(solution)/shard_map/all_to_all | solution.py:243
  68.0 0.1 collective-permute-start
  68.1 0.1 convert_reduce_fusion
  68.2 0.1 select_reduce_fusion.1
  68.4 0.6 reshape.487.kown_ref
  69.0 0.9 copy.80.rown_ref
  69.9 0.6 stack.2.ranges_ref
  70.5 1.8 %constant_dynamic-slice_fusion = (bf16[512,256]{1,0:T(8,128)(2,1)}, bf16[512,256]{1,0:T(8,128)(2,1)S(1)}) fusion(bf16[512,512]{1,0:T(8,128)(2,1)} %param.24, s32[]{:T(128)S(6)} %select_n.153, bf16[512,512]{1,0:T(8,128)(2,1)} %param.23), kind=kLoop, calls=%fused_computation.105 | loop fusion | bytes 1048580 | tf_op jit(solution)/shard_map/dynamic_slice | solution.py:228
  72.3 0.0 collective-permute-done
  72.3 2.0 %broadcast_select_fusion = (bf16[8,6,64,256]{3,2,1,0:T(8,128)(2,1)}, bf16[8,6,64,256]{3,2,1,0:T(8,128)(2,1)}) fusion(bf16[8,6,64,256]{3,2,1,0:T(8,128)(2,1)S(1)} %collective-permute-done, bf16[8,6,64,256]{3,2,1,0:T(8,128)(2,1)S(1)} %all-to-all-done.2, pred[]{:T(512)S(6)} %eq.58), kind=kLoop, calls=%fused_computation.6 | loop fusion | flops 1572864 | bytes 6291457 | tf_op jit(solution)/shard_map/jit(_where)/select_n | solution.py:220
  74.3 2.1 %gather_fusion.2 = bf16[48,64,256]{2,1,0:T(8,128)(2,1)S(1)} fusion(bf16[48,64,256]{2,1,0:T(8,128)(2,1)} %bitcast.55, s32[1024]{0:T(1024)S(1)} %pad_clamp_fusion), kind=kCustom, calls=%fused_computation.2 | custom fusion | bytes 3145920 | tf_op jit(solution)/shard_map/gather | solution.py:224
  76.3 2.1 %gather_fusion.1 = bf16[48,64,256]{2,1,0:T(8,128)(2,1)S(1)} fusion(bf16[48,64,256]{2,1,0:T(8,128)(2,1)} %bitcast.54, s32[1024]{0:T(1024)S(1)} %pad_clamp_fusion), kind=kCustom, calls=%fused_computation.1 | custom fusion | bytes 3145920 | tf_op jit(solution)/shard_map/gather | solution.py:221
  78.4 2.3 %pad_maximum_fusion.1.v_ref = bf16[3584,256]{1,0:T(8,128)(2,1)} fusion(bf16[512,256]{1,0:T(8,128)(2,1)} %get-tuple-element.51, bf16[3072,256]{1,0:T(8,128)(2,1)S(1)} %bitcast.53), kind=kLoop, calls=%fused_computation.4 | loop fusion | flops 3670016 | bytes 3670016 | tf_op jit(solution)/shard_map/concatenate | solution.py:230
  80.7 1.4 %pad_maximum_fusion.k_ref = bf16[3584,256]{1,0:T(8,128)(2,1)} fusion(bf16[512,256]{1,0:T(8,128)(2,1)S(1)} %get-tuple-element.52, bf16[3072,256]{1,0:T(8,128)(2,1)S(1)} %bitcast.52), kind=kLoop, calls=%fused_computation.3 | loop fusion | flops 3670016 | bytes 3670016 | tf_op jit(solution)/shard_map/concatenate | solution.py:229
  82.2 18.3 %shard_map.166 = bf16[512,512]{1,0:T(8,128)(2,1)} custom-call(s32[4,5]{1,0:T(4,128)} %stack.2.ranges_ref, bf16[512,512]{1,0:T(8,128)(2,1)} %q_ref.1, bf16[3584,256]{1,0:T(8,128)(2,1)} %pad_maximum_fusion.k_ref, bf16[3584,256]{1,0:T(8,128)(2,1)} %pad_maximum_fusion.1.v_ref, s32[14,1,256]{2,1,0:T(1,128)} %reshape.487.kown_ref, ...), custom_call_target="tpu_custom_call" | custom-call | tf_op jit(solution)/shard_map/pallas_call | solution.py:141
  100.5 2.1 %copy.81 = bf16[4,128,512]{1,2,0:T(8,128)(2,1)} copy(bf16[4,128,512]{2,1,0:T(8,128)(2,1)} %bitcast.61) | data formatting | bytes 1048576 | tf_op jit(solution)/shard_map/all_to_all | solution.py:249
  102.6 0.0 all-to-all-done
  102.6 3.8 %all-to-all-start.3 = ((bf16[4,128,512]{1,2,0:T(8,128)(2,1)}), bf16[4,128,512]{1,2,0:T(8,128)(2,1)S(1)}, u32[]{:S(2)}, u32[]{:S(2)}) async-start(bf16[4,128,512]{1,2,0:T(8,128)(2,1)} %copy.81), calls=%async_computation.3 | async-start | bytes 1048576 | tf_op jit(solution)/shard_map/all_to_all | solution.py:249
  106.4 1.2 convert_bitcast_fusion
  107.6 0.1 copy.86
  107.7 0.8 slice_convert_fusion
  108.5 5.9 %all-to-all-done.3 = bf16[4,128,512]{1,2,0:T(8,128)(2,1)S(1)} async-done(((bf16[4,128,512]{1,2,0:T(8,128)(2,1)}), bf16[4,128,512]{1,2,0:T(8,128)(2,1)S(1)}, u32[]{:S(2)}, u32[]{:S(2)}) %all-to-all-start.3) | async-done | bytes 524320 | tf_op jit(solution)/shard_map/all_to_all | solution.py:249
  114.4 4.7 %multiply_reduce_fusion.1 = (f32[128]{0:T(128)S(1)}, f32[128,2048]{1,0:T(8,128)S(1)}) fusion(bf16[128,2048]{0,1:T(8,128)(2,1)S(1)} %bitcast.57, bf16[2048,2048]{1,0:T(8,128)(2,1)} %all-gather.4.cloned.1.call-done), kind=kOutput, calls=%fused_computation.12 | convolution fusion | flops 1074265984 | bytes 9961984 | tf_op jit(solution)/shard_map/dot_general | solution.py:252
  119.1 0.2 add_convert_fusion.1
  119.4 0.0 all-gather.6.cloned.1.call-done
  119.4 0.0 all-gather.8.cloned.1.call-done
  119.4 2.5 %multiply_reduce_fusion = (f32[128]{0:T(128)S(1)}, f32[128,2048]{1,0:T(8,128)S(1)}) fusion(bf16[256,2048]{1,0:T(8,128)(2,1)} %all-gather.8.cloned.1.call-done, bf16[512,256]{1,0:T(8,128)(2,1)} %param.29, s32[]{:T(128)S(6)} %select_n.163, bf16[128,2048]{1,0:T(8,128)(2,1)S(1)} %add_convert_fusion.1, bf16[2048,256]{1,0:T(8,128)(2,1)} %all-gather.6.cloned.1.call-done), kind=kOutput, calls=%fused_computation.10 | convolution fusion | flops 269320064 | bytes 3736068 | tf_op jit(solution)/shard_map/dot_general | solution.py:264
  121.9 0.2 add_convert_fusion
  122.2 11.1 %all_to_all.62 = bf16[128,4,512]{2,0,1:T(8,128)(2,1)S(1)} all-to-all(bf16[128,4,512]{2,0,1:T(8,128)(2,1)S(1)} %bitcast.59), channel_id=1, replica_groups=mesh['req'=8,'tp'=4] {'tp'}, dimensions={1} | all-to-all | bytes 1048576 | tf_op jit(solution)/shard_map/all_to_all | solution.py:272
  133.3 0.8 copy.91
  (36 shorter events, 0.3 us)
Async XLA Ops:
  6.5 0.7 copy-start.7
  6.5 0.9 copy-start.5
  6.5 107.8 %all-gather.4.cloned.1.call-start = ((), (), s32[]{:S(2)}) async-start(), calls=%async_computation.5 | async-start | bytes 10485760 | tf_op jit(solution)/shard_map/all_gather | solution.py:235
  8.4 11.6 %all-to-all-start.1 = ((s32[8,1,6]{2,1,0:T(1,128)}), s32[8,1,6]{2,1,0:T(1,128)S(1)}, u32[]{:S(2)}, u32[]{:S(2)}) async-start(s32[8,1,6]{2,1,0:T(1,128)} %copy.79), calls=%async_computation.1 | async-start | bytes 8192 | tf_op jit(solution)/shard_map/all_to_all | solution.py:208
  14.7 104.7 %all-gather.6.cloned.1.call-start = ((), (), s32[]{:S(2)}) async-start(), calls=%async_computation.6 | async-start | bytes 1310720 | tf_op jit(solution)/shard_map/all_gather | solution.py:236
  22.0 4.5 %copy-start.6 = (s32[1,8]{1,0:T(1,128)S(1)}, s32[1,8]{1,0:T(1,128)}, u32[]{:S(2)}) copy-start(s32[1,8]{1,0:T(1,128)} %param.37) | copy-start | bytes 100
  22.0 5.0 %copy-start.1 = (s32[1,8]{1,0:T(1,128)S(1)}, s32[1,8]{1,0:T(1,128)}, u32[]{:S(2)}) copy-start(s32[1,8]{1,0:T(1,128)} %param.35) | copy-start | bytes 100
  22.0 5.2 %copy-start.4 = (s32[1,8]{1,0:T(1,128)S(1)}, s32[1,8]{1,0:T(1,128)}, u32[]{:S(2)}) copy-start(s32[1,8]{1,0:T(1,128)} %param.36) | copy-start | bytes 100
  22.0 5.7 %copy-start.2 = (bf16[512]{0:T(512)(128)(2,1)S(1)}, bf16[512]{0:T(512)(128)(2,1)}, u32[]{:S(2)}) copy-start(bf16[512]{0:T(512)(128)(2,1)} %param.28) | copy-start | bytes 3076
  22.1 5.7 %copy-start.3 = (bf16[512]{0:T(512)(128)(2,1)S(1)}, bf16[512]{0:T(512)(128)(2,1)}, u32[]{:S(2)}) copy-start(bf16[512]{0:T(512)(128)(2,1)} %param.32) | copy-start | bytes 3076
  22.1 5.8 %copy-start = (bf16[512,512]{1,0:T(8,128)(2,1)S(1)}, bf16[512,512]{1,0:T(8,128)(2,1)}, u32[]{:S(2)}) copy-start(bf16[512,512]{1,0:T(8,128)(2,1)} %param.21) | copy-start | bytes 1572868
  22.1 38.7 %all-to-all-start.2 = ((bf16[8,6,64,256]{3,2,1,0:T(8,128)(2,1)}), bf16[8,6,64,256]{3,2,1,0:T(8,128)(2,1)S(1)}, u32[]{:S(2)}, u32[]{:S(2)}) async-start(bf16[8,6,64,256]{3,2,1,0:T(8,128)(2,1)} %bitcast.11), calls=%async_computation.2 | async-start | bytes 3145728 | tf_op jit(solution)/shard_map/all_to_all | solution.py:217
  25.8 93.6 %all-gather.8.cloned.1.call-start = ((), (), s32[]{:S(2)}) async-start(), calls=%async_computation.7 | async-start | bytes 1310720 | tf_op jit(solution)/shard_map/all_gather | solution.py:237
  60.8 41.7 %all-to-all-start = ((bf16[4,136,512]{2,1,0:T(8,128)(2,1)}), bf16[4,136,512]{2,1,0:T(8,128)(2,1)}, u32[]{:S(2)}, u32[]{:S(2)}) async-start(bf16[4,136,512]{2,1,0:T(8,128)(2,1)} %pad_maximum_fusion.2), calls=%async_computation | async-start | bytes 1114112 | tf_op jit(solution)/shard_map/all_to_all | solution.py:243
  68.0 4.3 %collective-permute-start = (bf16[8,6,64,256]{3,2,1,0:T(8,128)(2,1)S(1)}, bf16[8,6,64,256]{3,2,1,0:T(8,128)(2,1)S(1)}, u32[]{:S(2)}, u32[]{:S(2)}) collective-permute-start(bf16[8,6,64,256]{3,2,1,0:T(8,128)(2,1)S(1)} %all-to-all-done.2), channel_id=1, source_target_pairs={{0,1},{1,0},{2,3},{3,2},{4,5},{5,4},{6,7},{7,6},{8,9},{9,8},{10,11... | collective-permute-start | bytes 4718600 | tf_op jit(solution)/shard_map/ppermute | solution.py:218
  102.6 11.8 %all-to-all-start.3 = ((bf16[4,128,512]{1,2,0:T(8,128)(2,1)}), bf16[4,128,512]{1,2,0:T(8,128)(2,1)S(1)}, u32[]{:S(2)}, u32[]{:S(2)}) async-start(bf16[4,128,512]{1,2,0:T(8,128)(2,1)} %copy.81), calls=%async_computation.3 | async-start | bytes 1048576 | tf_op jit(solution)/shard_map/all_to_all | solution.py:249
Sparse Core Ops, SparseCore 0:
  8.9 61.9 all-gather.3
  72.5 16.8 all-gather.5
  90.9 16.7 all-gather.7

commit v4 on v3

--- a/solution.py
+++ b/solution.py
@@ -47,15 +47,31 @@
 
 
 def attention_kernel(
-    ranges_ref, q_ref, k_ref, v_ref, kown_ref, kpos_ref, rown_ref, o_ref, s_scr, acc_scr
+    ranges_ref,
+    slots_ref,
+    meta_ref,
+    q_ref,
+    own_ref,
+    partner_ref,
+    fresh_k_ref,
+    fresh_v_ref,
+    kown_ref,
+    kpos_ref,
+    rown_ref,
+    o_ref,
+    s_scr,
+    acc_scr,
 ):
     block = pl.program_id(0)
     ctx_lo = ranges_ref[block, 0]
     ctx_n = ranges_ref[block, 1]
     new_lo = ranges_ref[block, 2]
     total = ctx_n + ranges_ref[block, 3]
-    first_new = ranges_ref[block, 4]
+    ctx_chunks = ranges_ref[block, 4]
+    keys_are_own = meta_ref[0] == 0
     heads = q_ref.shape[1] // HD
+    page_len = own_ref.shape[1]
+    per_chunk = KEY_CHUNK // page_len
     q = q_ref[...]
     stacked = jnp.concatenate([q[:, h * HD:(h + 1) * HD] for h in range(heads)], axis=0)
     row_owner = rown_ref[...]
@@ -63,12 +79,27 @@
     scale = 1.0 / math.sqrt(HD)
 
     def chunk_of(t):
-        return jnp.where(t < ctx_n, ctx_lo + t, first_new + new_lo + t - ctx_n)
+        return jnp.where(t < ctx_n, ctx_lo + t, ctx_chunks + new_lo + t - ctx_n)
+
+    def load_chunk(c, want_keys, fresh_ref):
+        pick_own = keys_are_own == want_keys
+
+        def cached():
+            pages = []
+            for i in range(per_chunk):
+                slot = slots_ref[c * per_chunk + i]
+                pages.append(jnp.where(pick_own, own_ref[slot], partner_ref[slot]))
+            return jnp.concatenate(pages, axis=0)
+
+        def fresh():
+            start = pl.multiple_of((c - ctx_chunks) * KEY_CHUNK, KEY_CHUNK)
+            return fresh_ref[pl.ds(start, KEY_CHUNK), :]
+
+        return lax.cond(c < ctx_chunks, cached, fresh)
 
     def scores_pass(t, highest):
         c = chunk_of(t)
-        start = pl.multiple_of(c * KEY_CHUNK, KEY_CHUNK)
-        keys = k_ref[pl.ds(start, KEY_CHUNK), :]
+        keys = load_chunk(c, True, fresh_k_ref)
         s = lax.dot_general(
             stacked, keys, (((1,), (1,)), ((), ())), preferred_element_type=jnp.float32
         ) * scale
@@ -89,13 +120,14 @@
         return summed + jnp.sum(e, axis=1, keepdims=True)
 
     summed = lax.fori_loop(0, total, exp_pass, jnp.zeros((heads * ROW_BLOCK, 1), jnp.float32))
+    inverse = 1.0 / summed
     acc_scr[...] = jnp.zeros(acc_scr.shape, jnp.float32)
 
     def value_pass(t, carry):
         c = chunk_of(t)
-        start = pl.multiple_of(c * KEY_CHUNK, KEY_CHUNK)
-        w = (s_scr[c] / summed).astype(jnp.bfloat16)
-        acc_scr[...] += jnp.dot(w, v_ref[pl.ds(start, KEY_CHUNK), :], preferred_element_type=jnp.float32)
+        w = (s_scr[c] * inverse).astype(jnp.bfloat16)
+        values = load_chunk(c, False, fresh_v_ref)
+        acc_scr[...] += jnp.dot(w, values, preferred_element_type=jnp.float32)
         return carry
 
     lax.fori_loop(0, total, value_pass, 0)
@@ -105,11 +137,14 @@
         )
 
 
-def sparse_attention(queries, keys, values, page_counts, last_fill, row_counts, page_len):
+def sparse_attention(
+    queries, own_pages, partner_pages, slots, new_keys, new_values, half, kv_head,
+    page_counts, last_fill, row_counts, page_total,
+):
     row_total = queries.shape[0]
-    key_total = keys.shape[0]
-    ctx_total = key_total - row_total
-    page_total = ctx_total // page_len
+    page_len = own_pages.shape[1]
+    ctx_total = page_total * page_len
+    key_total = ctx_total + row_total
     heads = queries.shape[1] // HD
     blocks = row_total // ROW_BLOCK
     chunks = key_total // KEY_CHUNK
@@ -137,21 +172,24 @@
     ranges = jnp.stack(
         [ctx_lo, ctx_n, new_lo, new_n, jnp.full((blocks,), ctx_chunks, jnp.int32)], axis=1
     ).astype(jnp.int32)
-    full = lambda b, r: (0, 0)
+    meta = jnp.stack([half, kv_head]).astype(jnp.int32)
+    whole = lambda b, r, s, m: (0, 0, 0)
     return pl.pallas_call(
         attention_kernel,
         grid_spec=pltpu.PrefetchScalarGridSpec(
-            num_scalar_prefetch=1,
+            num_scalar_prefetch=3,
             grid=(blocks,),
             in_specs=[
-                pl.BlockSpec((ROW_BLOCK, heads * HD), lambda b, r: (b, 0)),
-                pl.BlockSpec((key_total, HD), full),
-                pl.BlockSpec((key_total, HD), full),
-                pl.BlockSpec((chunks, 1, KEY_CHUNK), lambda b, r: (0, 0, 0)),
-                pl.BlockSpec((chunks, 1, KEY_CHUNK), lambda b, r: (0, 0, 0)),
-                pl.BlockSpec((ROW_BLOCK, 1), lambda b, r: (b, 0)),
+                pl.BlockSpec((ROW_BLOCK, heads * HD), lambda b, r, s, m: (b, 0)),
+                pl.BlockSpec(own_pages.shape, whole),
+                pl.BlockSpec(partner_pages.shape, whole),
+                pl.BlockSpec((row_total, HD), lambda b, r, s, m: (0, m[1])),
+                pl.BlockSpec((row_total, HD), lambda b, r, s, m: (0, m[1])),
+                pl.BlockSpec((chunks, 1, KEY_CHUNK), whole),
+                pl.BlockSpec((chunks, 1, KEY_CHUNK), whole),
+                pl.BlockSpec((ROW_BLOCK, 1), lambda b, r, s, m: (b, 0)),
             ],
-            out_specs=pl.BlockSpec((ROW_BLOCK, heads * HD), lambda b, r: (b, 0)),
+            out_specs=pl.BlockSpec((ROW_BLOCK, heads * HD), lambda b, r, s, m: (b, 0)),
             scratch_shapes=[
                 pltpu.VMEM((chunks, heads * ROW_BLOCK, KEY_CHUNK), jnp.float32),
                 pltpu.VMEM((heads * ROW_BLOCK, HD), jnp.float32),
@@ -160,9 +198,13 @@
         out_shape=jax.ShapeDtypeStruct((row_total, heads * HD), jnp.bfloat16),
     )(
         ranges,
+        slots.astype(jnp.int32),
+        meta,
         queries,
-        keys,
-        values,
+        own_pages,
+        partner_pages,
+        new_keys,
+        new_values,
         key_owner.reshape(chunks, 1, KEY_CHUNK),
         key_pos.reshape(chunks, 1, KEY_CHUNK),
         row_owner.reshape(row_total, 1),
@@ -210,26 +252,26 @@
     tp_count = lax.axis_size("tp")
     half = tp_index % 2
     partner = [(i, i ^ 1) for i in range(tp_count)]
-    own_cache = jnp.where(half == 0, cache_keys, cache_values)
-    head_cache = lax.dynamic_slice_in_dim(own_cache, kv_head * HD, HD, 2)
     arrival_index = holders * capacity + ranking
-    outgoing = head_cache[wanted]
+
+    def fetch_pages(cache):
+        return lax.dynamic_slice_in_dim(cache, kv_head * HD, HD, 2)[wanted]
+
+    outgoing = lax.cond(
+        half == 0, lambda: fetch_pages(cache_keys), lambda: fetch_pages(cache_values)
+    )
     arrived = lax.all_to_all(outgoing, "req", split_axis=0, concat_axis=0, tiled=True)
     swapped = lax.ppermute(arrived, "tp", partner)
-    key_pages = jnp.where(half == 0, arrived, swapped)
-    value_pages = jnp.where(half == 0, swapped, arrived)
-    context_keys = key_pages.reshape(req_count * capacity, page_len, HD)[arrival_index].reshape(
-        page_total * page_len, HD
-    )
-    context_values = value_pages.reshape(req_count * capacity, page_len, HD)[
-        arrival_index
-    ].reshape(page_total * page_len, HD)
-    fresh_keys = lax.dynamic_slice_in_dim(new_keys, kv_head * HD, HD, 1)
-    fresh_values = lax.dynamic_slice_in_dim(new_values, kv_head * HD, HD, 1)
-    all_keys = jnp.concatenate([context_keys, fresh_keys], axis=0)
-    all_values = jnp.concatenate([context_values, fresh_values], axis=0)
     attention = sparse_attention(
-        queries, all_keys, all_values, page_counts[0], last_fill[0], row_counts[0], page_len
+        queries,
+        arrived.reshape(-1, page_len, HD),
+        swapped.reshape(-1, page_len, HD),
+        arrival_index,
+        new_keys,
+        new_values,
+        half,
+        kv_head,
+        page_counts[0], last_fill[0], row_counts[0], page_total,
     )
     tp_size = lax.axis_size("tp")
     full_weight = lax.all_gather(out_weight, "tp", axis=0, tiled=True)

time: 142 us -> 138 us (0.972)
  other arithmetic: 12.9 us -> 4.04 us
  waiting for transfers between devices: 42 us -> 48.6 us
  local copies, waits for them, and re-layouts: 14.3 us -> 12.3 us
    all_to_all x1, waiting for transfers between devices: 5.86 us -> 10.7 us  [shards(): lax.all_to_all(attention, 'tp', split_axis=0, concat_axis=1, tiled=True)]
    select_n x3 -> x1, other arithmetic: 4.51 us -> 0.01 us  [fetch_pages(): return lax.dynamic_slice_in_dim(cache, kv_head * HD, HD, 2)[wanted]]
    concatenate x2 -> x0, other arithmetic: 3.73 us -> none  [the longest x1 2.31 us: shards(): all_values = jnp.concatenate([context_values, fresh_values], axis=0)]
    all_to_all x1, waiting for transfers between devices: 1.91 us -> 4.47 us  [shards(): lax.all_to_all(request_table, 'req', split_axis=0, concat_axis=0, tiled=T...]
    gather x3 -> x1, local copies, waits for them, and re-layouts: 6.08 us -> 3.77 us  [fetch_pages(): return lax.dynamic_slice_in_dim(cache, kv_head * HD, HD, 2)[wanted]]
  transfers between devices with their start and end apart: 8 -> 8, of which waited for: 3 -> 3; matrix products, arithmetic and copies ran while one was open for 22% -> 15% of each run, Pallas kernels for 13% -> 13%
where the time goes in v4:
time: 138 us; the launch traced here: 136 us
  waiting for transfers between devices  48.6 us (35%)
  starting transfers between devices  21.5 us (16%)
  Pallas kernels  18.3 us (13%)
  between operations  13.4 us (10%)
  local copies, waits for them, and re-layouts  12.3 us (9%)
  blocking collectives  10.8 us (8%)
  matrix products  7.21 us (5%)
  other arithmetic  4.04 us (3%)
    all_to_all x1, waiting for transfers between devices, shards(): lax.all_to_all(outgoing, 'req', split_axis=0, concat_axis=0, tiled=True)  31.3 us
    pallas_call x1, Pallas kernels, sparse_attention(): pl.pallas_call(attention_kernel, grid_spec=pltpu.PrefetchScalarGridSpec(n...  18.3 us
    all_to_all x1, blocking collectives, shards(): lax.all_to_all(row_out, 'tp', split_axis=1, concat_axis=0, tiled=True)  10.8 us
    all_to_all x1, waiting for transfers between devices, shards(): lax.all_to_all(attention, 'tp', split_axis=0, concat_axis=1, tiled=True)  10.7 us
    all_to_all x1, starting transfers between devices, shards(): lax.all_to_all(with_gains.reshape(-1, hidden.shape[1]), 'tp', split_axis=...  7.29 us
    all_to_all x1, starting transfers between devices, shards(): lax.all_to_all(request_table, 'req', split_axis=0, concat_axis=0, tiled=T...  6.38 us
    dot_general x1, matrix products, shards(): jnp.dot(row_attention, full_weight, preferred_element_type=jnp.float32)  4.74 us
    all_to_all x1, waiting for transfers between devices, shards(): lax.all_to_all(request_table, 'req', split_axis=0, concat_axis=0, tiled=T...  4.47 us
  transfers between devices with their start and end apart: 8, of which 3 were waited for; matrix products, arithmetic and copies ran while one was open for 15% of the time, Pallas kernels for 13%

profile of v4, /device:TPU:1, one launch (start us, length us, event | category | flops | bytes accessed | tf_op | source)
XLA Modules:
  0.0 136.1 jit_solution(15287120162187701678)
XLA Ops:
  6.5 0.0 all-gather.4.cloned.1.call-start
  6.5 0.0 copy-start
  6.5 0.7 all-gather.4.cloned.1.call-update
  7.3 0.1 copy-done.9
  7.3 0.2 convert_reduce_fusion.1
  7.5 0.0 copy-done.7
  7.6 0.2 select_reduce_fusion.2
  7.8 0.7 copy.82
  8.4 6.4 %all-to-all-start.1 = ((s32[8,1,6]{2,1,0:T(1,128)}), s32[8,1,6]{2,1,0:T(1,128)S(1)}, u32[]{:S(2)}, u32[]{:S(2)}) async-start(s32[8,1,6]{2,1,0:T(1,128)} %copy.82), calls=%async_computation.1 | async-start | bytes 8192 | tf_op jit(solution)/shard_map/all_to_all | solution.py:250
  14.8 0.0 all-gather.6.cloned.1.call-start
  14.9 0.7 all-gather.6.cloned.1.call-update
  15.6 4.5 %all-to-all-done.1 = s32[8,1,6]{2,1,0:T(1,128)S(1)} async-done(((s32[8,1,6]{2,1,0:T(1,128)}), s32[8,1,6]{2,1,0:T(1,128)S(1)}, u32[]{:S(2)}, u32[]{:S(2)}) %all-to-all-start.1) | async-done | bytes 224 | tf_op jit(solution)/shard_map/all_to_all | solution.py:250
  20.1 0.0 copy-done
  20.1 0.1 reshape.474
  20.2 1.9 %constant_dynamic-slice_fusion = bf16[48,64,256]{2,1,0:T(8,128)(2,1)} fusion(bf16[48,64,512]{2,1,0:T(8,128)(2,1)S(1)} %get-tuple-element.85, s32[]{:T(128)S(6)} %select_n.130), kind=kLoop, calls=%fused_computation.107 | loop fusion | bytes 3145732 | tf_op jit(solution)/shard_map/cond/branch_0_fun/dynamic_slice | solution.py:258
  22.1 3.8 %gather_fusion = bf16[48,64,256]{2,1,0:T(8,128)(2,1)} fusion(bf16[48,64,256]{2,1,0:T(8,128)(2,1)} %constant_dynamic-slice_fusion, s32[1024]{0:T(1024)S(1)} %pad_clamp_fusion), kind=kCustom, calls=%fused_computation | custom fusion | bytes 3145920 | tf_op jit(solution)/shard_map/cond/branch_0_fun/gather | solution.py:258
  25.9 0.0 copy-start.5
  25.9 0.0 copy-start.2
  25.9 3.7 %all-to-all-start.2 = ((bf16[8,6,64,256]{3,2,1,0:T(8,128)(2,1)}), bf16[8,6,64,256]{3,2,1,0:T(8,128)(2,1)S(1)}, u32[]{:S(2)}, u32[]{:S(2)}) async-start(bf16[8,6,64,256]{3,2,1,0:T(8,128)(2,1)} %bitcast.15), calls=%async_computation.2 | async-start | bytes 3145728 | tf_op jit(solution)/shard_map/all_to_all | solution.py:263
  29.6 0.0 all-gather.8.cloned.1.call-start
  29.7 0.7 all-gather.8.cloned.1.call-update
  30.4 0.0 copy-done.8
  30.4 0.2 reduce-window_clone.1
  30.6 0.1 convert_reduce_fusion.2
  30.7 0.1 slice.48
  30.8 0.1 slice.49
  30.8 0.0 copy-done.3
  30.9 0.2 reduce-window_1_clone.1
  31.0 0.0 copy-done.6
  31.0 0.2 select_reduce_fusion.3
  31.3 0.1 copy.69
  31.4 0.1 copy.73
  31.5 0.1 copy.77
  31.6 0.0 copy-done.4
  31.6 0.0 copy-done.5
  31.7 0.0 copy-done.2
  31.7 0.8 pad_maximum_fusion
  32.5 31.3 %all-to-all-done.2 = bf16[8,6,64,256]{3,2,1,0:T(8,128)(2,1)S(1)} async-done(((bf16[8,6,64,256]{3,2,1,0:T(8,128)(2,1)}), bf16[8,6,64,256]{3,2,1,0:T(8,128)(2,1)S(1)}, u32[]{:S(2)}, u32[]{:S(2)}) %all-to-all-start.2) | async-done | bytes 1572896 | tf_op jit(solution)/shard_map/all_to_all | solution.py:263
  63.8 7.3 %all-to-all-start = ((bf16[4,136,512]{2,1,0:T(8,128)(2,1)}), bf16[4,136,512]{2,1,0:T(8,128)(2,1)S(1)}, u32[]{:S(2)}, u32[]{:S(2)}) async-start(bf16[4,136,512]{2,1,0:T(8,128)(2,1)} %pad_maximum_fusion), calls=%async_computation | async-start | bytes 1114112 | tf_op jit(solution)/shard_map/all_to_all | solution.py:285
  71.1 0.1 collective-permute-start
  71.2 0.1 convert_reduce_fusion
  71.4 0.1 select_reduce_fusion.1
  71.5 0.6 reshape.468.kown_ref
  72.2 0.9 copy.84.rown_ref
  73.0 0.7 stack.16.ranges_ref
  73.7 0.7 pad_add_fusion.1.meta_ref
  74.4 0.6 multiply_add_fusion.1.slots_ref
  74.9 0.0 collective-permute-done
  74.9 0.0 copy-done.1
  74.9 18.3 %shard_map.165 = bf16[512,512]{1,0:T(8,128)(2,1)} custom-call(s32[4,5]{1,0:T(4,128)} %stack.16.ranges_ref, s32[48]{0:T(128)} %multiply_add_fusion.1.slots_ref, s32[2]{0:T(128)} %pad_add_fusion.1.meta_ref, bf16[512,512]{1,0:T(8,128)(2,1)} %q_ref.1, bf16[48,64,256]{2,1,0:T(8,128)(2,1)} %bitcast.50, bf16[48,64,256]{2,1,0:T(8,128)(2,1)} %bitcast.17.partner_ref, ...), custom_call_target="tpu_custom_call" | custom-call | tf_op jit(solution)/shard_map/pallas_call | solution.py:177
  93.3 2.1 %copy.85 = bf16[4,128,512]{1,2,0:T(8,128)(2,1)} copy(bf16[4,128,512]{2,1,0:T(8,128)(2,1)} %bitcast.55) | data formatting | bytes 1048576 | tf_op jit(solution)/shard_map/all_to_all | solution.py:291
  95.4 0.0 all-to-all-done
  95.4 3.9 %all-to-all-start.3 = ((bf16[4,128,512]{1,2,0:T(8,128)(2,1)}), bf16[4,128,512]{1,2,0:T(8,128)(2,1)S(1)}, u32[]{:S(2)}, u32[]{:S(2)}) async-start(bf16[4,128,512]{1,2,0:T(8,128)(2,1)} %copy.85), calls=%async_computation.3 | async-start | bytes 1048576 | tf_op jit(solution)/shard_map/all_to_all | solution.py:291
  99.2 0.1 convert_bitcast_fusion
  99.4 0.1 copy.90
  99.5 10.7 %all-to-all-done.3 = bf16[4,128,512]{1,2,0:T(8,128)(2,1)S(1)} async-done(((bf16[4,128,512]{1,2,0:T(8,128)(2,1)}), bf16[4,128,512]{1,2,0:T(8,128)(2,1)S(1)}, u32[]{:S(2)}, u32[]{:S(2)}) %all-to-all-start.3) | async-done | bytes 524320 | tf_op jit(solution)/shard_map/all_to_all | solution.py:291
  110.2 4.7 %multiply_reduce_fusion.1 = (f32[128]{0:T(128)S(1)}, f32[128,2048]{1,0:T(8,128)S(1)}) fusion(bf16[128,2048]{0,1:T(8,128)(2,1)S(1)} %bitcast.52, bf16[2048,2048]{1,0:T(8,128)(2,1)} %all-gather.4.cloned.1.call-done), kind=kOutput, calls=%fused_computation.5 | convolution fusion | flops 1074265984 | bytes 9961984 | tf_op jit(solution)/shard_map/dot_general | solution.py:294
  115.0 0.2 add_convert_fusion.1
  115.2 0.0 all-gather.6.cloned.1.call-done
  115.2 0.0 all-gather.8.cloned.1.call-done
  115.3 2.5 %multiply_reduce_fusion = (f32[128]{0:T(128)S(1)}, f32[128,2048]{1,0:T(8,128)S(1)}) fusion(bf16[256,2048]{1,0:T(8,128)(2,1)} %all-gather.8.cloned.1.call-done, bf16[512,256]{1,0:T(8,128)(2,1)} %param.31, s32[]{:T(128)S(6)} %select_n.137, bf16[128,2048]{1,0:T(8,128)(2,1)S(1)} %add_convert_fusion.1, bf16[2048,256]{1,0:T(8,128)(2,1)} %all-gather.6.cloned.1.call-done), kind=kOutput, calls=%fused_computation.3 | convolution fusion | flops 269320064 | bytes 3736068 | tf_op jit(solution)/shard_map/dot_general | solution.py:306
  117.7 0.2 add_convert_fusion
  118.0 10.8 %all_to_all.62 = bf16[128,4,512]{2,0,1:T(8,128)(2,1)S(1)} all-to-all(bf16[128,4,512]{2,0,1:T(8,128)(2,1)S(1)} %bitcast.57), channel_id=1, replica_groups=mesh['req'=8,'tp'=4] {'tp'}, dimensions={1} | all-to-all | bytes 1048576 | tf_op jit(solution)/shard_map/all_to_all | solution.py:314
  128.8 0.8 copy.101
  (36 shorter events, 0.3 us)
Async XLA Ops:
  6.5 103.7 %all-gather.4.cloned.1.call-start = ((), (), s32[]{:S(2)}) async-start(), calls=%async_computation.5 | async-start | bytes 10485760 | tf_op jit(solution)/shard_map/all_gather | solution.py:277
  6.5 13.5 %copy-start = (bf16[48,64,512]{2,1,0:T(8,128)(2,1)S(1)}, bf16[48,64,512]{2,1,0:T(8,128)(2,1)}, u32[]{:S(2)}) copy-start(bf16[48,64,512]{2,1,0:T(8,128)(2,1)} %param.28) | copy-start | bytes 9437188
  6.5 0.8 copy-start.9
  6.5 1.0 copy-start.7
  8.4 11.6 %all-to-all-start.1 = ((s32[8,1,6]{2,1,0:T(1,128)}), s32[8,1,6]{2,1,0:T(1,128)S(1)}, u32[]{:S(2)}, u32[]{:S(2)}) async-start(s32[8,1,6]{2,1,0:T(1,128)} %copy.82), calls=%async_computation.1 | async-start | bytes 8192 | tf_op jit(solution)/shard_map/all_to_all | solution.py:250
  14.8 100.4 %all-gather.6.cloned.1.call-start = ((), (), s32[]{:S(2)}) async-start(), calls=%async_computation.6 | async-start | bytes 1310720 | tf_op jit(solution)/shard_map/all_gather | solution.py:278
  25.9 4.5 %copy-start.8 = (s32[1,8]{1,0:T(1,128)S(1)}, s32[1,8]{1,0:T(1,128)}, u32[]{:S(2)}) copy-start(s32[1,8]{1,0:T(1,128)} %param.39) | copy-start | bytes 100
  25.9 5.0 %copy-start.3 = (s32[1,8]{1,0:T(1,128)S(1)}, s32[1,8]{1,0:T(1,128)}, u32[]{:S(2)}) copy-start(s32[1,8]{1,0:T(1,128)} %param.37) | copy-start | bytes 100
  25.9 5.2 %copy-start.6 = (s32[1,8]{1,0:T(1,128)S(1)}, s32[1,8]{1,0:T(1,128)}, u32[]{:S(2)}) copy-start(s32[1,8]{1,0:T(1,128)} %param.38) | copy-start | bytes 100
  25.9 5.7 %copy-start.4 = (bf16[512]{0:T(512)(128)(2,1)S(1)}, bf16[512]{0:T(512)(128)(2,1)}, u32[]{:S(2)}) copy-start(bf16[512]{0:T(512)(128)(2,1)} %param.30) | copy-start | bytes 3076
  25.9 5.7 %copy-start.5 = (bf16[512]{0:T(512)(128)(2,1)S(1)}, bf16[512]{0:T(512)(128)(2,1)}, u32[]{:S(2)}) copy-start(bf16[512]{0:T(512)(128)(2,1)} %param.34) | copy-start | bytes 3076
  25.9 5.8 %copy-start.2 = (bf16[512,512]{1,0:T(8,128)(2,1)S(1)}, bf16[512,512]{1,0:T(8,128)(2,1)}, u32[]{:S(2)}) copy-start(bf16[512,512]{1,0:T(8,128)(2,1)} %param.23) | copy-start | bytes 1572868
  25.9 37.9 %all-to-all-start.2 = ((bf16[8,6,64,256]{3,2,1,0:T(8,128)(2,1)}), bf16[8,6,64,256]{3,2,1,0:T(8,128)(2,1)S(1)}, u32[]{:S(2)}, u32[]{:S(2)}) async-start(bf16[8,6,64,256]{3,2,1,0:T(8,128)(2,1)} %bitcast.15), calls=%async_computation.2 | async-start | bytes 3145728 | tf_op jit(solution)/shard_map/all_to_all | solution.py:263
  29.6 85.6 %all-gather.8.cloned.1.call-start = ((), (), s32[]{:S(2)}) async-start(), calls=%async_computation.7 | async-start | bytes 1310720 | tf_op jit(solution)/shard_map/all_gather | solution.py:279
  63.8 11.1 %copy-start.1 = (bf16[8,6,64,256]{3,2,1,0:T(8,128)(2,1)}, bf16[8,6,64,256]{3,2,1,0:T(8,128)(2,1)S(1)}, u32[]{:S(2)}) copy-start(bf16[8,6,64,256]{3,2,1,0:T(8,128)(2,1)S(1)} %all-to-all-done.2) | copy-start | bytes 4718596
  63.8 31.5 %all-to-all-start = ((bf16[4,136,512]{2,1,0:T(8,128)(2,1)}), bf16[4,136,512]{2,1,0:T(8,128)(2,1)S(1)}, u32[]{:S(2)}, u32[]{:S(2)}) async-start(bf16[4,136,512]{2,1,0:T(8,128)(2,1)} %pad_maximum_fusion), calls=%async_computation | async-start | bytes 1114112 | tf_op jit(solution)/shard_map/all_to_all | solution.py:285
  71.1 3.8 %collective-permute-start = (bf16[8,6,64,256]{3,2,1,0:T(8,128)(2,1)S(1)}, bf16[8,6,64,256]{3,2,1,0:T(8,128)(2,1)}, u32[]{:S(2)}, u32[]{:S(2)}) collective-permute-start(bf16[8,6,64,256]{3,2,1,0:T(8,128)(2,1)S(1)} %all-to-all-done.2), channel_id=1, source_target_pairs={{0,1},{1,0},{2,3},{3,2},{4,5},{5,4},{6,7},{7,6},{8,9},{9,8},{10,11... | collective-permute-start | bytes 4718600 | tf_op jit(solution)/shard_map/ppermute | solution.py:264
  95.4 14.9 %all-to-all-start.3 = ((bf16[4,128,512]{1,2,0:T(8,128)(2,1)}), bf16[4,128,512]{1,2,0:T(8,128)(2,1)S(1)}, u32[]{:S(2)}, u32[]{:S(2)}) async-start(bf16[4,128,512]{1,2,0:T(8,128)(2,1)} %copy.85), calls=%async_computation.3 | async-start | bytes 1048576 | tf_op jit(solution)/shard_map/all_to_all | solution.py:291
Sparse Core Ops, SparseCore 0:
  8.9 60.7 all-gather.3
  71.3 16.6 all-gather.5
  89.6 19.4 all-gather.7

commit v5 on v4

--- a/solution.py
+++ b/solution.py
@@ -211,6 +211,33 @@
     )
 
 
+def rows_to_columns(x, axis_name):
+    count = lax.axis_size(axis_name)
+    me = lax.axis_index(axis_name)
+    parts = x.reshape(count, x.shape[0] // count, x.shape[1])
+    received = [parts[me]]
+    for shift in range(1, count):
+        outgoing = lax.dynamic_index_in_dim(parts, (me + shift) % count, 0, keepdims=False)
+        perm = [(i, (i + shift) % count) for i in range(count)]
+        received.append(lax.ppermute(outgoing, axis_name, perm))
+    order = (me - jnp.arange(count, dtype=jnp.int32)) % count
+    blocks = jnp.stack(received)[order]
+    return jnp.transpose(blocks, (1, 0, 2)).reshape(parts.shape[1], count * x.shape[1])
+
+
+def columns_to_rows(x, axis_name):
+    count = lax.axis_size(axis_name)
+    me = lax.axis_index(axis_name)
+    width = x.shape[1] // count
+    received = [lax.dynamic_slice_in_dim(x, me * width, width, 1)]
+    for shift in range(1, count):
+        outgoing = lax.dynamic_slice_in_dim(x, ((me + shift) % count) * width, width, 1)
+        perm = [(i, (i + shift) % count) for i in range(count)]
+        received.append(lax.ppermute(outgoing, axis_name, perm))
+    order = (me - jnp.arange(count, dtype=jnp.int32)) % count
+    return jnp.stack(received)[order].reshape(count * x.shape[0], width)
+
+
 def shards(
     hidden,
     queries,
@@ -255,7 +282,7 @@
     arrival_index = holders * capacity + ranking
 
     def fetch_pages(cache):
-        return lax.dynamic_slice_in_dim(cache, kv_head * HD, HD, 2)[wanted]
+        return cache.reshape(page_total, page_len, -1, HD)[wanted, :, kv_head]
 
     outgoing = lax.cond(
         half == 0, lambda: fetch_pages(cache_keys), lambda: fetch_pages(cache_values)
@@ -282,13 +309,11 @@
     with_gains = jnp.concatenate(
         [hidden_parts, jnp.broadcast_to(gain_rows[None], (tp_size, 8, hidden.shape[1]))], axis=1
     )
-    row_hidden_gains = lax.all_to_all(
-        with_gains.reshape(-1, hidden.shape[1]), "tp", split_axis=0, concat_axis=1, tiled=True
-    )
+    row_hidden_gains = rows_to_columns(with_gains.reshape(-1, hidden.shape[1]), "tp")
     row_hidden = row_hidden_gains[: hidden_parts.shape[1]]
     full_attn_gain = row_hidden_gains[hidden_parts.shape[1]]
     full_ple_gain = row_hidden_gains[hidden_parts.shape[1] + 1]
-    row_attention = lax.all_to_all(attention, "tp", split_axis=0, concat_axis=1, tiled=True)
+    row_attention = rows_to_columns(attention, "tp")
     part_rows = row_attention.shape[0]
     row_ple = lax.dynamic_slice_in_dim(ple_input, tp_index * part_rows, part_rows, 0)
     projected = jnp.dot(row_attention, full_weight, preferred_element_type=jnp.float32)
@@ -311,7 +336,7 @@
         * full_ple_gain.astype(jnp.float32)[None, :]
     )
     row_out = (mixed_state.astype(jnp.float32) + lift_normed).astype(jnp.bfloat16)
-    return lax.all_to_all(row_out, "tp", split_axis=1, concat_axis=0, tiled=True)
+    return columns_to_rows(row_out, "tp")
 
 
 def solution(mesh):

time: 138 us -> 132 us (0.957)
  blocking collectives: 10.8 us -> 0 us
  starting transfers between devices: 21.5 us -> 23.7 us
  local copies, waits for them, and re-layouts: 12.3 us -> 14.4 us
    ppermute x0 -> x9, waiting for transfers between devices: none -> 12.6 us  [the longest x3 6.56 us: columns_to_rows(): received.append(lax.ppermute(outgoing, axis_name, perm))]
    all_to_all x2 -> x0, starting transfers between devices: 11.2 us -> none  [the longest x1 7.29 us: shards(): lax.all_to_all(with_gains.reshape(-1, hidden.shape[1]), 'tp', split_axis=...]
    all_to_all x1 -> x0, blocking collectives: 10.8 us -> none  [shards(): lax.all_to_all(row_out, 'tp', split_axis=1, concat_axis=0, tiled=True)]
    all_to_all x2 -> x0, waiting for transfers between devices: 10.7 us -> none  [the longest x1 10.7 us: shards(): lax.all_to_all(attention, 'tp', split_axis=0, concat_axis=1, tiled=True)]
    ppermute x0 -> x9, starting transfers between devices: none -> 9.71 us  [the longest x6 8.03 us: rows_to_columns(): received.append(lax.ppermute(outgoing, axis_name, perm))]
    all_to_all x1, waiting for transfers between devices: 31.3 us -> 26.9 us  [shards(): lax.all_to_all(outgoing, 'req', split_axis=0, concat_axis=0, tiled=True)]
    all_gather x1, waiting for transfers between devices: 0.02 us -> 4.02 us  [shards(): full_proj_weight = lax.all_gather(ple_proj_weight, 'tp', axis=1, tiled=True)]
    ppermute x1, starting transfers between devices: 0.11 us -> 3.85 us  [shards(): swapped = lax.ppermute(arrived, 'tp', partner)]
  transfers between devices with their start and end apart: 8 -> 15, of which waited for: 3 -> 9; matrix products, arithmetic and copies ran while one was open for 15% -> 16% of each run, Pallas kernels for 13% -> 15%
where the time goes in v5:
time: 132 us; the launch traced here: 131 us
  waiting for transfers between devices  49.5 us (38%)
  starting transfers between devices  23.7 us (18%)
  Pallas kernels  19.6 us (15%)
  local copies, waits for them, and re-layouts  14.4 us (11%)
  between operations  13.5 us (10%)
  matrix products  7.21 us (5%)
  other arithmetic  3.46 us (3%)
    all_to_all x1, waiting for transfers between devices, shards(): lax.all_to_all(outgoing, 'req', split_axis=0, concat_axis=0, tiled=True)  26.9 us
    pallas_call x1, Pallas kernels, sparse_attention(): pl.pallas_call(attention_kernel, grid_spec=pltpu.PrefetchScalarGridSpec(n...  19.6 us
    ppermute x6, starting transfers between devices, rows_to_columns(): received.append(lax.ppermute(outgoing, axis_name, perm))  8.03 us
    ppermute x3, waiting for transfers between devices, columns_to_rows(): received.append(lax.ppermute(outgoing, axis_name, perm))  6.56 us
    all_to_all x1, starting transfers between devices, shards(): lax.all_to_all(request_table, 'req', split_axis=0, concat_axis=0, tiled=T...  6.38 us
    ppermute x6, waiting for transfers between devices, rows_to_columns(): received.append(lax.ppermute(outgoing, axis_name, perm))  6.02 us
    dot_general x1, matrix products, shards(): jnp.dot(row_attention, full_weight, preferred_element_type=jnp.float32)  4.75 us
    gather x1, local copies, waits for them, and re-layouts, fetch_pages(): return cache.reshape(page_total, page_len, -1, HD)[wanted, :, kv_head]  4.66 us
  transfers between devices with their start and end apart: 15, of which 9 were waited for; matrix products, arithmetic and copies ran while one was open for 16% of the time, Pallas kernels for 15%

profile of v5, /device:TPU:1, one launch (start us, length us, event | category | flops | bytes accessed | tf_op | source)
XLA Modules:
  0.0 131.4 jit_solution(5133417937448776991)
XLA Ops:
  6.5 0.7 all-gather.4.cloned.1.call-update
  7.3 0.1 copy-done.9
  7.3 0.2 convert_reduce_fusion.1
  7.6 0.2 select_reduce_fusion.2
  7.8 0.7 copy.95
  8.4 6.4 %all-to-all-start = ((s32[8,1,6]{2,1,0:T(1,128)}), s32[8,1,6]{2,1,0:T(1,128)S(1)}, u32[]{:S(2)}, u32[]{:S(2)}) async-start(s32[8,1,6]{2,1,0:T(1,128)} %copy.95), calls=%async_computation | async-start | bytes 8192 | tf_op jit(solution)/shard_map/all_to_all | solution.py:277
  14.8 0.0 all-gather.6.cloned.1.call-start
  14.9 0.7 all-gather.6.cloned.1.call-update
  15.6 4.5 %all-to-all-done = s32[8,1,6]{2,1,0:T(1,128)S(1)} async-done(((s32[8,1,6]{2,1,0:T(1,128)}), s32[8,1,6]{2,1,0:T(1,128)S(1)}, u32[]{:S(2)}, u32[]{:S(2)}) %all-to-all-start) | async-done | bytes 224 | tf_op jit(solution)/shard_map/all_to_all | solution.py:277
  20.1 0.1 reshape.537
  20.2 2.2 %copy.105 = bf16[48,8,2,8,256]{4,3,1,2,0:T(8,128)(2,1)} copy(bf16[48,8,2,8,256]{4,3,2,1,0:T(8,128)(2,1)S(1)} %bitcast.70) | data formatting | bytes 6291456 | tf_op jit(solution)/shard_map/cond/branch_0_fun/reshape | solution.py:285
  22.4 4.7 %gather_fusion.1 = bf16[48,64,256]{2,1,0:T(8,128)(2,1)} fusion(bf16[48,64,2,256]{3,1,2,0:T(8,128)(2,1)} %bitcast.71, s32[48]{0:T(128)S(1)} %reshape.537), kind=kCustom, calls=%fused_computation.1 | custom fusion | bytes 3146112 | tf_op jit(solution)/shard_map/cond/branch_0_fun/gather | solution.py:285
  27.0 3.7 %all-to-all-start.1 = ((bf16[8,6,64,256]{3,2,1,0:T(8,128)(2,1)}), bf16[8,6,64,256]{3,2,1,0:T(8,128)(2,1)S(1)}, u32[]{:S(2)}, u32[]{:S(2)}) async-start(bf16[8,6,64,256]{3,2,1,0:T(8,128)(2,1)} %bitcast.21), calls=%async_computation.1 | async-start | bytes 3145728 | tf_op jit(solution)/shard_map/all_to_all | solution.py:290
  30.7 0.0 all-gather.8.cloned.1.call-start
  31.0 0.1 fusion.1
  31.0 5.4 %collective-permute-start = (bf16[136,512]{1,0:T(8,128)(2,1)S(1)}, bf16[136,512]{1,0:T(8,128)(2,1)S(1)}, u32[]{:S(2)}, u32[]{:S(2)}) collective-permute-start(bf16[136,512]{1,0:T(8,128)(2,1)S(1)} %get-tuple-element.94), channel_id=1, source_target_pairs={{0,1},{1,2},{2,3},{3,0},{4,5},{5,6},{6,7},{7,4},{8,9},{9,10},{10,1... | collective-permute-start | bytes 417800 | tf_op jit(solution)/shard_map/ppermute | solution.py:222
  36.5 0.5 collective-permute-start.2
  37.0 0.2 reduce-window_clone.1
  37.2 0.1 convert_reduce_fusion.2
  37.3 0.1 slice.48
  37.4 0.1 slice.49
  37.5 0.2 reduce-window_1_clone.1
  37.7 0.1 convert_reduce_fusion
  37.8 0.2 select_reduce_fusion.3
  38.0 26.9 %all-to-all-done.1 = bf16[8,6,64,256]{3,2,1,0:T(8,128)(2,1)S(1)} async-done(((bf16[8,6,64,256]{3,2,1,0:T(8,128)(2,1)}), bf16[8,6,64,256]{3,2,1,0:T(8,128)(2,1)S(1)}, u32[]{:S(2)}, u32[]{:S(2)}) %all-to-all-start.1) | async-done | bytes 1572896 | tf_op jit(solution)/shard_map/all_to_all | solution.py:290
  65.0 3.8 %collective-permute-start.3 = (bf16[8,6,64,256]{3,2,1,0:T(8,128)(2,1)S(1)}, bf16[8,6,64,256]{3,2,1,0:T(8,128)(2,1)}, u32[]{:S(2)}, u32[]{:S(2)}) collective-permute-start(bf16[8,6,64,256]{3,2,1,0:T(8,128)(2,1)S(1)} %all-to-all-done.1), channel_id=1, source_target_pairs={{0,1},{1,0},{2,3},{3,2},{4,5},{5,4},{6,7},{7,6},{8,9},{9,8},{10,11... | collective-permute-start | bytes 4718600 | tf_op jit(solution)/shard_map/ppermute | solution.py:291
  68.8 0.1 copy.86
  68.9 0.1 copy.82
  69.0 0.1 copy.90
  69.1 0.1 select_reduce_fusion.1
  69.3 0.5 multiply_add_fusion.1.slots_ref
  69.8 0.6 pad_add_fusion.1.meta_ref
  70.4 0.6 reshape.522.kown_ref
  71.0 0.8 copy.98.rown_ref
  71.8 0.6 stack.59.ranges_ref
  72.5 0.1 fusion.45
  72.6 0.1 pad_maximum_fusion
  72.7 0.6 gather_fusion
  73.3 0.1 convert_bitcast_fusion
  73.4 0.1 copy.103
  73.6 19.6 %shard_map.165 = bf16[512,512]{1,0:T(8,128)(2,1)} custom-call(s32[4,5]{1,0:T(4,128)} %stack.59.ranges_ref, s32[48]{0:T(128)} %multiply_add_fusion.1.slots_ref, s32[2]{0:T(128)} %pad_add_fusion.1.meta_ref, bf16[512,512]{1,0:T(8,128)(2,1)} %q_ref.1, bf16[48,64,256]{2,1,0:T(8,128)(2,1)} %bitcast.72, bf16[48,64,256]{2,1,0:T(8,128)(2,1)} %bitcast.23.partner_ref, ...), custom_call_target="tpu_custom_call" | custom-call | tf_op jit(solution)/shard_map/pallas_call | solution.py:177
  93.1 1.1 constant_dynamic-slice_fusion.3
  94.3 1.3 collective-permute-start.4
  95.5 0.3 collective-permute-start.5
  95.9 0.5 collective-permute-start.6
  96.4 1.4 %collective-permute-done.4 = bf16[128,512]{1,0:T(8,128)(2,1)S(1)} collective-permute-done((bf16[128,512]{1,0:T(8,128)(2,1)S(1)}, bf16[128,512]{1,0:T(8,128)(2,1)S(1)}, u32[]{:S(2)}, u32[]{:S(2)}) %collective-permute-start.4) | collective-permute-done | bytes 131104 | tf_op jit(solution)/shard_map/ppermute | solution.py:222
  97.8 3.7 %collective-permute-done.5 = bf16[128,512]{1,0:T(8,128)(2,1)S(1)} collective-permute-done((bf16[128,512]{1,0:T(8,128)(2,1)S(1)}, bf16[128,512]{1,0:T(8,128)(2,1)S(1)}, u32[]{:S(2)}, u32[]{:S(2)}) %collective-permute-start.5) | collective-permute-done | bytes 131104 | tf_op jit(solution)/shard_map/ppermute | solution.py:222
  101.5 0.9 collective-permute-done.6
  102.4 0.1 pad_maximum_fusion.1
  102.5 0.6 gather_fusion.2
  103.1 0.3 copy.99
  103.4 0.0 all-gather.4.cloned.1.call-done
  103.4 4.8 %multiply_reduce_fusion.1 = (f32[128]{0:T(128)S(1)}, f32[128,2048]{1,0:T(8,128)S(1)}) fusion(bf16[128,2048]{0,1:T(8,128)(2,1)S(1)} %bitcast.74, bf16[2048,2048]{1,0:T(8,128)(2,1)} %all-gather.4.cloned.1.call-done), kind=kOutput, calls=%fused_computation.13 | convolution fusion | flops 1074265984 | bytes 9961984 | tf_op jit(solution)/shard_map/dot_general | solution.py:319
  108.1 0.2 add_convert_fusion.1
  108.4 4.0 %all-gather.8.cloned.1.call-done = bf16[256,2048]{1,0:T(8,128)(2,1)} async-done(((bf16[256,512]{1,0:T(8,128)(2,1)}), bf16[256,2048]{1,0:T(8,128)(2,1)}) %all-gather.8.cloned.1.call-update) | async-done | bytes 1048592 | tf_op jit(solution)/shard_map/all_gather | solution.py:306
  112.4 2.5 %multiply_reduce_fusion = (f32[128]{0:T(128)S(1)}, f32[128,2048]{1,0:T(8,128)S(1)}) fusion(bf16[256,2048]{1,0:T(8,128)(2,1)} %all-gather.8.cloned.1.call-done, bf16[512,256]{1,0:T(8,128)(2,1)} %param.31, s32[]{:T(128)S(6)} %select_n.229, bf16[128,2048]{1,0:T(8,128)(2,1)S(1)} %add_convert_fusion.1, bf16[2048,256]{1,0:T(8,128)(2,1)} %all-gather.6.cloned.1.call-done), kind=kOutput, calls=%fused_computation.11 | convolution fusion | flops 269320064 | bytes 3736068 | tf_op jit(solution)/shard_map/dot_general | solution.py:331
  114.9 0.2 add_convert_fusion
  115.2 0.3 collective-permute-start.7
  115.5 1.4 %collective-permute-start.8 = (bf16[128,512]{1,0:T(8,128)(2,1)S(1)}, bf16[128,512]{1,0:T(8,128)(2,1)S(1)}, u32[]{:S(2)}, u32[]{:S(2)}) collective-permute-start(bf16[128,512]{1,0:T(8,128)(2,1)S(1)} %get-tuple-element.99), channel_id=1, source_target_pairs={{0,2},{1,3},{2,0},{3,1},{4,6},{5,7},{6,4},{7,5},{8,10},{9,11},{10,... | collective-permute-start | bytes 393224 | tf_op jit(solution)/shard_map/ppermute | solution.py:236
  116.9 1.1 collective-permute-done.7
  118.0 4.7 %collective-permute-done.8 = bf16[128,512]{1,0:T(8,128)(2,1)S(1)} collective-permute-done((bf16[128,512]{1,0:T(8,128)(2,1)S(1)}, bf16[128,512]{1,0:T(8,128)(2,1)S(1)}, u32[]{:S(2)}, u32[]{:S(2)}) %collective-permute-start.8) | collective-permute-done | bytes 131104 | tf_op jit(solution)/shard_map/ppermute | solution.py:236
  122.7 0.8 collective-permute-done.9
  123.4 0.1 pad_maximum_fusion.2
  123.5 1.4 %gather_fusion.3 = bf16[4,128,512]{2,1,0:T(8,128)(2,1)} fusion(bf16[4,128,512]{2,1,0:T(8,128)(2,1)S(1)} %pad_maximum_fusion.2, s32[1024]{0:T(1024)S(1)} %pad_clamp_fusion), kind=kCustom, calls=%fused_computation.3 | custom fusion | bytes 1048592 | tf_op jit(solution)/shard_map/gather | solution.py:238
  (56 shorter events, 0.3 us)
Async XLA Ops:
  6.5 13.5 %copy-start = (bf16[48,64,512]{2,1,0:T(8,128)(2,1)S(1)}, bf16[48,64,512]{2,1,0:T(8,128)(2,1)}, u32[]{:S(2)}) copy-start(bf16[48,64,512]{2,1,0:T(8,128)(2,1)} %param.28) | copy-start | bytes 9437188
  6.5 0.8 copy-start.9
  6.5 1.0 copy-start.7
  6.5 96.8 %all-gather.4.cloned.1.call-start = ((), (), s32[]{:S(2)}) async-start(), calls=%async_computation.2 | async-start | bytes 10485760 | tf_op jit(solution)/shard_map/all_gather | solution.py:304
  8.4 11.6 %all-to-all-start = ((s32[8,1,6]{2,1,0:T(1,128)}), s32[8,1,6]{2,1,0:T(1,128)S(1)}, u32[]{:S(2)}, u32[]{:S(2)}) async-start(s32[8,1,6]{2,1,0:T(1,128)} %copy.95), calls=%async_computation | async-start | bytes 8192 | tf_op jit(solution)/shard_map/all_to_all | solution.py:277
  14.8 93.6 %all-gather.6.cloned.1.call-start = ((), (), s32[]{:S(2)}) async-start(), calls=%async_computation.3 | async-start | bytes 1310720 | tf_op jit(solution)/shard_map/all_gather | solution.py:305
  22.3 8.5 %copy-start.4 = (bf16[512]{0:T(512)(128)(2,1)S(1)}, bf16[512]{0:T(512)(128)(2,1)}, u32[]{:S(2)}) copy-start(bf16[512]{0:T(512)(128)(2,1)} %param.30) | copy-start | bytes 3076
  22.4 8.5 %copy-start.5 = (bf16[512]{0:T(512)(128)(2,1)S(1)}, bf16[512]{0:T(512)(128)(2,1)}, u32[]{:S(2)}) copy-start(bf16[512]{0:T(512)(128)(2,1)} %param.34) | copy-start | bytes 3076
  22.4 8.6 %copy-start.2 = (bf16[512,512]{1,0:T(8,128)(2,1)S(1)}, bf16[512,512]{1,0:T(8,128)(2,1)}, u32[]{:S(2)}) copy-start(bf16[512,512]{1,0:T(8,128)(2,1)} %param.23) | copy-start | bytes 1572868
  22.4 14.6 %copy-start.8 = (s32[1,8]{1,0:T(1,128)S(1)}, s32[1,8]{1,0:T(1,128)}, u32[]{:S(2)}) copy-start(s32[1,8]{1,0:T(1,128)} %param.39) | copy-start | bytes 100
  27.0 10.5 %copy-start.3 = (s32[1,8]{1,0:T(1,128)S(1)}, s32[1,8]{1,0:T(1,128)}, u32[]{:S(2)}) copy-start(s32[1,8]{1,0:T(1,128)} %param.37) | copy-start | bytes 100
  27.0 10.6 %copy-start.6 = (s32[1,8]{1,0:T(1,128)S(1)}, s32[1,8]{1,0:T(1,128)}, u32[]{:S(2)}) copy-start(s32[1,8]{1,0:T(1,128)} %param.38) | copy-start | bytes 100
  27.0 37.9 %all-to-all-start.1 = ((bf16[8,6,64,256]{3,2,1,0:T(8,128)(2,1)}), bf16[8,6,64,256]{3,2,1,0:T(8,128)(2,1)S(1)}, u32[]{:S(2)}, u32[]{:S(2)}) async-start(bf16[8,6,64,256]{3,2,1,0:T(8,128)(2,1)} %bitcast.21), calls=%async_computation.1 | async-start | bytes 3145728 | tf_op jit(solution)/shard_map/all_to_all | solution.py:290
  30.7 81.7 %all-gather.8.cloned.1.call-start = ((), (), s32[]{:S(2)}) async-start(), calls=%async_computation.4 | async-start | bytes 1310720 | tf_op jit(solution)/shard_map/all_gather | solution.py:306
  31.0 41.6 %collective-permute-start = (bf16[136,512]{1,0:T(8,128)(2,1)S(1)}, bf16[136,512]{1,0:T(8,128)(2,1)S(1)}, u32[]{:S(2)}, u32[]{:S(2)}) collective-permute-start(bf16[136,512]{1,0:T(8,128)(2,1)S(1)} %get-tuple-element.94), channel_id=1, source_target_pairs={{0,1},{1,2},{2,3},{3,0},{4,5},{5,6},{6,7},{7,4},{8,9},{9,10},{10,1... | collective-permute-start | bytes 417800 | tf_op jit(solution)/shard_map/ppermute | solution.py:222
  36.5 36.1 %collective-permute-start.1 = (bf16[136,512]{1,0:T(8,128)(2,1)S(1)}, bf16[136,512]{1,0:T(8,128)(2,1)S(1)}, u32[]{:S(2)}, u32[]{:S(2)}) collective-permute-start(bf16[136,512]{1,0:T(8,128)(2,1)S(1)} %get-tuple-element.95), channel_id=1, source_target_pairs={{0,2},{1,3},{2,0},{3,1},{4,6},{5,7},{6,4},{7,5},{8,10},{9,11},{10,... | collective-permute-start | bytes 417800 | tf_op jit(solution)/shard_map/ppermute | solution.py:222
  36.5 36.1 %collective-permute-start.2 = (bf16[136,512]{1,0:T(8,128)(2,1)S(1)}, bf16[136,512]{1,0:T(8,128)(2,1)S(1)}, u32[]{:S(2)}, u32[]{:S(2)}) collective-permute-start(bf16[136,512]{1,0:T(8,128)(2,1)S(1)} %get-tuple-element.96), channel_id=1, source_target_pairs={{0,3},{1,0},{2,1},{3,2},{4,7},{5,4},{6,5},{7,6},{8,11},{9,8},{10,9... | collective-permute-start | bytes 417800 | tf_op jit(solution)/shard_map/ppermute | solution.py:222
  65.0 8.6 %copy-start.1 = (bf16[8,6,64,256]{3,2,1,0:T(8,128)(2,1)}, bf16[8,6,64,256]{3,2,1,0:T(8,128)(2,1)S(1)}, u32[]{:S(2)}) copy-start(bf16[8,6,64,256]{3,2,1,0:T(8,128)(2,1)S(1)} %all-to-all-done.1) | copy-start | bytes 4718596
  65.0 8.6 %collective-permute-start.3 = (bf16[8,6,64,256]{3,2,1,0:T(8,128)(2,1)S(1)}, bf16[8,6,64,256]{3,2,1,0:T(8,128)(2,1)}, u32[]{:S(2)}, u32[]{:S(2)}) collective-permute-start(bf16[8,6,64,256]{3,2,1,0:T(8,128)(2,1)S(1)} %all-to-all-done.1), channel_id=1, source_target_pairs={{0,1},{1,0},{2,3},{3,2},{4,5},{5,4},{6,7},{7,6},{8,9},{9,8},{10,11... | collective-permute-start | bytes 4718600 | tf_op jit(solution)/shard_map/ppermute | solution.py:291
  94.3 3.6 %collective-permute-start.4 = (bf16[128,512]{1,0:T(8,128)(2,1)S(1)}, bf16[128,512]{1,0:T(8,128)(2,1)S(1)}, u32[]{:S(2)}, u32[]{:S(2)}) collective-permute-start(bf16[128,512]{1,0:T(8,128)(2,1)S(1)} %get-tuple-element.104), channel_id=1, source_target_pairs={{0,1},{1,2},{2,3},{3,0},{4,5},{5,6},{6,7},{7,4},{8,9},{9,10},{10,1... | collective-permute-start | bytes 393224 | tf_op jit(solution)/shard_map/ppermute | solution.py:222
  95.5 6.0 %collective-permute-start.5 = (bf16[128,512]{1,0:T(8,128)(2,1)S(1)}, bf16[128,512]{1,0:T(8,128)(2,1)S(1)}, u32[]{:S(2)}, u32[]{:S(2)}) collective-permute-start(bf16[128,512]{1,0:T(8,128)(2,1)S(1)} %get-tuple-element.103), channel_id=1, source_target_pairs={{0,2},{1,3},{2,0},{3,1},{4,6},{5,7},{6,4},{7,5},{8,10},{9,11},{10,... | collective-permute-start | bytes 393224 | tf_op jit(solution)/shard_map/ppermute | solution.py:222
  95.9 6.6 %collective-permute-start.6 = (bf16[128,512]{1,0:T(8,128)(2,1)S(1)}, bf16[128,512]{1,0:T(8,128)(2,1)S(1)}, u32[]{:S(2)}, u32[]{:S(2)}) collective-permute-start(bf16[128,512]{1,0:T(8,128)(2,1)S(1)} %get-tuple-element.102), channel_id=1, source_target_pairs={{0,3},{1,0},{2,1},{3,2},{4,7},{5,4},{6,5},{7,6},{8,11},{9,8},{10,9... | collective-permute-start | bytes 393224 | tf_op jit(solution)/shard_map/ppermute | solution.py:222
  115.2 2.8 %collective-permute-start.7 = (bf16[128,512]{1,0:T(8,128)(2,1)S(1)}, bf16[128,512]{1,0:T(8,128)(2,1)S(1)}, u32[]{:S(2)}, u32[]{:S(2)}) collective-permute-start(bf16[128,512]{1,0:T(8,128)(2,1)S(1)} %get-tuple-element.100), channel_id=1, source_target_pairs={{0,1},{1,2},{2,3},{3,0},{4,5},{5,6},{6,7},{7,4},{8,9},{9,10},{10,1... | collective-permute-start | bytes 393224 | tf_op jit(solution)/shard_map/ppermute | solution.py:236
  115.5 7.2 %collective-permute-start.8 = (bf16[128,512]{1,0:T(8,128)(2,1)S(1)}, bf16[128,512]{1,0:T(8,128)(2,1)S(1)}, u32[]{:S(2)}, u32[]{:S(2)}) collective-permute-start(bf16[128,512]{1,0:T(8,128)(2,1)S(1)} %get-tuple-element.99), channel_id=1, source_target_pairs={{0,2},{1,3},{2,0},{3,1},{4,6},{5,7},{6,4},{7,5},{8,10},{9,11},{10,... | collective-permute-start | bytes 393224 | tf_op jit(solution)/shard_map/ppermute | solution.py:236
  116.9 6.6 %collective-permute-start.9 = (bf16[128,512]{1,0:T(8,128)(2,1)S(1)}, bf16[128,512]{1,0:T(8,128)(2,1)S(1)}, u32[]{:S(2)}, u32[]{:S(2)}) collective-permute-start(bf16[128,512]{1,0:T(8,128)(2,1)S(1)} %get-tuple-element.98), channel_id=1, source_target_pairs={{0,3},{1,0},{2,1},{3,2},{4,7},{5,4},{6,5},{7,6},{8,11},{9,8},{10,9... | collective-permute-start | bytes 393224 | tf_op jit(solution)/shard_map/ppermute | solution.py:236
Sparse Core Ops, SparseCore 0:
  8.9 66.7 all-gather.3
  77.3 16.7 all-gather.5
  95.7 16.7 all-gather.7

commit v6 on v5

--- a/solution.py
+++ b/solution.py
@@ -211,6 +211,24 @@
     )
 
 
+def from_each(parts, axis_name):
+    count = lax.axis_size(axis_name)
+    me = lax.axis_index(axis_name)
+    received = [lax.dynamic_index_in_dim(parts, me, 0, keepdims=False)]
+    for shift in range(1, count):
+        outgoing = lax.dynamic_index_in_dim(parts, (me + shift) % count, 0, keepdims=False)
+        perm = [(i, (i + shift) % count) for i in range(count)]
+        received.append(lax.ppermute(outgoing, axis_name, perm))
+    order = (me - jnp.arange(count, dtype=jnp.int32)) % count
+    return jnp.stack(received)[order]
+
+
+def gather_over(x, axis_name, axis):
+    count = lax.axis_size(axis_name)
+    blocks = from_each(jnp.broadcast_to(x[None], (count,) + x.shape), axis_name)
+    return jnp.concatenate([blocks[j] for j in range(count)], axis=axis)
+
+
 def rows_to_columns(x, axis_name):
     count = lax.axis_size(axis_name)
     me = lax.axis_index(axis_name)
@@ -274,19 +292,18 @@
         ranking[:, None, None] == jnp.arange(capacity, dtype=jnp.int32)[None, None, :]
     )
     request_table = jnp.sum(jnp.where(matched, places[:, None, None] + 1, 0), axis=0) - 1
-    asked = lax.all_to_all(request_table, "req", split_axis=0, concat_axis=0, tiled=True)
+    if req_count <= 8:
+        asked = from_each(request_table, "req")
+    else:
+        asked = lax.all_to_all(request_table, "req", split_axis=0, concat_axis=0, tiled=True)
     wanted = jnp.maximum(asked, 0)
     tp_count = lax.axis_size("tp")
     half = tp_index % 2
     partner = [(i, i ^ 1) for i in range(tp_count)]
     arrival_index = holders * capacity + ranking
 
-    def fetch_pages(cache):
-        return cache.reshape(page_total, page_len, -1, HD)[wanted, :, kv_head]
-
-    outgoing = lax.cond(
-        half == 0, lambda: fetch_pages(cache_keys), lambda: fetch_pages(cache_values)
-    )
+    own_cache = jnp.where(half == 0, cache_keys, cache_values)
+    outgoing = lax.dynamic_slice_in_dim(own_cache, kv_head * HD, HD, 2)[wanted]
     arrived = lax.all_to_all(outgoing, "req", split_axis=0, concat_axis=0, tiled=True)
     swapped = lax.ppermute(arrived, "tp", partner)
     attention = sparse_attention(
@@ -302,8 +319,8 @@
     )
     tp_size = lax.axis_size("tp")
     full_weight = lax.all_gather(out_weight, "tp", axis=0, tiled=True)
-    full_gate_weight = lax.all_gather(ple_gate_weight, "tp", axis=0, tiled=True)
-    full_proj_weight = lax.all_gather(ple_proj_weight, "tp", axis=1, tiled=True)
+    full_gate_weight = gather_over(ple_gate_weight, "tp", 0)
+    full_proj_weight = gather_over(ple_proj_weight, "tp", 1)
     hidden_parts = hidden.reshape(tp_size, -1, hidden.shape[1])
     gain_rows = jnp.zeros((8, hidden.shape[1]), hidden.dtype).at[0].set(attn_gain).at[1].set(ple_gain)
     with_gains = jnp.concatenate(

time: 132 us -> 157 us (1.19)
  starting transfers between devices: 23.7 us -> 34.3 us
  other arithmetic: 3.46 us -> 9.7 us
  local copies, waits for them, and re-layouts: 14.4 us -> 17.8 us
  waiting for transfers between devices: 49.5 us -> 52.9 us
  Pallas kernels: 19.6 us -> 22.3 us
    ppermute x0 -> x13, starting transfers between devices: none -> 16.4 us  [from_each(): received.append(lax.ppermute(outgoing, axis_name, perm))]
    ppermute x0 -> x13, waiting for transfers between devices: none -> 16.2 us  [from_each(): received.append(lax.ppermute(outgoing, axis_name, perm))]
    all_to_all x1 -> x0, starting transfers between devices: 6.38 us -> none  [shards(): lax.all_to_all(request_table, 'req', split_axis=0, concat_axis=0, tiled=T...]
    all_to_all x1 -> x0, waiting for transfers between devices: 4.47 us -> none  [shards(): lax.all_to_all(request_table, 'req', split_axis=0, concat_axis=0, tiled=T...]
    all_gather x2 -> x0, waiting for transfers between devices: 4.04 us -> none  [the longest x1 4.02 us: shards(): full_proj_weight = lax.all_gather(ple_proj_weight, 'tp', axis=1, tiled=True)]
    another operation x2 -> x4, other arithmetic: 0.36 us -> 3.73 us  [the longest x2 3.37 us: from_each(): return jnp.stack(received)[order]]
    squeeze x0 -> x3, local copies, waits for them, and re-layouts: none -> 2.96 us  [the longest x2 2.94 us: gather_over(): return jnp.concatenate([blocks[j] for j in range(count)], axis=axis)]
    select_n x0 -> x2, other arithmetic: none -> 2.89 us  [the longest x1 2.88 us: shards(): own_cache = jnp.where(half == 0, cache_keys, cache_values)]
  transfers between devices with their start and end apart: 15 -> 25, of which waited for: 9 -> 12; matrix products, arithmetic and copies ran while one was open for 16% -> 16% of each run, Pallas kernels for 15% -> 14%
where the time goes in v6:
time: 157 us; the launch traced here: 158 us
  waiting for transfers between devices  52.9 us (34%)
  starting transfers between devices  34.3 us (22%)
  Pallas kernels  22.3 us (14%)
  local copies, waits for them, and re-layouts  17.8 us (11%)
  between operations  13.9 us (9%)
  other arithmetic  9.7 us (6%)
  matrix products  6.69 us (4%)
    all_to_all x1, waiting for transfers between devices, shards(): lax.all_to_all(outgoing, 'req', split_axis=0, concat_axis=0, tiled=True)  25.3 us
    pallas_call x1, Pallas kernels, sparse_attention(): pl.pallas_call(attention_kernel, grid_spec=pltpu.PrefetchScalarGridSpec(n...  22.3 us
    ppermute x13, starting transfers between devices, from_each(): received.append(lax.ppermute(outgoing, axis_name, perm))  16.4 us
    ppermute x13, waiting for transfers between devices, from_each(): received.append(lax.ppermute(outgoing, axis_name, perm))  16.2 us
    ppermute x6, starting transfers between devices, rows_to_columns(): received.append(lax.ppermute(outgoing, axis_name, perm))  6.67 us
    ppermute x3, waiting for transfers between devices, columns_to_rows(): received.append(lax.ppermute(outgoing, axis_name, perm))  5.78 us
    all_to_all x1, starting transfers between devices, shards(): lax.all_to_all(outgoing, 'req', split_axis=0, concat_axis=0, tiled=True)  5.24 us
    ppermute x6, waiting for transfers between devices, rows_to_columns(): received.append(lax.ppermute(outgoing, axis_name, perm))  4.89 us
  transfers between devices with their start and end apart: 25, of which 12 were waited for; matrix products, arithmetic and copies ran while one was open for 16% of the time, Pallas kernels for 14%

profile of v6, /device:TPU:1, one launch (start us, length us, event | category | flops | bytes accessed | tf_op | source)
XLA Modules:
  0.0 157.7 jit_solution(2919010579355485401)
XLA Ops:
  6.5 0.7 all-gather.2.cloned.1.call-update
  7.6 0.2 select_reduce_fusion.2
  7.9 2.1 %collective-permute-start.3 = (s32[6]{0:T(128)S(1)}, s32[6]{0:T(128)S(1)}, u32[]{:S(2)}, u32[]{:S(2)}) collective-permute-start(s32[6]{0:T(128)S(1)} %get-tuple-element.67), channel_id=1, source_target_pairs={{0,4},{4,8},{8,12},{12,16},{16,20},{20,24},{24,28},{28,0},{1,5},{5... | collective-permute-start | bytes 80 | tf_op jit(solution)/shard_map/ppermute | solution.py:221
  10.0 1.3 collective-permute-start.4
  11.3 2.3 %collective-permute-start.5 = (s32[6]{0:T(128)S(1)}, s32[6]{0:T(128)S(1)}, u32[]{:S(2)}, u32[]{:S(2)}) collective-permute-start(s32[6]{0:T(128)S(1)} %get-tuple-element.65), channel_id=1, source_target_pairs={{0,12},{4,16},{8,20},{12,24},{16,28},{20,0},{24,4},{28,8},{1,13},{... | collective-permute-start | bytes 80 | tf_op jit(solution)/shard_map/ppermute | solution.py:221
  13.6 1.0 collective-permute-start.6
  14.5 2.4 %collective-permute-start.7 = (s32[6]{0:T(128)S(1)}, s32[6]{0:T(128)S(1)}, u32[]{:S(2)}, u32[]{:S(2)}) collective-permute-start(s32[6]{0:T(128)S(1)} %get-tuple-element.63), channel_id=1, source_target_pairs={{0,20},{4,24},{8,28},{12,0},{16,4},{20,8},{24,12},{28,16},{1,21},{... | collective-permute-start | bytes 80 | tf_op jit(solution)/shard_map/ppermute | solution.py:221
  16.9 2.9 %dynamic-slice_select_fusion = bf16[48,64,256]{2,1,0:T(8,128)(2,1)S(1)} fusion(bf16[48,64,512]{2,1,0:T(8,128)(2,1)} %param.26, s32[]{:T(128)S(6)} %select_n.329, bf16[48,64,512]{2,1,0:T(8,128)(2,1)} %param.25, pred[]{:T(512)S(6)} %eq.155), kind=kLoop, calls=%fused_computation.7 | loop fusion | flops 786432 | bytes 4718597 | tf_op jit(solution)/shard_map/jit(_where)/select_n | solution.py:305
  19.8 0.7 collective-permute-start.8
  20.5 1.1 collective-permute-start.9
  21.7 0.6 collective-permute-done.8
  22.2 0.7 collective-permute-done.9
  23.0 0.6 gather_fusion.1
  23.6 1.9 %gather_fusion.2 = bf16[48,64,256]{2,1,0:T(8,128)(2,1)} fusion(bf16[48,64,256]{2,1,0:T(8,128)(2,1)S(1)} %dynamic-slice_select_fusion, s32[1024]{0:T(1024)S(1)} %pad_clamp_fusion), kind=kCustom, calls=%fused_computation.2 | custom fusion | bytes 3145920 | tf_op jit(solution)/shard_map/gather | solution.py:306
  25.6 5.2 %all-to-all-start = ((bf16[8,6,64,256]{3,2,1,0:T(8,128)(2,1)}), bf16[8,6,64,256]{3,2,1,0:T(8,128)(2,1)S(1)}, u32[]{:S(2)}, u32[]{:S(2)}) async-start(bf16[8,6,64,256]{3,2,1,0:T(8,128)(2,1)} %bitcast.33), calls=%async_computation | async-start | bytes 3145728 | tf_op jit(solution)/shard_map/all_to_all | solution.py:307
  31.0 5.3 %collective-permute-start = (bf16[136,512]{1,0:T(8,128)(2,1)S(1)}, bf16[136,512]{1,0:T(8,128)(2,1)S(1)}, u32[]{:S(2)}, u32[]{:S(2)}) collective-permute-start(bf16[136,512]{1,0:T(8,128)(2,1)S(1)} %get-tuple-element.50), channel_id=1, source_target_pairs={{0,1},{1,2},{2,3},{3,0},{4,5},{5,6},{6,7},{7,4},{8,9},{9,10},{10,1... | collective-permute-start | bytes 417800 | tf_op jit(solution)/shard_map/ppermute | solution.py:240
  36.3 0.3 collective-permute-start.1
  36.6 0.2 collective-permute-start.2
  36.8 1.5 collective-permute-start.14
  38.3 0.2 reduce-window_clone.1
  38.8 0.2 reduce-window_1_clone.1
  39.0 0.2 select_reduce_fusion.3
  39.8 25.3 %all-to-all-done = bf16[8,6,64,256]{3,2,1,0:T(8,128)(2,1)S(1)} async-done(((bf16[8,6,64,256]{3,2,1,0:T(8,128)(2,1)}), bf16[8,6,64,256]{3,2,1,0:T(8,128)(2,1)S(1)}, u32[]{:S(2)}, u32[]{:S(2)}) %all-to-all-start) | async-done | bytes 1572896 | tf_op jit(solution)/shard_map/all_to_all | solution.py:307
  65.2 3.8 %collective-permute-start.10 = (bf16[8,6,64,256]{3,2,1,0:T(8,128)(2,1)S(1)}, bf16[8,6,64,256]{3,2,1,0:T(8,128)(2,1)}, u32[]{:S(2)}, u32[]{:S(2)}) collective-permute-start(bf16[8,6,64,256]{3,2,1,0:T(8,128)(2,1)S(1)} %all-to-all-done), channel_id=1, source_target_pairs={{0,1},{1,0},{2,3},{3,2},{4,5},{5,4},{6,7},{7,6},{8,9},{9,8},{10,11... | collective-permute-start | bytes 4718600 | tf_op jit(solution)/shard_map/ppermute | solution.py:308
  69.0 0.5 multiply_add_fusion.1.slots_ref
  69.5 0.6 pad_add_fusion.1.meta_ref
  70.1 0.6 reshape.565.kown_ref
  70.7 0.9 copy.73.rown_ref
  71.6 0.6 stack.110.ranges_ref
  72.4 1.3 collective-permute-start.15
  73.7 0.3 collective-permute-start.16
  74.0 1.4 collective-permute-start.17
  75.5 0.6 gather_fusion
  76.2 1.1 copy.75
  77.3 0.3 collective-permute-start.18
  77.6 4.6 %collective-permute-done.15 = bf16[512,256]{1,0:T(8,128)(2,1)} collective-permute-done((bf16[512,256]{1,0:T(8,128)(2,1)S(1)}, bf16[512,256]{1,0:T(8,128)(2,1)}, u32[]{:S(2)}, u32[]{:S(2)}) %collective-permute-start.15) | collective-permute-done | bytes 262176 | tf_op jit(solution)/shard_map/ppermute | solution.py:221
  82.1 0.7 collective-permute-start.19
  82.9 4.9 %collective-permute-done.16 = bf16[512,256]{1,0:T(8,128)(2,1)} collective-permute-done((bf16[512,256]{1,0:T(8,128)(2,1)S(1)}, bf16[512,256]{1,0:T(8,128)(2,1)}, u32[]{:S(2)}, u32[]{:S(2)}) %collective-permute-start.16) | collective-permute-done | bytes 262176 | tf_op jit(solution)/shard_map/ppermute | solution.py:221
  87.8 1.2 pad_maximum_fusion
  89.0 1.7 %gather_fusion.4 = bf16[4,512,256]{2,1,0:T(8,128)(2,1)} fusion(bf16[4,512,256]{2,1,0:T(8,128)(2,1)S(1)} %pad_maximum_fusion, s32[1024]{0:T(1024)S(1)} %pad_clamp_fusion.2), kind=kCustom, calls=%fused_computation.4 | custom fusion | bytes 2097168 | tf_op jit(solution)/shard_map/gather | solution.py:223
  90.6 2.7 %collective-permute-done.18 = bf16[256,512]{1,0:T(8,128)(2,1)} collective-permute-done((bf16[256,512]{1,0:T(8,128)(2,1)S(1)}, bf16[256,512]{1,0:T(8,128)(2,1)}, u32[]{:S(2)}, u32[]{:S(2)}) %collective-permute-start.18) | collective-permute-done | bytes 262176 | tf_op jit(solution)/shard_map/ppermute | solution.py:221
  93.4 2.7 %collective-permute-done.19 = bf16[256,512]{1,0:T(8,128)(2,1)} collective-permute-done((bf16[256,512]{1,0:T(8,128)(2,1)S(1)}, bf16[256,512]{1,0:T(8,128)(2,1)}, u32[]{:S(2)}, u32[]{:S(2)}) %collective-permute-start.19) | collective-permute-done | bytes 262176 | tf_op jit(solution)/shard_map/ppermute | solution.py:221
  96.1 2.2 %pad_maximum_fusion.1 = bf16[4,256,512]{2,1,0:T(8,128)(2,1)} fusion(bf16[1,256,512]{2,1,0:T(8,128)(2,1)} %bitcast.59, bf16[1,256,512]{2,1,0:T(8,128)(2,1)} %bitcast.58, bf16[1,256,512]{2,1,0:T(8,128)(2,1)} %bitcast.57, bf16[1,256,512]{2,1,0:T(8,128)(2,1)S(1)} %bitcast.115), kind=kLoop, calls=%fused_computation.21 | loop fusion | flops 1572864 | bytes 2097152 | tf_op jit(solution)/shard_map/stack | solution.py:223
  98.3 1.8 %gather_fusion.5 = bf16[4,256,512]{2,1,0:T(8,128)(2,1)S(1)} fusion(bf16[4,256,512]{2,1,0:T(8,128)(2,1)} %pad_maximum_fusion.1, s32[1024]{0:T(1024)S(1)} %pad_clamp_fusion.2), kind=kCustom, calls=%fused_computation.5 | custom fusion | bytes 2097168 | tf_op jit(solution)/shard_map/gather | solution.py:223
  100.1 1.9 %slice_bitcast_fusion.7 = (bf16[512,256]{1,0:T(8,128)(2,1)S(1)}, bf16[512,256]{1,0:T(8,128)(2,1)S(1)}, bf16[512,256]{1,0:T(8,128)(2,1)S(1)}, bf16[512,256]{1,0:T(8,128)(2,1)}) fusion(bf16[4,512,256]{2,1,0:T(8,128)(2,1)} %gather_fusion.4), kind=kLoop, calls=%fused_computation.49 | loop fusion | bytes 2097152 | tf_op jit(solution)/shard_map/squeeze | solution.py:229
  102.1 22.3 %shard_map.163 = bf16[512,512]{1,0:T(8,128)(2,1)} custom-call(s32[4,5]{1,0:T(4,128)} %stack.110.ranges_ref, s32[48]{0:T(128)} %multiply_add_fusion.1.slots_ref, s32[2]{0:T(128)} %pad_add_fusion.1.meta_ref, bf16[512,512]{1,0:T(8,128)(2,1)} %q_ref.1, bf16[48,64,256]{2,1,0:T(8,128)(2,1)} %bitcast.106, bf16[48,64,256]{2,1,0:T(8,128)(2,1)} %bitcast.35.partner_ref, ...), custom_call_target="tpu_custom_call" | custom-call | tf_op jit(solution)/shard_map/pallas_call | solution.py:177
  124.4 1.1 constant_dynamic-slice_fusion.3
  125.7 0.7 collective-permute-start.13
  126.4 1.0 slice_bitcast_fusion.3
  127.4 0.5 collective-permute-done.11
  127.9 2.8 %collective-permute-done.12 = bf16[128,512]{1,0:T(8,128)(2,1)S(1)} collective-permute-done((bf16[128,512]{1,0:T(8,128)(2,1)S(1)}, bf16[128,512]{1,0:T(8,128)(2,1)S(1)}, u32[]{:S(2)}, u32[]{:S(2)}) %collective-permute-start.12) | collective-permute-done | bytes 131104 | tf_op jit(solution)/shard_map/ppermute | solution.py:240
  130.7 1.6 %collective-permute-done.13 = bf16[128,512]{1,0:T(8,128)(2,1)S(1)} collective-permute-done((bf16[128,512]{1,0:T(8,128)(2,1)S(1)}, bf16[128,512]{1,0:T(8,128)(2,1)S(1)}, u32[]{:S(2)}, u32[]{:S(2)}) %collective-permute-start.13) | collective-permute-done | bytes 131104 | tf_op jit(solution)/shard_map/ppermute | solution.py:240
  132.4 0.6 gather_fusion.3
  133.0 0.3 copy.74
  133.3 4.8 %multiply_reduce_fusion.1 = (f32[128]{0:T(128)S(1)}, f32[128,2048]{1,0:T(8,128)S(1)}) fusion(bf16[128,2048]{0,1:T(8,128)(2,1)S(1)} %bitcast.108, bf16[2048,2048]{1,0:T(8,128)(2,1)} %all-gather.2.cloned.1.call-done), kind=kOutput, calls=%fused_computation.34 | convolution fusion | flops 1074265984 | bytes 9961984 | tf_op jit(solution)/shard_map/dot_general | solution.py:336
  138.2 0.2 add_convert_fusion.1
  138.4 0.7 copy-done.5
  139.3 1.9 %multiply_reduce_fusion = (f32[128]{0:T(128)S(1)}, f32[128,2048]{1,0:T(8,128)S(1)}) fusion(bf16[256,512]{1,0:T(8,128)(2,1)} %get-tuple-element.46, bf16[256,512]{1,0:T(8,128)(2,1)S(1)} %copy-done.7, bf16[256,512]{1,0:T(8,128)(2,1)S(1)} %copy-done.8, bf16[256,512]{1,0:T(8,128)(2,1)S(1)} %copy-done.6, bf16[128,2048]{1,0:T(8,128)(2,1)S(1)} %add_convert_fusion.1, ...), kind=kOutput, calls=%fused_computation.32 | convolution fusion | flops 277708672 | bytes 3736068 | tf_op jit(solution)/shard_map/dot_general | solution.py:348
  141.2 0.2 add_convert_fusion
  141.6 1.3 collective-permute-start.21
  142.9 0.7 collective-permute-start.22
  143.6 4.7 %collective-permute-done.21 = bf16[128,512]{1,0:T(8,128)(2,1)S(1)} collective-permute-done((bf16[128,512]{1,0:T(8,128)(2,1)S(1)}, bf16[128,512]{1,0:T(8,128)(2,1)S(1)}, u32[]{:S(2)}, u32[]{:S(2)}) %collective-permute-start.21) | collective-permute-done | bytes 131104 | tf_op jit(solution)/shard_map/ppermute | solution.py:254
  148.3 1.1 collective-permute-done.22
  149.5 1.4 gather_fusion.6
  (96 shorter events, 2.6 us)
Async XLA Ops:
  6.5 0.8 copy-start.15
  6.5 1.0 copy-start.13
  6.5 126.7 %all-gather.2.cloned.1.call-start = ((), (), s32[]{:S(2)}) async-start(), calls=%async_computation.1 | async-start | bytes 10485760 | tf_op jit(solution)/shard_map/all_gather | solution.py:321
  7.9 11.9 %collective-permute-start.3 = (s32[6]{0:T(128)S(1)}, s32[6]{0:T(128)S(1)}, u32[]{:S(2)}, u32[]{:S(2)}) collective-permute-start(s32[6]{0:T(128)S(1)} %get-tuple-element.67), channel_id=1, source_target_pairs={{0,4},{4,8},{8,12},{12,16},{16,20},{20,24},{24,28},{28,0},{1,5},{5... | collective-permute-start | bytes 80 | tf_op jit(solution)/shard_map/ppermute | solution.py:221
  10.0 10.5 %collective-permute-start.4 = (s32[6]{0:T(128)S(1)}, s32[6]{0:T(128)S(1)}, u32[]{:S(2)}, u32[]{:S(2)}) collective-permute-start(s32[6]{0:T(128)S(1)} %get-tuple-element.66), channel_id=1, source_target_pairs={{0,8},{4,12},{8,16},{12,20},{16,24},{20,28},{24,0},{28,4},{1,9},{5... | collective-permute-start | bytes 80 | tf_op jit(solution)/shard_map/ppermute | solution.py:221
  11.3 10.4 %collective-permute-start.5 = (s32[6]{0:T(128)S(1)}, s32[6]{0:T(128)S(1)}, u32[]{:S(2)}, u32[]{:S(2)}) collective-permute-start(s32[6]{0:T(128)S(1)} %get-tuple-element.65), channel_id=1, source_target_pairs={{0,12},{4,16},{8,20},{12,24},{16,28},{20,0},{24,4},{28,8},{1,13},{... | collective-permute-start | bytes 80 | tf_op jit(solution)/shard_map/ppermute | solution.py:221
  13.6 8.1 %collective-permute-start.6 = (s32[6]{0:T(128)S(1)}, s32[6]{0:T(128)S(1)}, u32[]{:S(2)}, u32[]{:S(2)}) collective-permute-start(s32[6]{0:T(128)S(1)} %get-tuple-element.64), channel_id=1, source_target_pairs={{0,16},{4,20},{8,24},{12,28},{16,0},{20,4},{24,8},{28,12},{1,17},{... | collective-permute-start | bytes 80 | tf_op jit(solution)/shard_map/ppermute | solution.py:221
  14.5 7.2 %collective-permute-start.7 = (s32[6]{0:T(128)S(1)}, s32[6]{0:T(128)S(1)}, u32[]{:S(2)}, u32[]{:S(2)}) collective-permute-start(s32[6]{0:T(128)S(1)} %get-tuple-element.63), channel_id=1, source_target_pairs={{0,20},{4,24},{8,28},{12,0},{16,4},{20,8},{24,12},{28,16},{1,21},{... | collective-permute-start | bytes 80 | tf_op jit(solution)/shard_map/ppermute | solution.py:221
  19.8 2.4 %collective-permute-start.8 = (s32[6]{0:T(128)S(1)}, s32[6]{0:T(128)S(1)}, u32[]{:S(2)}, u32[]{:S(2)}) collective-permute-start(s32[6]{0:T(128)S(1)} %get-tuple-element.62), channel_id=1, source_target_pairs={{0,24},{4,28},{8,0},{12,4},{16,8},{20,12},{24,16},{28,20},{1,25},{... | collective-permute-start | bytes 80 | tf_op jit(solution)/shard_map/ppermute | solution.py:221
  20.5 2.4 %collective-permute-start.9 = (s32[6]{0:T(128)S(1)}, s32[6]{0:T(128)S(1)}, u32[]{:S(2)}, u32[]{:S(2)}) collective-permute-start(s32[6]{0:T(128)S(1)} %get-tuple-element.61), channel_id=1, source_target_pairs={{0,28},{4,0},{8,4},{12,8},{16,12},{20,16},{24,20},{28,24},{1,29},{... | collective-permute-start | bytes 80 | tf_op jit(solution)/shard_map/ppermute | solution.py:221
  25.5 5.3 %copy-start.10 = (bf16[512]{0:T(512)(128)(2,1)S(1)}, bf16[512]{0:T(512)(128)(2,1)}, u32[]{:S(2)}) copy-start(bf16[512]{0:T(512)(128)(2,1)} %param.28) | copy-start | bytes 3076
  25.5 5.3 %copy-start.11 = (bf16[512]{0:T(512)(128)(2,1)S(1)}, bf16[512]{0:T(512)(128)(2,1)}, u32[]{:S(2)}) copy-start(bf16[512]{0:T(512)(128)(2,1)} %param.32) | copy-start | bytes 3076
  25.5 5.4 %copy-start.2 = (bf16[512,512]{1,0:T(8,128)(2,1)S(1)}, bf16[512,512]{1,0:T(8,128)(2,1)}, u32[]{:S(2)}) copy-start(bf16[512,512]{1,0:T(8,128)(2,1)} %param.21) | copy-start | bytes 1572868
  25.5 11.3 %copy-start.3 = (bf16[512,256]{1,0:T(8,128)(2,1)S(1)}, bf16[512,256]{1,0:T(8,128)(2,1)}, u32[]{:S(2)}) copy-start(bf16[512,256]{1,0:T(8,128)(2,1)} %param.30) | copy-start | bytes 786436
  25.5 12.8 %copy-start.14 = (s32[1,8]{1,0:T(1,128)S(1)}, s32[1,8]{1,0:T(1,128)}, u32[]{:S(2)}) copy-start(s32[1,8]{1,0:T(1,128)} %param.37) | copy-start | bytes 100
  25.5 13.3 %copy-start.9 = (s32[1,8]{1,0:T(1,128)S(1)}, s32[1,8]{1,0:T(1,128)}, u32[]{:S(2)}) copy-start(s32[1,8]{1,0:T(1,128)} %param.35) | copy-start | bytes 100
  25.5 13.5 %copy-start.12 = (s32[1,8]{1,0:T(1,128)S(1)}, s32[1,8]{1,0:T(1,128)}, u32[]{:S(2)}) copy-start(s32[1,8]{1,0:T(1,128)} %param.36) | copy-start | bytes 100
  25.6 48.4 %copy-start.4 = (bf16[256,512]{1,0:T(8,128)(2,1)S(1)}, bf16[256,512]{1,0:T(8,128)(2,1)}, u32[]{:S(2)}) copy-start(bf16[256,512]{1,0:T(8,128)(2,1)} %param.31) | copy-start | bytes 786436
  25.6 39.6 %all-to-all-start = ((bf16[8,6,64,256]{3,2,1,0:T(8,128)(2,1)}), bf16[8,6,64,256]{3,2,1,0:T(8,128)(2,1)S(1)}, u32[]{:S(2)}, u32[]{:S(2)}) async-start(bf16[8,6,64,256]{3,2,1,0:T(8,128)(2,1)} %bitcast.33), calls=%async_computation | async-start | bytes 3145728 | tf_op jit(solution)/shard_map/all_to_all | solution.py:307
  31.0 41.4 %collective-permute-start = (bf16[136,512]{1,0:T(8,128)(2,1)S(1)}, bf16[136,512]{1,0:T(8,128)(2,1)S(1)}, u32[]{:S(2)}, u32[]{:S(2)}) collective-permute-start(bf16[136,512]{1,0:T(8,128)(2,1)S(1)} %get-tuple-element.50), channel_id=1, source_target_pairs={{0,1},{1,2},{2,3},{3,0},{4,5},{5,6},{6,7},{7,4},{8,9},{9,10},{10,1... | collective-permute-start | bytes 417800 | tf_op jit(solution)/shard_map/ppermute | solution.py:240
  36.3 37.3 %collective-permute-start.1 = (bf16[136,512]{1,0:T(8,128)(2,1)S(1)}, bf16[136,512]{1,0:T(8,128)(2,1)S(1)}, u32[]{:S(2)}, u32[]{:S(2)}) collective-permute-start(bf16[136,512]{1,0:T(8,128)(2,1)S(1)} %get-tuple-element.51), channel_id=1, source_target_pairs={{0,2},{1,3},{2,0},{3,1},{4,6},{5,7},{6,4},{7,5},{8,10},{9,11},{10,... | collective-permute-start | bytes 417800 | tf_op jit(solution)/shard_map/ppermute | solution.py:240
  36.6 37.4 %collective-permute-start.2 = (bf16[136,512]{1,0:T(8,128)(2,1)S(1)}, bf16[136,512]{1,0:T(8,128)(2,1)S(1)}, u32[]{:S(2)}, u32[]{:S(2)}) collective-permute-start(bf16[136,512]{1,0:T(8,128)(2,1)S(1)} %get-tuple-element.52), channel_id=1, source_target_pairs={{0,3},{1,0},{2,1},{3,2},{4,7},{5,4},{6,5},{7,6},{8,11},{9,8},{10,9... | collective-permute-start | bytes 417800 | tf_op jit(solution)/shard_map/ppermute | solution.py:240
  36.8 40.5 %collective-permute-start.14 = (bf16[512,256]{1,0:T(8,128)(2,1)S(1)}, bf16[512,256]{1,0:T(8,128)(2,1)S(1)}, u32[]{:S(2)}, u32[]{:S(2)}) collective-permute-start(bf16[512,256]{1,0:T(8,128)(2,1)S(1)} %copy-done.3), channel_id=1, source_target_pairs={{0,1},{1,2},{2,3},{3,0},{4,5},{5,6},{6,7},{7,4},{8,9},{9,10},{10,1... | collective-permute-start | bytes 786440 | tf_op jit(solution)/shard_map/ppermute | solution.py:221
  65.2 12.1 %copy-start = (bf16[8,6,64,256]{3,2,1,0:T(8,128)(2,1)}, bf16[8,6,64,256]{3,2,1,0:T(8,128)(2,1)S(1)}, u32[]{:S(2)}) copy-start(bf16[8,6,64,256]{3,2,1,0:T(8,128)(2,1)S(1)} %all-to-all-done) | copy-start | bytes 4718596
  65.2 36.9 %collective-permute-start.10 = (bf16[8,6,64,256]{3,2,1,0:T(8,128)(2,1)S(1)}, bf16[8,6,64,256]{3,2,1,0:T(8,128)(2,1)}, u32[]{:S(2)}, u32[]{:S(2)}) collective-permute-start(bf16[8,6,64,256]{3,2,1,0:T(8,128)(2,1)S(1)} %all-to-all-done), channel_id=1, source_target_pairs={{0,1},{1,0},{2,3},{3,2},{4,5},{5,4},{6,7},{7,6},{8,9},{9,8},{10,11... | collective-permute-start | bytes 4718600 | tf_op jit(solution)/shard_map/ppermute | solution.py:308
  72.4 9.8 %collective-permute-start.15 = (bf16[512,256]{1,0:T(8,128)(2,1)S(1)}, bf16[512,256]{1,0:T(8,128)(2,1)}, u32[]{:S(2)}, u32[]{:S(2)}) collective-permute-start(bf16[512,256]{1,0:T(8,128)(2,1)S(1)} %copy-done.3), channel_id=1, source_target_pairs={{0,2},{1,3},{2,0},{3,1},{4,6},{5,7},{6,4},{7,5},{8,10},{9,11},{10,... | collective-permute-start | bytes 786440 | tf_op jit(solution)/shard_map/ppermute | solution.py:221
  73.7 14.1 %collective-permute-start.16 = (bf16[512,256]{1,0:T(8,128)(2,1)S(1)}, bf16[512,256]{1,0:T(8,128)(2,1)}, u32[]{:S(2)}, u32[]{:S(2)}) collective-permute-start(bf16[512,256]{1,0:T(8,128)(2,1)S(1)} %copy-done.3), channel_id=1, source_target_pairs={{0,3},{1,0},{2,1},{3,2},{4,7},{5,4},{6,5},{7,6},{8,11},{9,8},{10,9... | collective-permute-start | bytes 786440 | tf_op jit(solution)/shard_map/ppermute | solution.py:221
  74.0 16.6 %collective-permute-start.17 = (bf16[256,512]{1,0:T(8,128)(2,1)S(1)}, bf16[256,512]{1,0:T(8,128)(2,1)}, u32[]{:S(2)}, u32[]{:S(2)}) collective-permute-start(bf16[256,512]{1,0:T(8,128)(2,1)S(1)} %copy-done.4), channel_id=1, source_target_pairs={{0,1},{1,2},{2,3},{3,0},{4,5},{5,6},{6,7},{7,4},{8,9},{9,10},{10,1... | collective-permute-start | bytes 786440 | tf_op jit(solution)/shard_map/ppermute | solution.py:221
  77.3 16.1 %collective-permute-start.18 = (bf16[256,512]{1,0:T(8,128)(2,1)S(1)}, bf16[256,512]{1,0:T(8,128)(2,1)}, u32[]{:S(2)}, u32[]{:S(2)}) collective-permute-start(bf16[256,512]{1,0:T(8,128)(2,1)S(1)} %copy-done.4), channel_id=1, source_target_pairs={{0,2},{1,3},{2,0},{3,1},{4,6},{5,7},{6,4},{7,5},{8,10},{9,11},{10,... | collective-permute-start | bytes 786440 | tf_op jit(solution)/shard_map/ppermute | solution.py:221
  82.1 13.9 %collective-permute-start.19 = (bf16[256,512]{1,0:T(8,128)(2,1)S(1)}, bf16[256,512]{1,0:T(8,128)(2,1)}, u32[]{:S(2)}, u32[]{:S(2)}) collective-permute-start(bf16[256,512]{1,0:T(8,128)(2,1)S(1)} %copy-done.4), channel_id=1, source_target_pairs={{0,3},{1,0},{2,1},{3,2},{4,7},{5,4},{6,5},{7,6},{8,11},{9,8},{10,9... | collective-permute-start | bytes 786440 | tf_op jit(solution)/shard_map/ppermute | solution.py:221
  125.5 2.4 %collective-permute-start.11 = (bf16[128,512]{1,0:T(8,128)(2,1)S(1)}, bf16[128,512]{1,0:T(8,128)(2,1)S(1)}, u32[]{:S(2)}, u32[]{:S(2)}) collective-permute-start(bf16[128,512]{1,0:T(8,128)(2,1)S(1)} %get-tuple-element.60), channel_id=1, source_target_pairs={{0,1},{1,2},{2,3},{3,0},{4,5},{5,6},{6,7},{7,4},{8,9},{9,10},{10,1... | collective-permute-start | bytes 393224 | tf_op jit(solution)/shard_map/ppermute | solution.py:240
  125.6 5.1 %collective-permute-start.12 = (bf16[128,512]{1,0:T(8,128)(2,1)S(1)}, bf16[128,512]{1,0:T(8,128)(2,1)S(1)}, u32[]{:S(2)}, u32[]{:S(2)}) collective-permute-start(bf16[128,512]{1,0:T(8,128)(2,1)S(1)} %get-tuple-element.59), channel_id=1, source_target_pairs={{0,2},{1,3},{2,0},{3,1},{4,6},{5,7},{6,4},{7,5},{8,10},{9,11},{10,... | collective-permute-start | bytes 393224 | tf_op jit(solution)/shard_map/ppermute | solution.py:240
  125.7 6.6 %collective-permute-start.13 = (bf16[128,512]{1,0:T(8,128)(2,1)S(1)}, bf16[128,512]{1,0:T(8,128)(2,1)S(1)}, u32[]{:S(2)}, u32[]{:S(2)}) collective-permute-start(bf16[128,512]{1,0:T(8,128)(2,1)S(1)} %get-tuple-element.58), channel_id=1, source_target_pairs={{0,3},{1,0},{2,1},{3,2},{4,7},{5,4},{6,5},{7,6},{8,11},{9,8},{10,9... | collective-permute-start | bytes 393224 | tf_op jit(solution)/shard_map/ppermute | solution.py:240
  133.3 4.9 %copy-start.1 = (f32[4,16,8,512]{3,2,0,1:T(8,128)S(1)}, f32[4,16,8,512]{3,2,0,1:T(8,128)}, u32[]{:S(2)}) copy-start(f32[4,16,8,512]{3,2,0,1:T(8,128)} %copy.75) | copy-start | bytes 3145732
  138.1 1.0 copy-start.5
  138.1 1.0 copy-start.6
  138.1 1.1 copy-start.7
  138.1 1.2 copy-start.8
  141.5 2.2 %collective-permute-start.20 = (bf16[128,512]{1,0:T(8,128)(2,1)S(1)}, bf16[128,512]{1,0:T(8,128)(2,1)S(1)}, u32[]{:S(2)}, u32[]{:S(2)}) collective-permute-start(bf16[128,512]{1,0:T(8,128)(2,1)S(1)} %get-tuple-element.56), channel_id=1, source_target_pairs={{0,1},{1,2},{2,3},{3,0},{4,5},{5,6},{6,7},{7,4},{8,9},{9,10},{10,1... | collective-permute-start | bytes 393224 | tf_op jit(solution)/shard_map/ppermute | solution.py:254
  141.6 6.7 %collective-permute-start.21 = (bf16[128,512]{1,0:T(8,128)(2,1)S(1)}, bf16[128,512]{1,0:T(8,128)(2,1)S(1)}, u32[]{:S(2)}, u32[]{:S(2)}) collective-permute-start(bf16[128,512]{1,0:T(8,128)(2,1)S(1)} %get-tuple-element.55), channel_id=1, source_target_pairs={{0,2},{1,3},{2,0},{3,1},{4,6},{5,7},{6,4},{7,5},{8,10},{9,11},{10,... | collective-permute-start | bytes 393224 | tf_op jit(solution)/shard_map/ppermute | solution.py:254
  142.9 6.5 %collective-permute-start.22 = (bf16[128,512]{1,0:T(8,128)(2,1)S(1)}, bf16[128,512]{1,0:T(8,128)(2,1)S(1)}, u32[]{:S(2)}, u32[]{:S(2)}) collective-permute-start(bf16[128,512]{1,0:T(8,128)(2,1)S(1)} %get-tuple-element.54), channel_id=1, source_target_pairs={{0,3},{1,0},{2,1},{3,2},{4,7},{5,4},{6,5},{7,6},{8,11},{9,8},{10,9... | collective-permute-start | bytes 393224 | tf_op jit(solution)/shard_map/ppermute | solution.py:254
Sparse Core Ops, SparseCore 0:
  8.9 71.0 all-gather.1

commit v7 on v5

--- a/solution.py
+++ b/solution.py
@@ -301,9 +301,11 @@
         page_counts[0], last_fill[0], row_counts[0], page_total,
     )
     tp_size = lax.axis_size("tp")
-    full_weight = lax.all_gather(out_weight, "tp", axis=0, tiled=True)
-    full_gate_weight = lax.all_gather(ple_gate_weight, "tp", axis=0, tiled=True)
-    full_proj_weight = lax.all_gather(ple_proj_weight, "tp", axis=1, tiled=True)
+    joined = jnp.concatenate([out_weight, ple_gate_weight, ple_proj_weight.T], axis=1)
+    full_joined = lax.all_gather(joined, "tp", axis=0, tiled=True)
+    full_weight = full_joined[:, : out_weight.shape[1]]
+    full_gate_weight = full_joined[:, out_weight.shape[1] : out_weight.shape[1] + ple_gate_weight.shape[1]]
+    full_proj_weight_t = full_joined[:, out_weight.shape[1] + ple_gate_weight.shape[1] :]
     hidden_parts = hidden.reshape(tp_size, -1, hidden.shape[1])
     gain_rows = jnp.zeros((8, hidden.shape[1]), hidden.dtype).at[0].set(attn_gain).at[1].set(ple_gain)
     with_gains = jnp.concatenate(
@@ -328,7 +330,9 @@
     activated = (jax.nn.gelu(gate, approximate=True) * row_ple.astype(jnp.float32)).astype(
         jnp.bfloat16
     )
-    lifted = jnp.dot(activated, full_proj_weight, preferred_element_type=jnp.float32)
+    lifted = lax.dot_general(
+        activated, full_proj_weight_t, (((1,), (1,)), ((), ())), preferred_element_type=jnp.float32
+    )
     lift_squares = jnp.sum(lifted * lifted, axis=1)
     lift_normed = (
         lifted

time: 132 us -> 133 us (level)
  waiting for transfers between devices: 49.5 us -> 44.7 us
  other arithmetic: 3.46 us -> 7.07 us
    all_gather x3 -> x1, waiting for transfers between devices: 4.06 us -> 0.02 us  [shards(): full_joined = lax.all_gather(joined, 'tp', axis=0, tiled=True)]
    concatenate x0 -> x1, other arithmetic: none -> 3.52 us  [shards(): jnp.concatenate([out_weight, ple_gate_weight, ple_proj_weight.T], axis=1)]
    unnamed x3 -> x1, waiting for transfers between devices: 1.42 us -> 0.02 us
  transfers between devices with their start and end apart: 15 -> 13, of which waited for: 9 -> 7; matrix products, arithmetic and copies ran while one was open for 16% -> 12% of each run, Pallas kernels for 15% -> 15%
where the time goes in v7:
time: 133 us; the launch traced here: 132 us
  waiting for transfers between devices  44.7 us (34%)
  starting transfers between devices  23.2 us (17%)
  Pallas kernels  20.3 us (15%)
  local copies, waits for them, and re-layouts  15.6 us (12%)
  between operations  13.8 us (10%)
  matrix products  7.35 us (6%)
  other arithmetic  7.07 us (5%)
    all_to_all x1, waiting for transfers between devices, shards(): lax.all_to_all(outgoing, 'req', split_axis=0, concat_axis=0, tiled=True)  27.6 us
    pallas_call x1, Pallas kernels, sparse_attention(): pl.pallas_call(attention_kernel, grid_spec=pltpu.PrefetchScalarGridSpec(n...  20.3 us
    ppermute x6, starting transfers between devices, rows_to_columns(): received.append(lax.ppermute(outgoing, axis_name, perm))  7.37 us
    all_to_all x1, starting transfers between devices, shards(): lax.all_to_all(request_table, 'req', split_axis=0, concat_axis=0, tiled=T...  6.38 us
    ppermute x6, waiting for transfers between devices, rows_to_columns(): received.append(lax.ppermute(outgoing, axis_name, perm))  6 us
    ppermute x3, waiting for transfers between devices, columns_to_rows(): received.append(lax.ppermute(outgoing, axis_name, perm))  5.78 us
    all_to_all x1, waiting for transfers between devices, shards(): lax.all_to_all(request_table, 'req', split_axis=0, concat_axis=0, tiled=T...  5.24 us
    dot_general x1, matrix products, shards(): jnp.dot(row_attention, full_weight, preferred_element_type=jnp.float32)  4.74 us
  transfers between devices with their start and end apart: 13, of which 7 were waited for; matrix products, arithmetic and copies ran while one was open for 12% of the time, Pallas kernels for 15%

profile of v7, /device:TPU:1, one launch (start us, length us, event | category | flops | bytes accessed | tf_op | source)
XLA Modules:
  0.0 132.0 jit_solution(11772111069529930853)
XLA Ops:
  6.5 0.9 copy-done.3
  7.5 0.1 copy.104
  7.6 0.0 copy-start.8
  7.6 0.0 copy-start
  7.7 3.5 %pad_maximum_fusion = bf16[512,2560]{1,0:T(8,128)(2,1)} fusion(bf16[512,256]{1,0:T(8,128)(2,1)S(1)} %copy.104, bf16[512,256]{1,0:T(8,128)(2,1)} %param.32, bf16[512,2048]{1,0:T(8,128)(2,1)} %param.29), kind=kLoop, calls=%fused_computation.7 | loop fusion | flops 7864320 | bytes 5242880 | tf_op jit(solution)/shard_map/concatenate | solution.py:304
  11.2 0.0 all-gather.2.cloned.1.call-update
  11.2 0.2 convert_reduce_fusion.1
  11.4 0.2 select_reduce_fusion.2
  11.6 0.7 copy.99
  12.3 6.4 %all-to-all-start = ((s32[8,1,6]{2,1,0:T(1,128)}), s32[8,1,6]{2,1,0:T(1,128)S(1)}, u32[]{:S(2)}, u32[]{:S(2)}) async-start(s32[8,1,6]{2,1,0:T(1,128)} %copy.99), calls=%async_computation | async-start | bytes 8192 | tf_op jit(solution)/shard_map/all_to_all | solution.py:277
  18.7 5.2 %all-to-all-done = s32[8,1,6]{2,1,0:T(1,128)S(1)} async-done(((s32[8,1,6]{2,1,0:T(1,128)}), s32[8,1,6]{2,1,0:T(1,128)S(1)}, u32[]{:S(2)}, u32[]{:S(2)}) %all-to-all-start) | async-done | bytes 224 | tf_op jit(solution)/shard_map/all_to_all | solution.py:277
  23.9 0.1 reshape.537
  24.0 2.3 %copy.110 = bf16[48,8,2,8,256]{4,3,1,2,0:T(8,128)(2,1)} copy(bf16[48,8,2,8,256]{4,3,2,1,0:T(8,128)(2,1)S(1)} %bitcast.68) | data formatting | bytes 6291456 | tf_op jit(solution)/shard_map/cond/branch_0_fun/reshape | solution.py:285
  26.3 4.7 %gather_fusion.1 = bf16[48,64,256]{2,1,0:T(8,128)(2,1)} fusion(bf16[48,64,2,256]{3,1,2,0:T(8,128)(2,1)} %bitcast.69, s32[48]{0:T(128)S(1)} %reshape.537), kind=kCustom, calls=%fused_computation.1 | custom fusion | bytes 3146112 | tf_op jit(solution)/shard_map/cond/branch_0_fun/gather | solution.py:285
  31.0 3.6 %all-to-all-start.1 = ((bf16[8,6,64,256]{3,2,1,0:T(8,128)(2,1)}), bf16[8,6,64,256]{3,2,1,0:T(8,128)(2,1)S(1)}, u32[]{:S(2)}, u32[]{:S(2)}) async-start(bf16[8,6,64,256]{3,2,1,0:T(8,128)(2,1)} %bitcast.21), calls=%async_computation.1 | async-start | bytes 3145728 | tf_op jit(solution)/shard_map/all_to_all | solution.py:290
  34.8 0.1 fusion.7
  34.9 4.9 %collective-permute-start = (bf16[136,512]{1,0:T(8,128)(2,1)S(1)}, bf16[136,512]{1,0:T(8,128)(2,1)S(1)}, u32[]{:S(2)}, u32[]{:S(2)}) collective-permute-start(bf16[136,512]{1,0:T(8,128)(2,1)S(1)} %get-tuple-element.94), channel_id=1, source_target_pairs={{0,1},{1,2},{2,3},{3,0},{4,5},{5,6},{6,7},{7,4},{8,9},{9,10},{10,1... | collective-permute-start | bytes 417800 | tf_op jit(solution)/shard_map/ppermute | solution.py:222
  39.8 0.4 collective-permute-start.2
  40.2 0.2 reduce-window_clone.1
  40.4 0.1 convert_reduce_fusion.2
  40.5 0.1 slice.57
  40.6 0.1 slice.58
  40.7 0.2 reduce-window_1_clone.1
  40.9 0.1 convert_reduce_fusion
  41.0 0.2 select_reduce_fusion.3
  41.2 27.6 %all-to-all-done.1 = bf16[8,6,64,256]{3,2,1,0:T(8,128)(2,1)S(1)} async-done(((bf16[8,6,64,256]{3,2,1,0:T(8,128)(2,1)}), bf16[8,6,64,256]{3,2,1,0:T(8,128)(2,1)S(1)}, u32[]{:S(2)}, u32[]{:S(2)}) %all-to-all-start.1) | async-done | bytes 1572896 | tf_op jit(solution)/shard_map/all_to_all | solution.py:290
  68.9 3.8 %collective-permute-start.3 = (bf16[8,6,64,256]{3,2,1,0:T(8,128)(2,1)S(1)}, bf16[8,6,64,256]{3,2,1,0:T(8,128)(2,1)}, u32[]{:S(2)}, u32[]{:S(2)}) collective-permute-start(bf16[8,6,64,256]{3,2,1,0:T(8,128)(2,1)S(1)} %all-to-all-done.1), channel_id=1, source_target_pairs={{0,1},{1,0},{2,3},{3,2},{4,5},{5,4},{6,7},{7,6},{8,9},{9,8},{10,11... | collective-permute-start | bytes 4718600 | tf_op jit(solution)/shard_map/ppermute | solution.py:291
  72.7 0.1 copy.90
  72.8 0.1 copy.86
  72.9 0.1 copy.94
  73.0 0.1 select_reduce_fusion.1
  73.1 0.6 multiply_add_fusion.1.slots_ref
  73.7 0.7 pad_add_fusion.1.meta_ref
  74.4 0.6 reshape.522.kown_ref
  75.0 0.9 copy.102.rown_ref
  75.9 0.6 stack.59.ranges_ref
  76.5 0.1 fusion.58
  76.7 0.1 pad_maximum_fusion.1
  76.7 0.6 gather_fusion
  77.3 0.1 convert_bitcast_fusion
  77.5 0.1 copy.108
  77.6 20.3 %shard_map.165 = bf16[512,512]{1,0:T(8,128)(2,1)} custom-call(s32[4,5]{1,0:T(4,128)} %stack.59.ranges_ref, s32[48]{0:T(128)} %multiply_add_fusion.1.slots_ref, s32[2]{0:T(128)} %pad_add_fusion.1.meta_ref, bf16[512,512]{1,0:T(8,128)(2,1)} %q_ref.1, bf16[48,64,256]{2,1,0:T(8,128)(2,1)} %bitcast.70, bf16[48,64,256]{2,1,0:T(8,128)(2,1)} %bitcast.23.partner_ref, ...), custom_call_target="tpu_custom_call" | custom-call | tf_op jit(solution)/shard_map/pallas_call | solution.py:177
  97.9 1.1 constant_dynamic-slice_fusion.3
  99.0 1.2 collective-permute-start.4
  100.2 0.3 collective-permute-start.5
  100.5 0.6 collective-permute-start.6
  101.1 1.5 %collective-permute-done.4 = bf16[128,512]{1,0:T(8,128)(2,1)S(1)} collective-permute-done((bf16[128,512]{1,0:T(8,128)(2,1)S(1)}, bf16[128,512]{1,0:T(8,128)(2,1)S(1)}, u32[]{:S(2)}, u32[]{:S(2)}) %collective-permute-start.4) | collective-permute-done | bytes 131104 | tf_op jit(solution)/shard_map/ppermute | solution.py:222
  102.5 3.5 %collective-permute-done.5 = bf16[128,512]{1,0:T(8,128)(2,1)S(1)} collective-permute-done((bf16[128,512]{1,0:T(8,128)(2,1)S(1)}, bf16[128,512]{1,0:T(8,128)(2,1)S(1)}, u32[]{:S(2)}, u32[]{:S(2)}) %collective-permute-start.5) | collective-permute-done | bytes 131104 | tf_op jit(solution)/shard_map/ppermute | solution.py:222
  106.1 1.0 collective-permute-done.6
  107.1 0.1 pad_maximum_fusion.2
  107.1 0.6 gather_fusion.2
  107.7 0.3 copy.103
  108.0 0.0 all-gather.2.cloned.1.call-done
  108.0 4.7 %multiply_reduce_fusion.1 = (f32[128]{0:T(128)S(1)}, f32[128,2048]{1,0:T(8,128)S(1)}) fusion(bf16[128,2048]{0,1:T(8,128)(2,1)S(1)} %bitcast.77, bf16[2048,2560]{1,0:T(8,128)(2,1)} %all-gather.2.cloned.1.call-done), kind=kOutput, calls=%fused_computation.20 | convolution fusion | flops 1074265984 | bytes 9961984 | tf_op jit(solution)/shard_map/dot_general | solution.py:321
  112.8 0.2 add_convert_fusion.1
  113.0 2.6 %multiply_reduce_fusion = (f32[128]{0:T(128)S(1)}, f32[128,2048]{1,0:T(8,128)S(1)}) fusion(bf16[2048,2560]{1,0:T(8,128)(2,1)} %all-gather.2.cloned.1.call-done, bf16[128,2048]{1,0:T(8,128)(2,1)S(1)} %add_convert_fusion.1, bf16[512,256]{1,0:T(8,128)(2,1)} %param.31, s32[]{:T(128)S(6)} %select_n.229), kind=kOutput, calls=%fused_computation.18 | convolution fusion | flops 269320064 | bytes 3736068 | tf_op jit(solution)/shard_map/dot_general | solution.py:333
  115.6 0.2 add_convert_fusion
  115.9 0.1 collective-permute-start.7
  116.0 1.3 collective-permute-start.8
  117.2 0.7 collective-permute-start.9
  118.0 4.5 %collective-permute-done.8 = bf16[128,512]{1,0:T(8,128)(2,1)S(1)} collective-permute-done((bf16[128,512]{1,0:T(8,128)(2,1)S(1)}, bf16[128,512]{1,0:T(8,128)(2,1)S(1)}, u32[]{:S(2)}, u32[]{:S(2)}) %collective-permute-start.8) | collective-permute-done | bytes 131104 | tf_op jit(solution)/shard_map/ppermute | solution.py:236
  122.5 1.2 collective-permute-done.9
  123.7 0.1 pad_maximum_fusion.3
  123.8 1.4 %gather_fusion.3 = bf16[4,128,512]{2,1,0:T(8,128)(2,1)} fusion(bf16[4,128,512]{2,1,0:T(8,128)(2,1)S(1)} %pad_maximum_fusion.3, s32[1024]{0:T(1024)S(1)} %pad_clamp_fusion), kind=kCustom, calls=%fused_computation.3 | custom fusion | bytes 1048592 | tf_op jit(solution)/shard_map/gather | solution.py:238
  (54 shorter events, 0.3 us)
Async XLA Ops:
  6.5 0.9 copy-start.3
  6.5 101.5 %all-gather.2.cloned.1.call-start = ((), (), s32[]{:S(2)}) async-start(), calls=%async_computation.2 | async-start | bytes 13107200 | tf_op jit(solution)/shard_map/all_gather | solution.py:305
  7.6 3.6 %copy-start.10 = (s32[48,1]{0,1:T(1,128)S(1)}, s32[48,1]{0,1:T(1,128)}, u32[]{:S(2)}) copy-start(s32[48,1]{0,1:T(1,128)} %param.35) | copy-start | bytes 580
  7.6 3.8 %copy-start.8 = (s32[48,1]{0,1:T(1,128)S(1)}, s32[48,1]{0,1:T(1,128)}, u32[]{:S(2)}) copy-start(s32[48,1]{0,1:T(1,128)} %param.36) | copy-start | bytes 580
  7.6 16.3 %copy-start = (bf16[48,64,512]{2,1,0:T(8,128)(2,1)S(1)}, bf16[48,64,512]{2,1,0:T(8,128)(2,1)}, u32[]{:S(2)}) copy-start(bf16[48,64,512]{2,1,0:T(8,128)(2,1)} %param.28) | copy-start | bytes 9437188
  12.3 11.6 %all-to-all-start = ((s32[8,1,6]{2,1,0:T(1,128)}), s32[8,1,6]{2,1,0:T(1,128)S(1)}, u32[]{:S(2)}, u32[]{:S(2)}) async-start(s32[8,1,6]{2,1,0:T(1,128)} %copy.99), calls=%async_computation | async-start | bytes 8192 | tf_op jit(solution)/shard_map/all_to_all | solution.py:277
  26.3 8.4 %copy-start.5 = (bf16[512]{0:T(512)(128)(2,1)S(1)}, bf16[512]{0:T(512)(128)(2,1)}, u32[]{:S(2)}) copy-start(bf16[512]{0:T(512)(128)(2,1)} %param.30) | copy-start | bytes 3076
  26.3 8.4 %copy-start.6 = (bf16[512]{0:T(512)(128)(2,1)S(1)}, bf16[512]{0:T(512)(128)(2,1)}, u32[]{:S(2)}) copy-start(bf16[512]{0:T(512)(128)(2,1)} %param.34) | copy-start | bytes 3076
  26.3 8.5 %copy-start.2 = (bf16[512,512]{1,0:T(8,128)(2,1)S(1)}, bf16[512,512]{1,0:T(8,128)(2,1)}, u32[]{:S(2)}) copy-start(bf16[512,512]{1,0:T(8,128)(2,1)} %param.23) | copy-start | bytes 1572868
  26.3 13.9 %copy-start.9 = (s32[1,8]{1,0:T(1,128)S(1)}, s32[1,8]{1,0:T(1,128)}, u32[]{:S(2)}) copy-start(s32[1,8]{1,0:T(1,128)} %param.39) | copy-start | bytes 100
  26.3 14.4 %copy-start.4 = (s32[1,8]{1,0:T(1,128)S(1)}, s32[1,8]{1,0:T(1,128)}, u32[]{:S(2)}) copy-start(s32[1,8]{1,0:T(1,128)} %param.37) | copy-start | bytes 100
  26.3 14.6 %copy-start.7 = (s32[1,8]{1,0:T(1,128)S(1)}, s32[1,8]{1,0:T(1,128)}, u32[]{:S(2)}) copy-start(s32[1,8]{1,0:T(1,128)} %param.38) | copy-start | bytes 100
  31.0 37.8 %all-to-all-start.1 = ((bf16[8,6,64,256]{3,2,1,0:T(8,128)(2,1)}), bf16[8,6,64,256]{3,2,1,0:T(8,128)(2,1)S(1)}, u32[]{:S(2)}, u32[]{:S(2)}) async-start(bf16[8,6,64,256]{3,2,1,0:T(8,128)(2,1)} %bitcast.21), calls=%async_computation.1 | async-start | bytes 3145728 | tf_op jit(solution)/shard_map/all_to_all | solution.py:290
  34.9 41.7 %collective-permute-start = (bf16[136,512]{1,0:T(8,128)(2,1)S(1)}, bf16[136,512]{1,0:T(8,128)(2,1)S(1)}, u32[]{:S(2)}, u32[]{:S(2)}) collective-permute-start(bf16[136,512]{1,0:T(8,128)(2,1)S(1)} %get-tuple-element.94), channel_id=1, source_target_pairs={{0,1},{1,2},{2,3},{3,0},{4,5},{5,6},{6,7},{7,4},{8,9},{9,10},{10,1... | collective-permute-start | bytes 417800 | tf_op jit(solution)/shard_map/ppermute | solution.py:222
  39.8 36.9 %collective-permute-start.1 = (bf16[136,512]{1,0:T(8,128)(2,1)S(1)}, bf16[136,512]{1,0:T(8,128)(2,1)S(1)}, u32[]{:S(2)}, u32[]{:S(2)}) collective-permute-start(bf16[136,512]{1,0:T(8,128)(2,1)S(1)} %get-tuple-element.95), channel_id=1, source_target_pairs={{0,2},{1,3},{2,0},{3,1},{4,6},{5,7},{6,4},{7,5},{8,10},{9,11},{10,... | collective-permute-start | bytes 417800 | tf_op jit(solution)/shard_map/ppermute | solution.py:222
  39.8 36.9 %collective-permute-start.2 = (bf16[136,512]{1,0:T(8,128)(2,1)S(1)}, bf16[136,512]{1,0:T(8,128)(2,1)S(1)}, u32[]{:S(2)}, u32[]{:S(2)}) collective-permute-start(bf16[136,512]{1,0:T(8,128)(2,1)S(1)} %get-tuple-element.96), channel_id=1, source_target_pairs={{0,3},{1,0},{2,1},{3,2},{4,7},{5,4},{6,5},{7,6},{8,11},{9,8},{10,9... | collective-permute-start | bytes 417800 | tf_op jit(solution)/shard_map/ppermute | solution.py:222
  68.9 8.7 %copy-start.1 = (bf16[8,6,64,256]{3,2,1,0:T(8,128)(2,1)}, bf16[8,6,64,256]{3,2,1,0:T(8,128)(2,1)S(1)}, u32[]{:S(2)}) copy-start(bf16[8,6,64,256]{3,2,1,0:T(8,128)(2,1)S(1)} %all-to-all-done.1) | copy-start | bytes 4718596
  68.9 8.7 %collective-permute-start.3 = (bf16[8,6,64,256]{3,2,1,0:T(8,128)(2,1)S(1)}, bf16[8,6,64,256]{3,2,1,0:T(8,128)(2,1)}, u32[]{:S(2)}, u32[]{:S(2)}) collective-permute-start(bf16[8,6,64,256]{3,2,1,0:T(8,128)(2,1)S(1)} %all-to-all-done.1), channel_id=1, source_target_pairs={{0,1},{1,0},{2,3},{3,2},{4,5},{5,4},{6,7},{7,6},{8,9},{9,8},{10,11... | collective-permute-start | bytes 4718600 | tf_op jit(solution)/shard_map/ppermute | solution.py:291
  99.0 3.5 %collective-permute-start.4 = (bf16[128,512]{1,0:T(8,128)(2,1)S(1)}, bf16[128,512]{1,0:T(8,128)(2,1)S(1)}, u32[]{:S(2)}, u32[]{:S(2)}) collective-permute-start(bf16[128,512]{1,0:T(8,128)(2,1)S(1)} %get-tuple-element.104), channel_id=1, source_target_pairs={{0,1},{1,2},{2,3},{3,0},{4,5},{5,6},{6,7},{7,4},{8,9},{9,10},{10,1... | collective-permute-start | bytes 393224 | tf_op jit(solution)/shard_map/ppermute | solution.py:222
  100.2 5.8 %collective-permute-start.5 = (bf16[128,512]{1,0:T(8,128)(2,1)S(1)}, bf16[128,512]{1,0:T(8,128)(2,1)S(1)}, u32[]{:S(2)}, u32[]{:S(2)}) collective-permute-start(bf16[128,512]{1,0:T(8,128)(2,1)S(1)} %get-tuple-element.103), channel_id=1, source_target_pairs={{0,2},{1,3},{2,0},{3,1},{4,6},{5,7},{6,4},{7,5},{8,10},{9,11},{10,... | collective-permute-start | bytes 393224 | tf_op jit(solution)/shard_map/ppermute | solution.py:222
  100.5 6.6 %collective-permute-start.6 = (bf16[128,512]{1,0:T(8,128)(2,1)S(1)}, bf16[128,512]{1,0:T(8,128)(2,1)S(1)}, u32[]{:S(2)}, u32[]{:S(2)}) collective-permute-start(bf16[128,512]{1,0:T(8,128)(2,1)S(1)} %get-tuple-element.102), channel_id=1, source_target_pairs={{0,3},{1,0},{2,1},{3,2},{4,7},{5,4},{6,5},{7,6},{8,11},{9,8},{10,9... | collective-permute-start | bytes 393224 | tf_op jit(solution)/shard_map/ppermute | solution.py:222
  115.9 2.0 %collective-permute-start.7 = (bf16[128,512]{1,0:T(8,128)(2,1)S(1)}, bf16[128,512]{1,0:T(8,128)(2,1)S(1)}, u32[]{:S(2)}, u32[]{:S(2)}) collective-permute-start(bf16[128,512]{1,0:T(8,128)(2,1)S(1)} %get-tuple-element.100), channel_id=1, source_target_pairs={{0,1},{1,2},{2,3},{3,0},{4,5},{5,6},{6,7},{7,4},{8,9},{9,10},{10,1... | collective-permute-start | bytes 393224 | tf_op jit(solution)/shard_map/ppermute | solution.py:236
  116.0 6.5 %collective-permute-start.8 = (bf16[128,512]{1,0:T(8,128)(2,1)S(1)}, bf16[128,512]{1,0:T(8,128)(2,1)S(1)}, u32[]{:S(2)}, u32[]{:S(2)}) collective-permute-start(bf16[128,512]{1,0:T(8,128)(2,1)S(1)} %get-tuple-element.99), channel_id=1, source_target_pairs={{0,2},{1,3},{2,0},{3,1},{4,6},{5,7},{6,4},{7,5},{8,10},{9,11},{10,... | collective-permute-start | bytes 393224 | tf_op jit(solution)/shard_map/ppermute | solution.py:236
  117.2 6.5 %collective-permute-start.9 = (bf16[128,512]{1,0:T(8,128)(2,1)S(1)}, bf16[128,512]{1,0:T(8,128)(2,1)S(1)}, u32[]{:S(2)}, u32[]{:S(2)}) collective-permute-start(bf16[128,512]{1,0:T(8,128)(2,1)S(1)} %get-tuple-element.98), channel_id=1, source_target_pairs={{0,3},{1,0},{2,1},{3,2},{4,7},{5,4},{6,5},{7,6},{8,11},{9,8},{10,9... | collective-permute-start | bytes 393224 | tf_op jit(solution)/shard_map/ppermute | solution.py:236
Sparse Core Ops, SparseCore 0:
  11.3 78.6 all-gather.1

commit v8 on v7

--- a/solution.py
+++ b/solution.py
@@ -137,15 +137,11 @@
         )
 
 
-def sparse_attention(
-    queries, own_pages, partner_pages, slots, new_keys, new_values, half, kv_head,
-    page_counts, last_fill, row_counts, page_total,
+def attention_tables(
+    slots, half, kv_head, page_counts, last_fill, row_counts, page_total, page_len, row_total
 ):
-    row_total = queries.shape[0]
-    page_len = own_pages.shape[1]
     ctx_total = page_total * page_len
     key_total = ctx_total + row_total
-    heads = queries.shape[1] // HD
     blocks = row_total // ROW_BLOCK
     chunks = key_total // KEY_CHUNK
     ctx_chunks = ctx_total // KEY_CHUNK
@@ -173,6 +169,21 @@
         [ctx_lo, ctx_n, new_lo, new_n, jnp.full((blocks,), ctx_chunks, jnp.int32)], axis=1
     ).astype(jnp.int32)
     meta = jnp.stack([half, kv_head]).astype(jnp.int32)
+    return (
+        ranges,
+        slots.astype(jnp.int32),
+        meta,
+        key_owner.reshape(chunks, 1, KEY_CHUNK),
+        key_pos.reshape(chunks, 1, KEY_CHUNK),
+        row_owner.reshape(row_total, 1),
+    )
+
+
+def sparse_attention(queries, own_pages, partner_pages, new_keys, new_values, tables):
+    ranges, slots, meta, key_owner, key_pos, row_owner = tables
+    row_total = queries.shape[0]
+    heads = queries.shape[1] // HD
+    blocks = row_total // ROW_BLOCK
     whole = lambda b, r, s, m: (0, 0, 0)
     return pl.pallas_call(
         attention_kernel,
@@ -185,29 +196,29 @@
                 pl.BlockSpec(partner_pages.shape, whole),
                 pl.BlockSpec((row_total, HD), lambda b, r, s, m: (0, m[1])),
                 pl.BlockSpec((row_total, HD), lambda b, r, s, m: (0, m[1])),
-                pl.BlockSpec((chunks, 1, KEY_CHUNK), whole),
-                pl.BlockSpec((chunks, 1, KEY_CHUNK), whole),
+                pl.BlockSpec(key_owner.shape, whole),
+                pl.BlockSpec(key_pos.shape, whole),
                 pl.BlockSpec((ROW_BLOCK, 1), lambda b, r, s, m: (b, 0)),
             ],
             out_specs=pl.BlockSpec((ROW_BLOCK, heads * HD), lambda b, r, s, m: (b, 0)),
             scratch_shapes=[
-                pltpu.VMEM((chunks, heads * ROW_BLOCK, KEY_CHUNK), jnp.float32),
+                pltpu.VMEM((key_owner.shape[0], heads * ROW_BLOCK, KEY_CHUNK), jnp.float32),
                 pltpu.VMEM((heads * ROW_BLOCK, HD), jnp.float32),
             ],
         ),
         out_shape=jax.ShapeDtypeStruct((row_total, heads * HD), jnp.bfloat16),
     )(
         ranges,
-        slots.astype(jnp.int32),
+        slots,
         meta,
         queries,
         own_pages,
         partner_pages,
         new_keys,
         new_values,
-        key_owner.reshape(chunks, 1, KEY_CHUNK),
-        key_pos.reshape(chunks, 1, KEY_CHUNK),
-        row_owner.reshape(row_total, 1),
+        key_owner,
+        key_pos,
+        row_owner,
     )
 
 
@@ -275,30 +286,27 @@
     )
     request_table = jnp.sum(jnp.where(matched, places[:, None, None] + 1, 0), axis=0) - 1
     asked = lax.all_to_all(request_table, "req", split_axis=0, concat_axis=0, tiled=True)
-    wanted = jnp.maximum(asked, 0)
     tp_count = lax.axis_size("tp")
     half = tp_index % 2
     partner = [(i, i ^ 1) for i in range(tp_count)]
     arrival_index = holders * capacity + ranking
-
-    def fetch_pages(cache):
-        return cache.reshape(page_total, page_len, -1, HD)[wanted, :, kv_head]
-
-    outgoing = lax.cond(
-        half == 0, lambda: fetch_pages(cache_keys), lambda: fetch_pages(cache_values)
-    )
+    tables = attention_tables(
+        arrival_index, half, kv_head, page_counts[0], last_fill[0], row_counts[0],
+        page_total, page_len, row_total,
+    )
+    asked, tables = lax.optimization_barrier((asked, tables))
+    wanted = jnp.maximum(asked, 0)
+    own_cache = jnp.where(half == 0, cache_keys, cache_values)
+    outgoing = lax.dynamic_slice_in_dim(own_cache, kv_head * HD, HD, 2)[wanted]
     arrived = lax.all_to_all(outgoing, "req", split_axis=0, concat_axis=0, tiled=True)
     swapped = lax.ppermute(arrived, "tp", partner)
     attention = sparse_attention(
         queries,
         arrived.reshape(-1, page_len, HD),
         swapped.reshape(-1, page_len, HD),
-        arrival_index,
         new_keys,
         new_values,
-        half,
-        kv_head,
-        page_counts[0], last_fill[0], row_counts[0], page_total,
+        tables,
     )
     tp_size = lax.axis_size("tp")
     joined = jnp.concatenate([out_weight, ple_gate_weight, ple_proj_weight.T], axis=1)

time: 133 us -> 141 us (1.060)
  blocking collectives: 0 us -> 41.2 us
  waiting for transfers between devices: 44.7 us -> 24.2 us
  starting transfers between devices: 23.2 us -> 13.7 us
  local copies, waits for them, and re-layouts: 15.6 us -> 9.26 us
  other arithmetic: 7.07 us -> 11.1 us
    all_to_all x0 -> x1, blocking collectives: none -> 41.2 us  [shards(): lax.all_to_all(outgoing, 'req', split_axis=0, concat_axis=0, tiled=True)]
    all_to_all x1 -> x0, waiting for transfers between devices: 27.6 us -> none  [shards(): lax.all_to_all(outgoing, 'req', split_axis=0, concat_axis=0, tiled=True)]
    ppermute x6, waiting for transfers between devices: 6 us -> 18.2 us  [rows_to_columns(): received.append(lax.ppermute(outgoing, axis_name, perm))]
    all_to_all x1, waiting for transfers between devices: 5.24 us -> 0.01 us  [shards(): lax.all_to_all(request_table, 'req', split_axis=0, concat_axis=0, tiled=T...]
    gather x1, local copies, waits for them, and re-layouts: 4.69 us -> 0.66 us  [shards(): outgoing = lax.dynamic_slice_in_dim(own_cache, kv_head * HD, HD, 2)[wanted]]
    all_to_all x1 -> x0, starting transfers between devices: 3.6 us -> none  [shards(): lax.all_to_all(outgoing, 'req', split_axis=0, concat_axis=0, tiled=True)]
    ppermute x6, starting transfers between devices: 7.37 us -> 4.14 us  [rows_to_columns(): received.append(lax.ppermute(outgoing, axis_name, perm))]
    select_n x2 -> x3, other arithmetic: 0.01 us -> 3.08 us  [the longest x1 3.06 us: shards(): own_cache = jnp.where(half == 0, cache_keys, cache_values)]
  transfers between devices with their start and end apart: 13 -> 12, of which waited for: 7 -> 8; matrix products, arithmetic and copies ran while one was open for 12% -> 10% of each run, Pallas kernels for 15% -> 14%
where the time goes in v8:
time: 141 us; the launch traced here: 140 us
  blocking collectives  41.2 us (29%)
  waiting for transfers between devices  24.2 us (17%)
  Pallas kernels  19.7 us (14%)
  between operations  13.8 us (10%)
  starting transfers between devices  13.7 us (10%)
  other arithmetic  11.1 us (8%)
  local copies, waits for them, and re-layouts  9.26 us (7%)
  matrix products  7.36 us (5%)
    all_to_all x1, blocking collectives, shards(): lax.all_to_all(outgoing, 'req', split_axis=0, concat_axis=0, tiled=True)  41.2 us
    pallas_call x1, Pallas kernels, sparse_attention(): pl.pallas_call(attention_kernel, grid_spec=pltpu.PrefetchScalarGridSpec(n...  19.7 us
    ppermute x6, waiting for transfers between devices, rows_to_columns(): received.append(lax.ppermute(outgoing, axis_name, perm))  18.2 us
    all_to_all x1, starting transfers between devices, shards(): lax.all_to_all(request_table, 'req', split_axis=0, concat_axis=0, tiled=T...  6.38 us
    ppermute x3, waiting for transfers between devices, columns_to_rows(): received.append(lax.ppermute(outgoing, axis_name, perm))  6 us
    dot_general x1, matrix products, shards(): jnp.dot(row_attention, full_weight, preferred_element_type=jnp.float32)  4.74 us
    ppermute x6, starting transfers between devices, rows_to_columns(): received.append(lax.ppermute(outgoing, axis_name, perm))  4.14 us
    concatenate x1, other arithmetic, shards(): jnp.concatenate([out_weight, ple_gate_weight, ple_proj_weight.T], axis=1)  3.42 us
  transfers between devices with their start and end apart: 12, of which 8 were waited for; matrix products, arithmetic and copies ran while one was open for 10% of the time, Pallas kernels for 14%

profile of v8, /device:TPU:1, one launch (start us, length us, event | category | flops | bytes accessed | tf_op | source)
XLA Modules:
  0.0 140.3 jit_solution(9161716791058969172)
XLA Ops:
  6.5 1.1 copy.96
  7.6 0.0 copy-start.7
  7.7 3.4 %pad_maximum_fusion = bf16[512,2560]{1,0:T(8,128)(2,1)} fusion(bf16[512,256]{1,0:T(8,128)(2,1)S(1)} %copy.96, bf16[512,256]{1,0:T(8,128)(2,1)} %param.30, bf16[512,2048]{1,0:T(8,128)(2,1)} %param.27), kind=kLoop, calls=%fused_computation.6 | loop fusion | flops 7864320 | bytes 5242880 | tf_op jit(solution)/shard_map/concatenate | solution.py:312
  11.1 0.0 all-gather.2.cloned.1.call-update
  11.1 0.2 convert_reduce_fusion.1
  11.4 0.2 select_reduce_fusion.2
  11.6 0.7 copy.81
  12.2 6.4 %all-to-all-start = ((s32[8,1,6]{2,1,0:T(1,128)}), s32[8,1,6]{2,1,0:T(1,128)S(1)}, u32[]{:S(2)}, u32[]{:S(2)}) async-start(s32[8,1,6]{2,1,0:T(1,128)} %copy.81), calls=%async_computation | async-start | bytes 8192 | tf_op jit(solution)/shard_map/all_to_all | solution.py:288
  18.6 0.2 reduce-window_clone.1
  18.8 0.1 convert_reduce_fusion.2
  18.9 0.1 slice.57
  19.0 0.1 slice.58
  19.1 0.2 reduce-window_1_clone.1
  19.3 0.2 select_reduce_fusion.3
  19.5 0.1 copy.86
  19.6 0.1 copy.82
  19.7 0.1 copy.90
  19.8 0.1 convert_reduce_fusion
  19.9 0.1 select_reduce_fusion.1
  20.1 0.6 reshape.512.kown_ref
  20.7 0.6 pad_add_fusion.1.meta_ref
  21.3 3.1 %dynamic-slice_select_fusion = bf16[48,64,256]{2,1,0:T(8,128)(2,1)S(1)} fusion(bf16[48,64,512]{2,1,0:T(8,128)(2,1)} %param.26, s32[]{:T(128)S(6)} %select_n.231, bf16[48,64,512]{2,1,0:T(8,128)(2,1)} %param.25, pred[]{:T(512)S(6)} %eq.147), kind=kLoop, calls=%fused_computation.7 | loop fusion | flops 786432 | bytes 4718597 | tf_op jit(solution)/shard_map/jit(_where)/select_n | solution.py:299
  24.4 0.6 multiply_add_fusion.1.slots_ref
  25.0 0.6 stack.59.ranges_ref
  25.7 0.1 reshape.531
  25.8 0.7 gather_fusion.1
  26.5 41.2 %all_to_all.14 = bf16[8,6,64,256]{3,2,1,0:T(8,128)(2,1)S(1)} all-to-all(bf16[8,6,64,256]{3,2,1,0:T(8,128)(2,1)S(1)} %bitcast.62), channel_id=1, replica_groups=mesh['req'=8,'tp'=4] {'req'}, dimensions={0} | all-to-all | bytes 3145728 | tf_op jit(solution)/shard_map/all_to_all | solution.py:301
  67.6 2.0 %collective-permute-start.3 = (bf16[8,6,64,256]{3,2,1,0:T(8,128)(2,1)S(1)}, bf16[8,6,64,256]{3,2,1,0:T(8,128)(2,1)}, u32[]{:S(2)}, u32[]{:S(2)}) collective-permute-start(bf16[8,6,64,256]{3,2,1,0:T(8,128)(2,1)S(1)} %all_to_all.14), channel_id=1, source_target_pairs={{0,1},{1,0},{2,3},{3,2},{4,5},{5,4},{6,7},{7,6},{8,9},{9,8},{10,11... | collective-permute-start | bytes 4718600 | tf_op jit(solution)/shard_map/ppermute | solution.py:302
  69.8 1.1 fusion.7
  70.9 1.6 %collective-permute-start = (bf16[136,512]{1,0:T(8,128)(2,1)S(1)}, bf16[136,512]{1,0:T(8,128)(2,1)S(1)}, u32[]{:S(2)}, u32[]{:S(2)}) collective-permute-start(bf16[136,512]{1,0:T(8,128)(2,1)S(1)} %get-tuple-element.56), channel_id=1, source_target_pairs={{0,1},{1,2},{2,3},{3,0},{4,5},{5,6},{6,7},{7,4},{8,9},{9,10},{10,1... | collective-permute-start | bytes 417800 | tf_op jit(solution)/shard_map/ppermute | solution.py:233
  72.6 0.2 collective-permute-start.1
  72.8 0.3 collective-permute-start.2
  73.0 0.1 fusion.55
  73.2 0.9 copy.94.rown_ref
  74.0 4.8 %collective-permute-done = bf16[136,512]{1,0:T(8,128)(2,1)S(1)} collective-permute-done((bf16[136,512]{1,0:T(8,128)(2,1)S(1)}, bf16[136,512]{1,0:T(8,128)(2,1)S(1)}, u32[]{:S(2)}, u32[]{:S(2)}) %collective-permute-start) | collective-permute-done | bytes 139296 | tf_op jit(solution)/shard_map/ppermute | solution.py:233
  78.8 7.0 %collective-permute-done.1 = bf16[136,512]{1,0:T(8,128)(2,1)S(1)} collective-permute-done((bf16[136,512]{1,0:T(8,128)(2,1)S(1)}, bf16[136,512]{1,0:T(8,128)(2,1)S(1)}, u32[]{:S(2)}, u32[]{:S(2)}) %collective-permute-start.1) | collective-permute-done | bytes 139296 | tf_op jit(solution)/shard_map/ppermute | solution.py:233
  85.8 0.6 collective-permute-done.2
  86.4 0.1 pad_maximum_fusion.1
  86.5 0.6 gather_fusion
  87.1 0.1 convert_bitcast_fusion
  87.2 0.1 copy.99
  87.4 19.7 %shard_map.166 = bf16[512,512]{1,0:T(8,128)(2,1)} custom-call(s32[4,5]{1,0:T(4,128)} %stack.59.ranges_ref, s32[48]{0:T(128)} %multiply_add_fusion.1.slots_ref, s32[2]{0:T(128)} %pad_add_fusion.1.meta_ref, bf16[512,512]{1,0:T(8,128)(2,1)} %q_ref.1, bf16[48,64,256]{2,1,0:T(8,128)(2,1)} %bitcast.63, bf16[48,64,256]{2,1,0:T(8,128)(2,1)} %bitcast.24.partner_ref, ...), custom_call_target="tpu_custom_call" | custom-call | tf_op jit(solution)/shard_map/pallas_call | solution.py:188
  107.1 1.1 constant_dynamic-slice_fusion.3
  108.2 0.1 collective-permute-start.4
  108.3 1.2 collective-permute-start.5
  109.5 0.7 collective-permute-start.6
  110.3 4.5 %collective-permute-done.5 = bf16[128,512]{1,0:T(8,128)(2,1)S(1)} collective-permute-done((bf16[128,512]{1,0:T(8,128)(2,1)S(1)}, bf16[128,512]{1,0:T(8,128)(2,1)S(1)}, u32[]{:S(2)}, u32[]{:S(2)}) %collective-permute-start.5) | collective-permute-done | bytes 131104 | tf_op jit(solution)/shard_map/ppermute | solution.py:233
  114.8 1.2 collective-permute-done.6
  116.0 0.1 pad_maximum_fusion.2
  116.1 0.6 gather_fusion.2
  116.7 0.3 copy.95
  116.9 0.0 all-gather.2.cloned.1.call-done
  117.0 4.7 %multiply_reduce_fusion.1 = (f32[128]{0:T(128)S(1)}, f32[128,2048]{1,0:T(8,128)S(1)}) fusion(bf16[128,2048]{0,1:T(8,128)(2,1)S(1)} %bitcast.70, bf16[2048,2560]{1,0:T(8,128)(2,1)} %all-gather.2.cloned.1.call-done), kind=kOutput, calls=%fused_computation.20 | convolution fusion | flops 1074265984 | bytes 9961984 | tf_op jit(solution)/shard_map/dot_general | solution.py:329
  121.7 0.2 add_convert_fusion.1
  121.9 2.6 %multiply_reduce_fusion = (f32[128]{0:T(128)S(1)}, f32[128,2048]{1,0:T(8,128)S(1)}) fusion(bf16[2048,2560]{1,0:T(8,128)(2,1)} %all-gather.2.cloned.1.call-done, bf16[128,2048]{1,0:T(8,128)(2,1)S(1)} %add_convert_fusion.1, bf16[512,256]{1,0:T(8,128)(2,1)} %param.29, s32[]{:T(128)S(6)} %select_n.232), kind=kOutput, calls=%fused_computation.18 | convolution fusion | flops 269320064 | bytes 3736068 | tf_op jit(solution)/shard_map/dot_general | solution.py:341
  124.6 0.2 add_convert_fusion
  124.9 0.1 collective-permute-start.7
  124.9 0.5 collective-permute-start.8
  125.4 0.6 collective-permute-start.9
  126.0 0.9 collective-permute-done.7
  126.9 3.4 %collective-permute-done.8 = bf16[128,512]{1,0:T(8,128)(2,1)S(1)} collective-permute-done((bf16[128,512]{1,0:T(8,128)(2,1)S(1)}, bf16[128,512]{1,0:T(8,128)(2,1)S(1)}, u32[]{:S(2)}, u32[]{:S(2)}) %collective-permute-start.8) | collective-permute-done | bytes 131104 | tf_op jit(solution)/shard_map/ppermute | solution.py:247
  130.3 1.7 %collective-permute-done.9 = bf16[128,512]{1,0:T(8,128)(2,1)S(1)} collective-permute-done((bf16[128,512]{1,0:T(8,128)(2,1)S(1)}, bf16[128,512]{1,0:T(8,128)(2,1)S(1)}, u32[]{:S(2)}, u32[]{:S(2)}) %collective-permute-start.9) | collective-permute-done | bytes 131104 | tf_op jit(solution)/shard_map/ppermute | solution.py:247
  132.0 0.1 pad_maximum_fusion.3
  132.1 1.4 gather_fusion.3
  (46 shorter events, 0.3 us)
Async XLA Ops:
  6.5 110.4 %all-gather.2.cloned.1.call-start = ((), (), s32[]{:S(2)}) async-start(), calls=%async_computation.2 | async-start | bytes 13107200 | tf_op jit(solution)/shard_map/all_gather | solution.py:313
  7.6 3.5 %copy-start.7 = (s32[48,1]{0,1:T(1,128)S(1)}, s32[48,1]{0,1:T(1,128)}, u32[]{:S(2)}) copy-start(s32[48,1]{0,1:T(1,128)} %param.33) | copy-start | bytes 580
  7.6 3.7 %copy-start.5 = (s32[48,1]{0,1:T(1,128)S(1)}, s32[48,1]{0,1:T(1,128)}, u32[]{:S(2)}) copy-start(s32[48,1]{0,1:T(1,128)} %param.34) | copy-start | bytes 580
  7.6 11.0 %copy-start.6 = (s32[1,8]{1,0:T(1,128)S(1)}, s32[1,8]{1,0:T(1,128)}, u32[]{:S(2)}) copy-start(s32[1,8]{1,0:T(1,128)} %param.37) | copy-start | bytes 100
  7.7 11.4 %copy-start.1 = (s32[1,8]{1,0:T(1,128)S(1)}, s32[1,8]{1,0:T(1,128)}, u32[]{:S(2)}) copy-start(s32[1,8]{1,0:T(1,128)} %param.35) | copy-start | bytes 100
  7.7 11.6 %copy-start.4 = (s32[1,8]{1,0:T(1,128)S(1)}, s32[1,8]{1,0:T(1,128)}, u32[]{:S(2)}) copy-start(s32[1,8]{1,0:T(1,128)} %param.36) | copy-start | bytes 100
  12.2 13.4 %all-to-all-start = ((s32[8,1,6]{2,1,0:T(1,128)}), s32[8,1,6]{2,1,0:T(1,128)S(1)}, u32[]{:S(2)}, u32[]{:S(2)}) async-start(s32[8,1,6]{2,1,0:T(1,128)} %copy.81), calls=%async_computation | async-start | bytes 8192 | tf_op jit(solution)/shard_map/all_to_all | solution.py:288
  25.8 43.9 %copy-start.2 = (bf16[512]{0:T(512)(128)(2,1)S(1)}, bf16[512]{0:T(512)(128)(2,1)}, u32[]{:S(2)}) copy-start(bf16[512]{0:T(512)(128)(2,1)} %param.28) | copy-start | bytes 3076
  25.8 43.9 %copy-start.3 = (bf16[512]{0:T(512)(128)(2,1)S(1)}, bf16[512]{0:T(512)(128)(2,1)}, u32[]{:S(2)}) copy-start(bf16[512]{0:T(512)(128)(2,1)} %param.32) | copy-start | bytes 3076
  67.6 19.7 %copy-start = (bf16[8,6,64,256]{3,2,1,0:T(8,128)(2,1)}, bf16[8,6,64,256]{3,2,1,0:T(8,128)(2,1)S(1)}, u32[]{:S(2)}) copy-start(bf16[8,6,64,256]{3,2,1,0:T(8,128)(2,1)S(1)} %all_to_all.14) | copy-start | bytes 4718596
  67.6 19.7 %collective-permute-start.3 = (bf16[8,6,64,256]{3,2,1,0:T(8,128)(2,1)S(1)}, bf16[8,6,64,256]{3,2,1,0:T(8,128)(2,1)}, u32[]{:S(2)}, u32[]{:S(2)}) collective-permute-start(bf16[8,6,64,256]{3,2,1,0:T(8,128)(2,1)S(1)} %all_to_all.14), channel_id=1, source_target_pairs={{0,1},{1,0},{2,3},{3,2},{4,5},{5,4},{6,7},{7,6},{8,9},{9,8},{10,11... | collective-permute-start | bytes 4718600 | tf_op jit(solution)/shard_map/ppermute | solution.py:302
  70.9 7.9 %collective-permute-start = (bf16[136,512]{1,0:T(8,128)(2,1)S(1)}, bf16[136,512]{1,0:T(8,128)(2,1)S(1)}, u32[]{:S(2)}, u32[]{:S(2)}) collective-permute-start(bf16[136,512]{1,0:T(8,128)(2,1)S(1)} %get-tuple-element.56), channel_id=1, source_target_pairs={{0,1},{1,2},{2,3},{3,0},{4,5},{5,6},{6,7},{7,4},{8,9},{9,10},{10,1... | collective-permute-start | bytes 417800 | tf_op jit(solution)/shard_map/ppermute | solution.py:233
  72.6 13.2 %collective-permute-start.1 = (bf16[136,512]{1,0:T(8,128)(2,1)S(1)}, bf16[136,512]{1,0:T(8,128)(2,1)S(1)}, u32[]{:S(2)}, u32[]{:S(2)}) collective-permute-start(bf16[136,512]{1,0:T(8,128)(2,1)S(1)} %get-tuple-element.57), channel_id=1, source_target_pairs={{0,2},{1,3},{2,0},{3,1},{4,6},{5,7},{6,4},{7,5},{8,10},{9,11},{10,... | collective-permute-start | bytes 417800 | tf_op jit(solution)/shard_map/ppermute | solution.py:233
  72.8 13.7 %collective-permute-start.2 = (bf16[136,512]{1,0:T(8,128)(2,1)S(1)}, bf16[136,512]{1,0:T(8,128)(2,1)S(1)}, u32[]{:S(2)}, u32[]{:S(2)}) collective-permute-start(bf16[136,512]{1,0:T(8,128)(2,1)S(1)} %get-tuple-element.58), channel_id=1, source_target_pairs={{0,3},{1,0},{2,1},{3,2},{4,7},{5,4},{6,5},{7,6},{8,11},{9,8},{10,9... | collective-permute-start | bytes 417800 | tf_op jit(solution)/shard_map/ppermute | solution.py:233
  108.2 2.1 %collective-permute-start.4 = (bf16[128,512]{1,0:T(8,128)(2,1)S(1)}, bf16[128,512]{1,0:T(8,128)(2,1)S(1)}, u32[]{:S(2)}, u32[]{:S(2)}) collective-permute-start(bf16[128,512]{1,0:T(8,128)(2,1)S(1)} %get-tuple-element.66), channel_id=1, source_target_pairs={{0,1},{1,2},{2,3},{3,0},{4,5},{5,6},{6,7},{7,4},{8,9},{9,10},{10,1... | collective-permute-start | bytes 393224 | tf_op jit(solution)/shard_map/ppermute | solution.py:233
  108.3 6.5 %collective-permute-start.5 = (bf16[128,512]{1,0:T(8,128)(2,1)S(1)}, bf16[128,512]{1,0:T(8,128)(2,1)S(1)}, u32[]{:S(2)}, u32[]{:S(2)}) collective-permute-start(bf16[128,512]{1,0:T(8,128)(2,1)S(1)} %get-tuple-element.65), channel_id=1, source_target_pairs={{0,2},{1,3},{2,0},{3,1},{4,6},{5,7},{6,4},{7,5},{8,10},{9,11},{10,... | collective-permute-start | bytes 393224 | tf_op jit(solution)/shard_map/ppermute | solution.py:233
  109.5 6.5 %collective-permute-start.6 = (bf16[128,512]{1,0:T(8,128)(2,1)S(1)}, bf16[128,512]{1,0:T(8,128)(2,1)S(1)}, u32[]{:S(2)}, u32[]{:S(2)}) collective-permute-start(bf16[128,512]{1,0:T(8,128)(2,1)S(1)} %get-tuple-element.64), channel_id=1, source_target_pairs={{0,3},{1,0},{2,1},{3,2},{4,7},{5,4},{6,5},{7,6},{8,11},{9,8},{10,9... | collective-permute-start | bytes 393224 | tf_op jit(solution)/shard_map/ppermute | solution.py:233
  124.9 2.0 %collective-permute-start.7 = (bf16[128,512]{1,0:T(8,128)(2,1)S(1)}, bf16[128,512]{1,0:T(8,128)(2,1)S(1)}, u32[]{:S(2)}, u32[]{:S(2)}) collective-permute-start(bf16[128,512]{1,0:T(8,128)(2,1)S(1)} %get-tuple-element.62), channel_id=1, source_target_pairs={{0,1},{1,2},{2,3},{3,0},{4,5},{5,6},{6,7},{7,4},{8,9},{9,10},{10,1... | collective-permute-start | bytes 393224 | tf_op jit(solution)/shard_map/ppermute | solution.py:247
  124.9 5.4 %collective-permute-start.8 = (bf16[128,512]{1,0:T(8,128)(2,1)S(1)}, bf16[128,512]{1,0:T(8,128)(2,1)S(1)}, u32[]{:S(2)}, u32[]{:S(2)}) collective-permute-start(bf16[128,512]{1,0:T(8,128)(2,1)S(1)} %get-tuple-element.61), channel_id=1, source_target_pairs={{0,2},{1,3},{2,0},{3,1},{4,6},{5,7},{6,4},{7,5},{8,10},{9,11},{10,... | collective-permute-start | bytes 393224 | tf_op jit(solution)/shard_map/ppermute | solution.py:247
  125.4 6.6 %collective-permute-start.9 = (bf16[128,512]{1,0:T(8,128)(2,1)S(1)}, bf16[128,512]{1,0:T(8,128)(2,1)S(1)}, u32[]{:S(2)}, u32[]{:S(2)}) collective-permute-start(bf16[128,512]{1,0:T(8,128)(2,1)S(1)} %get-tuple-element.60), channel_id=1, source_target_pairs={{0,3},{1,0},{2,1},{3,2},{4,7},{5,4},{6,5},{7,6},{8,11},{9,8},{10,9... | collective-permute-start | bytes 393224 | tf_op jit(solution)/shard_map/ppermute | solution.py:247
Sparse Core Ops, SparseCore 0:
  11.3 78.7 all-gather.1

commit v9 on v5

--- a/solution.py
+++ b/solution.py
@@ -281,12 +281,8 @@
     partner = [(i, i ^ 1) for i in range(tp_count)]
     arrival_index = holders * capacity + ranking
 
-    def fetch_pages(cache):
-        return cache.reshape(page_total, page_len, -1, HD)[wanted, :, kv_head]
-
-    outgoing = lax.cond(
-        half == 0, lambda: fetch_pages(cache_keys), lambda: fetch_pages(cache_values)
-    )
+    own_cache = jnp.where(half == 0, cache_keys, cache_values)
+    outgoing = lax.dynamic_slice_in_dim(own_cache, kv_head * HD, HD, 2)[wanted]
     arrived = lax.all_to_all(outgoing, "req", split_axis=0, concat_axis=0, tiled=True)
     swapped = lax.ppermute(arrived, "tp", partner)
     attention = sparse_attention(

time: 132 us -> 134 us (1.015)
  waiting for transfers between devices: 49.5 us -> 58.1 us
  local copies, waits for them, and re-layouts: 14.4 us -> 9.47 us
  starting transfers between devices: 23.7 us -> 20.7 us
  other arithmetic: 3.46 us -> 6.1 us
    all_gather x1, waiting for transfers between devices: 4.02 us -> 11.4 us  [shards(): full_proj_weight = lax.all_gather(ple_proj_weight, 'tp', axis=1, tiled=True)]
    all_to_all x1, waiting for transfers between devices: 26.9 us -> 29.9 us  [shards(): lax.all_to_all(outgoing, 'req', split_axis=0, concat_axis=0, tiled=True)]
    gather x1, local copies, waits for them, and re-layouts: 4.66 us -> 1.95 us  [shards(): outgoing = lax.dynamic_slice_in_dim(own_cache, kv_head * HD, HD, 2)[wanted]]
    select_n x0 -> x1, other arithmetic: none -> 2.53 us  [shards(): own_cache = jnp.where(half == 0, cache_keys, cache_values)]
    ppermute x6, starting transfers between devices: 8.03 us -> 5.78 us  [rows_to_columns(): received.append(lax.ppermute(outgoing, axis_name, perm))]
    reshape x1 -> x0, local copies, waits for them, and re-layouts: 2.2 us -> none  [fetch_pages(): return cache.reshape(page_total, page_len, -1, HD)[wanted, :, kv_head]]
    all_to_all x1, waiting for transfers between devices: 4.47 us -> 2.71 us  [shards(): lax.all_to_all(request_table, 'req', split_axis=0, concat_axis=0, tiled=T...]
  transfers between devices with their start and end apart: 15 -> 15, of which waited for: 9 -> 9; matrix products, arithmetic and copies ran while one was open for 16% -> 14% of each run, Pallas kernels for 15% -> 14%
where the time goes in v9:
time: 134 us
  waiting for transfers between devices  58.1 us (43%)
  starting transfers between devices  20.7 us (15%)
  Pallas kernels  19 us (14%)
  between operations  13.5 us (10%)
  local copies, waits for them, and re-layouts  9.47 us (7%)
  matrix products  7.2 us (5%)
  other arithmetic  6.1 us (5%)
    all_to_all x1, waiting for transfers between devices, shards(): lax.all_to_all(outgoing, 'req', split_axis=0, concat_axis=0, tiled=True)  29.9 us
    pallas_call x1, Pallas kernels, sparse_attention(): pl.pallas_call(attention_kernel, grid_spec=pltpu.PrefetchScalarGridSpec(n...  19 us
    all_gather x1, waiting for transfers between devices, shards(): full_proj_weight = lax.all_gather(ple_proj_weight, 'tp', axis=1, tiled=True)  11.4 us
    ppermute x3, waiting for transfers between devices, columns_to_rows(): received.append(lax.ppermute(outgoing, axis_name, perm))  6.56 us
    all_to_all x1, starting transfers between devices, shards(): lax.all_to_all(request_table, 'req', split_axis=0, concat_axis=0, tiled=T...  6.38 us
    ppermute x6, waiting for transfers between devices, rows_to_columns(): received.append(lax.ppermute(outgoing, axis_name, perm))  6.07 us
    ppermute x6, starting transfers between devices, rows_to_columns(): received.append(lax.ppermute(outgoing, axis_name, perm))  5.78 us
    dot_general x1, matrix products, shards(): jnp.dot(row_attention, full_weight, preferred_element_type=jnp.float32)  4.74 us
  transfers between devices with their start and end apart: 15, of which 9 were waited for; matrix products, arithmetic and copies ran while one was open for 14% of the time, Pallas kernels for 14%

profile of v9, /device:TPU:1, one launch (start us, length us, event | category | flops | bytes accessed | tf_op | source)
XLA Modules:
  0.0 134.1 jit_solution(6104450274982479346)
XLA Ops:
  6.5 0.7 all-gather.4.cloned.1.call-update
  7.3 0.0 all-gather.6.cloned.1.call-start
  7.3 0.7 all-gather.6.cloned.1.call-update
  8.0 0.2 convert_reduce_fusion.1
  8.2 0.2 select_reduce_fusion.2
  8.4 0.7 copy.89
  9.1 6.4 %all-to-all-start = ((s32[8,1,6]{2,1,0:T(1,128)}), s32[8,1,6]{2,1,0:T(1,128)S(1)}, u32[]{:S(2)}, u32[]{:S(2)}) async-start(s32[8,1,6]{2,1,0:T(1,128)} %copy.89), calls=%async_computation | async-start | bytes 8192 | tf_op jit(solution)/shard_map/all_to_all | solution.py:277
  15.5 2.5 %dynamic-slice_select_fusion = bf16[48,64,256]{2,1,0:T(8,128)(2,1)S(1)} fusion(bf16[48,64,512]{2,1,0:T(8,128)(2,1)} %param.26, s32[]{:T(128)S(6)} %select_n.225, bf16[48,64,512]{2,1,0:T(8,128)(2,1)} %param.25, pred[]{:T(512)S(6)} %eq.138), kind=kLoop, calls=%fused_computation.4 | loop fusion | flops 786432 | bytes 4718597 | tf_op jit(solution)/shard_map/jit(_where)/select_n | solution.py:284
  18.0 2.7 %all-to-all-done = s32[8,1,6]{2,1,0:T(1,128)S(1)} async-done(((s32[8,1,6]{2,1,0:T(1,128)}), s32[8,1,6]{2,1,0:T(1,128)S(1)}, u32[]{:S(2)}, u32[]{:S(2)}) %all-to-all-start) | async-done | bytes 224 | tf_op jit(solution)/shard_map/all_to_all | solution.py:277
  20.8 0.1 reshape.543
  20.8 1.9 %gather_fusion.1 = bf16[48,64,256]{2,1,0:T(8,128)(2,1)} fusion(bf16[48,64,256]{2,1,0:T(8,128)(2,1)S(1)} %dynamic-slice_select_fusion, s32[1024]{0:T(1024)S(1)} %pad_clamp_fusion), kind=kCustom, calls=%fused_computation.1 | custom fusion | bytes 3145920 | tf_op jit(solution)/shard_map/gather | solution.py:285
  22.8 3.7 %all-to-all-start.1 = ((bf16[8,6,64,256]{3,2,1,0:T(8,128)(2,1)}), bf16[8,6,64,256]{3,2,1,0:T(8,128)(2,1)S(1)}, u32[]{:S(2)}, u32[]{:S(2)}) async-start(bf16[8,6,64,256]{3,2,1,0:T(8,128)(2,1)} %bitcast.19), calls=%async_computation.1 | async-start | bytes 3145728 | tf_op jit(solution)/shard_map/all_to_all | solution.py:286
  26.6 0.0 all-gather.8.cloned.1.call-start
  26.8 0.1 fusion.1
  26.9 3.3 %collective-permute-start = (bf16[136,512]{1,0:T(8,128)(2,1)S(1)}, bf16[136,512]{1,0:T(8,128)(2,1)S(1)}, u32[]{:S(2)}, u32[]{:S(2)}) collective-permute-start(bf16[136,512]{1,0:T(8,128)(2,1)S(1)} %get-tuple-element.42), channel_id=1, source_target_pairs={{0,1},{1,2},{2,3},{3,0},{4,5},{5,6},{6,7},{7,4},{8,9},{9,10},{10,1... | collective-permute-start | bytes 417800 | tf_op jit(solution)/shard_map/ppermute | solution.py:222
  30.1 0.3 collective-permute-start.1
  30.4 0.2 collective-permute-start.2
  30.6 0.2 reduce-window_clone.1
  30.8 0.1 convert_reduce_fusion.2
  30.9 0.1 slice.48
  31.0 0.1 slice.49
  31.1 0.2 reduce-window_1_clone.1
  31.3 0.1 convert_reduce_fusion
  31.4 0.2 select_reduce_fusion.3
  31.6 29.9 %all-to-all-done.1 = bf16[8,6,64,256]{3,2,1,0:T(8,128)(2,1)S(1)} async-done(((bf16[8,6,64,256]{3,2,1,0:T(8,128)(2,1)}), bf16[8,6,64,256]{3,2,1,0:T(8,128)(2,1)S(1)}, u32[]{:S(2)}, u32[]{:S(2)}) %all-to-all-start.1) | async-done | bytes 1572896 | tf_op jit(solution)/shard_map/all_to_all | solution.py:286
  61.5 3.1 %collective-permute-start.3 = (bf16[8,6,64,256]{3,2,1,0:T(8,128)(2,1)S(1)}, bf16[8,6,64,256]{3,2,1,0:T(8,128)(2,1)}, u32[]{:S(2)}, u32[]{:S(2)}) collective-permute-start(bf16[8,6,64,256]{3,2,1,0:T(8,128)(2,1)S(1)} %all-to-all-done.1), channel_id=1, source_target_pairs={{0,1},{1,0},{2,3},{3,2},{4,5},{5,4},{6,7},{7,6},{8,9},{9,8},{10,11... | collective-permute-start | bytes 4718600 | tf_op jit(solution)/shard_map/ppermute | solution.py:287
  64.6 0.1 copy.80
  64.7 0.1 copy.76
  64.8 0.1 copy.84
  64.9 0.1 select_reduce_fusion.1
  65.1 0.6 multiply_add_fusion.1.slots_ref
  65.7 0.7 pad_add_fusion.1.meta_ref
  66.3 0.6 reshape.526.kown_ref
  66.9 0.8 copy.90.rown_ref
  67.8 0.7 stack.59.ranges_ref
  68.4 0.1 fusion.42
  68.6 0.1 pad_maximum_fusion
  68.7 0.6 gather_fusion
  69.3 0.1 convert_bitcast_fusion
  69.4 0.1 copy.94
  69.5 19.0 %shard_map.163 = bf16[512,512]{1,0:T(8,128)(2,1)} custom-call(s32[4,5]{1,0:T(4,128)} %stack.59.ranges_ref, s32[48]{0:T(128)} %multiply_add_fusion.1.slots_ref, s32[2]{0:T(128)} %pad_add_fusion.1.meta_ref, bf16[512,512]{1,0:T(8,128)(2,1)} %q_ref.1, bf16[48,64,256]{2,1,0:T(8,128)(2,1)} %bitcast.63, bf16[48,64,256]{2,1,0:T(8,128)(2,1)} %bitcast.21.partner_ref, ...), custom_call_target="tpu_custom_call" | custom-call | tf_op jit(solution)/shard_map/pallas_call | solution.py:177
  88.5 1.1 constant_dynamic-slice_fusion.3
  89.6 1.2 collective-permute-start.4
  90.8 0.2 collective-permute-start.5
  91.1 0.6 collective-permute-start.6
  91.7 1.4 %collective-permute-done.4 = bf16[128,512]{1,0:T(8,128)(2,1)S(1)} collective-permute-done((bf16[128,512]{1,0:T(8,128)(2,1)S(1)}, bf16[128,512]{1,0:T(8,128)(2,1)S(1)}, u32[]{:S(2)}, u32[]{:S(2)}) %collective-permute-start.4) | collective-permute-done | bytes 131104 | tf_op jit(solution)/shard_map/ppermute | solution.py:222
  93.1 3.7 %collective-permute-done.5 = bf16[128,512]{1,0:T(8,128)(2,1)S(1)} collective-permute-done((bf16[128,512]{1,0:T(8,128)(2,1)S(1)}, bf16[128,512]{1,0:T(8,128)(2,1)S(1)}, u32[]{:S(2)}, u32[]{:S(2)}) %collective-permute-start.5) | collective-permute-done | bytes 131104 | tf_op jit(solution)/shard_map/ppermute | solution.py:222
  96.8 0.9 collective-permute-done.6
  97.8 0.1 pad_maximum_fusion.1
  97.8 0.6 gather_fusion.2
  98.4 0.3 copy.91
  98.7 0.0 all-gather.4.cloned.1.call-done
  98.7 4.7 %multiply_reduce_fusion.1 = (f32[128]{0:T(128)S(1)}, f32[128,2048]{1,0:T(8,128)S(1)}) fusion(bf16[128,2048]{0,1:T(8,128)(2,1)S(1)} %bitcast.65, bf16[2048,2048]{1,0:T(8,128)(2,1)} %all-gather.4.cloned.1.call-done), kind=kOutput, calls=%fused_computation.13 | convolution fusion | flops 1074265984 | bytes 9961984 | tf_op jit(solution)/shard_map/dot_general | solution.py:315
  103.5 0.2 add_convert_fusion.1
  103.7 11.4 %all-gather.8.cloned.1.call-done = bf16[256,2048]{1,0:T(8,128)(2,1)} async-done(((bf16[256,512]{1,0:T(8,128)(2,1)}), bf16[256,2048]{1,0:T(8,128)(2,1)}) %all-gather.8.cloned.1.call-update) | async-done | bytes 1048592 | tf_op jit(solution)/shard_map/all_gather | solution.py:302
  115.1 2.5 %multiply_reduce_fusion = (f32[128]{0:T(128)S(1)}, f32[128,2048]{1,0:T(8,128)S(1)}) fusion(bf16[256,2048]{1,0:T(8,128)(2,1)} %all-gather.8.cloned.1.call-done, bf16[512,256]{1,0:T(8,128)(2,1)} %param.29, s32[]{:T(128)S(6)} %select_n.232, bf16[128,2048]{1,0:T(8,128)(2,1)S(1)} %add_convert_fusion.1, bf16[2048,256]{1,0:T(8,128)(2,1)} %all-gather.6.cloned.1.call-done), kind=kOutput, calls=%fused_computation.11 | convolution fusion | flops 269320064 | bytes 3736068 | tf_op jit(solution)/shard_map/dot_general | solution.py:327
  117.6 0.2 add_convert_fusion
  117.9 0.3 collective-permute-start.7
  118.1 1.4 %collective-permute-start.8 = (bf16[128,512]{1,0:T(8,128)(2,1)S(1)}, bf16[128,512]{1,0:T(8,128)(2,1)S(1)}, u32[]{:S(2)}, u32[]{:S(2)}) collective-permute-start(bf16[128,512]{1,0:T(8,128)(2,1)S(1)} %get-tuple-element.47), channel_id=1, source_target_pairs={{0,2},{1,3},{2,0},{3,1},{4,6},{5,7},{6,4},{7,5},{8,10},{9,11},{10,... | collective-permute-start | bytes 393224 | tf_op jit(solution)/shard_map/ppermute | solution.py:236
  119.6 1.1 collective-permute-done.7
  120.7 4.7 %collective-permute-done.8 = bf16[128,512]{1,0:T(8,128)(2,1)S(1)} collective-permute-done((bf16[128,512]{1,0:T(8,128)(2,1)S(1)}, bf16[128,512]{1,0:T(8,128)(2,1)S(1)}, u32[]{:S(2)}, u32[]{:S(2)}) %collective-permute-start.8) | collective-permute-done | bytes 131104 | tf_op jit(solution)/shard_map/ppermute | solution.py:236
  125.3 0.8 collective-permute-done.9
  126.1 0.1 pad_maximum_fusion.2
  126.2 1.4 %gather_fusion.3 = bf16[4,128,512]{2,1,0:T(8,128)(2,1)} fusion(bf16[4,128,512]{2,1,0:T(8,128)(2,1)S(1)} %pad_maximum_fusion.2, s32[1024]{0:T(1024)S(1)} %pad_clamp_fusion.1), kind=kCustom, calls=%fused_computation.3 | custom fusion | bytes 1048592 | tf_op jit(solution)/shard_map/gather | solution.py:238
  (53 shorter events, 0.4 us)
Async XLA Ops:
  6.5 1.5 %copy-start.8 = (s32[48,1]{0,1:T(1,128)S(1)}, s32[48,1]{0,1:T(1,128)}, u32[]{:S(2)}) copy-start(s32[48,1]{0,1:T(1,128)} %param.33) | copy-start | bytes 580
  6.5 1.7 %copy-start.6 = (s32[48,1]{0,1:T(1,128)S(1)}, s32[48,1]{0,1:T(1,128)}, u32[]{:S(2)}) copy-start(s32[48,1]{0,1:T(1,128)} %param.34) | copy-start | bytes 580
  6.5 92.2 %all-gather.4.cloned.1.call-start = ((), (), s32[]{:S(2)}) async-start(), calls=%async_computation.2 | async-start | bytes 10485760 | tf_op jit(solution)/shard_map/all_gather | solution.py:300
  7.3 96.5 %all-gather.6.cloned.1.call-start = ((), (), s32[]{:S(2)}) async-start(), calls=%async_computation.3 | async-start | bytes 1310720 | tf_op jit(solution)/shard_map/all_gather | solution.py:301
  9.1 11.6 %all-to-all-start = ((s32[8,1,6]{2,1,0:T(1,128)}), s32[8,1,6]{2,1,0:T(1,128)S(1)}, u32[]{:S(2)}, u32[]{:S(2)}) async-start(s32[8,1,6]{2,1,0:T(1,128)} %copy.89), calls=%async_computation | async-start | bytes 8192 | tf_op jit(solution)/shard_map/all_to_all | solution.py:277
  22.8 3.9 %copy-start.3 = (bf16[512]{0:T(512)(128)(2,1)S(1)}, bf16[512]{0:T(512)(128)(2,1)}, u32[]{:S(2)}) copy-start(bf16[512]{0:T(512)(128)(2,1)} %param.28) | copy-start | bytes 3076
  22.8 3.9 %copy-start.4 = (bf16[512]{0:T(512)(128)(2,1)S(1)}, bf16[512]{0:T(512)(128)(2,1)}, u32[]{:S(2)}) copy-start(bf16[512]{0:T(512)(128)(2,1)} %param.32) | copy-start | bytes 3076
  22.8 4.0 %copy-start.1 = (bf16[512,512]{1,0:T(8,128)(2,1)S(1)}, bf16[512,512]{1,0:T(8,128)(2,1)}, u32[]{:S(2)}) copy-start(bf16[512,512]{1,0:T(8,128)(2,1)} %param.21) | copy-start | bytes 1572868
  22.8 7.8 %copy-start.7 = (s32[1,8]{1,0:T(1,128)S(1)}, s32[1,8]{1,0:T(1,128)}, u32[]{:S(2)}) copy-start(s32[1,8]{1,0:T(1,128)} %param.37) | copy-start | bytes 100
  22.8 8.3 %copy-start.2 = (s32[1,8]{1,0:T(1,128)S(1)}, s32[1,8]{1,0:T(1,128)}, u32[]{:S(2)}) copy-start(s32[1,8]{1,0:T(1,128)} %param.35) | copy-start | bytes 100
  22.8 8.5 %copy-start.5 = (s32[1,8]{1,0:T(1,128)S(1)}, s32[1,8]{1,0:T(1,128)}, u32[]{:S(2)}) copy-start(s32[1,8]{1,0:T(1,128)} %param.36) | copy-start | bytes 100
  22.8 38.7 %all-to-all-start.1 = ((bf16[8,6,64,256]{3,2,1,0:T(8,128)(2,1)}), bf16[8,6,64,256]{3,2,1,0:T(8,128)(2,1)S(1)}, u32[]{:S(2)}, u32[]{:S(2)}) async-start(bf16[8,6,64,256]{3,2,1,0:T(8,128)(2,1)} %bitcast.19), calls=%async_computation.1 | async-start | bytes 3145728 | tf_op jit(solution)/shard_map/all_to_all | solution.py:286
  26.6 88.5 %all-gather.8.cloned.1.call-start = ((), (), s32[]{:S(2)}) async-start(), calls=%async_computation.4 | async-start | bytes 1310720 | tf_op jit(solution)/shard_map/all_gather | solution.py:302
  26.9 41.7 %collective-permute-start = (bf16[136,512]{1,0:T(8,128)(2,1)S(1)}, bf16[136,512]{1,0:T(8,128)(2,1)S(1)}, u32[]{:S(2)}, u32[]{:S(2)}) collective-permute-start(bf16[136,512]{1,0:T(8,128)(2,1)S(1)} %get-tuple-element.42), channel_id=1, source_target_pairs={{0,1},{1,2},{2,3},{3,0},{4,5},{5,6},{6,7},{7,4},{8,9},{9,10},{10,1... | collective-permute-start | bytes 417800 | tf_op jit(solution)/shard_map/ppermute | solution.py:222
  30.1 38.5 %collective-permute-start.1 = (bf16[136,512]{1,0:T(8,128)(2,1)S(1)}, bf16[136,512]{1,0:T(8,128)(2,1)S(1)}, u32[]{:S(2)}, u32[]{:S(2)}) collective-permute-start(bf16[136,512]{1,0:T(8,128)(2,1)S(1)} %get-tuple-element.43), channel_id=1, source_target_pairs={{0,2},{1,3},{2,0},{3,1},{4,6},{5,7},{6,4},{7,5},{8,10},{9,11},{10,... | collective-permute-start | bytes 417800 | tf_op jit(solution)/shard_map/ppermute | solution.py:222
  30.4 38.2 %collective-permute-start.2 = (bf16[136,512]{1,0:T(8,128)(2,1)S(1)}, bf16[136,512]{1,0:T(8,128)(2,1)S(1)}, u32[]{:S(2)}, u32[]{:S(2)}) collective-permute-start(bf16[136,512]{1,0:T(8,128)(2,1)S(1)} %get-tuple-element.44), channel_id=1, source_target_pairs={{0,3},{1,0},{2,1},{3,2},{4,7},{5,4},{6,5},{7,6},{8,11},{9,8},{10,9... | collective-permute-start | bytes 417800 | tf_op jit(solution)/shard_map/ppermute | solution.py:222
  61.5 7.9 %copy-start = (bf16[8,6,64,256]{3,2,1,0:T(8,128)(2,1)}, bf16[8,6,64,256]{3,2,1,0:T(8,128)(2,1)S(1)}, u32[]{:S(2)}) copy-start(bf16[8,6,64,256]{3,2,1,0:T(8,128)(2,1)S(1)} %all-to-all-done.1) | copy-start | bytes 4718596
  61.5 8.0 %collective-permute-start.3 = (bf16[8,6,64,256]{3,2,1,0:T(8,128)(2,1)S(1)}, bf16[8,6,64,256]{3,2,1,0:T(8,128)(2,1)}, u32[]{:S(2)}, u32[]{:S(2)}) collective-permute-start(bf16[8,6,64,256]{3,2,1,0:T(8,128)(2,1)S(1)} %all-to-all-done.1), channel_id=1, source_target_pairs={{0,1},{1,0},{2,3},{3,2},{4,5},{5,4},{6,7},{7,6},{8,9},{9,8},{10,11... | collective-permute-start | bytes 4718600 | tf_op jit(solution)/shard_map/ppermute | solution.py:287
  89.6 3.5 %collective-permute-start.4 = (bf16[128,512]{1,0:T(8,128)(2,1)S(1)}, bf16[128,512]{1,0:T(8,128)(2,1)S(1)}, u32[]{:S(2)}, u32[]{:S(2)}) collective-permute-start(bf16[128,512]{1,0:T(8,128)(2,1)S(1)} %get-tuple-element.52), channel_id=1, source_target_pairs={{0,1},{1,2},{2,3},{3,0},{4,5},{5,6},{6,7},{7,4},{8,9},{9,10},{10,1... | collective-permute-start | bytes 393224 | tf_op jit(solution)/shard_map/ppermute | solution.py:222
  90.8 6.0 %collective-permute-start.5 = (bf16[128,512]{1,0:T(8,128)(2,1)S(1)}, bf16[128,512]{1,0:T(8,128)(2,1)S(1)}, u32[]{:S(2)}, u32[]{:S(2)}) collective-permute-start(bf16[128,512]{1,0:T(8,128)(2,1)S(1)} %get-tuple-element.51), channel_id=1, source_target_pairs={{0,2},{1,3},{2,0},{3,1},{4,6},{5,7},{6,4},{7,5},{8,10},{9,11},{10,... | collective-permute-start | bytes 393224 | tf_op jit(solution)/shard_map/ppermute | solution.py:222
  91.1 6.7 %collective-permute-start.6 = (bf16[128,512]{1,0:T(8,128)(2,1)S(1)}, bf16[128,512]{1,0:T(8,128)(2,1)S(1)}, u32[]{:S(2)}, u32[]{:S(2)}) collective-permute-start(bf16[128,512]{1,0:T(8,128)(2,1)S(1)} %get-tuple-element.50), channel_id=1, source_target_pairs={{0,3},{1,0},{2,1},{3,2},{4,7},{5,4},{6,5},{7,6},{8,11},{9,8},{10,9... | collective-permute-start | bytes 393224 | tf_op jit(solution)/shard_map/ppermute | solution.py:222
  117.9 2.8 %collective-permute-start.7 = (bf16[128,512]{1,0:T(8,128)(2,1)S(1)}, bf16[128,512]{1,0:T(8,128)(2,1)S(1)}, u32[]{:S(2)}, u32[]{:S(2)}) collective-permute-start(bf16[128,512]{1,0:T(8,128)(2,1)S(1)} %get-tuple-element.48), channel_id=1, source_target_pairs={{0,1},{1,2},{2,3},{3,0},{4,5},{5,6},{6,7},{7,4},{8,9},{9,10},{10,1... | collective-permute-start | bytes 393224 | tf_op jit(solution)/shard_map/ppermute | solution.py:236
  118.1 7.2 %collective-permute-start.8 = (bf16[128,512]{1,0:T(8,128)(2,1)S(1)}, bf16[128,512]{1,0:T(8,128)(2,1)S(1)}, u32[]{:S(2)}, u32[]{:S(2)}) collective-permute-start(bf16[128,512]{1,0:T(8,128)(2,1)S(1)} %get-tuple-element.47), channel_id=1, source_target_pairs={{0,2},{1,3},{2,0},{3,1},{4,6},{5,7},{6,4},{7,5},{8,10},{9,11},{10,... | collective-permute-start | bytes 393224 | tf_op jit(solution)/shard_map/ppermute | solution.py:236
  119.5 6.6 %collective-permute-start.9 = (bf16[128,512]{1,0:T(8,128)(2,1)S(1)}, bf16[128,512]{1,0:T(8,128)(2,1)S(1)}, u32[]{:S(2)}, u32[]{:S(2)}) collective-permute-start(bf16[128,512]{1,0:T(8,128)(2,1)S(1)} %get-tuple-element.46), channel_id=1, source_target_pairs={{0,3},{1,0},{2,1},{3,2},{4,7},{5,4},{6,5},{7,6},{8,11},{9,8},{10,9... | collective-permute-start | bytes 393224 | tf_op jit(solution)/shard_map/ppermute | solution.py:236
Sparse Core Ops, SparseCore 0:
  8.9 66.7 all-gather.3
  77.3 16.8 all-gather.5
  95.7 19.3 all-gather.7

commit v10 on v9

--- a/solution.py
+++ b/solution.py
@@ -298,8 +298,11 @@
     )
     tp_size = lax.axis_size("tp")
     full_weight = lax.all_gather(out_weight, "tp", axis=0, tiled=True)
-    full_gate_weight = lax.all_gather(ple_gate_weight, "tp", axis=0, tiled=True)
-    full_proj_weight = lax.all_gather(ple_proj_weight, "tp", axis=1, tiled=True)
+    ple_joined = lax.all_gather(
+        jnp.concatenate([ple_gate_weight, ple_proj_weight.T], axis=1), "tp", axis=0, tiled=True
+    )
+    full_gate_weight = ple_joined[:, : ple_gate_weight.shape[1]]
+    full_proj_weight_t = ple_joined[:, ple_gate_weight.shape[1] :]
     hidden_parts = hidden.reshape(tp_size, -1, hidden.shape[1])
     gain_rows = jnp.zeros((8, hidden.shape[1]), hidden.dtype).at[0].set(attn_gain).at[1].set(ple_gain)
     with_gains = jnp.concatenate(
@@ -324,7 +327,9 @@
     activated = (jax.nn.gelu(gate, approximate=True) * row_ple.astype(jnp.float32)).astype(
         jnp.bfloat16
     )
-    lifted = jnp.dot(activated, full_proj_weight, preferred_element_type=jnp.float32)
+    lifted = lax.dot_general(
+        activated, full_proj_weight_t, (((1,), (1,)), ((), ())), preferred_element_type=jnp.float32
+    )
     lift_squares = jnp.sum(lifted * lifted, axis=1)
     lift_normed = (
         lifted

time: 134 us -> 128 us (0.955)
  waiting for transfers between devices: 58.1 us -> 50.8 us
    all_gather x2 -> x1, waiting for transfers between devices: 11.4 us -> 0.02 us  [shards(): lax.all_gather(jnp.concatenate([ple_gate_weight, ple_proj_weight.T], axis...]
    ppermute x6, waiting for transfers between devices: 6.07 us -> 12.6 us  [rows_to_columns(): received.append(lax.ppermute(outgoing, axis_name, perm))]
  transfers between devices with their start and end apart: 15 -> 14, of which waited for: 9 -> 8; matrix products, arithmetic and copies ran while one was open for 14% -> 15% of each run, Pallas kernels for 14% -> 15%
where the time goes in v10:
time: 128 us
  waiting for transfers between devices  50.8 us (40%)
  starting transfers between devices  20.2 us (16%)
  Pallas kernels  19 us (15%)
  between operations  13.9 us (11%)
  local copies, waits for them, and re-layouts  9.55 us (7%)
  matrix products  7.38 us (6%)
  other arithmetic  6.95 us (5%)
    all_to_all x1, waiting for transfers between devices, shards(): lax.all_to_all(outgoing, 'req', split_axis=0, concat_axis=0, tiled=True)  28.9 us
    pallas_call x1, Pallas kernels, sparse_attention(): pl.pallas_call(attention_kernel, grid_spec=pltpu.PrefetchScalarGridSpec(n...  19 us
    ppermute x6, waiting for transfers between devices, rows_to_columns(): received.append(lax.ppermute(outgoing, axis_name, perm))  12.6 us
    all_to_all x1, starting transfers between devices, shards(): lax.all_to_all(request_table, 'req', split_axis=0, concat_axis=0, tiled=T...  6.38 us
    ppermute x3, waiting for transfers between devices, columns_to_rows(): received.append(lax.ppermute(outgoing, axis_name, perm))  5.78 us
    ppermute x6, starting transfers between devices, rows_to_columns(): received.append(lax.ppermute(outgoing, axis_name, perm))  5.75 us
    dot_general x1, matrix products, shards(): jnp.dot(row_attention, full_weight, preferred_element_type=jnp.float32)  4.74 us
    all_to_all x1, starting transfers between devices, shards(): lax.all_to_all(outgoing, 'req', split_axis=0, concat_axis=0, tiled=True)  3.75 us
  transfers between devices with their start and end apart: 14, of which 8 were waited for; matrix products, arithmetic and copies ran while one was open for 15% of the time, Pallas kernels for 15%

profile of v10, /device:TPU:1, one launch (start us, length us, event | category | flops | bytes accessed | tf_op | source)
XLA Modules:
  0.0 127.7 jit_solution(9218546627457191326)
XLA Ops:
  6.5 0.7 all-gather.3.cloned.1.call-update
  7.3 0.2 convert_reduce_fusion.1
  7.5 0.2 select_reduce_fusion.2
  7.7 0.7 copy.93
  8.4 6.4 %all-to-all-start = ((s32[8,1,6]{2,1,0:T(1,128)}), s32[8,1,6]{2,1,0:T(1,128)S(1)}, u32[]{:S(2)}, u32[]{:S(2)}) async-start(s32[8,1,6]{2,1,0:T(1,128)} %copy.93), calls=%async_computation | async-start | bytes 8192 | tf_op jit(solution)/shard_map/all_to_all | solution.py:277
  14.7 2.6 %dynamic-slice_select_fusion = bf16[48,64,256]{2,1,0:T(8,128)(2,1)S(1)} fusion(bf16[48,64,512]{2,1,0:T(8,128)(2,1)} %param.26, s32[]{:T(128)S(6)} %select_n.225, bf16[48,64,512]{2,1,0:T(8,128)(2,1)} %param.25, pred[]{:T(512)S(6)} %eq.138), kind=kLoop, calls=%fused_computation.4 | loop fusion | flops 786432 | bytes 4718597 | tf_op jit(solution)/shard_map/jit(_where)/select_n | solution.py:284
  17.3 2.7 %all-to-all-done = s32[8,1,6]{2,1,0:T(1,128)S(1)} async-done(((s32[8,1,6]{2,1,0:T(1,128)}), s32[8,1,6]{2,1,0:T(1,128)S(1)}, u32[]{:S(2)}, u32[]{:S(2)}) %all-to-all-start) | async-done | bytes 224 | tf_op jit(solution)/shard_map/all_to_all | solution.py:277
  20.0 0.1 reshape.543
  20.1 1.9 %gather_fusion.1 = bf16[48,64,256]{2,1,0:T(8,128)(2,1)} fusion(bf16[48,64,256]{2,1,0:T(8,128)(2,1)S(1)} %dynamic-slice_select_fusion, s32[1024]{0:T(1024)S(1)} %pad_clamp_fusion), kind=kCustom, calls=%fused_computation.1 | custom fusion | bytes 3145920 | tf_op jit(solution)/shard_map/gather | solution.py:285
  22.0 3.7 %all-to-all-start.1 = ((bf16[8,6,64,256]{3,2,1,0:T(8,128)(2,1)}), bf16[8,6,64,256]{3,2,1,0:T(8,128)(2,1)S(1)}, u32[]{:S(2)}, u32[]{:S(2)}) async-start(bf16[8,6,64,256]{3,2,1,0:T(8,128)(2,1)} %bitcast.19), calls=%async_computation.1 | async-start | bytes 3145728 | tf_op jit(solution)/shard_map/all_to_all | solution.py:286
  25.8 0.0 all-gather.5.cloned.1.call-start
  26.0 0.1 fusion.5
  26.1 3.2 %collective-permute-start = (bf16[136,512]{1,0:T(8,128)(2,1)S(1)}, bf16[136,512]{1,0:T(8,128)(2,1)S(1)}, u32[]{:S(2)}, u32[]{:S(2)}) collective-permute-start(bf16[136,512]{1,0:T(8,128)(2,1)S(1)} %get-tuple-element.42), channel_id=1, source_target_pairs={{0,1},{1,2},{2,3},{3,0},{4,5},{5,6},{6,7},{7,4},{8,9},{9,10},{10,1... | collective-permute-start | bytes 417800 | tf_op jit(solution)/shard_map/ppermute | solution.py:222
  29.3 0.3 collective-permute-start.1
  29.6 0.2 collective-permute-start.2
  29.8 0.1 copy.96
  29.9 0.8 pad_maximum_fusion.2
  30.8 0.2 reduce-window_clone.1
  31.0 0.1 convert_reduce_fusion.2
  31.1 0.1 slice.54
  31.2 0.1 slice.55
  31.3 0.2 reduce-window_1_clone.1
  31.5 0.1 convert_reduce_fusion
  31.6 0.2 select_reduce_fusion.3
  31.8 28.9 %all-to-all-done.1 = bf16[8,6,64,256]{3,2,1,0:T(8,128)(2,1)S(1)} async-done(((bf16[8,6,64,256]{3,2,1,0:T(8,128)(2,1)}), bf16[8,6,64,256]{3,2,1,0:T(8,128)(2,1)S(1)}, u32[]{:S(2)}, u32[]{:S(2)}) %all-to-all-start.1) | async-done | bytes 1572896 | tf_op jit(solution)/shard_map/all_to_all | solution.py:286
  60.7 3.1 %collective-permute-start.3 = (bf16[8,6,64,256]{3,2,1,0:T(8,128)(2,1)S(1)}, bf16[8,6,64,256]{3,2,1,0:T(8,128)(2,1)}, u32[]{:S(2)}, u32[]{:S(2)}) collective-permute-start(bf16[8,6,64,256]{3,2,1,0:T(8,128)(2,1)S(1)} %all-to-all-done.1), channel_id=1, source_target_pairs={{0,1},{1,0},{2,3},{3,2},{4,5},{5,4},{6,7},{7,6},{8,9},{9,8},{10,11... | collective-permute-start | bytes 4718600 | tf_op jit(solution)/shard_map/ppermute | solution.py:287
  63.8 0.1 copy.84
  63.9 0.1 copy.80
  64.0 0.1 copy.88
  64.1 0.1 select_reduce_fusion.1
  64.2 0.6 multiply_add_fusion.1.slots_ref
  64.8 0.7 pad_add_fusion.1.meta_ref
  65.5 0.6 reshape.526.kown_ref
  66.1 0.8 copy.94.rown_ref
  66.9 0.7 stack.59.ranges_ref
  67.6 0.1 fusion.53
  67.8 0.1 pad_maximum_fusion
  67.9 0.6 gather_fusion
  68.5 0.1 convert_bitcast_fusion
  68.6 0.1 copy.99
  68.7 19.0 %shard_map.163 = bf16[512,512]{1,0:T(8,128)(2,1)} custom-call(s32[4,5]{1,0:T(4,128)} %stack.59.ranges_ref, s32[48]{0:T(128)} %multiply_add_fusion.1.slots_ref, s32[2]{0:T(128)} %pad_add_fusion.1.meta_ref, bf16[512,512]{1,0:T(8,128)(2,1)} %q_ref.1, bf16[48,64,256]{2,1,0:T(8,128)(2,1)} %bitcast.62, bf16[48,64,256]{2,1,0:T(8,128)(2,1)} %bitcast.21.partner_ref, ...), custom_call_target="tpu_custom_call" | custom-call | tf_op jit(solution)/shard_map/pallas_call | solution.py:177
  87.7 1.1 constant_dynamic-slice_fusion.3
  88.8 1.2 collective-permute-start.4
  90.0 0.3 collective-permute-start.5
  90.3 0.6 collective-permute-start.6
  90.9 4.9 %collective-permute-done.4 = bf16[128,512]{1,0:T(8,128)(2,1)S(1)} collective-permute-done((bf16[128,512]{1,0:T(8,128)(2,1)S(1)}, bf16[128,512]{1,0:T(8,128)(2,1)S(1)}, u32[]{:S(2)}, u32[]{:S(2)}) %collective-permute-start.4) | collective-permute-done | bytes 131104 | tf_op jit(solution)/shard_map/ppermute | solution.py:222
  95.7 6.7 %collective-permute-done.5 = bf16[128,512]{1,0:T(8,128)(2,1)S(1)} collective-permute-done((bf16[128,512]{1,0:T(8,128)(2,1)S(1)}, bf16[128,512]{1,0:T(8,128)(2,1)S(1)}, u32[]{:S(2)}, u32[]{:S(2)}) %collective-permute-start.5) | collective-permute-done | bytes 131104 | tf_op jit(solution)/shard_map/ppermute | solution.py:222
  102.5 1.0 collective-permute-done.6
  103.5 0.1 pad_maximum_fusion.1
  103.6 0.6 gather_fusion.2
  104.1 0.3 copy.95
  104.4 0.0 all-gather.3.cloned.1.call-done
  104.4 4.7 %multiply_reduce_fusion.1 = (f32[128]{0:T(128)S(1)}, f32[128,2048]{1,0:T(8,128)S(1)}) fusion(bf16[128,2048]{0,1:T(8,128)(2,1)S(1)} %bitcast.64, bf16[2048,2048]{1,0:T(8,128)(2,1)} %all-gather.3.cloned.1.call-done), kind=kOutput, calls=%fused_computation.17 | convolution fusion | flops 1074265984 | bytes 9961984 | tf_op jit(solution)/shard_map/dot_general | solution.py:318
  109.2 0.2 add_convert_fusion.1
  109.4 2.6 %multiply_reduce_fusion = (f32[128]{0:T(128)S(1)}, f32[128,2048]{1,0:T(8,128)S(1)}) fusion(bf16[2048,512]{0,1:T(8,128)(2,1)} %all-gather.5.cloned.1.call-done, bf16[128,2048]{1,0:T(8,128)(2,1)S(1)} %add_convert_fusion.1, bf16[512,256]{1,0:T(8,128)(2,1)} %param.29, s32[]{:T(128)S(6)} %select_n.232), kind=kOutput, calls=%fused_computation.15 | convolution fusion | flops 269320064 | bytes 3736068 | tf_op jit(solution)/shard_map/dot_general | solution.py:330
  112.1 0.2 add_convert_fusion
  112.4 0.1 collective-permute-start.7
  112.5 0.5 collective-permute-start.8
  112.9 0.7 collective-permute-start.9
  113.6 0.8 collective-permute-done.7
  114.4 3.2 %collective-permute-done.8 = bf16[128,512]{1,0:T(8,128)(2,1)S(1)} collective-permute-done((bf16[128,512]{1,0:T(8,128)(2,1)S(1)}, bf16[128,512]{1,0:T(8,128)(2,1)S(1)}, u32[]{:S(2)}, u32[]{:S(2)}) %collective-permute-start.8) | collective-permute-done | bytes 131104 | tf_op jit(solution)/shard_map/ppermute | solution.py:236
  117.6 1.8 %collective-permute-done.9 = bf16[128,512]{1,0:T(8,128)(2,1)S(1)} collective-permute-done((bf16[128,512]{1,0:T(8,128)(2,1)S(1)}, bf16[128,512]{1,0:T(8,128)(2,1)S(1)}, u32[]{:S(2)}, u32[]{:S(2)}) %collective-permute-start.9) | collective-permute-done | bytes 131104 | tf_op jit(solution)/shard_map/ppermute | solution.py:236
  119.4 0.1 pad_maximum_fusion.3
  119.5 1.4 %gather_fusion.3 = bf16[4,128,512]{2,1,0:T(8,128)(2,1)} fusion(bf16[4,128,512]{2,1,0:T(8,128)(2,1)S(1)} %pad_maximum_fusion.3, s32[1024]{0:T(1024)S(1)} %pad_clamp_fusion.1), kind=kCustom, calls=%fused_computation.3 | custom fusion | bytes 1048592 | tf_op jit(solution)/shard_map/gather | solution.py:238
  (56 shorter events, 0.4 us)
Async XLA Ops:
  6.5 0.7 copy-start.10
  6.5 0.9 copy-start.8
  6.5 97.9 %all-gather.3.cloned.1.call-start = ((), (), s32[]{:S(2)}) async-start(), calls=%async_computation.2 | async-start | bytes 10485760 | tf_op jit(solution)/shard_map/all_gather | solution.py:300
  8.4 11.6 %all-to-all-start = ((s32[8,1,6]{2,1,0:T(1,128)}), s32[8,1,6]{2,1,0:T(1,128)S(1)}, u32[]{:S(2)}, u32[]{:S(2)}) async-start(s32[8,1,6]{2,1,0:T(1,128)} %copy.93), calls=%async_computation | async-start | bytes 8192 | tf_op jit(solution)/shard_map/all_to_all | solution.py:277
  22.0 3.9 %copy-start.5 = (bf16[512]{0:T(512)(128)(2,1)S(1)}, bf16[512]{0:T(512)(128)(2,1)}, u32[]{:S(2)}) copy-start(bf16[512]{0:T(512)(128)(2,1)} %param.28) | copy-start | bytes 3076
  22.0 3.9 %copy-start.6 = (bf16[512]{0:T(512)(128)(2,1)S(1)}, bf16[512]{0:T(512)(128)(2,1)}, u32[]{:S(2)}) copy-start(bf16[512]{0:T(512)(128)(2,1)} %param.32) | copy-start | bytes 3076
  22.0 4.0 %copy-start.1 = (bf16[512,512]{1,0:T(8,128)(2,1)S(1)}, bf16[512,512]{1,0:T(8,128)(2,1)}, u32[]{:S(2)}) copy-start(bf16[512,512]{1,0:T(8,128)(2,1)} %param.21) | copy-start | bytes 1572868
  22.0 7.8 %copy-start.2 = (bf16[512,256]{1,0:T(8,128)(2,1)S(1)}, bf16[512,256]{1,0:T(8,128)(2,1)}, u32[]{:S(2)}) copy-start(bf16[512,256]{1,0:T(8,128)(2,1)} %param.30) | copy-start | bytes 786436
  22.0 8.0 %copy-start.3 = (bf16[256,512]{1,0:T(8,128)(2,1)S(1)}, bf16[256,512]{1,0:T(8,128)(2,1)}, u32[]{:S(2)}) copy-start(bf16[256,512]{1,0:T(8,128)(2,1)} %param.31) | copy-start | bytes 786436
  22.0 38.7 %all-to-all-start.1 = ((bf16[8,6,64,256]{3,2,1,0:T(8,128)(2,1)}), bf16[8,6,64,256]{3,2,1,0:T(8,128)(2,1)S(1)}, u32[]{:S(2)}, u32[]{:S(2)}) async-start(bf16[8,6,64,256]{3,2,1,0:T(8,128)(2,1)} %bitcast.19), calls=%async_computation.1 | async-start | bytes 3145728 | tf_op jit(solution)/shard_map/all_to_all | solution.py:286
  25.7 5.1 %copy-start.9 = (s32[1,8]{1,0:T(1,128)S(1)}, s32[1,8]{1,0:T(1,128)}, u32[]{:S(2)}) copy-start(s32[1,8]{1,0:T(1,128)} %param.37) | copy-start | bytes 100
  25.8 5.5 %copy-start.4 = (s32[1,8]{1,0:T(1,128)S(1)}, s32[1,8]{1,0:T(1,128)}, u32[]{:S(2)}) copy-start(s32[1,8]{1,0:T(1,128)} %param.35) | copy-start | bytes 100
  25.8 5.7 %copy-start.7 = (s32[1,8]{1,0:T(1,128)S(1)}, s32[1,8]{1,0:T(1,128)}, u32[]{:S(2)}) copy-start(s32[1,8]{1,0:T(1,128)} %param.36) | copy-start | bytes 100
  25.8 83.7 %all-gather.5.cloned.1.call-start = ((), (), s32[]{:S(2)}) async-start(), calls=%async_computation.3 | async-start | bytes 2621440 | tf_op jit(solution)/shard_map/all_gather | solution.py:301
  26.1 41.7 %collective-permute-start = (bf16[136,512]{1,0:T(8,128)(2,1)S(1)}, bf16[136,512]{1,0:T(8,128)(2,1)S(1)}, u32[]{:S(2)}, u32[]{:S(2)}) collective-permute-start(bf16[136,512]{1,0:T(8,128)(2,1)S(1)} %get-tuple-element.42), channel_id=1, source_target_pairs={{0,1},{1,2},{2,3},{3,0},{4,5},{5,6},{6,7},{7,4},{8,9},{9,10},{10,1... | collective-permute-start | bytes 417800 | tf_op jit(solution)/shard_map/ppermute | solution.py:222
  29.3 38.5 %collective-permute-start.1 = (bf16[136,512]{1,0:T(8,128)(2,1)S(1)}, bf16[136,512]{1,0:T(8,128)(2,1)S(1)}, u32[]{:S(2)}, u32[]{:S(2)}) collective-permute-start(bf16[136,512]{1,0:T(8,128)(2,1)S(1)} %get-tuple-element.43), channel_id=1, source_target_pairs={{0,2},{1,3},{2,0},{3,1},{4,6},{5,7},{6,4},{7,5},{8,10},{9,11},{10,... | collective-permute-start | bytes 417800 | tf_op jit(solution)/shard_map/ppermute | solution.py:222
  29.6 38.2 %collective-permute-start.2 = (bf16[136,512]{1,0:T(8,128)(2,1)S(1)}, bf16[136,512]{1,0:T(8,128)(2,1)S(1)}, u32[]{:S(2)}, u32[]{:S(2)}) collective-permute-start(bf16[136,512]{1,0:T(8,128)(2,1)S(1)} %get-tuple-element.44), channel_id=1, source_target_pairs={{0,3},{1,0},{2,1},{3,2},{4,7},{5,4},{6,5},{7,6},{8,11},{9,8},{10,9... | collective-permute-start | bytes 417800 | tf_op jit(solution)/shard_map/ppermute | solution.py:222
  60.7 7.9 %copy-start = (bf16[8,6,64,256]{3,2,1,0:T(8,128)(2,1)}, bf16[8,6,64,256]{3,2,1,0:T(8,128)(2,1)S(1)}, u32[]{:S(2)}) copy-start(bf16[8,6,64,256]{3,2,1,0:T(8,128)(2,1)S(1)} %all-to-all-done.1) | copy-start | bytes 4718596
  60.7 8.0 %collective-permute-start.3 = (bf16[8,6,64,256]{3,2,1,0:T(8,128)(2,1)S(1)}, bf16[8,6,64,256]{3,2,1,0:T(8,128)(2,1)}, u32[]{:S(2)}, u32[]{:S(2)}) collective-permute-start(bf16[8,6,64,256]{3,2,1,0:T(8,128)(2,1)S(1)} %all-to-all-done.1), channel_id=1, source_target_pairs={{0,1},{1,0},{2,3},{3,2},{4,5},{5,4},{6,7},{7,6},{8,9},{9,8},{10,11... | collective-permute-start | bytes 4718600 | tf_op jit(solution)/shard_map/ppermute | solution.py:287
  88.8 6.9 %collective-permute-start.4 = (bf16[128,512]{1,0:T(8,128)(2,1)S(1)}, bf16[128,512]{1,0:T(8,128)(2,1)S(1)}, u32[]{:S(2)}, u32[]{:S(2)}) collective-permute-start(bf16[128,512]{1,0:T(8,128)(2,1)S(1)} %get-tuple-element.52), channel_id=1, source_target_pairs={{0,1},{1,2},{2,3},{3,0},{4,5},{5,6},{6,7},{7,4},{8,9},{9,10},{10,1... | collective-permute-start | bytes 393224 | tf_op jit(solution)/shard_map/ppermute | solution.py:222
  90.0 12.5 %collective-permute-start.5 = (bf16[128,512]{1,0:T(8,128)(2,1)S(1)}, bf16[128,512]{1,0:T(8,128)(2,1)S(1)}, u32[]{:S(2)}, u32[]{:S(2)}) collective-permute-start(bf16[128,512]{1,0:T(8,128)(2,1)S(1)} %get-tuple-element.51), channel_id=1, source_target_pairs={{0,2},{1,3},{2,0},{3,1},{4,6},{5,7},{6,4},{7,5},{8,10},{9,11},{10,... | collective-permute-start | bytes 393224 | tf_op jit(solution)/shard_map/ppermute | solution.py:222
  90.3 13.2 %collective-permute-start.6 = (bf16[128,512]{1,0:T(8,128)(2,1)S(1)}, bf16[128,512]{1,0:T(8,128)(2,1)S(1)}, u32[]{:S(2)}, u32[]{:S(2)}) collective-permute-start(bf16[128,512]{1,0:T(8,128)(2,1)S(1)} %get-tuple-element.50), channel_id=1, source_target_pairs={{0,3},{1,0},{2,1},{3,2},{4,7},{5,4},{6,5},{7,6},{8,11},{9,8},{10,9... | collective-permute-start | bytes 393224 | tf_op jit(solution)/shard_map/ppermute | solution.py:222
  112.4 2.0 %collective-permute-start.7 = (bf16[128,512]{1,0:T(8,128)(2,1)S(1)}, bf16[128,512]{1,0:T(8,128)(2,1)S(1)}, u32[]{:S(2)}, u32[]{:S(2)}) collective-permute-start(bf16[128,512]{1,0:T(8,128)(2,1)S(1)} %get-tuple-element.48), channel_id=1, source_target_pairs={{0,1},{1,2},{2,3},{3,0},{4,5},{5,6},{6,7},{7,4},{8,9},{9,10},{10,1... | collective-permute-start | bytes 393224 | tf_op jit(solution)/shard_map/ppermute | solution.py:236
  112.5 5.2 %collective-permute-start.8 = (bf16[128,512]{1,0:T(8,128)(2,1)S(1)}, bf16[128,512]{1,0:T(8,128)(2,1)S(1)}, u32[]{:S(2)}, u32[]{:S(2)}) collective-permute-start(bf16[128,512]{1,0:T(8,128)(2,1)S(1)} %get-tuple-element.47), channel_id=1, source_target_pairs={{0,2},{1,3},{2,0},{3,1},{4,6},{5,7},{6,4},{7,5},{8,10},{9,11},{10,... | collective-permute-start | bytes 393224 | tf_op jit(solution)/shard_map/ppermute | solution.py:236
  112.9 6.5 %collective-permute-start.9 = (bf16[128,512]{1,0:T(8,128)(2,1)S(1)}, bf16[128,512]{1,0:T(8,128)(2,1)S(1)}, u32[]{:S(2)}, u32[]{:S(2)}) collective-permute-start(bf16[128,512]{1,0:T(8,128)(2,1)S(1)} %get-tuple-element.46), channel_id=1, source_target_pairs={{0,3},{1,0},{2,1},{3,2},{4,7},{5,4},{6,5},{7,6},{8,11},{9,8},{10,9... | collective-permute-start | bytes 393224 | tf_op jit(solution)/shard_map/ppermute | solution.py:236
Sparse Core Ops, SparseCore 0:
  8.9 66.7 all-gather.2
  77.3 28.2 all-gather.4

commit v11 on v10

--- a/solution.py
+++ b/solution.py
@@ -113,24 +113,17 @@
         0, total, scores_pass, jnp.full((heads * ROW_BLOCK, 1), -1e30, jnp.float32)
     )
 
-    def exp_pass(t, summed):
+    acc_scr[...] = jnp.zeros(acc_scr.shape, jnp.float32)
+
+    def value_pass(t, summed):
         c = chunk_of(t)
         e = jnp.exp(s_scr[c] - highest)
-        s_scr[c] = e
+        values = load_chunk(c, False, fresh_v_ref)
+        acc_scr[...] += jnp.dot(e.astype(jnp.bfloat16), values, preferred_element_type=jnp.float32)
         return summed + jnp.sum(e, axis=1, keepdims=True)
 
-    summed = lax.fori_loop(0, total, exp_pass, jnp.zeros((heads * ROW_BLOCK, 1), jnp.float32))
-    inverse = 1.0 / summed
-    acc_scr[...] = jnp.zeros(acc_scr.shape, jnp.float32)
-
-    def value_pass(t, carry):
-        c = chunk_of(t)
-        w = (s_scr[c] * inverse).astype(jnp.bfloat16)
-        values = load_chunk(c, False, fresh_v_ref)
-        acc_scr[...] += jnp.dot(w, values, preferred_element_type=jnp.float32)
-        return carry
-
-    lax.fori_loop(0, total, value_pass, 0)
+    summed = lax.fori_loop(0, total, value_pass, jnp.zeros((heads * ROW_BLOCK, 1), jnp.float32))
+    acc_scr[...] = acc_scr[...] / summed
     for h in range(heads):
         o_ref[:, h * HD:(h + 1) * HD] = acc_scr[h * ROW_BLOCK:(h + 1) * ROW_BLOCK, :].astype(
             jnp.bfloat16

time: 128 us -> 128 us (level)
  no operation moved by 1% of the time
where the time goes in v11:
time: 128 us
  waiting for transfers between devices  50.8 us (40%)
  starting transfers between devices  20.7 us (16%)
  Pallas kernels  18.6 us (15%)
  between operations  13.9 us (11%)
  local copies, waits for them, and re-layouts  9.55 us (7%)
  matrix products  7.39 us (6%)
  other arithmetic  6.95 us (5%)
    all_to_all x1, waiting for transfers between devices, shards(): lax.all_to_all(outgoing, 'req', split_axis=0, concat_axis=0, tiled=True)  28.9 us
    pallas_call x1, Pallas kernels, sparse_attention(): pl.pallas_call(attention_kernel, grid_spec=pltpu.PrefetchScalarGridSpec(n...  18.6 us
    ppermute x6, waiting for transfers between devices, rows_to_columns(): received.append(lax.ppermute(outgoing, axis_name, perm))  12.6 us
    all_to_all x1, starting transfers between devices, shards(): lax.all_to_all(request_table, 'req', split_axis=0, concat_axis=0, tiled=T...  6.38 us
    ppermute x3, waiting for transfers between devices, columns_to_rows(): received.append(lax.ppermute(outgoing, axis_name, perm))  5.78 us
    ppermute x6, starting transfers between devices, rows_to_columns(): received.append(lax.ppermute(outgoing, axis_name, perm))  5.75 us
    dot_general x1, matrix products, shards(): jnp.dot(row_attention, full_weight, preferred_element_type=jnp.float32)  4.75 us
    all_to_all x1, starting transfers between devices, shards(): lax.all_to_all(outgoing, 'req', split_axis=0, concat_axis=0, tiled=True)  3.75 us
  transfers between devices with their start and end apart: 14, of which 8 were waited for; matrix products, arithmetic and copies ran while one was open for 15% of the time, Pallas kernels for 15%

profile of v11, /device:TPU:1, one launch (start us, length us, event | category | flops | bytes accessed | tf_op | source)
XLA Modules:
  0.0 127.8 jit_solution(9417980493315414992)
XLA Ops:
  6.5 0.7 all-gather.3.cloned.1.call-update
  7.3 0.2 convert_reduce_fusion.1
  7.5 0.2 select_reduce_fusion.2
  7.7 0.7 copy.93
  8.4 6.4 %all-to-all-start = ((s32[8,1,6]{2,1,0:T(1,128)}), s32[8,1,6]{2,1,0:T(1,128)S(1)}, u32[]{:S(2)}, u32[]{:S(2)}) async-start(s32[8,1,6]{2,1,0:T(1,128)} %copy.93), calls=%async_computation | async-start | bytes 8192 | tf_op jit(solution)/shard_map/all_to_all | solution.py:270
  14.7 2.6 %dynamic-slice_select_fusion = bf16[48,64,256]{2,1,0:T(8,128)(2,1)S(1)} fusion(bf16[48,64,512]{2,1,0:T(8,128)(2,1)} %param.26, s32[]{:T(128)S(6)} %select_n.225, bf16[48,64,512]{2,1,0:T(8,128)(2,1)} %param.25, pred[]{:T(512)S(6)} %eq.138), kind=kLoop, calls=%fused_computation.4 | loop fusion | flops 786432 | bytes 4718597 | tf_op jit(solution)/shard_map/jit(_where)/select_n | solution.py:277
  17.3 2.7 %all-to-all-done = s32[8,1,6]{2,1,0:T(1,128)S(1)} async-done(((s32[8,1,6]{2,1,0:T(1,128)}), s32[8,1,6]{2,1,0:T(1,128)S(1)}, u32[]{:S(2)}, u32[]{:S(2)}) %all-to-all-start) | async-done | bytes 224 | tf_op jit(solution)/shard_map/all_to_all | solution.py:270
  20.0 0.1 reshape.543
  20.1 1.9 %gather_fusion.1 = bf16[48,64,256]{2,1,0:T(8,128)(2,1)} fusion(bf16[48,64,256]{2,1,0:T(8,128)(2,1)S(1)} %dynamic-slice_select_fusion, s32[1024]{0:T(1024)S(1)} %pad_clamp_fusion), kind=kCustom, calls=%fused_computation.1 | custom fusion | bytes 3145920 | tf_op jit(solution)/shard_map/gather | solution.py:278
  22.0 3.7 %all-to-all-start.1 = ((bf16[8,6,64,256]{3,2,1,0:T(8,128)(2,1)}), bf16[8,6,64,256]{3,2,1,0:T(8,128)(2,1)S(1)}, u32[]{:S(2)}, u32[]{:S(2)}) async-start(bf16[8,6,64,256]{3,2,1,0:T(8,128)(2,1)} %bitcast.19), calls=%async_computation.1 | async-start | bytes 3145728 | tf_op jit(solution)/shard_map/all_to_all | solution.py:279
  25.8 0.0 all-gather.5.cloned.1.call-start
  26.0 0.1 fusion.5
  26.1 3.2 %collective-permute-start = (bf16[136,512]{1,0:T(8,128)(2,1)S(1)}, bf16[136,512]{1,0:T(8,128)(2,1)S(1)}, u32[]{:S(2)}, u32[]{:S(2)}) collective-permute-start(bf16[136,512]{1,0:T(8,128)(2,1)S(1)} %get-tuple-element.42), channel_id=1, source_target_pairs={{0,1},{1,2},{2,3},{3,0},{4,5},{5,6},{6,7},{7,4},{8,9},{9,10},{10,1... | collective-permute-start | bytes 417800 | tf_op jit(solution)/shard_map/ppermute | solution.py:215
  29.3 0.3 collective-permute-start.1
  29.6 0.2 collective-permute-start.2
  29.8 0.1 copy.96
  29.9 0.8 pad_maximum_fusion.2
  30.8 0.2 reduce-window_clone.1
  31.0 0.1 convert_reduce_fusion.2
  31.1 0.1 slice.54
  31.2 0.1 slice.55
  31.3 0.2 reduce-window_1_clone.1
  31.5 0.1 convert_reduce_fusion
  31.6 0.2 select_reduce_fusion.3
  31.8 28.9 %all-to-all-done.1 = bf16[8,6,64,256]{3,2,1,0:T(8,128)(2,1)S(1)} async-done(((bf16[8,6,64,256]{3,2,1,0:T(8,128)(2,1)}), bf16[8,6,64,256]{3,2,1,0:T(8,128)(2,1)S(1)}, u32[]{:S(2)}, u32[]{:S(2)}) %all-to-all-start.1) | async-done | bytes 1572896 | tf_op jit(solution)/shard_map/all_to_all | solution.py:279
  60.7 3.1 %collective-permute-start.3 = (bf16[8,6,64,256]{3,2,1,0:T(8,128)(2,1)S(1)}, bf16[8,6,64,256]{3,2,1,0:T(8,128)(2,1)}, u32[]{:S(2)}, u32[]{:S(2)}) collective-permute-start(bf16[8,6,64,256]{3,2,1,0:T(8,128)(2,1)S(1)} %all-to-all-done.1), channel_id=1, source_target_pairs={{0,1},{1,0},{2,3},{3,2},{4,5},{5,4},{6,7},{7,6},{8,9},{9,8},{10,11... | collective-permute-start | bytes 4718600 | tf_op jit(solution)/shard_map/ppermute | solution.py:280
  63.8 0.1 copy.84
  63.9 0.1 copy.80
  64.0 0.1 copy.88
  64.1 0.1 select_reduce_fusion.1
  64.2 0.6 multiply_add_fusion.1.slots_ref
  64.8 0.7 pad_add_fusion.1.meta_ref
  65.5 0.6 reshape.526.kown_ref
  66.1 0.8 copy.94.rown_ref
  66.9 0.7 stack.59.ranges_ref
  67.6 0.1 fusion.53
  67.8 0.1 pad_maximum_fusion
  67.9 0.6 gather_fusion
  68.5 0.1 convert_bitcast_fusion
  68.6 0.1 copy.99
  68.7 18.6 %shard_map.163 = bf16[512,512]{1,0:T(8,128)(2,1)} custom-call(s32[4,5]{1,0:T(4,128)} %stack.59.ranges_ref, s32[48]{0:T(128)} %multiply_add_fusion.1.slots_ref, s32[2]{0:T(128)} %pad_add_fusion.1.meta_ref, bf16[512,512]{1,0:T(8,128)(2,1)} %q_ref.1, bf16[48,64,256]{2,1,0:T(8,128)(2,1)} %bitcast.62, bf16[48,64,256]{2,1,0:T(8,128)(2,1)} %bitcast.21.partner_ref, ...), custom_call_target="tpu_custom_call" | custom-call | tf_op jit(solution)/shard_map/pallas_call | solution.py:170
  87.2 1.1 constant_dynamic-slice_fusion.3
  88.4 1.2 collective-permute-start.4
  89.6 0.3 collective-permute-start.5
  89.8 0.6 collective-permute-start.6
  90.4 4.9 %collective-permute-done.4 = bf16[128,512]{1,0:T(8,128)(2,1)S(1)} collective-permute-done((bf16[128,512]{1,0:T(8,128)(2,1)S(1)}, bf16[128,512]{1,0:T(8,128)(2,1)S(1)}, u32[]{:S(2)}, u32[]{:S(2)}) %collective-permute-start.4) | collective-permute-done | bytes 131104 | tf_op jit(solution)/shard_map/ppermute | solution.py:215
  95.3 6.7 %collective-permute-done.5 = bf16[128,512]{1,0:T(8,128)(2,1)S(1)} collective-permute-done((bf16[128,512]{1,0:T(8,128)(2,1)S(1)}, bf16[128,512]{1,0:T(8,128)(2,1)S(1)}, u32[]{:S(2)}, u32[]{:S(2)}) %collective-permute-start.5) | collective-permute-done | bytes 131104 | tf_op jit(solution)/shard_map/ppermute | solution.py:215
  102.1 1.0 collective-permute-done.6
  103.1 0.1 pad_maximum_fusion.1
  103.1 0.6 gather_fusion.2
  103.7 0.3 copy.95
  104.0 0.0 all-gather.3.cloned.1.call-done
  104.0 4.8 %multiply_reduce_fusion.1 = (f32[128]{0:T(128)S(1)}, f32[128,2048]{1,0:T(8,128)S(1)}) fusion(bf16[128,2048]{0,1:T(8,128)(2,1)S(1)} %bitcast.64, bf16[2048,2048]{1,0:T(8,128)(2,1)} %all-gather.3.cloned.1.call-done), kind=kOutput, calls=%fused_computation.17 | convolution fusion | flops 1074265984 | bytes 9961984 | tf_op jit(solution)/shard_map/dot_general | solution.py:311
  108.8 0.2 add_convert_fusion.1
  109.0 2.6 %multiply_reduce_fusion = (f32[128]{0:T(128)S(1)}, f32[128,2048]{1,0:T(8,128)S(1)}) fusion(bf16[2048,512]{0,1:T(8,128)(2,1)} %all-gather.5.cloned.1.call-done, bf16[128,2048]{1,0:T(8,128)(2,1)S(1)} %add_convert_fusion.1, bf16[512,256]{1,0:T(8,128)(2,1)} %param.29, s32[]{:T(128)S(6)} %select_n.232), kind=kOutput, calls=%fused_computation.15 | convolution fusion | flops 269320064 | bytes 3736068 | tf_op jit(solution)/shard_map/dot_general | solution.py:323
  111.7 0.2 add_convert_fusion
  112.0 0.1 collective-permute-start.7
  112.1 0.9 collective-permute-start.8
  113.0 0.7 collective-permute-start.9
  113.7 0.3 collective-permute-done.7
  114.0 4.2 %collective-permute-done.8 = bf16[128,512]{1,0:T(8,128)(2,1)S(1)} collective-permute-done((bf16[128,512]{1,0:T(8,128)(2,1)S(1)}, bf16[128,512]{1,0:T(8,128)(2,1)S(1)}, u32[]{:S(2)}, u32[]{:S(2)}) %collective-permute-start.8) | collective-permute-done | bytes 131104 | tf_op jit(solution)/shard_map/ppermute | solution.py:229
  118.1 1.3 %collective-permute-done.9 = bf16[128,512]{1,0:T(8,128)(2,1)S(1)} collective-permute-done((bf16[128,512]{1,0:T(8,128)(2,1)S(1)}, bf16[128,512]{1,0:T(8,128)(2,1)S(1)}, u32[]{:S(2)}, u32[]{:S(2)}) %collective-permute-start.9) | collective-permute-done | bytes 131104 | tf_op jit(solution)/shard_map/ppermute | solution.py:229
  119.5 0.1 pad_maximum_fusion.3
  119.6 1.4 %gather_fusion.3 = bf16[4,128,512]{2,1,0:T(8,128)(2,1)} fusion(bf16[4,128,512]{2,1,0:T(8,128)(2,1)S(1)} %pad_maximum_fusion.3, s32[1024]{0:T(1024)S(1)} %pad_clamp_fusion.1), kind=kCustom, calls=%fused_computation.3 | custom fusion | bytes 1048592 | tf_op jit(solution)/shard_map/gather | solution.py:231
  (56 shorter events, 0.4 us)
Async XLA Ops:
  6.5 0.7 copy-start.10
  6.5 0.9 copy-start.8
  6.5 97.5 %all-gather.3.cloned.1.call-start = ((), (), s32[]{:S(2)}) async-start(), calls=%async_computation.2 | async-start | bytes 10485760 | tf_op jit(solution)/shard_map/all_gather | solution.py:293
  8.4 11.6 %all-to-all-start = ((s32[8,1,6]{2,1,0:T(1,128)}), s32[8,1,6]{2,1,0:T(1,128)S(1)}, u32[]{:S(2)}, u32[]{:S(2)}) async-start(s32[8,1,6]{2,1,0:T(1,128)} %copy.93), calls=%async_computation | async-start | bytes 8192 | tf_op jit(solution)/shard_map/all_to_all | solution.py:270
  22.0 3.9 %copy-start.5 = (bf16[512]{0:T(512)(128)(2,1)S(1)}, bf16[512]{0:T(512)(128)(2,1)}, u32[]{:S(2)}) copy-start(bf16[512]{0:T(512)(128)(2,1)} %param.28) | copy-start | bytes 3076
  22.0 3.9 %copy-start.6 = (bf16[512]{0:T(512)(128)(2,1)S(1)}, bf16[512]{0:T(512)(128)(2,1)}, u32[]{:S(2)}) copy-start(bf16[512]{0:T(512)(128)(2,1)} %param.32) | copy-start | bytes 3076
  22.0 4.0 %copy-start.1 = (bf16[512,512]{1,0:T(8,128)(2,1)S(1)}, bf16[512,512]{1,0:T(8,128)(2,1)}, u32[]{:S(2)}) copy-start(bf16[512,512]{1,0:T(8,128)(2,1)} %param.21) | copy-start | bytes 1572868
  22.0 7.8 %copy-start.2 = (bf16[512,256]{1,0:T(8,128)(2,1)S(1)}, bf16[512,256]{1,0:T(8,128)(2,1)}, u32[]{:S(2)}) copy-start(bf16[512,256]{1,0:T(8,128)(2,1)} %param.30) | copy-start | bytes 786436
  22.0 8.0 %copy-start.3 = (bf16[256,512]{1,0:T(8,128)(2,1)S(1)}, bf16[256,512]{1,0:T(8,128)(2,1)}, u32[]{:S(2)}) copy-start(bf16[256,512]{1,0:T(8,128)(2,1)} %param.31) | copy-start | bytes 786436
  22.0 38.7 %all-to-all-start.1 = ((bf16[8,6,64,256]{3,2,1,0:T(8,128)(2,1)}), bf16[8,6,64,256]{3,2,1,0:T(8,128)(2,1)S(1)}, u32[]{:S(2)}, u32[]{:S(2)}) async-start(bf16[8,6,64,256]{3,2,1,0:T(8,128)(2,1)} %bitcast.19), calls=%async_computation.1 | async-start | bytes 3145728 | tf_op jit(solution)/shard_map/all_to_all | solution.py:279
  25.7 5.1 %copy-start.9 = (s32[1,8]{1,0:T(1,128)S(1)}, s32[1,8]{1,0:T(1,128)}, u32[]{:S(2)}) copy-start(s32[1,8]{1,0:T(1,128)} %param.37) | copy-start | bytes 100
  25.8 5.5 %copy-start.4 = (s32[1,8]{1,0:T(1,128)S(1)}, s32[1,8]{1,0:T(1,128)}, u32[]{:S(2)}) copy-start(s32[1,8]{1,0:T(1,128)} %param.35) | copy-start | bytes 100
  25.8 5.7 %copy-start.7 = (s32[1,8]{1,0:T(1,128)S(1)}, s32[1,8]{1,0:T(1,128)}, u32[]{:S(2)}) copy-start(s32[1,8]{1,0:T(1,128)} %param.36) | copy-start | bytes 100
  25.8 83.3 %all-gather.5.cloned.1.call-start = ((), (), s32[]{:S(2)}) async-start(), calls=%async_computation.3 | async-start | bytes 2621440 | tf_op jit(solution)/shard_map/all_gather | solution.py:294
  26.1 41.7 %collective-permute-start = (bf16[136,512]{1,0:T(8,128)(2,1)S(1)}, bf16[136,512]{1,0:T(8,128)(2,1)S(1)}, u32[]{:S(2)}, u32[]{:S(2)}) collective-permute-start(bf16[136,512]{1,0:T(8,128)(2,1)S(1)} %get-tuple-element.42), channel_id=1, source_target_pairs={{0,1},{1,2},{2,3},{3,0},{4,5},{5,6},{6,7},{7,4},{8,9},{9,10},{10,1... | collective-permute-start | bytes 417800 | tf_op jit(solution)/shard_map/ppermute | solution.py:215
  29.3 38.5 %collective-permute-start.1 = (bf16[136,512]{1,0:T(8,128)(2,1)S(1)}, bf16[136,512]{1,0:T(8,128)(2,1)S(1)}, u32[]{:S(2)}, u32[]{:S(2)}) collective-permute-start(bf16[136,512]{1,0:T(8,128)(2,1)S(1)} %get-tuple-element.43), channel_id=1, source_target_pairs={{0,2},{1,3},{2,0},{3,1},{4,6},{5,7},{6,4},{7,5},{8,10},{9,11},{10,... | collective-permute-start | bytes 417800 | tf_op jit(solution)/shard_map/ppermute | solution.py:215
  29.6 38.2 %collective-permute-start.2 = (bf16[136,512]{1,0:T(8,128)(2,1)S(1)}, bf16[136,512]{1,0:T(8,128)(2,1)S(1)}, u32[]{:S(2)}, u32[]{:S(2)}) collective-permute-start(bf16[136,512]{1,0:T(8,128)(2,1)S(1)} %get-tuple-element.44), channel_id=1, source_target_pairs={{0,3},{1,0},{2,1},{3,2},{4,7},{5,4},{6,5},{7,6},{8,11},{9,8},{10,9... | collective-permute-start | bytes 417800 | tf_op jit(solution)/shard_map/ppermute | solution.py:215
  60.7 7.9 %copy-start = (bf16[8,6,64,256]{3,2,1,0:T(8,128)(2,1)}, bf16[8,6,64,256]{3,2,1,0:T(8,128)(2,1)S(1)}, u32[]{:S(2)}) copy-start(bf16[8,6,64,256]{3,2,1,0:T(8,128)(2,1)S(1)} %all-to-all-done.1) | copy-start | bytes 4718596
  60.7 8.0 %collective-permute-start.3 = (bf16[8,6,64,256]{3,2,1,0:T(8,128)(2,1)S(1)}, bf16[8,6,64,256]{3,2,1,0:T(8,128)(2,1)}, u32[]{:S(2)}, u32[]{:S(2)}) collective-permute-start(bf16[8,6,64,256]{3,2,1,0:T(8,128)(2,1)S(1)} %all-to-all-done.1), channel_id=1, source_target_pairs={{0,1},{1,0},{2,3},{3,2},{4,5},{5,4},{6,7},{7,6},{8,9},{9,8},{10,11... | collective-permute-start | bytes 4718600 | tf_op jit(solution)/shard_map/ppermute | solution.py:280
  88.4 6.9 %collective-permute-start.4 = (bf16[128,512]{1,0:T(8,128)(2,1)S(1)}, bf16[128,512]{1,0:T(8,128)(2,1)S(1)}, u32[]{:S(2)}, u32[]{:S(2)}) collective-permute-start(bf16[128,512]{1,0:T(8,128)(2,1)S(1)} %get-tuple-element.52), channel_id=1, source_target_pairs={{0,1},{1,2},{2,3},{3,0},{4,5},{5,6},{6,7},{7,4},{8,9},{9,10},{10,1... | collective-permute-start | bytes 393224 | tf_op jit(solution)/shard_map/ppermute | solution.py:215
  89.6 12.5 %collective-permute-start.5 = (bf16[128,512]{1,0:T(8,128)(2,1)S(1)}, bf16[128,512]{1,0:T(8,128)(2,1)S(1)}, u32[]{:S(2)}, u32[]{:S(2)}) collective-permute-start(bf16[128,512]{1,0:T(8,128)(2,1)S(1)} %get-tuple-element.51), channel_id=1, source_target_pairs={{0,2},{1,3},{2,0},{3,1},{4,6},{5,7},{6,4},{7,5},{8,10},{9,11},{10,... | collective-permute-start | bytes 393224 | tf_op jit(solution)/shard_map/ppermute | solution.py:215
  89.8 13.2 %collective-permute-start.6 = (bf16[128,512]{1,0:T(8,128)(2,1)S(1)}, bf16[128,512]{1,0:T(8,128)(2,1)S(1)}, u32[]{:S(2)}, u32[]{:S(2)}) collective-permute-start(bf16[128,512]{1,0:T(8,128)(2,1)S(1)} %get-tuple-element.50), channel_id=1, source_target_pairs={{0,3},{1,0},{2,1},{3,2},{4,7},{5,4},{6,5},{7,6},{8,11},{9,8},{10,9... | collective-permute-start | bytes 393224 | tf_op jit(solution)/shard_map/ppermute | solution.py:215
  112.0 2.0 %collective-permute-start.7 = (bf16[128,512]{1,0:T(8,128)(2,1)S(1)}, bf16[128,512]{1,0:T(8,128)(2,1)S(1)}, u32[]{:S(2)}, u32[]{:S(2)}) collective-permute-start(bf16[128,512]{1,0:T(8,128)(2,1)S(1)} %get-tuple-element.48), channel_id=1, source_target_pairs={{0,1},{1,2},{2,3},{3,0},{4,5},{5,6},{6,7},{7,4},{8,9},{9,10},{10,1... | collective-permute-start | bytes 393224 | tf_op jit(solution)/shard_map/ppermute | solution.py:229
  112.1 6.1 %collective-permute-start.8 = (bf16[128,512]{1,0:T(8,128)(2,1)S(1)}, bf16[128,512]{1,0:T(8,128)(2,1)S(1)}, u32[]{:S(2)}, u32[]{:S(2)}) collective-permute-start(bf16[128,512]{1,0:T(8,128)(2,1)S(1)} %get-tuple-element.47), channel_id=1, source_target_pairs={{0,2},{1,3},{2,0},{3,1},{4,6},{5,7},{6,4},{7,5},{8,10},{9,11},{10,... | collective-permute-start | bytes 393224 | tf_op jit(solution)/shard_map/ppermute | solution.py:229
  113.0 6.5 %collective-permute-start.9 = (bf16[128,512]{1,0:T(8,128)(2,1)S(1)}, bf16[128,512]{1,0:T(8,128)(2,1)S(1)}, u32[]{:S(2)}, u32[]{:S(2)}) collective-permute-start(bf16[128,512]{1,0:T(8,128)(2,1)S(1)} %get-tuple-element.46), channel_id=1, source_target_pairs={{0,3},{1,0},{2,1},{3,2},{4,7},{5,4},{6,5},{7,6},{8,11},{9,8},{10,9... | collective-permute-start | bytes 393224 | tf_op jit(solution)/shard_map/ppermute | solution.py:229
Sparse Core Ops, SparseCore 0:
  8.9 66.7 all-gather.2
  77.3 28.2 all-gather.4

commit v12 on v10

--- a/solution.py
+++ b/solution.py
@@ -50,6 +50,7 @@
     ranges_ref,
     slots_ref,
     meta_ref,
+    order_ref,
     q_ref,
     own_ref,
     partner_ref,
@@ -62,7 +63,7 @@
     s_scr,
     acc_scr,
 ):
-    block = pl.program_id(0)
+    block = order_ref[pl.program_id(0)]
     ctx_lo = ranges_ref[block, 0]
     ctx_n = ranges_ref[block, 1]
     new_lo = ranges_ref[block, 2]
@@ -139,7 +140,7 @@
 
 def sparse_attention(
     queries, own_pages, partner_pages, slots, new_keys, new_values, half, kv_head,
-    page_counts, last_fill, row_counts, page_total,
+    page_counts, last_fill, row_counts, page_total, order,
 ):
     row_total = queries.shape[0]
     page_len = own_pages.shape[1]
@@ -173,33 +174,14 @@
         [ctx_lo, ctx_n, new_lo, new_n, jnp.full((blocks,), ctx_chunks, jnp.int32)], axis=1
     ).astype(jnp.int32)
     meta = jnp.stack([half, kv_head]).astype(jnp.int32)
-    whole = lambda b, r, s, m: (0, 0, 0)
-    return pl.pallas_call(
-        attention_kernel,
-        grid_spec=pltpu.PrefetchScalarGridSpec(
-            num_scalar_prefetch=3,
-            grid=(blocks,),
-            in_specs=[
-                pl.BlockSpec((ROW_BLOCK, heads * HD), lambda b, r, s, m: (b, 0)),
-                pl.BlockSpec(own_pages.shape, whole),
-                pl.BlockSpec(partner_pages.shape, whole),
-                pl.BlockSpec((row_total, HD), lambda b, r, s, m: (0, m[1])),
-                pl.BlockSpec((row_total, HD), lambda b, r, s, m: (0, m[1])),
-                pl.BlockSpec((chunks, 1, KEY_CHUNK), whole),
-                pl.BlockSpec((chunks, 1, KEY_CHUNK), whole),
-                pl.BlockSpec((ROW_BLOCK, 1), lambda b, r, s, m: (b, 0)),
-            ],
-            out_specs=pl.BlockSpec((ROW_BLOCK, heads * HD), lambda b, r, s, m: (b, 0)),
-            scratch_shapes=[
-                pltpu.VMEM((chunks, heads * ROW_BLOCK, KEY_CHUNK), jnp.float32),
-                pltpu.VMEM((heads * ROW_BLOCK, HD), jnp.float32),
-            ],
-        ),
-        out_shape=jax.ShapeDtypeStruct((row_total, heads * HD), jnp.bfloat16),
-    )(
+    whole = lambda b, r, s, m, o: (0, 0, 0)
+    by_order = lambda b, r, s, m, o: (o[b], 0)
+    by_head = lambda b, r, s, m, o: (0, m[1])
+    operands = (
         ranges,
         slots.astype(jnp.int32),
         meta,
+        order.astype(jnp.int32),
         queries,
         own_pages,
         partner_pages,
@@ -209,6 +191,29 @@
         key_pos.reshape(chunks, 1, KEY_CHUNK),
         row_owner.reshape(row_total, 1),
     )
+    return pl.pallas_call(
+        attention_kernel,
+        grid_spec=pltpu.PrefetchScalarGridSpec(
+            num_scalar_prefetch=4,
+            grid=(order.shape[0],),
+            in_specs=[
+                pl.BlockSpec((ROW_BLOCK, heads * HD), by_order),
+                pl.BlockSpec(own_pages.shape, whole),
+                pl.BlockSpec(partner_pages.shape, whole),
+                pl.BlockSpec((row_total, HD), by_head),
+                pl.BlockSpec((row_total, HD), by_head),
+                pl.BlockSpec((chunks, 1, KEY_CHUNK), whole),
+                pl.BlockSpec((chunks, 1, KEY_CHUNK), whole),
+                pl.BlockSpec((ROW_BLOCK, 1), by_order),
+            ],
+            out_specs=pl.BlockSpec((ROW_BLOCK, heads * HD), lambda b, r, s, m, o: (b, 0)),
+            scratch_shapes=[
+                pltpu.VMEM((chunks, heads * ROW_BLOCK, KEY_CHUNK), jnp.float32),
+                pltpu.VMEM((heads * ROW_BLOCK, HD), jnp.float32),
+            ],
+        ),
+        out_shape=jax.ShapeDtypeStruct((order.shape[0] * ROW_BLOCK, heads * HD), jnp.bfloat16),
+    )(*operands)
 
 
 def rows_to_columns(x, axis_name):
@@ -285,17 +290,28 @@
     outgoing = lax.dynamic_slice_in_dim(own_cache, kv_head * HD, HD, 2)[wanted]
     arrived = lax.all_to_all(outgoing, "req", split_axis=0, concat_axis=0, tiled=True)
     swapped = lax.ppermute(arrived, "tp", partner)
-    attention = sparse_attention(
-        queries,
-        arrived.reshape(-1, page_len, HD),
-        swapped.reshape(-1, page_len, HD),
-        arrival_index,
-        new_keys,
-        new_values,
-        half,
-        kv_head,
-        page_counts[0], last_fill[0], row_counts[0], page_total,
-    )
+    assert row_total == ROW_BLOCK * tp_count
+    sends = (tp_index + jnp.arange(1, tp_count, dtype=jnp.int32)) % tp_count
+
+    def attend(order):
+        return sparse_attention(
+            queries,
+            arrived.reshape(-1, page_len, HD),
+            swapped.reshape(-1, page_len, HD),
+            arrival_index,
+            new_keys,
+            new_values,
+            half,
+            kv_head,
+            page_counts[0],
+            last_fill[0],
+            row_counts[0],
+            page_total,
+            order,
+        )
+
+    sent_blocks = attend(sends)
+    own_block = attend(tp_index.reshape(1).astype(jnp.int32))
     tp_size = lax.axis_size("tp")
     full_weight = lax.all_gather(out_weight, "tp", axis=0, tiled=True)
     ple_joined = lax.all_gather(
@@ -312,7 +328,15 @@
     row_hidden = row_hidden_gains[: hidden_parts.shape[1]]
     full_attn_gain = row_hidden_gains[hidden_parts.shape[1]]
     full_ple_gain = row_hidden_gains[hidden_parts.shape[1] + 1]
-    row_attention = rows_to_columns(attention, "tp")
+    received = [own_block]
+    for shift in range(1, tp_count):
+        perm = [(i, (i + shift) % tp_count) for i in range(tp_count)]
+        piece = sent_blocks[(shift - 1) * ROW_BLOCK : shift * ROW_BLOCK]
+        received.append(lax.ppermute(piece, "tp", perm))
+    source_order = (tp_index - jnp.arange(tp_count, dtype=jnp.int32)) % tp_count
+    row_attention = jnp.transpose(jnp.stack(received)[source_order], (1, 0, 2)).reshape(
+        ROW_BLOCK, tp_count * own_block.shape[1]
+    )
     part_rows = row_attention.shape[0]
     row_ple = lax.dynamic_slice_in_dim(ple_input, tp_index * part_rows, part_rows, 0)
     projected = jnp.dot(row_attention, full_weight, preferred_element_type=jnp.float32)

time: 128 us -> 133 us (1.039); the launches traced: 128 us -> 131 us
  waiting for transfers between devices: 50.8 us -> 42.4 us
  other arithmetic: 6.95 us -> 12.6 us
  local copies, waits for them, and re-layouts: 9.55 us -> 13.6 us
  Pallas kernels: 19 us -> 21 us
    ppermute x6 -> x3, waiting for transfers between devices: 12.6 us -> 0.01 us  [rows_to_columns(): received.append(lax.ppermute(outgoing, axis_name, perm))]
    ppermute x0 -> x3, waiting for transfers between devices: none -> 4 us  [shards(): received.append(lax.ppermute(piece, 'tp', perm))]
    ppermute x6 -> x3, starting transfers between devices: 5.75 us -> 3.6 us  [rows_to_columns(): received.append(lax.ppermute(outgoing, axis_name, perm))]
    pallas_call x1 -> x2, Pallas kernels: 19 us -> 21 us  [sparse_attention(): pl.pallas_call(attention_kernel, grid_spec=pltpu.PrefetchScalarGridSpec(n...]
    another operation x2 -> x1, other arithmetic: 0.14 us -> 1.96 us  [rows_to_columns(): blocks = jnp.stack(received)[order]]
  transfers between devices with their start and end apart: 14 -> 14, of which waited for: 8 -> 6; matrix products, arithmetic and copies ran while one was open for 15% -> 21% of each run, Pallas kernels for 15% -> 16%
where the time goes in v12:
time: 133 us; the launch traced here: 131 us
  waiting for transfers between devices  42.4 us (32%)
  Pallas kernels  21 us (16%)
  starting transfers between devices  19.7 us (15%)
  between operations  13.9 us (10%)
  local copies, waits for them, and re-layouts  13.6 us (10%)
  other arithmetic  12.6 us (9%)
  matrix products  7.46 us (6%)
    all_to_all x1, waiting for transfers between devices, shards(): lax.all_to_all(outgoing, 'req', split_axis=0, concat_axis=0, tiled=True)  28.3 us
    pallas_call x2, Pallas kernels, sparse_attention(): pl.pallas_call(attention_kernel, grid_spec=pltpu.PrefetchScalarGridSpec(n...  21 us
    ppermute x3, waiting for transfers between devices, columns_to_rows(): received.append(lax.ppermute(outgoing, axis_name, perm))  6.56 us
    all_to_all x1, starting transfers between devices, shards(): lax.all_to_all(request_table, 'req', split_axis=0, concat_axis=0, tiled=T...  6.38 us
    dot_general x1, matrix products, shards(): jnp.dot(row_attention, full_weight, preferred_element_type=jnp.float32)  4.83 us
    ppermute x3, waiting for transfers between devices, shards(): received.append(lax.ppermute(piece, 'tp', perm))  4 us
    all_to_all x1, starting transfers between devices, shards(): lax.all_to_all(outgoing, 'req', split_axis=0, concat_axis=0, tiled=True)  3.75 us
    ppermute x3, starting transfers between devices, rows_to_columns(): received.append(lax.ppermute(outgoing, axis_name, perm))  3.6 us
  transfers between devices with their start and end apart: 14, of which 6 were waited for; matrix products, arithmetic and copies ran while one was open for 21% of the time, Pallas kernels for 16%

profile of v12, /device:TPU:1, one launch (start us, length us, event | category | flops | bytes accessed | tf_op | source)
XLA Modules:
  0.0 130.6 jit_solution(11408956709550719508)
XLA Ops:
  6.5 0.7 all-gather.3.cloned.1.call-update
  7.3 0.2 convert_reduce_fusion.1
  7.5 0.2 select_reduce_fusion.2
  7.7 0.7 copy.80
  8.4 6.4 %all-to-all-start = ((s32[8,1,6]{2,1,0:T(1,128)}), s32[8,1,6]{2,1,0:T(1,128)S(1)}, u32[]{:S(2)}, u32[]{:S(2)}) async-start(s32[8,1,6]{2,1,0:T(1,128)} %copy.80), calls=%async_computation | async-start | bytes 8192 | tf_op jit(solution)/shard_map/all_to_all | solution.py:282
  14.7 2.5 %dynamic-slice_select_fusion = bf16[48,64,256]{2,1,0:T(8,128)(2,1)S(1)} fusion(bf16[48,64,512]{2,1,0:T(8,128)(2,1)} %param.26, s32[]{:T(128)S(6)} %select_n.234, bf16[48,64,512]{2,1,0:T(8,128)(2,1)} %param.25, pred[]{:T(512)S(6)} %eq.73), kind=kLoop, calls=%fused_computation.4 | loop fusion | flops 786432 | bytes 4718597 | tf_op jit(solution)/shard_map/jit(_where)/select_n | solution.py:289
  17.2 2.8 %all-to-all-done = s32[8,1,6]{2,1,0:T(1,128)S(1)} async-done(((s32[8,1,6]{2,1,0:T(1,128)}), s32[8,1,6]{2,1,0:T(1,128)S(1)}, u32[]{:S(2)}, u32[]{:S(2)}) %all-to-all-start) | async-done | bytes 224 | tf_op jit(solution)/shard_map/all_to_all | solution.py:282
  20.0 0.1 reshape.548
  20.1 1.9 %gather_fusion.1 = bf16[48,64,256]{2,1,0:T(8,128)(2,1)} fusion(bf16[48,64,256]{2,1,0:T(8,128)(2,1)S(1)} %dynamic-slice_select_fusion, s32[1024]{0:T(1024)S(1)} %pad_clamp_fusion), kind=kCustom, calls=%fused_computation.1 | custom fusion | bytes 3145920 | tf_op jit(solution)/shard_map/gather | solution.py:290
  22.0 3.7 %all-to-all-start.1 = ((bf16[8,6,64,256]{3,2,1,0:T(8,128)(2,1)}), bf16[8,6,64,256]{3,2,1,0:T(8,128)(2,1)S(1)}, u32[]{:S(2)}, u32[]{:S(2)}) async-start(bf16[8,6,64,256]{3,2,1,0:T(8,128)(2,1)} %bitcast.20), calls=%async_computation.1 | async-start | bytes 3145728 | tf_op jit(solution)/shard_map/all_to_all | solution.py:291
  25.8 0.0 all-gather.5.cloned.1.call-start
  26.0 0.8 fusion.5
  26.8 3.2 %collective-permute-start = (bf16[136,512]{1,0:T(8,128)(2,1)}, bf16[136,512]{1,0:T(8,128)(2,1)}, u32[]{:S(2)}, u32[]{:S(2)}) collective-permute-start(bf16[136,512]{1,0:T(8,128)(2,1)} %get-tuple-element.42), channel_id=1, source_target_pairs={{0,1},{1,2},{2,3},{3,0},{4,5},{5,6},{6,7},{7,4},{8,9},{9,10},{10,1... | collective-permute-start | bytes 417800 | tf_op jit(solution)/shard_map/ppermute | solution.py:227
  30.0 0.3 collective-permute-start.1
  30.2 0.2 collective-permute-start.2
  30.4 0.1 copy.84
  30.5 0.8 pad_maximum_fusion.2
  31.4 0.2 reduce-window_clone.1
  31.6 0.1 convert_reduce_fusion.2
  31.7 0.1 slice.65
  31.8 0.1 slice.66
  31.9 0.2 reduce-window_1_clone.1
  32.1 0.1 convert_reduce_fusion
  32.2 0.2 select_reduce_fusion.3
  32.4 28.3 %all-to-all-done.1 = bf16[8,6,64,256]{3,2,1,0:T(8,128)(2,1)S(1)} async-done(((bf16[8,6,64,256]{3,2,1,0:T(8,128)(2,1)}), bf16[8,6,64,256]{3,2,1,0:T(8,128)(2,1)S(1)}, u32[]{:S(2)}, u32[]{:S(2)}) %all-to-all-start.1) | async-done | bytes 1572896 | tf_op jit(solution)/shard_map/all_to_all | solution.py:291
  60.7 3.1 %collective-permute-start.3 = (bf16[8,6,64,256]{3,2,1,0:T(8,128)(2,1)S(1)}, bf16[8,6,64,256]{3,2,1,0:T(8,128)(2,1)S(1)}, u32[]{:S(2)}, u32[]{:S(2)}) collective-permute-start(bf16[8,6,64,256]{3,2,1,0:T(8,128)(2,1)S(1)} %all-to-all-done.1), channel_id=1, source_target_pairs={{0,1},{1,0},{2,3},{3,2},{4,5},{5,4},{6,7},{7,6},{8,9},{9,8},{10,11... | collective-permute-start | bytes 4718600 | tf_op jit(solution)/shard_map/ppermute | solution.py:292
  63.8 0.1 select_reduce_fusion.1
  63.9 0.1 copy.71
  64.0 0.1 copy.67
  64.1 0.1 copy.75
  64.2 0.5 and_select_fusion.order_ref
  64.7 0.5 multiply_add_fusion.1.slots_ref
  65.3 0.6 pad_add_fusion.1.meta_ref
  65.9 0.6 reshape.532.kown_ref
  66.5 0.9 copy.81.rown_ref
  67.3 0.7 stack.70.ranges_ref
  68.0 0.1 fusion.53
  68.2 2.0 %pad_maximum_fusion = bf16[4,136,512]{2,1,0:T(8,128)(2,1)} fusion(bf16[1,136,512]{2,1,0:T(8,128)(2,1)} %bitcast.6, bf16[1,136,512]{2,1,0:T(8,128)(2,1)} %bitcast.4, bf16[1,136,512]{2,1,0:T(8,128)(2,1)} %bitcast.2, bf16[1,136,512]{2,1,0:T(8,128)(2,1)S(1)} %get-tuple-element.41), kind=kLoop, calls=%fused_computation.18 | loop fusion | flops 835584 | bytes 1114112 | tf_op jit(solution)/shard_map/stack | solution.py:229
  70.1 2.5 %gather_fusion = bf16[4,136,512]{2,1,0:T(8,128)(2,1)} fusion(bf16[4,136,512]{2,1,0:T(8,128)(2,1)} %pad_maximum_fusion, s32[1024]{0:T(1024)S(1)} %pad_clamp_fusion.1), kind=kCustom, calls=%fused_computation | custom fusion | bytes 1114128 | tf_op jit(solution)/shard_map/gather | solution.py:229
  72.6 1.2 convert_bitcast_fusion
  73.8 1.1 copy.87
  74.8 1.2 copy-done.1
  76.1 16.2 %shard_map.164 = bf16[384,512]{1,0:T(8,128)(2,1)} custom-call(s32[4,5]{1,0:T(4,128)} %stack.70.ranges_ref, s32[48]{0:T(128)} %multiply_add_fusion.1.slots_ref, s32[2]{0:T(128)} %pad_add_fusion.1.meta_ref, s32[3]{0:T(128)} %and_select_fusion.order_ref, bf16[512,512]{1,0:T(8,128)(2,1)} %q_ref.3, bf16[48,64,256]{2,1,0:T(8,128)(2,1)} %bitcast.57, ...), custom_call_target="tpu_custom_call" | custom-call | tf_op jit(solution)/shard_map/pallas_call | solution.py:194
  92.3 1.1 fusion.64
  93.3 0.1 collective-permute-start.4
  93.4 0.1 collective-permute-start.5
  93.5 0.4 collective-permute-start.6
  93.9 0.8 slice_convert_fusion
  94.7 4.8 %shard_map.163 = bf16[128,512]{1,0:T(8,128)(2,1)} custom-call(s32[4,5]{1,0:T(4,128)} %stack.70.ranges_ref, s32[48]{0:T(128)} %multiply_add_fusion.1.slots_ref, s32[2]{0:T(128)} %pad_add_fusion.1.meta_ref, s32[1]{0:T(128)} %bitcast.17.order_ref, bf16[512,512]{1,0:T(8,128)(2,1)} %q_ref.3, bf16[48,64,256]{2,1,0:T(8,128)(2,1)} %bitcast.58, ...), custom_call_target="tpu_custom_call" | custom-call | tf_op jit(solution)/shard_map/pallas_call | solution.py:194
  99.6 2.7 %collective-permute-done.5 = bf16[128,512]{1,0:T(8,128)(2,1)S(1)} collective-permute-done((bf16[128,512]{1,0:T(8,128)(2,1)S(1)}, bf16[128,512]{1,0:T(8,128)(2,1)S(1)}, u32[]{:S(2)}, u32[]{:S(2)}) %collective-permute-start.5) | collective-permute-done | bytes 131104 | tf_op jit(solution)/shard_map/ppermute | solution.py:335
  102.3 1.3 collective-permute-done.6
  103.6 1.0 pad_maximum_fusion.1
  104.5 0.6 gather_fusion.2
  105.1 0.3 copy.83
  105.4 4.8 %multiply_reduce_fusion.1 = (f32[128]{0:T(128)S(1)}, f32[128,2048]{1,0:T(8,128)S(1)}) fusion(bf16[128,2048]{0,1:T(8,128)(2,1)S(1)} %bitcast.62, bf16[2048,2048]{1,0:T(8,128)(2,1)} %all-gather.3.cloned.1.call-done), kind=kOutput, calls=%fused_computation.17 | convolution fusion | flops 1074265984 | bytes 9961984 | tf_op jit(solution)/shard_map/dot_general | solution.py:342
  110.3 0.2 add_convert_fusion.1
  110.5 2.6 %multiply_reduce_fusion = (f32[128]{0:T(128)S(1)}, f32[128,2048]{1,0:T(8,128)S(1)}) fusion(bf16[2048,512]{0,1:T(8,128)(2,1)} %all-gather.5.cloned.1.call-done, bf16[128,2048]{1,0:T(8,128)(2,1)S(1)} %add_convert_fusion.1, bf16[512,256]{1,0:T(8,128)(2,1)} %param.29, s32[]{:T(128)S(6)} %select_n.242), kind=kOutput, calls=%fused_computation.15 | convolution fusion | flops 269320064 | bytes 3736068 | tf_op jit(solution)/shard_map/dot_general | solution.py:354
  113.2 0.2 add_convert_fusion
  113.5 0.1 collective-permute-start.7
  113.5 2.2 %collective-permute-start.8 = (bf16[128,512]{1,0:T(8,128)(2,1)S(1)}, bf16[128,512]{1,0:T(8,128)(2,1)S(1)}, u32[]{:S(2)}, u32[]{:S(2)}) collective-permute-start(bf16[128,512]{1,0:T(8,128)(2,1)S(1)} %get-tuple-element.47), channel_id=1, source_target_pairs={{0,2},{1,3},{2,0},{3,1},{4,6},{5,7},{6,4},{7,5},{8,10},{9,11},{10,... | collective-permute-start | bytes 393224 | tf_op jit(solution)/shard_map/ppermute | solution.py:241
  115.8 5.9 %collective-permute-done.8 = bf16[128,512]{1,0:T(8,128)(2,1)S(1)} collective-permute-done((bf16[128,512]{1,0:T(8,128)(2,1)S(1)}, bf16[128,512]{1,0:T(8,128)(2,1)S(1)}, u32[]{:S(2)}, u32[]{:S(2)}) %collective-permute-start.8) | collective-permute-done | bytes 131104 | tf_op jit(solution)/shard_map/ppermute | solution.py:241
  121.7 0.6 collective-permute-done.9
  122.3 0.1 pad_maximum_fusion.3
  122.4 1.4 %gather_fusion.3 = bf16[4,128,512]{2,1,0:T(8,128)(2,1)} fusion(bf16[4,128,512]{2,1,0:T(8,128)(2,1)S(1)} %pad_maximum_fusion.3, s32[1024]{0:T(1024)S(1)} %pad_clamp_fusion.1), kind=kCustom, calls=%fused_computation.3 | custom fusion | bytes 1048592 | tf_op jit(solution)/shard_map/gather | solution.py:243
  (62 shorter events, 0.4 us)
Async XLA Ops:
  6.5 0.7 copy-start.12
  6.5 0.9 copy-start.10
  6.5 98.9 %all-gather.3.cloned.1.call-start = ((), (), s32[]{:S(2)}) async-start(), calls=%async_computation.2 | async-start | bytes 10485760 | tf_op jit(solution)/shard_map/all_gather | solution.py:316
  8.4 11.6 %all-to-all-start = ((s32[8,1,6]{2,1,0:T(1,128)}), s32[8,1,6]{2,1,0:T(1,128)S(1)}, u32[]{:S(2)}, u32[]{:S(2)}) async-start(s32[8,1,6]{2,1,0:T(1,128)} %copy.80), calls=%async_computation | async-start | bytes 8192 | tf_op jit(solution)/shard_map/all_to_all | solution.py:282
  22.0 3.9 %copy-start.7 = (bf16[512]{0:T(512)(128)(2,1)S(1)}, bf16[512]{0:T(512)(128)(2,1)}, u32[]{:S(2)}) copy-start(bf16[512]{0:T(512)(128)(2,1)} %param.28) | copy-start | bytes 3076
  22.0 3.9 %copy-start.8 = (bf16[512]{0:T(512)(128)(2,1)S(1)}, bf16[512]{0:T(512)(128)(2,1)}, u32[]{:S(2)}) copy-start(bf16[512]{0:T(512)(128)(2,1)} %param.32) | copy-start | bytes 3076
  22.0 4.0 %copy-start.3 = (bf16[512,512]{1,0:T(8,128)(2,1)S(1)}, bf16[512,512]{1,0:T(8,128)(2,1)}, u32[]{:S(2)}) copy-start(bf16[512,512]{1,0:T(8,128)(2,1)} %param.21) | copy-start | bytes 1572868
  22.0 8.4 %copy-start.4 = (bf16[512,256]{1,0:T(8,128)(2,1)S(1)}, bf16[512,256]{1,0:T(8,128)(2,1)}, u32[]{:S(2)}) copy-start(bf16[512,256]{1,0:T(8,128)(2,1)} %param.30) | copy-start | bytes 786436
  22.0 8.6 %copy-start.5 = (bf16[256,512]{1,0:T(8,128)(2,1)S(1)}, bf16[256,512]{1,0:T(8,128)(2,1)}, u32[]{:S(2)}) copy-start(bf16[256,512]{1,0:T(8,128)(2,1)} %param.31) | copy-start | bytes 786436
  22.0 38.7 %all-to-all-start.1 = ((bf16[8,6,64,256]{3,2,1,0:T(8,128)(2,1)}), bf16[8,6,64,256]{3,2,1,0:T(8,128)(2,1)S(1)}, u32[]{:S(2)}, u32[]{:S(2)}) async-start(bf16[8,6,64,256]{3,2,1,0:T(8,128)(2,1)} %bitcast.20), calls=%async_computation.1 | async-start | bytes 3145728 | tf_op jit(solution)/shard_map/all_to_all | solution.py:291
  25.7 5.7 %copy-start.11 = (s32[1,8]{1,0:T(1,128)S(1)}, s32[1,8]{1,0:T(1,128)}, u32[]{:S(2)}) copy-start(s32[1,8]{1,0:T(1,128)} %param.37) | copy-start | bytes 100
  25.8 6.1 %copy-start.6 = (s32[1,8]{1,0:T(1,128)S(1)}, s32[1,8]{1,0:T(1,128)}, u32[]{:S(2)}) copy-start(s32[1,8]{1,0:T(1,128)} %param.35) | copy-start | bytes 100
  25.8 6.3 %copy-start.9 = (s32[1,8]{1,0:T(1,128)S(1)}, s32[1,8]{1,0:T(1,128)}, u32[]{:S(2)}) copy-start(s32[1,8]{1,0:T(1,128)} %param.36) | copy-start | bytes 100
  25.8 84.7 %all-gather.5.cloned.1.call-start = ((), (), s32[]{:S(2)}) async-start(), calls=%async_computation.3 | async-start | bytes 2621440 | tf_op jit(solution)/shard_map/all_gather | solution.py:317
  26.8 41.3 %collective-permute-start = (bf16[136,512]{1,0:T(8,128)(2,1)}, bf16[136,512]{1,0:T(8,128)(2,1)}, u32[]{:S(2)}, u32[]{:S(2)}) collective-permute-start(bf16[136,512]{1,0:T(8,128)(2,1)} %get-tuple-element.42), channel_id=1, source_target_pairs={{0,1},{1,2},{2,3},{3,0},{4,5},{5,6},{6,7},{7,4},{8,9},{9,10},{10,1... | collective-permute-start | bytes 417800 | tf_op jit(solution)/shard_map/ppermute | solution.py:227
  30.0 38.2 %collective-permute-start.1 = (bf16[136,512]{1,0:T(8,128)(2,1)}, bf16[136,512]{1,0:T(8,128)(2,1)}, u32[]{:S(2)}, u32[]{:S(2)}) collective-permute-start(bf16[136,512]{1,0:T(8,128)(2,1)} %get-tuple-element.43), channel_id=1, source_target_pairs={{0,2},{1,3},{2,0},{3,1},{4,6},{5,7},{6,4},{7,5},{8,10},{9,11},{10,... | collective-permute-start | bytes 417800 | tf_op jit(solution)/shard_map/ppermute | solution.py:227
  30.2 37.9 %collective-permute-start.2 = (bf16[136,512]{1,0:T(8,128)(2,1)S(1)}, bf16[136,512]{1,0:T(8,128)(2,1)}, u32[]{:S(2)}, u32[]{:S(2)}) collective-permute-start(bf16[136,512]{1,0:T(8,128)(2,1)S(1)} %get-tuple-element.44), channel_id=1, source_target_pairs={{0,3},{1,0},{2,1},{3,2},{4,7},{5,4},{6,5},{7,6},{8,11},{9,8},{10,9... | collective-permute-start | bytes 417800 | tf_op jit(solution)/shard_map/ppermute | solution.py:227
  60.7 13.0 %copy-start = (bf16[8,6,64,256]{3,2,1,0:T(8,128)(2,1)}, bf16[8,6,64,256]{3,2,1,0:T(8,128)(2,1)S(1)}, u32[]{:S(2)}) copy-start(bf16[8,6,64,256]{3,2,1,0:T(8,128)(2,1)S(1)} %all-to-all-done.1) | copy-start | bytes 4718596
  60.7 14.1 %collective-permute-start.3 = (bf16[8,6,64,256]{3,2,1,0:T(8,128)(2,1)S(1)}, bf16[8,6,64,256]{3,2,1,0:T(8,128)(2,1)S(1)}, u32[]{:S(2)}, u32[]{:S(2)}) collective-permute-start(bf16[8,6,64,256]{3,2,1,0:T(8,128)(2,1)S(1)} %all-to-all-done.1), channel_id=1, source_target_pairs={{0,1},{1,0},{2,3},{3,2},{4,5},{5,4},{6,7},{7,6},{8,9},{9,8},{10,11... | collective-permute-start | bytes 4718600 | tf_op jit(solution)/shard_map/ppermute | solution.py:292
  74.8 1.2 copy-start.1
  93.3 6.3 %collective-permute-start.4 = (bf16[128,512]{1,0:T(8,128)(2,1)S(1)}, bf16[128,512]{1,0:T(8,128)(2,1)S(1)}, u32[]{:S(2)}, u32[]{:S(2)}) collective-permute-start(bf16[128,512]{1,0:T(8,128)(2,1)S(1)} %get-tuple-element.49), channel_id=1, source_target_pairs={{0,1},{1,2},{2,3},{3,0},{4,5},{5,6},{6,7},{7,4},{8,9},{9,10},{10,1... | collective-permute-start | bytes 393224 | tf_op jit(solution)/shard_map/ppermute | solution.py:335
  93.4 8.9 %collective-permute-start.5 = (bf16[128,512]{1,0:T(8,128)(2,1)S(1)}, bf16[128,512]{1,0:T(8,128)(2,1)S(1)}, u32[]{:S(2)}, u32[]{:S(2)}) collective-permute-start(bf16[128,512]{1,0:T(8,128)(2,1)S(1)} %get-tuple-element.51), channel_id=1, source_target_pairs={{0,2},{1,3},{2,0},{3,1},{4,6},{5,7},{6,4},{7,5},{8,10},{9,11},{10,... | collective-permute-start | bytes 393224 | tf_op jit(solution)/shard_map/ppermute | solution.py:335
  93.5 10.1 %collective-permute-start.6 = (bf16[128,512]{1,0:T(8,128)(2,1)S(1)}, bf16[128,512]{1,0:T(8,128)(2,1)S(1)}, u32[]{:S(2)}, u32[]{:S(2)}) collective-permute-start(bf16[128,512]{1,0:T(8,128)(2,1)S(1)} %get-tuple-element.50), channel_id=1, source_target_pairs={{0,3},{1,0},{2,1},{3,2},{4,7},{5,4},{6,5},{7,6},{8,11},{9,8},{10,9... | collective-permute-start | bytes 393224 | tf_op jit(solution)/shard_map/ppermute | solution.py:335
  105.4 4.8 %copy-start.2 = (f32[4,16,8,512]{3,2,0,1:T(8,128)S(1)}, f32[4,16,8,512]{3,2,0,1:T(8,128)}, u32[]{:S(2)}) copy-start(f32[4,16,8,512]{3,2,0,1:T(8,128)} %copy.87) | copy-start | bytes 3145732
  113.5 2.3 %collective-permute-start.7 = (bf16[128,512]{1,0:T(8,128)(2,1)S(1)}, bf16[128,512]{1,0:T(8,128)(2,1)S(1)}, u32[]{:S(2)}, u32[]{:S(2)}) collective-permute-start(bf16[128,512]{1,0:T(8,128)(2,1)S(1)} %get-tuple-element.48), channel_id=1, source_target_pairs={{0,1},{1,2},{2,3},{3,0},{4,5},{5,6},{6,7},{7,4},{8,9},{9,10},{10,1... | collective-permute-start | bytes 393224 | tf_op jit(solution)/shard_map/ppermute | solution.py:241
  113.5 8.2 %collective-permute-start.8 = (bf16[128,512]{1,0:T(8,128)(2,1)S(1)}, bf16[128,512]{1,0:T(8,128)(2,1)S(1)}, u32[]{:S(2)}, u32[]{:S(2)}) collective-permute-start(bf16[128,512]{1,0:T(8,128)(2,1)S(1)} %get-tuple-element.47), channel_id=1, source_target_pairs={{0,2},{1,3},{2,0},{3,1},{4,6},{5,7},{6,4},{7,5},{8,10},{9,11},{10,... | collective-permute-start | bytes 393224 | tf_op jit(solution)/shard_map/ppermute | solution.py:241
  115.8 6.6 %collective-permute-start.9 = (bf16[128,512]{1,0:T(8,128)(2,1)S(1)}, bf16[128,512]{1,0:T(8,128)(2,1)S(1)}, u32[]{:S(2)}, u32[]{:S(2)}) collective-permute-start(bf16[128,512]{1,0:T(8,128)(2,1)S(1)} %get-tuple-element.46), channel_id=1, source_target_pairs={{0,3},{1,0},{2,1},{3,2},{4,7},{5,4},{6,5},{7,6},{8,11},{9,8},{10,9... | collective-permute-start | bytes 393224 | tf_op jit(solution)/shard_map/ppermute | solution.py:241
Sparse Core Ops, SparseCore 0:
  8.9 66.7 all-gather.2
  77.3 26.8 all-gather.4

commit v13 on v10

--- a/solution.py
+++ b/solution.py
@@ -104,8 +104,9 @@
             stacked, keys, (((1,), (1,)), ((), ())), preferred_element_type=jnp.float32
         ) * scale
         seen = (kown_ref[c] == row_owner) & (kpos_ref[c] <= row_index)
-        seen = jnp.concatenate([seen] * heads, axis=0)
-        s = jnp.where(seen, s, -1e30)
+        s = jnp.where(seen[None], s.reshape(heads, ROW_BLOCK, KEY_CHUNK), -1e30).reshape(
+            heads * ROW_BLOCK, KEY_CHUNK
+        )
         s_scr[c] = s
         return jnp.maximum(highest, jnp.max(s, axis=1, keepdims=True))
 
@@ -312,10 +313,25 @@
     row_hidden = row_hidden_gains[: hidden_parts.shape[1]]
     full_attn_gain = row_hidden_gains[hidden_parts.shape[1]]
     full_ple_gain = row_hidden_gains[hidden_parts.shape[1] + 1]
-    row_attention = rows_to_columns(attention, "tp")
-    part_rows = row_attention.shape[0]
+    parts = attention.reshape(tp_size, -1, attention.shape[1])
+    width = attention.shape[1]
+    projected = jnp.dot(
+        parts[tp_index],
+        lax.dynamic_slice_in_dim(full_weight, tp_index * width, width, 0),
+        preferred_element_type=jnp.float32,
+    )
+    for shift in range(1, tp_size):
+        outgoing = lax.dynamic_index_in_dim(parts, (tp_index + shift) % tp_size, 0, keepdims=False)
+        perm = [(i, (i + shift) % tp_size) for i in range(tp_size)]
+        piece = lax.ppermute(outgoing, "tp", perm)
+        source = (tp_index - shift) % tp_size
+        projected = projected + jnp.dot(
+            piece,
+            lax.dynamic_slice_in_dim(full_weight, source * width, width, 0),
+            preferred_element_type=jnp.float32,
+        )
+    part_rows = parts.shape[1]
     row_ple = lax.dynamic_slice_in_dim(ple_input, tp_index * part_rows, part_rows, 0)
-    projected = jnp.dot(row_attention, full_weight, preferred_element_type=jnp.float32)
     squares = jnp.sum(projected * projected, axis=1)
     normed = (
         projected

time: 128 us -> 126 us (0.984)
  waiting for transfers between devices: 50.8 us -> 43.5 us
  matrix products: 7.38 us -> 11.1 us
  Pallas kernels: 19 us -> 20.9 us
    ppermute x6 -> x3, waiting for transfers between devices: 12.6 us -> 0.01 us  [rows_to_columns(): received.append(lax.ppermute(outgoing, axis_name, perm))]
    ppermute x0 -> x3, waiting for transfers between devices: none -> 4.76 us  [shards(): piece = lax.ppermute(outgoing, 'tp', perm)]
    dot_general x1 -> x4, matrix products: 4.74 us -> 8.42 us  [the longest x3 6.29 us: shards(): jnp.dot(piece, lax.dynamic_slice_in_dim(full_weight, source * width, widt...]
    ppermute x6 -> x3, starting transfers between devices: 5.75 us -> 3.7 us  [rows_to_columns(): received.append(lax.ppermute(outgoing, axis_name, perm))]
    pallas_call x1, Pallas kernels: 19 us -> 20.9 us  [sparse_attention(): pl.pallas_call(attention_kernel, grid_spec=pltpu.PrefetchScalarGridSpec(n...]
    ppermute x0 -> x3, starting transfers between devices: none -> 1.75 us  [shards(): piece = lax.ppermute(outgoing, 'tp', perm)]
  transfers between devices with their start and end apart: 14 -> 14, of which waited for: 8 -> 8; matrix products, arithmetic and copies ran while one was open for 15% -> 18% of each run, Pallas kernels for 15% -> 17%
where the time goes in v13:
time: 126 us
  waiting for transfers between devices  43.5 us (35%)
  starting transfers between devices  21.1 us (17%)
  Pallas kernels  20.9 us (17%)
  between operations  13.9 us (11%)
  matrix products  11.1 us (9%)
  local copies, waits for them, and re-layouts  8.63 us (7%)
  other arithmetic  6.88 us (5%)
    all_to_all x1, waiting for transfers between devices, shards(): lax.all_to_all(outgoing, 'req', split_axis=0, concat_axis=0, tiled=True)  28.8 us
    pallas_call x1, Pallas kernels, sparse_attention(): pl.pallas_call(attention_kernel, grid_spec=pltpu.PrefetchScalarGridSpec(n...  20.9 us
    ppermute x3, waiting for transfers between devices, columns_to_rows(): received.append(lax.ppermute(outgoing, axis_name, perm))  6.56 us
    all_to_all x1, starting transfers between devices, shards(): lax.all_to_all(request_table, 'req', split_axis=0, concat_axis=0, tiled=T...  6.38 us
    dot_general x3, matrix products, shards(): jnp.dot(piece, lax.dynamic_slice_in_dim(full_weight, source * width, widt...  6.29 us
    ppermute x3, waiting for transfers between devices, shards(): piece = lax.ppermute(outgoing, 'tp', perm)  4.76 us
    all_to_all x1, starting transfers between devices, shards(): lax.all_to_all(outgoing, 'req', split_axis=0, concat_axis=0, tiled=True)  3.75 us
    ppermute x3, starting transfers between devices, rows_to_columns(): received.append(lax.ppermute(outgoing, axis_name, perm))  3.7 us
  transfers between devices with their start and end apart: 14, of which 8 were waited for; matrix products, arithmetic and copies ran while one was open for 18% of the time, Pallas kernels for 17%

profile of v13, /device:TPU:1, one launch (start us, length us, event | category | flops | bytes accessed | tf_op | source)
XLA Modules:
  0.0 125.9 jit_solution(9365453927619417815)
XLA Ops:
  6.5 0.7 all-gather.3.cloned.1.call-update
  7.3 0.2 convert_reduce_fusion.1
  7.5 0.2 select_reduce_fusion.2
  7.7 0.7 copy.76
  8.4 6.4 %all-to-all-start = ((s32[8,1,6]{2,1,0:T(1,128)}), s32[8,1,6]{2,1,0:T(1,128)S(1)}, u32[]{:S(2)}, u32[]{:S(2)}) async-start(s32[8,1,6]{2,1,0:T(1,128)} %copy.76), calls=%async_computation | async-start | bytes 8192 | tf_op jit(solution)/shard_map/all_to_all | solution.py:278
  14.7 2.6 %dynamic-slice_select_fusion = bf16[48,64,256]{2,1,0:T(8,128)(2,1)S(1)} fusion(bf16[48,64,512]{2,1,0:T(8,128)(2,1)} %param.26, s32[]{:T(128)S(6)} %select_n.244, bf16[48,64,512]{2,1,0:T(8,128)(2,1)} %param.25, pred[]{:T(512)S(6)} %eq.140), kind=kLoop, calls=%fused_computation.12 | loop fusion | flops 786432 | bytes 4718597 | tf_op jit(solution)/shard_map/jit(_where)/select_n | solution.py:285
  17.3 2.7 %all-to-all-done = s32[8,1,6]{2,1,0:T(1,128)S(1)} async-done(((s32[8,1,6]{2,1,0:T(1,128)}), s32[8,1,6]{2,1,0:T(1,128)S(1)}, u32[]{:S(2)}, u32[]{:S(2)}) %all-to-all-start) | async-done | bytes 224 | tf_op jit(solution)/shard_map/all_to_all | solution.py:278
  20.0 0.1 reshape.539
  20.1 1.9 %gather_fusion.1 = bf16[48,64,256]{2,1,0:T(8,128)(2,1)} fusion(bf16[48,64,256]{2,1,0:T(8,128)(2,1)S(1)} %dynamic-slice_select_fusion, s32[1024]{0:T(1024)S(1)} %pad_clamp_fusion), kind=kCustom, calls=%fused_computation.1 | custom fusion | bytes 3145920 | tf_op jit(solution)/shard_map/gather | solution.py:286
  22.0 0.0 copy-start.3
  22.0 3.7 %all-to-all-start.1 = ((bf16[8,6,64,256]{3,2,1,0:T(8,128)(2,1)}), bf16[8,6,64,256]{3,2,1,0:T(8,128)(2,1)S(1)}, u32[]{:S(2)}, u32[]{:S(2)}) async-start(bf16[8,6,64,256]{3,2,1,0:T(8,128)(2,1)} %bitcast.19), calls=%async_computation.1 | async-start | bytes 3145728 | tf_op jit(solution)/shard_map/all_to_all | solution.py:287
  25.8 0.0 all-gather.5.cloned.1.call-start
  26.0 0.1 fusion.12
  26.1 3.2 %collective-permute-start = (bf16[136,512]{1,0:T(8,128)(2,1)S(1)}, bf16[136,512]{1,0:T(8,128)(2,1)S(1)}, u32[]{:S(2)}, u32[]{:S(2)}) collective-permute-start(bf16[136,512]{1,0:T(8,128)(2,1)S(1)} %get-tuple-element.42), channel_id=1, source_target_pairs={{0,1},{1,2},{2,3},{3,0},{4,5},{5,6},{6,7},{7,4},{8,9},{9,10},{10,1... | collective-permute-start | bytes 417800 | tf_op jit(solution)/shard_map/ppermute | solution.py:223
  29.3 0.3 collective-permute-start.1
  29.6 0.2 collective-permute-start.2
  29.8 0.1 copy.78
  29.9 0.8 pad_maximum_fusion.1
  30.8 0.0 all-gather.5.cloned.1.call-update
  30.8 0.2 reduce-window_clone.1
  31.0 0.1 convert_reduce_fusion.2
  31.1 0.1 slice.54
  31.2 0.1 slice.55
  31.3 0.2 reduce-window_1_clone.1
  31.5 0.1 convert_reduce_fusion
  31.6 0.2 select_reduce_fusion.3
  31.8 0.1 select_reduce_fusion.1
  32.0 28.8 %all-to-all-done.1 = bf16[8,6,64,256]{3,2,1,0:T(8,128)(2,1)S(1)} async-done(((bf16[8,6,64,256]{3,2,1,0:T(8,128)(2,1)}), bf16[8,6,64,256]{3,2,1,0:T(8,128)(2,1)S(1)}, u32[]{:S(2)}, u32[]{:S(2)}) %all-to-all-start.1) | async-done | bytes 1572896 | tf_op jit(solution)/shard_map/all_to_all | solution.py:287
  60.7 3.1 %collective-permute-start.3 = (bf16[8,6,64,256]{3,2,1,0:T(8,128)(2,1)S(1)}, bf16[8,6,64,256]{3,2,1,0:T(8,128)(2,1)}, u32[]{:S(2)}, u32[]{:S(2)}) collective-permute-start(bf16[8,6,64,256]{3,2,1,0:T(8,128)(2,1)S(1)} %all-to-all-done.1), channel_id=1, source_target_pairs={{0,1},{1,0},{2,3},{3,2},{4,5},{5,4},{6,7},{7,6},{8,9},{9,8},{10,11... | collective-permute-start | bytes 4718600 | tf_op jit(solution)/shard_map/ppermute | solution.py:288
  63.8 0.1 copy.67
  63.9 0.1 copy.63
  64.0 0.1 copy.71
  64.1 0.6 multiply_add_fusion.1.slots_ref
  64.7 0.7 pad_add_fusion.1.meta_ref
  65.3 0.6 reshape.523.kown_ref
  65.9 0.8 copy.77.rown_ref
  66.8 0.7 stack.47.ranges_ref
  67.5 0.1 fusion.66
  67.6 0.1 pad_maximum_fusion
  67.7 0.6 gather_fusion
  68.3 0.1 convert_bitcast_fusion
  68.4 0.1 copy.81
  68.6 20.9 %shard_map.163 = bf16[512,512]{1,0:T(8,128)(2,1)} custom-call(s32[4,5]{1,0:T(4,128)} %stack.47.ranges_ref, s32[48]{0:T(128)} %multiply_add_fusion.1.slots_ref, s32[2]{0:T(128)} %pad_add_fusion.1.meta_ref, bf16[512,512]{1,0:T(8,128)(2,1)} %q_ref.1, bf16[48,64,256]{2,1,0:T(8,128)(2,1)} %bitcast.61, bf16[48,64,256]{2,1,0:T(8,128)(2,1)} %bitcast.21.partner_ref, ...), custom_call_target="tpu_custom_call" | custom-call | tf_op jit(solution)/shard_map/pallas_call | solution.py:178
  89.5 1.1 dynamic-slice_bitcast_fusion.2
  90.5 1.3 %collective-permute-start.4 = (bf16[128,512]{1,0:T(8,128)(2,1)S(1)}, bf16[128,512]{1,0:T(8,128)(2,1)S(1)}, u32[]{:S(2)}, u32[]{:S(2)}) collective-permute-start(bf16[128,512]{1,0:T(8,128)(2,1)S(1)} %get-tuple-element.51), channel_id=1, source_target_pairs={{0,1},{1,2},{2,3},{3,0},{4,5},{5,6},{6,7},{7,4},{8,9},{9,10},{10,1... | collective-permute-start | bytes 393224 | tf_op jit(solution)/shard_map/ppermute | solution.py:326
  91.9 0.4 collective-permute-start.5
  92.3 2.1 %fusion.5 = f32[128,2048]{1,0:T(8,128)S(1)} fusion(bf16[2048,2048]{1,0:T(8,128)(2,1)} %all-gather.3.cloned.1.call-done, s32[]{:T(128)S(6)} %select_n.251, bf16[4,128,512]{2,1,0:T(8,128)(2,1)} %bitcast.66, s32[]{:T(128)S(6)} %select_n.223), kind=kOutput, calls=%fused_computation.10 | convolution fusion | flops 268435456 | bytes 3276808 | tf_op jit(solution)/shard_map/dot_general | solution.py:318
  94.4 3.3 %collective-permute-done.4 = bf16[128,512]{1,0:T(8,128)(2,1)S(1)} collective-permute-done((bf16[128,512]{1,0:T(8,128)(2,1)S(1)}, bf16[128,512]{1,0:T(8,128)(2,1)S(1)}, u32[]{:S(2)}, u32[]{:S(2)}) %collective-permute-start.4) | collective-permute-done | bytes 131104 | tf_op jit(solution)/shard_map/ppermute | solution.py:326
  97.7 2.0 %convolution_add_fusion.1 = f32[128,2048]{1,0:T(8,128)S(1)} fusion(f32[128,2048]{1,0:T(8,128)S(1)} %fusion.5, bf16[128,512]{1,0:T(8,128)(2,1)S(1)} %collective-permute-done.4, bf16[2048,2048]{1,0:T(8,128)(2,1)} %all-gather.3.cloned.1.call-done, s32[]{:T(128)S(6)} %select_n.253), kind=kOutput, calls=%fused_computation.5 | convolution fusion | flops 268697600 | bytes 4325380 | tf_op jit(solution)/shard_map/dot_general | solution.py:328
  99.7 1.1 collective-permute-done.6
  100.8 2.0 %fusion.1 = f32[128,2048]{1,0:T(8,128)S(1)} fusion(bf16[128,512]{1,0:T(8,128)(2,1)S(1)} %collective-permute-done.6, bf16[2048,2048]{1,0:T(8,128)(2,1)} %all-gather.3.cloned.1.call-done, s32[]{:T(128)S(6)} %select_n.257), kind=kOutput, calls=%fused_computation.6 | convolution fusion | flops 268435456 | bytes 3276804 | tf_op jit(solution)/shard_map/dot_general | solution.py:328
  102.9 0.4 collective-permute-done.5
  103.3 2.2 %multiply_reduce_fusion.1 = (f32[128]{0:T(128)S(1)}, f32[128,2048]{1,0:T(8,128)S(1)}) fusion(f32[128,2048]{1,0:T(8,128)S(1)} %fusion.1, f32[128,2048]{1,0:T(8,128)S(1)} %convolution_add_fusion.1, bf16[128,512]{1,0:T(8,128)(2,1)S(1)} %collective-permute-done.5, bf16[2048,2048]{1,0:T(8,128)(2,1)} %all-gather.3.cloned.1.call-done, s32[]{:T(128)S(6)} %select_n.255), kind=kOutput, calls=%fused_computation.25 | convolution fusion | flops 269483904 | bytes 5374468 | tf_op jit(solution)/shard_map/dot_general | solution.py:328
  105.5 0.2 add_convert_fusion.1
  105.7 0.0 all-gather.5.cloned.1.call-done
  105.8 2.6 %multiply_reduce_fusion = (f32[128]{0:T(128)S(1)}, f32[128,2048]{1,0:T(8,128)S(1)}) fusion(bf16[2048,512]{0,1:T(8,128)(2,1)} %all-gather.5.cloned.1.call-done, bf16[128,2048]{1,0:T(8,128)(2,1)S(1)} %add_convert_fusion.1, bf16[512,256]{1,0:T(8,128)(2,1)} %param.29, s32[]{:T(128)S(6)} %select_n.258), kind=kOutput, calls=%fused_computation.23 | convolution fusion | flops 269320064 | bytes 3736068 | tf_op jit(solution)/shard_map/dot_general | solution.py:346
  108.4 0.2 add_convert_fusion
  108.7 1.1 collective-permute-start.7
  109.8 1.3 %collective-permute-start.8 = (bf16[128,512]{1,0:T(8,128)(2,1)S(1)}, bf16[128,512]{1,0:T(8,128)(2,1)S(1)}, u32[]{:S(2)}, u32[]{:S(2)}) collective-permute-start(bf16[128,512]{1,0:T(8,128)(2,1)S(1)} %get-tuple-element.47), channel_id=1, source_target_pairs={{0,2},{1,3},{2,0},{3,1},{4,6},{5,7},{6,4},{7,5},{8,10},{9,11},{10,... | collective-permute-start | bytes 393224 | tf_op jit(solution)/shard_map/ppermute | solution.py:237
  111.1 1.4 %collective-permute-done.7 = bf16[128,512]{1,0:T(8,128)(2,1)S(1)} collective-permute-done((bf16[128,512]{1,0:T(8,128)(2,1)S(1)}, bf16[128,512]{1,0:T(8,128)(2,1)S(1)}, u32[]{:S(2)}, u32[]{:S(2)}) %collective-permute-start.7) | collective-permute-done | bytes 131104 | tf_op jit(solution)/shard_map/ppermute | solution.py:237
  112.5 4.5 %collective-permute-done.8 = bf16[128,512]{1,0:T(8,128)(2,1)S(1)} collective-permute-done((bf16[128,512]{1,0:T(8,128)(2,1)S(1)}, bf16[128,512]{1,0:T(8,128)(2,1)S(1)}, u32[]{:S(2)}, u32[]{:S(2)}) %collective-permute-start.8) | collective-permute-done | bytes 131104 | tf_op jit(solution)/shard_map/ppermute | solution.py:237
  117.0 0.6 collective-permute-done.9
  117.7 0.1 pad_maximum_fusion.2
  117.7 1.4 %gather_fusion.2 = bf16[4,128,512]{2,1,0:T(8,128)(2,1)} fusion(bf16[4,128,512]{2,1,0:T(8,128)(2,1)S(1)} %pad_maximum_fusion.2, s32[1024]{0:T(1024)S(1)} %pad_clamp_fusion.1), kind=kCustom, calls=%fused_computation.2 | custom fusion | bytes 1048592 | tf_op jit(solution)/shard_map/gather | solution.py:239
  (56 shorter events, 0.3 us)
Async XLA Ops:
  6.5 0.7 copy-start.10
  6.5 0.9 copy-start.8
  6.5 85.8 %all-gather.3.cloned.1.call-start = ((), (), s32[]{:S(2)}) async-start(), calls=%async_computation.2 | async-start | bytes 10485760 | tf_op jit(solution)/shard_map/all_gather | solution.py:301
  8.4 11.6 %all-to-all-start = ((s32[8,1,6]{2,1,0:T(1,128)}), s32[8,1,6]{2,1,0:T(1,128)S(1)}, u32[]{:S(2)}, u32[]{:S(2)}) async-start(s32[8,1,6]{2,1,0:T(1,128)} %copy.76), calls=%async_computation | async-start | bytes 8192 | tf_op jit(solution)/shard_map/all_to_all | solution.py:278
  22.0 3.9 %copy-start.5 = (bf16[512]{0:T(512)(128)(2,1)S(1)}, bf16[512]{0:T(512)(128)(2,1)}, u32[]{:S(2)}) copy-start(bf16[512]{0:T(512)(128)(2,1)} %param.28) | copy-start | bytes 3076
  22.0 3.9 %copy-start.6 = (bf16[512]{0:T(512)(128)(2,1)S(1)}, bf16[512]{0:T(512)(128)(2,1)}, u32[]{:S(2)}) copy-start(bf16[512]{0:T(512)(128)(2,1)} %param.32) | copy-start | bytes 3076
  22.0 4.0 %copy-start.1 = (bf16[512,512]{1,0:T(8,128)(2,1)S(1)}, bf16[512,512]{1,0:T(8,128)(2,1)}, u32[]{:S(2)}) copy-start(bf16[512,512]{1,0:T(8,128)(2,1)} %param.21) | copy-start | bytes 1572868
  22.0 7.8 %copy-start.2 = (bf16[512,256]{1,0:T(8,128)(2,1)S(1)}, bf16[512,256]{1,0:T(8,128)(2,1)}, u32[]{:S(2)}) copy-start(bf16[512,256]{1,0:T(8,128)(2,1)} %param.30) | copy-start | bytes 786436
  22.0 8.0 %copy-start.3 = (bf16[256,512]{1,0:T(8,128)(2,1)S(1)}, bf16[256,512]{1,0:T(8,128)(2,1)}, u32[]{:S(2)}) copy-start(bf16[256,512]{1,0:T(8,128)(2,1)} %param.31) | copy-start | bytes 786436
  22.0 38.7 %all-to-all-start.1 = ((bf16[8,6,64,256]{3,2,1,0:T(8,128)(2,1)}), bf16[8,6,64,256]{3,2,1,0:T(8,128)(2,1)S(1)}, u32[]{:S(2)}, u32[]{:S(2)}) async-start(bf16[8,6,64,256]{3,2,1,0:T(8,128)(2,1)} %bitcast.19), calls=%async_computation.1 | async-start | bytes 3145728 | tf_op jit(solution)/shard_map/all_to_all | solution.py:287
  25.7 5.1 %copy-start.9 = (s32[1,8]{1,0:T(1,128)S(1)}, s32[1,8]{1,0:T(1,128)}, u32[]{:S(2)}) copy-start(s32[1,8]{1,0:T(1,128)} %param.37) | copy-start | bytes 100
  25.8 5.5 %copy-start.4 = (s32[1,8]{1,0:T(1,128)S(1)}, s32[1,8]{1,0:T(1,128)}, u32[]{:S(2)}) copy-start(s32[1,8]{1,0:T(1,128)} %param.35) | copy-start | bytes 100
  25.8 5.7 %copy-start.7 = (s32[1,8]{1,0:T(1,128)S(1)}, s32[1,8]{1,0:T(1,128)}, u32[]{:S(2)}) copy-start(s32[1,8]{1,0:T(1,128)} %param.36) | copy-start | bytes 100
  25.8 80.0 %all-gather.5.cloned.1.call-start = ((), (), s32[]{:S(2)}) async-start(), calls=%async_computation.3 | async-start | bytes 2621440 | tf_op jit(solution)/shard_map/all_gather | solution.py:302
  26.1 41.5 %collective-permute-start = (bf16[136,512]{1,0:T(8,128)(2,1)S(1)}, bf16[136,512]{1,0:T(8,128)(2,1)S(1)}, u32[]{:S(2)}, u32[]{:S(2)}) collective-permute-start(bf16[136,512]{1,0:T(8,128)(2,1)S(1)} %get-tuple-element.42), channel_id=1, source_target_pairs={{0,1},{1,2},{2,3},{3,0},{4,5},{5,6},{6,7},{7,4},{8,9},{9,10},{10,1... | collective-permute-start | bytes 417800 | tf_op jit(solution)/shard_map/ppermute | solution.py:223
  29.3 38.3 %collective-permute-start.1 = (bf16[136,512]{1,0:T(8,128)(2,1)S(1)}, bf16[136,512]{1,0:T(8,128)(2,1)S(1)}, u32[]{:S(2)}, u32[]{:S(2)}) collective-permute-start(bf16[136,512]{1,0:T(8,128)(2,1)S(1)} %get-tuple-element.43), channel_id=1, source_target_pairs={{0,2},{1,3},{2,0},{3,1},{4,6},{5,7},{6,4},{7,5},{8,10},{9,11},{10,... | collective-permute-start | bytes 417800 | tf_op jit(solution)/shard_map/ppermute | solution.py:223
  29.6 38.1 %collective-permute-start.2 = (bf16[136,512]{1,0:T(8,128)(2,1)S(1)}, bf16[136,512]{1,0:T(8,128)(2,1)S(1)}, u32[]{:S(2)}, u32[]{:S(2)}) collective-permute-start(bf16[136,512]{1,0:T(8,128)(2,1)S(1)} %get-tuple-element.44), channel_id=1, source_target_pairs={{0,3},{1,0},{2,1},{3,2},{4,7},{5,4},{6,5},{7,6},{8,11},{9,8},{10,9... | collective-permute-start | bytes 417800 | tf_op jit(solution)/shard_map/ppermute | solution.py:223
  60.7 7.7 %copy-start = (bf16[8,6,64,256]{3,2,1,0:T(8,128)(2,1)}, bf16[8,6,64,256]{3,2,1,0:T(8,128)(2,1)S(1)}, u32[]{:S(2)}) copy-start(bf16[8,6,64,256]{3,2,1,0:T(8,128)(2,1)S(1)} %all-to-all-done.1) | copy-start | bytes 4718596
  60.7 7.8 %collective-permute-start.3 = (bf16[8,6,64,256]{3,2,1,0:T(8,128)(2,1)S(1)}, bf16[8,6,64,256]{3,2,1,0:T(8,128)(2,1)}, u32[]{:S(2)}, u32[]{:S(2)}) collective-permute-start(bf16[8,6,64,256]{3,2,1,0:T(8,128)(2,1)S(1)} %all-to-all-done.1), channel_id=1, source_target_pairs={{0,1},{1,0},{2,3},{3,2},{4,5},{5,4},{6,7},{7,6},{8,9},{9,8},{10,11... | collective-permute-start | bytes 4718600 | tf_op jit(solution)/shard_map/ppermute | solution.py:288
  90.5 7.2 %collective-permute-start.4 = (bf16[128,512]{1,0:T(8,128)(2,1)S(1)}, bf16[128,512]{1,0:T(8,128)(2,1)S(1)}, u32[]{:S(2)}, u32[]{:S(2)}) collective-permute-start(bf16[128,512]{1,0:T(8,128)(2,1)S(1)} %get-tuple-element.51), channel_id=1, source_target_pairs={{0,1},{1,2},{2,3},{3,0},{4,5},{5,6},{6,7},{7,4},{8,9},{9,10},{10,1... | collective-permute-start | bytes 393224 | tf_op jit(solution)/shard_map/ppermute | solution.py:326
  91.9 9.0 %collective-permute-start.6 = (bf16[128,512]{1,0:T(8,128)(2,1)S(1)}, bf16[128,512]{1,0:T(8,128)(2,1)S(1)}, u32[]{:S(2)}, u32[]{:S(2)}) collective-permute-start(bf16[128,512]{1,0:T(8,128)(2,1)S(1)} %get-tuple-element.50), channel_id=1, source_target_pairs={{0,3},{1,0},{2,1},{3,2},{4,7},{5,4},{6,5},{7,6},{8,11},{9,8},{10,9... | collective-permute-start | bytes 393224 | tf_op jit(solution)/shard_map/ppermute | solution.py:326
  91.9 11.4 %collective-permute-start.5 = (bf16[128,512]{1,0:T(8,128)(2,1)S(1)}, bf16[128,512]{1,0:T(8,128)(2,1)S(1)}, u32[]{:S(2)}, u32[]{:S(2)}) collective-permute-start(bf16[128,512]{1,0:T(8,128)(2,1)S(1)} %get-tuple-element.49), channel_id=1, source_target_pairs={{0,2},{1,3},{2,0},{3,1},{4,6},{5,7},{6,4},{7,5},{8,10},{9,11},{10,... | collective-permute-start | bytes 393224 | tf_op jit(solution)/shard_map/ppermute | solution.py:326
  108.7 3.8 %collective-permute-start.7 = (bf16[128,512]{1,0:T(8,128)(2,1)S(1)}, bf16[128,512]{1,0:T(8,128)(2,1)S(1)}, u32[]{:S(2)}, u32[]{:S(2)}) collective-permute-start(bf16[128,512]{1,0:T(8,128)(2,1)S(1)} %get-tuple-element.48), channel_id=1, source_target_pairs={{0,1},{1,2},{2,3},{3,0},{4,5},{5,6},{6,7},{7,4},{8,9},{9,10},{10,1... | collective-permute-start | bytes 393224 | tf_op jit(solution)/shard_map/ppermute | solution.py:237
  109.8 7.2 %collective-permute-start.8 = (bf16[128,512]{1,0:T(8,128)(2,1)S(1)}, bf16[128,512]{1,0:T(8,128)(2,1)S(1)}, u32[]{:S(2)}, u32[]{:S(2)}) collective-permute-start(bf16[128,512]{1,0:T(8,128)(2,1)S(1)} %get-tuple-element.47), channel_id=1, source_target_pairs={{0,2},{1,3},{2,0},{3,1},{4,6},{5,7},{6,4},{7,5},{8,10},{9,11},{10,... | collective-permute-start | bytes 393224 | tf_op jit(solution)/shard_map/ppermute | solution.py:237
  111.1 6.6 %collective-permute-start.9 = (bf16[128,512]{1,0:T(8,128)(2,1)S(1)}, bf16[128,512]{1,0:T(8,128)(2,1)S(1)}, u32[]{:S(2)}, u32[]{:S(2)}) collective-permute-start(bf16[128,512]{1,0:T(8,128)(2,1)S(1)} %get-tuple-element.46), channel_id=1, source_target_pairs={{0,3},{1,0},{2,1},{3,2},{4,7},{5,4},{6,5},{7,6},{8,11},{9,8},{10,9... | collective-permute-start | bytes 393224 | tf_op jit(solution)/shard_map/ppermute | solution.py:237
Sparse Core Ops, SparseCore 0:
  8.9 66.7 all-gather.2
  77.3 27.0 all-gather.4

commit v14 on v13

--- a/solution.py
+++ b/solution.py
@@ -299,20 +299,27 @@
     )
     tp_size = lax.axis_size("tp")
     full_weight = lax.all_gather(out_weight, "tp", axis=0, tiled=True)
-    ple_joined = lax.all_gather(
-        jnp.concatenate([ple_gate_weight, ple_proj_weight.T], axis=1), "tp", axis=0, tiled=True
-    )
-    full_gate_weight = ple_joined[:, : ple_gate_weight.shape[1]]
-    full_proj_weight_t = ple_joined[:, ple_gate_weight.shape[1] :]
+    ple_joined = jnp.concatenate([ple_gate_weight, ple_proj_weight.T], axis=1)
+    assert ple_joined.shape[1] == hidden.shape[1]
     hidden_parts = hidden.reshape(tp_size, -1, hidden.shape[1])
     gain_rows = jnp.zeros((8, hidden.shape[1]), hidden.dtype).at[0].set(attn_gain).at[1].set(ple_gain)
-    with_gains = jnp.concatenate(
-        [hidden_parts, jnp.broadcast_to(gain_rows[None], (tp_size, 8, hidden.shape[1]))], axis=1
-    )
-    row_hidden_gains = rows_to_columns(with_gains.reshape(-1, hidden.shape[1]), "tp")
-    row_hidden = row_hidden_gains[: hidden_parts.shape[1]]
-    full_attn_gain = row_hidden_gains[hidden_parts.shape[1]]
-    full_ple_gain = row_hidden_gains[hidden_parts.shape[1] + 1]
+    with_all = jnp.concatenate(
+        [
+            hidden_parts,
+            jnp.broadcast_to(gain_rows[None], (tp_size, 8, hidden.shape[1])),
+            jnp.broadcast_to(ple_joined[None], (tp_size,) + ple_joined.shape),
+        ],
+        axis=1,
+    )
+    row_all = rows_to_columns(with_all.reshape(-1, hidden.shape[1]), "tp")
+    part_rows = hidden_parts.shape[1]
+    row_hidden = row_all[:part_rows]
+    full_attn_gain = row_all[part_rows]
+    full_ple_gain = row_all[part_rows + 1]
+    ple_blocks = row_all[part_rows + 8 :].reshape(ple_joined.shape[0], tp_size, hidden.shape[1])
+    ple_blocks = jnp.transpose(ple_blocks, (1, 0, 2)).reshape(-1, hidden.shape[1])
+    full_gate_weight = ple_blocks[:, : ple_gate_weight.shape[1]]
+    full_proj_weight_t = ple_blocks[:, ple_gate_weight.shape[1] :]
     parts = attention.reshape(tp_size, -1, attention.shape[1])
     width = attention.shape[1]
     projected = jnp.dot(
@@ -330,7 +337,6 @@
             lax.dynamic_slice_in_dim(full_weight, source * width, width, 0),
             preferred_element_type=jnp.float32,
         )
-    part_rows = parts.shape[1]
     row_ple = lax.dynamic_slice_in_dim(ple_input, tp_index * part_rows, part_rows, 0)
     squares = jnp.sum(projected * projected, axis=1)
     normed = (

time: 126 us -> 158 us (1.25)
  waiting for transfers between devices: 43.5 us -> 60 us
  other arithmetic: 6.88 us -> 14.3 us
  local copies, waits for them, and re-layouts: 8.63 us -> 14 us
    ppermute x3, waiting for transfers between devices: 0.01 us -> 21.8 us  [rows_to_columns(): received.append(lax.ppermute(outgoing, axis_name, perm))]
    ppermute x3, waiting for transfers between devices: 4.76 us -> 0.09 us  [shards(): piece = lax.ppermute(outgoing, 'tp', perm)]
    slice x0 -> x1, local copies, waits for them, and re-layouts: none -> 1.8 us  [shards(): row_all[part_rows + 8:]]
    another operation x1, other arithmetic: 0.07 us -> 1.82 us  [rows_to_columns(): blocks = jnp.stack(received)[order]]
    gather x1, local copies, waits for them, and re-layouts: 0.58 us -> 2.29 us  [rows_to_columns(): blocks = jnp.stack(received)[order]]
  transfers between devices with their start and end apart: 14 -> 13, of which waited for: 8 -> 8; matrix products, arithmetic and copies ran while one was open for 18% -> 19% of each run, Pallas kernels for 17% -> 13%
where the time goes in v14:
time: 158 us; the launch traced here: 156 us
  waiting for transfers between devices  60 us (38%)
  starting transfers between devices  21.9 us (14%)
  Pallas kernels  20.9 us (13%)
  other arithmetic  14.3 us (9%)
  local copies, waits for them, and re-layouts  14 us (9%)
  between operations  13.8 us (9%)
  matrix products  11.5 us (7%)
    all_to_all x1, waiting for transfers between devices, shards(): lax.all_to_all(outgoing, 'req', split_axis=0, concat_axis=0, tiled=True)  28.5 us
    ppermute x3, waiting for transfers between devices, rows_to_columns(): received.append(lax.ppermute(outgoing, axis_name, perm))  21.8 us
    pallas_call x1, Pallas kernels, sparse_attention(): pl.pallas_call(attention_kernel, grid_spec=pltpu.PrefetchScalarGridSpec(n...  20.9 us
    ppermute x3, waiting for transfers between devices, columns_to_rows(): received.append(lax.ppermute(outgoing, axis_name, perm))  6.56 us
    all_to_all x1, starting transfers between devices, shards(): lax.all_to_all(request_table, 'req', split_axis=0, concat_axis=0, tiled=T...  6.38 us
    dot_general x3, matrix products, shards(): jnp.dot(piece, lax.dynamic_slice_in_dim(full_weight, source * width, widt...  6.34 us
    all_to_all x1, starting transfers between devices, shards(): lax.all_to_all(outgoing, 'req', split_axis=0, concat_axis=0, tiled=True)  4.43 us
    ppermute x3, starting transfers between devices, rows_to_columns(): received.append(lax.ppermute(outgoing, axis_name, perm))  3.78 us
  transfers between devices with their start and end apart: 13, of which 8 were waited for; matrix products, arithmetic and copies ran while one was open for 19% of the time, Pallas kernels for 13%

profile of v14, /device:TPU:1, one launch (start us, length us, event | category | flops | bytes accessed | tf_op | source)
XLA Modules:
  0.0 156.5 jit_solution(2840222841762545129)
XLA Ops:
  6.5 0.7 all-gather.2.cloned.1.call-update
  7.3 0.9 convert_reduce_fusion.1
  8.2 0.7 add_bitcast_fusion.2
  8.8 0.7 iota_compare_fusion.4
  9.5 0.2 select_reduce_fusion.2
  9.7 0.7 copy.81
  10.4 6.4 %all-to-all-start = ((s32[8,1,6]{2,1,0:T(1,128)}), s32[8,1,6]{2,1,0:T(1,128)S(1)}, u32[]{:S(2)}, u32[]{:S(2)}) async-start(s32[8,1,6]{2,1,0:T(1,128)} %copy.81), calls=%async_computation | async-start | bytes 8192 | tf_op jit(solution)/shard_map/all_to_all | solution.py:278
  16.8 2.9 %dynamic-slice_select_fusion = bf16[48,64,256]{2,1,0:T(8,128)(2,1)S(1)} fusion(bf16[48,64,512]{2,1,0:T(8,128)(2,1)} %param.26, s32[]{:T(128)S(6)} %select_n.244, bf16[48,64,512]{2,1,0:T(8,128)(2,1)} %param.25, pred[]{:T(512)S(6)} %eq.140), kind=kLoop, calls=%fused_computation.14 | loop fusion | flops 786432 | bytes 4718597 | tf_op jit(solution)/shard_map/jit(_where)/select_n | solution.py:285
  19.6 2.4 %all-to-all-done = s32[8,1,6]{2,1,0:T(1,128)S(1)} async-done(((s32[8,1,6]{2,1,0:T(1,128)}), s32[8,1,6]{2,1,0:T(1,128)S(1)}, u32[]{:S(2)}, u32[]{:S(2)}) %all-to-all-start) | async-done | bytes 224 | tf_op jit(solution)/shard_map/all_to_all | solution.py:278
  22.1 1.9 %gather_fusion.1 = bf16[48,64,256]{2,1,0:T(8,128)(2,1)} fusion(bf16[48,64,256]{2,1,0:T(8,128)(2,1)S(1)} %dynamic-slice_select_fusion, s32[1024]{0:T(1024)S(1)} %pad_clamp_fusion), kind=kCustom, calls=%fused_computation.1 | custom fusion | bytes 3145920 | tf_op jit(solution)/shard_map/gather | solution.py:286
  24.1 4.4 %all-to-all-start.1 = ((bf16[8,6,64,256]{3,2,1,0:T(8,128)(2,1)}), bf16[8,6,64,256]{3,2,1,0:T(8,128)(2,1)}, u32[]{:S(2)}, u32[]{:S(2)}) async-start(bf16[8,6,64,256]{3,2,1,0:T(8,128)(2,1)} %bitcast.20), calls=%async_computation.1 | async-start | bytes 3145728 | tf_op jit(solution)/shard_map/all_to_all | solution.py:287
  28.6 0.1 copy.65
  28.8 0.2 copy.66
  29.1 0.2 broadcast_in_dim.115
  29.3 0.3 copy-done.2
  29.6 0.2 pad_maximum_fusion
  29.9 0.2 constant_dynamic-slice_fusion.3
  30.1 3.3 %collective-permute-start = (bf16[648,512]{1,0:T(8,128)(2,1)S(1)}, bf16[648,512]{1,0:T(8,128)(2,1)S(1)}, u32[]{:S(2)}, u32[]{:S(2)}) collective-permute-start(bf16[648,512]{1,0:T(8,128)(2,1)S(1)} %get-tuple-element.44), channel_id=1, source_target_pairs={{0,1},{1,2},{2,3},{3,0},{4,5},{5,6},{6,7},{7,4},{8,9},{9,10},{10,1... | collective-permute-start | bytes 1990664 | tf_op jit(solution)/shard_map/ppermute | solution.py:223
  33.4 0.2 collective-permute-start.1
  33.7 0.2 collective-permute-start.2
  33.9 0.2 reduce-window_clone.1
  34.1 0.1 convert_reduce_fusion.2
  34.2 0.1 slice.58
  34.3 0.1 slice.59
  34.4 0.2 reduce-window_1_clone.1
  34.6 0.1 convert_reduce_fusion
  34.7 0.2 select_reduce_fusion.3
  34.9 0.1 select_reduce_fusion.1
  35.1 28.5 %all-to-all-done.1 = bf16[8,6,64,256]{3,2,1,0:T(8,128)(2,1)} async-done(((bf16[8,6,64,256]{3,2,1,0:T(8,128)(2,1)}), bf16[8,6,64,256]{3,2,1,0:T(8,128)(2,1)}, u32[]{:S(2)}, u32[]{:S(2)}) %all-to-all-start.1) | async-done | bytes 1572896 | tf_op jit(solution)/shard_map/all_to_all | solution.py:287
  63.6 3.1 %collective-permute-start.3 = (bf16[8,6,64,256]{3,2,1,0:T(8,128)(2,1)}, bf16[8,6,64,256]{3,2,1,0:T(8,128)(2,1)}, u32[]{:S(2)}, u32[]{:S(2)}) collective-permute-start(bf16[8,6,64,256]{3,2,1,0:T(8,128)(2,1)} %all-to-all-done.1), channel_id=1, source_target_pairs={{0,1},{1,0},{2,3},{3,2},{4,5},{5,4},{6,7},{7,6},{8,9},{9,8},{10,11... | collective-permute-start | bytes 4718600 | tf_op jit(solution)/shard_map/ppermute | solution.py:288
  66.7 0.1 copy.72
  66.7 0.1 copy.68
  66.8 0.1 copy.76
  66.9 0.6 reshape.530.kown_ref
  67.6 0.9 copy.82.rown_ref
  68.5 0.7 stack.47.ranges_ref
  69.1 0.1 fusion.59
  69.3 0.7 pad_add_fusion.1.meta_ref
  69.9 0.5 multiply_add_fusion.1.slots_ref
  70.5 21.2 %collective-permute-done.1 = bf16[648,512]{1,0:T(8,128)(2,1)} collective-permute-done((bf16[648,512]{1,0:T(8,128)(2,1)S(1)}, bf16[648,512]{1,0:T(8,128)(2,1)}, u32[]{:S(2)}, u32[]{:S(2)}) %collective-permute-start.1) | collective-permute-done | bytes 663584 | tf_op jit(solution)/shard_map/ppermute | solution.py:223
  91.7 0.6 collective-permute-done.2
  92.3 1.8 %pad_maximum_fusion.1 = bf16[4,648,512]{2,1,0:T(8,128)(2,1)S(1)} fusion(bf16[1,648,512]{2,1,0:T(8,128)(2,1)} %bitcast.7, bf16[1,648,512]{2,1,0:T(8,128)(2,1)} %bitcast.5, bf16[1,648,512]{2,1,0:T(8,128)(2,1)} %bitcast.71, bf16[1,648,512]{2,1,0:T(8,128)(2,1)S(1)} %get-tuple-element.41), kind=kLoop, calls=%fused_computation.4 | loop fusion | flops 3981312 | bytes 5308416 | tf_op jit(solution)/shard_map/stack | solution.py:225
  94.1 2.3 %gather_fusion = bf16[4,648,512]{2,1,0:T(8,128)(2,1)} fusion(bf16[4,648,512]{2,1,0:T(8,128)(2,1)S(1)} %pad_maximum_fusion.1, s32[1024]{0:T(1024)S(1)} %pad_clamp_fusion.1), kind=kCustom, calls=%fused_computation | custom fusion | bytes 5308432 | tf_op jit(solution)/shard_map/gather | solution.py:225
  96.4 1.8 %slice.73 = bf16[512,4,512]{2,0,1:T(8,128)(2,1)S(1)} slice(bf16[648,4,512]{2,0,1:T(8,128)(2,1)} %bitcast.64), slice={[136:648], [0:4], [0:512]} | slice | bytes 4194304 | tf_op jit(solution)/shard_map/slice | solution.py:319
  98.2 1.2 convert_bitcast_fusion
  99.4 0.1 copy.85
  99.5 0.8 slice_convert_fusion
  100.4 20.9 %shard_map.163 = bf16[512,512]{1,0:T(8,128)(2,1)} custom-call(s32[4,5]{1,0:T(4,128)} %stack.47.ranges_ref, s32[48]{0:T(128)} %multiply_add_fusion.1.slots_ref, s32[2]{0:T(128)} %pad_add_fusion.1.meta_ref, bf16[512,512]{1,0:T(8,128)(2,1)} %q_ref.1, bf16[48,64,256]{2,1,0:T(8,128)(2,1)} %bitcast.21.own_ref, bf16[48,64,256]{2,1,0:T(8,128)(2,1)} %bitcast.22.partner_ref, ...), custom_call_target="tpu_custom_call" | custom-call | tf_op jit(solution)/shard_map/pallas_call | solution.py:178
  121.3 1.8 %dynamic-slice_bitcast_fusion.5 = (bf16[128,512]{1,0:T(8,128)(2,1)}, bf16[128,512]{1,0:T(8,128)(2,1)}, bf16[128,512]{1,0:T(8,128)(2,1)}) fusion(bf16[4,128,512]{2,1,0:T(8,128)(2,1)} %bitcast.68, s32[]{:T(128)S(6)} %select_n.227, s32[]{:T(128)S(6)} %select_n.229, s32[]{:T(128)S(6)} %select_n.225), kind=kLoop, calls=%fused_computation.43 | loop fusion | bytes 786444 | tf_op jit(solution)/shard_map/jit(dynamic_index_in_dim)/squeeze | solution.py:331
  123.1 0.5 collective-permute-start.6
  123.6 1.2 collective-permute-start.5
  124.8 2.1 %fusion.5 = f32[128,2048]{1,0:T(8,128)S(1)} fusion(bf16[2048,2048]{1,0:T(8,128)(2,1)} %all-gather.2.cloned.1.call-done, s32[]{:T(128)S(6)} %select_n.251, bf16[4,128,512]{2,1,0:T(8,128)(2,1)} %bitcast.69, s32[]{:T(128)S(6)} %select_n.223), kind=kOutput, calls=%fused_computation.12 | convolution fusion | flops 268435456 | bytes 3276808 | tf_op jit(solution)/shard_map/dot_general | solution.py:325
  126.9 2.1 %convolution_add_fusion.1 = f32[128,2048]{1,0:T(8,128)S(1)} fusion(f32[128,2048]{1,0:T(8,128)S(1)} %fusion.5, bf16[128,512]{1,0:T(8,128)(2,1)S(1)} %collective-permute-done.4, bf16[2048,2048]{1,0:T(8,128)(2,1)} %all-gather.2.cloned.1.call-done, s32[]{:T(128)S(6)} %select_n.253), kind=kOutput, calls=%fused_computation.7 | convolution fusion | flops 268697600 | bytes 4325380 | tf_op jit(solution)/shard_map/dot_general | solution.py:335
  129.1 2.0 %fusion.1 = f32[128,2048]{1,0:T(8,128)S(1)} fusion(bf16[128,512]{1,0:T(8,128)(2,1)S(1)} %collective-permute-done.6, bf16[2048,2048]{1,0:T(8,128)(2,1)} %all-gather.2.cloned.1.call-done, s32[]{:T(128)S(6)} %select_n.257), kind=kOutput, calls=%fused_computation.8 | convolution fusion | flops 268435456 | bytes 3276804 | tf_op jit(solution)/shard_map/dot_general | solution.py:335
  131.1 2.2 %multiply_reduce_fusion.1 = (f32[128]{0:T(128)S(1)}, f32[128,2048]{1,0:T(8,128)S(1)}) fusion(f32[128,2048]{1,0:T(8,128)S(1)} %fusion.1, f32[128,2048]{1,0:T(8,128)S(1)} %convolution_add_fusion.1, bf16[128,512]{1,0:T(8,128)(2,1)S(1)} %collective-permute-done.5, bf16[2048,2048]{1,0:T(8,128)(2,1)} %all-gather.2.cloned.1.call-done, s32[]{:T(128)S(6)} %select_n.255), kind=kOutput, calls=%fused_computation.23 | convolution fusion | flops 269483904 | bytes 5374468 | tf_op jit(solution)/shard_map/dot_general | solution.py:335
  133.4 1.0 add_convert_fusion.1
  134.4 3.0 %multiply_reduce_fusion = (f32[128]{0:T(128)S(1)}, f32[128,2048]{1,0:T(8,128)}) fusion(bf16[2048,512]{1,0:T(8,128)(2,1)S(1)} %bitcast.70, bf16[128,2048]{1,0:T(8,128)(2,1)} %add_convert_fusion.1, bf16[512,256]{1,0:T(8,128)(2,1)} %param.29, s32[]{:T(128)S(6)} %select_n.258), kind=kOutput, calls=%fused_computation.21 | convolution fusion | flops 269320064 | bytes 3736068 | tf_op jit(solution)/shard_map/dot_general | solution.py:352
  137.5 1.5 add_convert_fusion
  139.0 1.5 collective-permute-start.7
  140.5 1.0 collective-permute-start.8
  141.5 1.7 %collective-permute-done.7 = bf16[128,512]{1,0:T(8,128)(2,1)S(1)} collective-permute-done((bf16[128,512]{1,0:T(8,128)(2,1)S(1)}, bf16[128,512]{1,0:T(8,128)(2,1)S(1)}, u32[]{:S(2)}, u32[]{:S(2)}) %collective-permute-start.7) | collective-permute-done | bytes 131104 | tf_op jit(solution)/shard_map/ppermute | solution.py:237
  143.2 4.3 %collective-permute-done.8 = bf16[128,512]{1,0:T(8,128)(2,1)S(1)} collective-permute-done((bf16[128,512]{1,0:T(8,128)(2,1)S(1)}, bf16[128,512]{1,0:T(8,128)(2,1)S(1)}, u32[]{:S(2)}, u32[]{:S(2)}) %collective-permute-start.8) | collective-permute-done | bytes 131104 | tf_op jit(solution)/shard_map/ppermute | solution.py:237
  147.4 0.6 collective-permute-done.9
  148.1 1.5 gather_fusion.2
  (59 shorter events, 0.6 us)
Async XLA Ops:
  6.5 118.3 %all-gather.2.cloned.1.call-start = ((), (), s32[]{:S(2)}) async-start(), calls=%async_computation.2 | async-start | bytes 10485760 | tf_op jit(solution)/shard_map/all_gather | solution.py:301
  10.4 11.6 %all-to-all-start = ((s32[8,1,6]{2,1,0:T(1,128)}), s32[8,1,6]{2,1,0:T(1,128)S(1)}, u32[]{:S(2)}, u32[]{:S(2)}) async-start(s32[8,1,6]{2,1,0:T(1,128)} %copy.81), calls=%async_computation | async-start | bytes 8192 | tf_op jit(solution)/shard_map/all_to_all | solution.py:278
  22.1 6.4 %copy-start.3 = (bf16[512,256]{1,0:T(8,128)(2,1)S(1)}, bf16[512,256]{1,0:T(8,128)(2,1)}, u32[]{:S(2)}) copy-start(bf16[512,256]{1,0:T(8,128)(2,1)} %param.30) | copy-start | bytes 786436
  24.1 4.7 %copy-start.4 = (bf16[256,512]{1,0:T(8,128)(2,1)S(1)}, bf16[256,512]{1,0:T(8,128)(2,1)}, u32[]{:S(2)}) copy-start(bf16[256,512]{1,0:T(8,128)(2,1)} %param.31) | copy-start | bytes 786436
  24.1 4.9 %copy-start.7 = (bf16[512]{0:T(512)(128)(2,1)S(1)}, bf16[512]{0:T(512)(128)(2,1)}, u32[]{:S(2)}) copy-start(bf16[512]{0:T(512)(128)(2,1)} %param.28) | copy-start | bytes 3076
  24.1 4.9 %copy-start.8 = (bf16[512]{0:T(512)(128)(2,1)S(1)}, bf16[512]{0:T(512)(128)(2,1)}, u32[]{:S(2)}) copy-start(bf16[512]{0:T(512)(128)(2,1)} %param.32) | copy-start | bytes 3076
  24.1 39.5 %all-to-all-start.1 = ((bf16[8,6,64,256]{3,2,1,0:T(8,128)(2,1)}), bf16[8,6,64,256]{3,2,1,0:T(8,128)(2,1)}, u32[]{:S(2)}, u32[]{:S(2)}) async-start(bf16[8,6,64,256]{3,2,1,0:T(8,128)(2,1)} %bitcast.20), calls=%async_computation.1 | async-start | bytes 3145728 | tf_op jit(solution)/shard_map/all_to_all | solution.py:287
  28.6 1.1 copy-start.2
  29.9 4.0 %copy-start.10 = (s32[1,8]{1,0:T(1,128)S(1)}, s32[1,8]{1,0:T(1,128)}, u32[]{:S(2)}) copy-start(s32[1,8]{1,0:T(1,128)} %param.37) | copy-start | bytes 100
  29.9 4.5 %copy-start.6 = (s32[1,8]{1,0:T(1,128)S(1)}, s32[1,8]{1,0:T(1,128)}, u32[]{:S(2)}) copy-start(s32[1,8]{1,0:T(1,128)} %param.35) | copy-start | bytes 100
  29.9 4.7 %copy-start.9 = (s32[1,8]{1,0:T(1,128)S(1)}, s32[1,8]{1,0:T(1,128)}, u32[]{:S(2)}) copy-start(s32[1,8]{1,0:T(1,128)} %param.36) | copy-start | bytes 100
  29.9 40.0 %copy-start.11 = (s32[48,1]{0,1:T(1,128)S(1)}, s32[48,1]{0,1:T(1,128)}, u32[]{:S(2)}) copy-start(s32[48,1]{0,1:T(1,128)} %param.33) | copy-start | bytes 580
  30.1 40.4 %collective-permute-start = (bf16[648,512]{1,0:T(8,128)(2,1)S(1)}, bf16[648,512]{1,0:T(8,128)(2,1)S(1)}, u32[]{:S(2)}, u32[]{:S(2)}) collective-permute-start(bf16[648,512]{1,0:T(8,128)(2,1)S(1)} %get-tuple-element.44), channel_id=1, source_target_pairs={{0,1},{1,2},{2,3},{3,0},{4,5},{5,6},{6,7},{7,4},{8,9},{9,10},{10,1... | collective-permute-start | bytes 1990664 | tf_op jit(solution)/shard_map/ppermute | solution.py:223
  33.4 58.2 %collective-permute-start.1 = (bf16[648,512]{1,0:T(8,128)(2,1)S(1)}, bf16[648,512]{1,0:T(8,128)(2,1)}, u32[]{:S(2)}, u32[]{:S(2)}) collective-permute-start(bf16[648,512]{1,0:T(8,128)(2,1)S(1)} %get-tuple-element.43), channel_id=1, source_target_pairs={{0,2},{1,3},{2,0},{3,1},{4,6},{5,7},{6,4},{7,5},{8,10},{9,11},{10,... | collective-permute-start | bytes 1990664 | tf_op jit(solution)/shard_map/ppermute | solution.py:223
  33.7 58.6 %collective-permute-start.2 = (bf16[648,512]{1,0:T(8,128)(2,1)S(1)}, bf16[648,512]{1,0:T(8,128)(2,1)}, u32[]{:S(2)}, u32[]{:S(2)}) collective-permute-start(bf16[648,512]{1,0:T(8,128)(2,1)S(1)} %get-tuple-element.42), channel_id=1, source_target_pairs={{0,3},{1,0},{2,1},{3,2},{4,7},{5,4},{6,5},{7,6},{8,11},{9,8},{10,9... | collective-permute-start | bytes 1990664 | tf_op jit(solution)/shard_map/ppermute | solution.py:223
  63.6 36.8 %collective-permute-start.3 = (bf16[8,6,64,256]{3,2,1,0:T(8,128)(2,1)}, bf16[8,6,64,256]{3,2,1,0:T(8,128)(2,1)}, u32[]{:S(2)}, u32[]{:S(2)}) collective-permute-start(bf16[8,6,64,256]{3,2,1,0:T(8,128)(2,1)} %all-to-all-done.1), channel_id=1, source_target_pairs={{0,1},{1,0},{2,3},{3,2},{4,5},{5,4},{6,7},{7,6},{8,9},{9,8},{10,11... | collective-permute-start | bytes 4718600 | tf_op jit(solution)/shard_map/ppermute | solution.py:288
  69.9 24.2 %copy-start.5 = (s32[1024]{0:T(1024)}, s32[1024]{0:T(1024)S(1)}, u32[]{:S(2)}) copy-start(s32[1024]{0:T(1024)S(1)} %pad_clamp_fusion.1) | copy-start | bytes 12292
  70.5 21.8 %copy-start.1 = (bf16[648,512]{1,0:T(8,128)(2,1)}, bf16[648,512]{1,0:T(8,128)(2,1)S(1)}, u32[]{:S(2)}) copy-start(bf16[648,512]{1,0:T(8,128)(2,1)S(1)} %collective-permute-done) | copy-start | bytes 1990660
  123.1 3.8 %collective-permute-start.4 = (bf16[128,512]{1,0:T(8,128)(2,1)}, bf16[128,512]{1,0:T(8,128)(2,1)S(1)}, u32[]{:S(2)}, u32[]{:S(2)}) collective-permute-start(bf16[128,512]{1,0:T(8,128)(2,1)} %get-tuple-element.51), channel_id=1, source_target_pairs={{0,1},{1,2},{2,3},{3,0},{4,5},{5,6},{6,7},{7,4},{8,9},{9,10},{10,1... | collective-permute-start | bytes 393224 | tf_op jit(solution)/shard_map/ppermute | solution.py:333
  123.1 6.0 %collective-permute-start.6 = (bf16[128,512]{1,0:T(8,128)(2,1)}, bf16[128,512]{1,0:T(8,128)(2,1)S(1)}, u32[]{:S(2)}, u32[]{:S(2)}) collective-permute-start(bf16[128,512]{1,0:T(8,128)(2,1)} %get-tuple-element.50), channel_id=1, source_target_pairs={{0,3},{1,0},{2,1},{3,2},{4,7},{5,4},{6,5},{7,6},{8,11},{9,8},{10,9... | collective-permute-start | bytes 393224 | tf_op jit(solution)/shard_map/ppermute | solution.py:333
  123.6 7.5 %collective-permute-start.5 = (bf16[128,512]{1,0:T(8,128)(2,1)}, bf16[128,512]{1,0:T(8,128)(2,1)S(1)}, u32[]{:S(2)}, u32[]{:S(2)}) collective-permute-start(bf16[128,512]{1,0:T(8,128)(2,1)} %get-tuple-element.49), channel_id=1, source_target_pairs={{0,2},{1,3},{2,0},{3,1},{4,6},{5,7},{6,4},{7,5},{8,10},{9,11},{10,... | collective-permute-start | bytes 393224 | tf_op jit(solution)/shard_map/ppermute | solution.py:333
  134.4 3.1 %copy-start = (bf16[128,2048]{1,0:T(8,128)(2,1)S(1)}, bf16[128,2048]{1,0:T(8,128)(2,1)}, u32[]{:S(2)}) copy-start(bf16[128,2048]{1,0:T(8,128)(2,1)} %add_convert_fusion.1) | copy-start | bytes 1572868
  139.0 4.2 %collective-permute-start.7 = (bf16[128,512]{1,0:T(8,128)(2,1)S(1)}, bf16[128,512]{1,0:T(8,128)(2,1)S(1)}, u32[]{:S(2)}, u32[]{:S(2)}) collective-permute-start(bf16[128,512]{1,0:T(8,128)(2,1)S(1)} %get-tuple-element.48), channel_id=1, source_target_pairs={{0,1},{1,2},{2,3},{3,0},{4,5},{5,6},{6,7},{7,4},{8,9},{9,10},{10,1... | collective-permute-start | bytes 393224 | tf_op jit(solution)/shard_map/ppermute | solution.py:237
  140.5 7.0 %collective-permute-start.8 = (bf16[128,512]{1,0:T(8,128)(2,1)S(1)}, bf16[128,512]{1,0:T(8,128)(2,1)S(1)}, u32[]{:S(2)}, u32[]{:S(2)}) collective-permute-start(bf16[128,512]{1,0:T(8,128)(2,1)S(1)} %get-tuple-element.47), channel_id=1, source_target_pairs={{0,2},{1,3},{2,0},{3,1},{4,6},{5,7},{6,4},{7,5},{8,10},{9,11},{10,... | collective-permute-start | bytes 393224 | tf_op jit(solution)/shard_map/ppermute | solution.py:237
  141.5 6.6 %collective-permute-start.9 = (bf16[128,512]{1,0:T(8,128)(2,1)S(1)}, bf16[128,512]{1,0:T(8,128)(2,1)S(1)}, u32[]{:S(2)}, u32[]{:S(2)}) collective-permute-start(bf16[128,512]{1,0:T(8,128)(2,1)S(1)} %get-tuple-element.46), channel_id=1, source_target_pairs={{0,3},{1,0},{2,1},{3,2},{4,7},{5,4},{6,5},{7,6},{8,11},{9,8},{10,9... | collective-permute-start | bytes 393224 | tf_op jit(solution)/shard_map/ppermute | solution.py:237
Sparse Core Ops, SparseCore 0:
  8.9 89.2 all-gather.1

commit v15 on v13

--- a/solution.py
+++ b/solution.py
@@ -1,3 +1,4 @@
+import functools
 import math
 
 import jax
@@ -37,7 +38,7 @@
     return jnp.concatenate([context_mask, causal], axis=1)
 
 
-ROW_BLOCK = 128
+ROW_BLOCK = 64
 KEY_CHUNK = 256
 
 
@@ -47,28 +48,28 @@
 
 
 def attention_kernel(
-    ranges_ref,
-    slots_ref,
-    meta_ref,
+    scalars_ref,
     q_ref,
     own_ref,
     partner_ref,
     fresh_k_ref,
     fresh_v_ref,
-    kown_ref,
-    kpos_ref,
+    kinfo_ref,
     rown_ref,
     o_ref,
     s_scr,
     acc_scr,
+    *,
+    slot_base,
+    meta_base,
 ):
     block = pl.program_id(0)
-    ctx_lo = ranges_ref[block, 0]
-    ctx_n = ranges_ref[block, 1]
-    new_lo = ranges_ref[block, 2]
-    total = ctx_n + ranges_ref[block, 3]
-    ctx_chunks = ranges_ref[block, 4]
-    keys_are_own = meta_ref[0] == 0
+    ctx_lo = scalars_ref[block * 5]
+    ctx_n = scalars_ref[block * 5 + 1]
+    new_lo = scalars_ref[block * 5 + 2]
+    total = ctx_n + scalars_ref[block * 5 + 3]
+    ctx_chunks = scalars_ref[block * 5 + 4]
+    keys_are_own = scalars_ref[meta_base] == 0
     heads = q_ref.shape[1] // HD
     page_len = own_ref.shape[1]
     per_chunk = KEY_CHUNK // page_len
@@ -87,7 +88,7 @@
         def cached():
             pages = []
             for i in range(per_chunk):
-                slot = slots_ref[c * per_chunk + i]
+                slot = scalars_ref[slot_base + c * per_chunk + i]
                 pages.append(jnp.where(pick_own, own_ref[slot], partner_ref[slot]))
             return jnp.concatenate(pages, axis=0)
 
@@ -103,7 +104,8 @@
         s = lax.dot_general(
             stacked, keys, (((1,), (1,)), ((), ())), preferred_element_type=jnp.float32
         ) * scale
-        seen = (kown_ref[c] == row_owner) & (kpos_ref[c] <= row_index)
+        info = kinfo_ref[c]
+        seen = (info[0:1] == row_owner) & (info[1:2] <= row_index)
         s = jnp.where(seen[None], s.reshape(heads, ROW_BLOCK, KEY_CHUNK), -1e30).reshape(
             heads * ROW_BLOCK, KEY_CHUNK
         )
@@ -174,23 +176,29 @@
         [ctx_lo, ctx_n, new_lo, new_n, jnp.full((blocks,), ctx_chunks, jnp.int32)], axis=1
     ).astype(jnp.int32)
     meta = jnp.stack([half, kv_head]).astype(jnp.int32)
-    whole = lambda b, r, s, m: (0, 0, 0)
+    slot_base = ranges.size
+    meta_base = slot_base + slots.shape[0]
+    scalars = jnp.concatenate([ranges.reshape(-1), slots.astype(jnp.int32), meta])
+    key_info = jnp.stack(
+        [key_owner.reshape(chunks, KEY_CHUNK), key_pos.reshape(chunks, KEY_CHUNK)], axis=1
+    )
+    whole = lambda b, s: (0, 0, 0)
+    by_head = lambda b, s: (0, s[meta_base + 1])
     return pl.pallas_call(
-        attention_kernel,
+        functools.partial(attention_kernel, slot_base=slot_base, meta_base=meta_base),
         grid_spec=pltpu.PrefetchScalarGridSpec(
-            num_scalar_prefetch=3,
+            num_scalar_prefetch=1,
             grid=(blocks,),
             in_specs=[
-                pl.BlockSpec((ROW_BLOCK, heads * HD), lambda b, r, s, m: (b, 0)),
+                pl.BlockSpec((ROW_BLOCK, heads * HD), lambda b, s: (b, 0)),
                 pl.BlockSpec(own_pages.shape, whole),
                 pl.BlockSpec(partner_pages.shape, whole),
-                pl.BlockSpec((row_total, HD), lambda b, r, s, m: (0, m[1])),
-                pl.BlockSpec((row_total, HD), lambda b, r, s, m: (0, m[1])),
-                pl.BlockSpec((chunks, 1, KEY_CHUNK), whole),
-                pl.BlockSpec((chunks, 1, KEY_CHUNK), whole),
-                pl.BlockSpec((ROW_BLOCK, 1), lambda b, r, s, m: (b, 0)),
+                pl.BlockSpec((row_total, HD), by_head),
+                pl.BlockSpec((row_total, HD), by_head),
+                pl.BlockSpec((chunks, 2, KEY_CHUNK), whole),
+                pl.BlockSpec((ROW_BLOCK, 1), lambda b, s: (b, 0)),
             ],
-            out_specs=pl.BlockSpec((ROW_BLOCK, heads * HD), lambda b, r, s, m: (b, 0)),
+            out_specs=pl.BlockSpec((ROW_BLOCK, heads * HD), lambda b, s: (b, 0)),
             scratch_shapes=[
                 pltpu.VMEM((chunks, heads * ROW_BLOCK, KEY_CHUNK), jnp.float32),
                 pltpu.VMEM((heads * ROW_BLOCK, HD), jnp.float32),
@@ -198,16 +206,13 @@
         ),
         out_shape=jax.ShapeDtypeStruct((row_total, heads * HD), jnp.bfloat16),
     )(
-        ranges,
-        slots.astype(jnp.int32),
-        meta,
+        scalars,
         queries,
         own_pages,
         partner_pages,
         new_keys,
         new_values,
-        key_owner.reshape(chunks, 1, KEY_CHUNK),
-        key_pos.reshape(chunks, 1, KEY_CHUNK),
+        key_info,
         row_owner.reshape(row_total, 1),
     )
 

time: 126 us -> 128 us (1.016); the launches traced: 126 us -> 126 us
  Pallas kernels: 20.9 us -> 23.1 us
  local copies, waits for them, and re-layouts: 8.63 us -> 7.28 us
    pallas_call x1, Pallas kernels: 20.9 us -> 23.1 us  [sparse_attention(): pl.pallas_call(functools.partial(attention_kernel, slot_base=slot_base, m...]
  transfers between devices with their start and end apart: 14 -> 14, of which waited for: 8 -> 7; matrix products, arithmetic and copies ran while one was open for 18% -> 16% of each run, Pallas kernels for 17% -> 18%
where the time goes in v15:
time: 128 us; the launch traced here: 126 us
  waiting for transfers between devices  43.1 us (34%)
  Pallas kernels  23.1 us (18%)
  starting transfers between devices  20.8 us (16%)
  between operations  13.9 us (11%)
  matrix products  11.1 us (9%)
  local copies, waits for them, and re-layouts  7.28 us (6%)
  other arithmetic  6.81 us (5%)
    all_to_all x1, waiting for transfers between devices, shards(): lax.all_to_all(outgoing, 'req', split_axis=0, concat_axis=0, tiled=True)  28.8 us
    pallas_call x1, Pallas kernels, sparse_attention(): pl.pallas_call(functools.partial(attention_kernel, slot_base=slot_base, m...  23.1 us
    ppermute x3, waiting for transfers between devices, columns_to_rows(): received.append(lax.ppermute(outgoing, axis_name, perm))  6.56 us
    all_to_all x1, starting transfers between devices, shards(): lax.all_to_all(request_table, 'req', split_axis=0, concat_axis=0, tiled=T...  6.38 us
    dot_general x3, matrix products, shards(): jnp.dot(piece, lax.dynamic_slice_in_dim(full_weight, source * width, widt...  6.31 us
    ppermute x3, waiting for transfers between devices, shards(): piece = lax.ppermute(outgoing, 'tp', perm)  4.39 us
    all_to_all x1, starting transfers between devices, shards(): lax.all_to_all(outgoing, 'req', split_axis=0, concat_axis=0, tiled=True)  3.75 us
    ppermute x3, starting transfers between devices, rows_to_columns(): received.append(lax.ppermute(outgoing, axis_name, perm))  3.7 us
  transfers between devices with their start and end apart: 14, of which 7 were waited for; matrix products, arithmetic and copies ran while one was open for 16% of the time, Pallas kernels for 18%

profile of v15, /device:TPU:1, one launch (start us, length us, event | category | flops | bytes accessed | tf_op | source)
XLA Modules:
  0.0 126.1 jit_solution(2931714375364524257)
XLA Ops:
  6.5 0.7 all-gather.3.cloned.1.call-update
  7.3 0.2 convert_reduce_fusion.1
  7.5 0.2 select_reduce_fusion.2
  7.7 0.7 copy.32
  8.4 6.4 %all-to-all-start = ((s32[8,1,6]{2,1,0:T(1,128)}), s32[8,1,6]{2,1,0:T(1,128)S(1)}, u32[]{:S(2)}, u32[]{:S(2)}) async-start(s32[8,1,6]{2,1,0:T(1,128)} %copy.32), calls=%async_computation | async-start | bytes 8192 | tf_op jit(solution)/shard_map/all_to_all | solution.py:283
  14.7 2.6 %dynamic-slice_select_fusion = bf16[48,64,256]{2,1,0:T(8,128)(2,1)S(1)} fusion(bf16[48,64,512]{2,1,0:T(8,128)(2,1)} %param.26, s32[]{:T(128)S(6)} %select_n.244, bf16[48,64,512]{2,1,0:T(8,128)(2,1)} %param.25, pred[]{:T(512)S(6)} %eq.140), kind=kLoop, calls=%fused_computation.12 | loop fusion | flops 786432 | bytes 4718597 | tf_op jit(solution)/shard_map/jit(_where)/select_n | solution.py:290
  17.3 2.7 %all-to-all-done = s32[8,1,6]{2,1,0:T(1,128)S(1)} async-done(((s32[8,1,6]{2,1,0:T(1,128)}), s32[8,1,6]{2,1,0:T(1,128)S(1)}, u32[]{:S(2)}, u32[]{:S(2)}) %all-to-all-start) | async-done | bytes 224 | tf_op jit(solution)/shard_map/all_to_all | solution.py:283
  20.0 0.1 reshape.538
  20.1 1.9 %gather_fusion.1 = bf16[48,64,256]{2,1,0:T(8,128)(2,1)} fusion(bf16[48,64,256]{2,1,0:T(8,128)(2,1)S(1)} %dynamic-slice_select_fusion, s32[1024]{0:T(1024)S(1)} %pad_clamp_fusion), kind=kCustom, calls=%fused_computation.1 | custom fusion | bytes 3145920 | tf_op jit(solution)/shard_map/gather | solution.py:291
  22.0 0.0 copy-start.3
  22.0 3.7 %all-to-all-start.1 = ((bf16[8,6,64,256]{3,2,1,0:T(8,128)(2,1)}), bf16[8,6,64,256]{3,2,1,0:T(8,128)(2,1)S(1)}, u32[]{:S(2)}, u32[]{:S(2)}) async-start(bf16[8,6,64,256]{3,2,1,0:T(8,128)(2,1)} %bitcast.20), calls=%async_computation.1 | async-start | bytes 3145728 | tf_op jit(solution)/shard_map/all_to_all | solution.py:292
  25.7 0.0 copy-start.10
  25.8 0.0 copy-start.5
  25.8 0.0 copy-start.8
  25.8 0.0 copy-start.4
  25.8 0.0 all-gather.5.cloned.1.call-start
  26.0 0.1 fusion.12
  26.1 3.2 %collective-permute-start = (bf16[136,512]{1,0:T(8,128)(2,1)S(1)}, bf16[136,512]{1,0:T(8,128)(2,1)S(1)}, u32[]{:S(2)}, u32[]{:S(2)}) collective-permute-start(bf16[136,512]{1,0:T(8,128)(2,1)S(1)} %get-tuple-element.38), channel_id=1, source_target_pairs={{0,1},{1,2},{2,3},{3,0},{4,5},{5,6},{6,7},{7,4},{8,9},{9,10},{10,1... | collective-permute-start | bytes 417800 | tf_op jit(solution)/shard_map/ppermute | solution.py:228
  29.3 0.3 collective-permute-start.1
  29.6 0.2 collective-permute-start.2
  29.8 0.1 copy.34
  29.9 0.8 pad_maximum_fusion.1
  30.8 0.0 all-gather.5.cloned.1.call-update
  30.8 0.2 reduce-window_clone.1
  31.0 0.1 convert_reduce_fusion.2
  31.1 0.1 slice.54
  31.2 0.1 slice.55
  31.3 0.2 reduce-window_1_clone.1
  31.5 0.1 convert_reduce_fusion
  31.6 0.2 select_reduce_fusion.3
  31.8 0.1 select_reduce_fusion.1
  32.0 28.8 %all-to-all-done.1 = bf16[8,6,64,256]{3,2,1,0:T(8,128)(2,1)S(1)} async-done(((bf16[8,6,64,256]{3,2,1,0:T(8,128)(2,1)}), bf16[8,6,64,256]{3,2,1,0:T(8,128)(2,1)S(1)}, u32[]{:S(2)}, u32[]{:S(2)}) %all-to-all-start.1) | async-done | bytes 1572896 | tf_op jit(solution)/shard_map/all_to_all | solution.py:292
  60.7 3.1 %collective-permute-start.3 = (bf16[8,6,64,256]{3,2,1,0:T(8,128)(2,1)S(1)}, bf16[8,6,64,256]{3,2,1,0:T(8,128)(2,1)}, u32[]{:S(2)}, u32[]{:S(2)}) collective-permute-start(bf16[8,6,64,256]{3,2,1,0:T(8,128)(2,1)S(1)} %all-to-all-done.1), channel_id=1, source_target_pairs={{0,1},{1,0},{2,3},{3,2},{4,5},{5,4},{6,7},{7,6},{8,9},{9,8},{10,11... | collective-permute-start | bytes 4718600 | tf_op jit(solution)/shard_map/ppermute | solution.py:293
  63.9 0.1 copy.30
  64.0 0.1 reshape.520
  64.1 0.6 pad_add_fusion.2.scalars_ref
  64.7 0.9 copy.33.rown_ref
  65.6 0.6 pad_add_fusion.kinfo_ref
  66.2 0.0 collective-permute-done.1
  66.2 0.1 pad_maximum_fusion
  66.3 0.6 gather_fusion
  66.9 0.1 convert_bitcast_fusion
  67.0 0.1 copy.37
  67.2 23.1 %shard_map.163 = bf16[512,512]{1,0:T(8,128)(2,1)} custom-call(s32[90]{0:T(128)} %pad_add_fusion.2.scalars_ref, bf16[512,512]{1,0:T(8,128)(2,1)} %q_ref.1, bf16[48,64,256]{2,1,0:T(8,128)(2,1)} %bitcast.88, bf16[48,64,256]{2,1,0:T(8,128)(2,1)} %bitcast.22.partner_ref, bf16[512,512]{1,0:T(8,128)(2,1)} %fresh_k_ref.1, bf16[512,512]{1,0:T(8,128)(2,1)} %fresh_v_ref.1, ...), custom_call_target="tpu_custom_call" | custom-call | tf_op jit(solution)/shard_map/pallas_call | solution.py:187
  90.2 1.1 dynamic-slice_bitcast_fusion.2
  91.3 1.3 %collective-permute-start.4 = (bf16[128,512]{1,0:T(8,128)(2,1)S(1)}, bf16[128,512]{1,0:T(8,128)(2,1)S(1)}, u32[]{:S(2)}, u32[]{:S(2)}) collective-permute-start(bf16[128,512]{1,0:T(8,128)(2,1)S(1)} %get-tuple-element.47), channel_id=1, source_target_pairs={{0,1},{1,2},{2,3},{3,0},{4,5},{5,6},{6,7},{7,4},{8,9},{9,10},{10,1... | collective-permute-start | bytes 393224 | tf_op jit(solution)/shard_map/ppermute | solution.py:331
  92.6 0.4 collective-permute-start.5
  93.0 2.1 %fusion.5 = f32[128,2048]{1,0:T(8,128)S(1)} fusion(bf16[2048,2048]{1,0:T(8,128)(2,1)} %all-gather.3.cloned.1.call-done, s32[]{:T(128)S(6)} %select_n.251, bf16[4,128,512]{2,1,0:T(8,128)(2,1)} %bitcast.93, s32[]{:T(128)S(6)} %select_n.223), kind=kOutput, calls=%fused_computation.10 | convolution fusion | flops 268435456 | bytes 3276808 | tf_op jit(solution)/shard_map/dot_general | solution.py:323
  95.1 3.3 %collective-permute-done.4 = bf16[128,512]{1,0:T(8,128)(2,1)S(1)} collective-permute-done((bf16[128,512]{1,0:T(8,128)(2,1)S(1)}, bf16[128,512]{1,0:T(8,128)(2,1)S(1)}, u32[]{:S(2)}, u32[]{:S(2)}) %collective-permute-start.4) | collective-permute-done | bytes 131104 | tf_op jit(solution)/shard_map/ppermute | solution.py:331
  98.4 2.0 %convolution_add_fusion.1 = f32[128,2048]{1,0:T(8,128)S(1)} fusion(f32[128,2048]{1,0:T(8,128)S(1)} %fusion.5, bf16[128,512]{1,0:T(8,128)(2,1)S(1)} %collective-permute-done.4, bf16[2048,2048]{1,0:T(8,128)(2,1)} %all-gather.3.cloned.1.call-done, s32[]{:T(128)S(6)} %select_n.253), kind=kOutput, calls=%fused_computation.5 | convolution fusion | flops 268697600 | bytes 4325380 | tf_op jit(solution)/shard_map/dot_general | solution.py:333
  100.4 1.1 collective-permute-done.6
  101.5 2.1 %fusion.1 = f32[128,2048]{1,0:T(8,128)S(1)} fusion(bf16[128,512]{1,0:T(8,128)(2,1)S(1)} %collective-permute-done.6, bf16[2048,2048]{1,0:T(8,128)(2,1)} %all-gather.3.cloned.1.call-done, s32[]{:T(128)S(6)} %select_n.257), kind=kOutput, calls=%fused_computation.6 | convolution fusion | flops 268435456 | bytes 3276804 | tf_op jit(solution)/shard_map/dot_general | solution.py:333
  103.6 2.2 %multiply_reduce_fusion.1 = (f32[128]{0:T(128)S(1)}, f32[128,2048]{1,0:T(8,128)S(1)}) fusion(f32[128,2048]{1,0:T(8,128)S(1)} %fusion.1, f32[128,2048]{1,0:T(8,128)S(1)} %convolution_add_fusion.1, bf16[128,512]{1,0:T(8,128)(2,1)S(1)} %collective-permute-done.5, bf16[2048,2048]{1,0:T(8,128)(2,1)} %all-gather.3.cloned.1.call-done, s32[]{:T(128)S(6)} %select_n.255), kind=kOutput, calls=%fused_computation.25 | convolution fusion | flops 269483904 | bytes 5374468 | tf_op jit(solution)/shard_map/dot_general | solution.py:333
  105.8 0.2 add_convert_fusion.1
  106.1 0.0 all-gather.5.cloned.1.call-done
  106.1 2.6 %multiply_reduce_fusion = (f32[128]{0:T(128)S(1)}, f32[128,2048]{1,0:T(8,128)S(1)}) fusion(bf16[2048,512]{0,1:T(8,128)(2,1)} %all-gather.5.cloned.1.call-done, bf16[128,2048]{1,0:T(8,128)(2,1)S(1)} %add_convert_fusion.1, bf16[512,256]{1,0:T(8,128)(2,1)} %param.29, s32[]{:T(128)S(6)} %select_n.258), kind=kOutput, calls=%fused_computation.23 | convolution fusion | flops 269320064 | bytes 3736068 | tf_op jit(solution)/shard_map/dot_general | solution.py:351
  108.7 0.2 add_convert_fusion
  109.0 1.4 %collective-permute-start.7 = (bf16[128,512]{1,0:T(8,128)(2,1)S(1)}, bf16[128,512]{1,0:T(8,128)(2,1)S(1)}, u32[]{:S(2)}, u32[]{:S(2)}) collective-permute-start(bf16[128,512]{1,0:T(8,128)(2,1)S(1)} %get-tuple-element.44), channel_id=1, source_target_pairs={{0,1},{1,2},{2,3},{3,0},{4,5},{5,6},{6,7},{7,4},{8,9},{9,10},{10,1... | collective-permute-start | bytes 393224 | tf_op jit(solution)/shard_map/ppermute | solution.py:242
  110.5 0.8 collective-permute-start.8
  111.3 1.9 %collective-permute-done.7 = bf16[128,512]{1,0:T(8,128)(2,1)S(1)} collective-permute-done((bf16[128,512]{1,0:T(8,128)(2,1)S(1)}, bf16[128,512]{1,0:T(8,128)(2,1)S(1)}, u32[]{:S(2)}, u32[]{:S(2)}) %collective-permute-start.7) | collective-permute-done | bytes 131104 | tf_op jit(solution)/shard_map/ppermute | solution.py:242
  113.2 4.0 %collective-permute-done.8 = bf16[128,512]{1,0:T(8,128)(2,1)S(1)} collective-permute-done((bf16[128,512]{1,0:T(8,128)(2,1)S(1)}, bf16[128,512]{1,0:T(8,128)(2,1)S(1)}, u32[]{:S(2)}, u32[]{:S(2)}) %collective-permute-start.8) | collective-permute-done | bytes 131104 | tf_op jit(solution)/shard_map/ppermute | solution.py:242
  117.2 0.6 collective-permute-done.9
  117.8 0.1 pad_maximum_fusion.2
  117.9 1.4 %gather_fusion.2 = bf16[4,128,512]{2,1,0:T(8,128)(2,1)} fusion(bf16[4,128,512]{2,1,0:T(8,128)(2,1)S(1)} %pad_maximum_fusion.2, s32[1024]{0:T(1024)S(1)} %pad_clamp_fusion.1), kind=kCustom, calls=%fused_computation.2 | custom fusion | bytes 1048592 | tf_op jit(solution)/shard_map/gather | solution.py:244
  (56 shorter events, 0.4 us)
Async XLA Ops:
  6.5 0.7 copy-start.11
  6.5 0.9 copy-start.9
  6.5 86.4 %all-gather.3.cloned.1.call-start = ((), (), s32[]{:S(2)}) async-start(), calls=%async_computation.2 | async-start | bytes 10485760 | tf_op jit(solution)/shard_map/all_gather | solution.py:306
  8.4 11.6 %all-to-all-start = ((s32[8,1,6]{2,1,0:T(1,128)}), s32[8,1,6]{2,1,0:T(1,128)S(1)}, u32[]{:S(2)}, u32[]{:S(2)}) async-start(s32[8,1,6]{2,1,0:T(1,128)} %copy.32), calls=%async_computation | async-start | bytes 8192 | tf_op jit(solution)/shard_map/all_to_all | solution.py:283
  22.0 3.9 %copy-start.6 = (bf16[512]{0:T(512)(128)(2,1)S(1)}, bf16[512]{0:T(512)(128)(2,1)}, u32[]{:S(2)}) copy-start(bf16[512]{0:T(512)(128)(2,1)} %param.28) | copy-start | bytes 3076
  22.0 3.9 %copy-start.7 = (bf16[512]{0:T(512)(128)(2,1)S(1)}, bf16[512]{0:T(512)(128)(2,1)}, u32[]{:S(2)}) copy-start(bf16[512]{0:T(512)(128)(2,1)} %param.32) | copy-start | bytes 3076
  22.0 4.1 %copy-start.1 = (bf16[512,512]{1,0:T(8,128)(2,1)S(1)}, bf16[512,512]{1,0:T(8,128)(2,1)}, u32[]{:S(2)}) copy-start(bf16[512,512]{1,0:T(8,128)(2,1)} %param.21) | copy-start | bytes 1572868
  22.0 7.8 %copy-start.2 = (bf16[512,256]{1,0:T(8,128)(2,1)S(1)}, bf16[512,256]{1,0:T(8,128)(2,1)}, u32[]{:S(2)}) copy-start(bf16[512,256]{1,0:T(8,128)(2,1)} %param.30) | copy-start | bytes 786436
  22.0 8.0 %copy-start.3 = (bf16[256,512]{1,0:T(8,128)(2,1)S(1)}, bf16[256,512]{1,0:T(8,128)(2,1)}, u32[]{:S(2)}) copy-start(bf16[256,512]{1,0:T(8,128)(2,1)} %param.31) | copy-start | bytes 786436
  22.0 38.7 %all-to-all-start.1 = ((bf16[8,6,64,256]{3,2,1,0:T(8,128)(2,1)}), bf16[8,6,64,256]{3,2,1,0:T(8,128)(2,1)S(1)}, u32[]{:S(2)}, u32[]{:S(2)}) async-start(bf16[8,6,64,256]{3,2,1,0:T(8,128)(2,1)} %bitcast.20), calls=%async_computation.1 | async-start | bytes 3145728 | tf_op jit(solution)/shard_map/all_to_all | solution.py:292
  25.7 5.1 %copy-start.10 = (s32[1,8]{1,0:T(1,128)S(1)}, s32[1,8]{1,0:T(1,128)}, u32[]{:S(2)}) copy-start(s32[1,8]{1,0:T(1,128)} %param.37) | copy-start | bytes 100
  25.8 5.5 %copy-start.5 = (s32[1,8]{1,0:T(1,128)S(1)}, s32[1,8]{1,0:T(1,128)}, u32[]{:S(2)}) copy-start(s32[1,8]{1,0:T(1,128)} %param.35) | copy-start | bytes 100
  25.8 5.7 %copy-start.8 = (s32[1,8]{1,0:T(1,128)S(1)}, s32[1,8]{1,0:T(1,128)}, u32[]{:S(2)}) copy-start(s32[1,8]{1,0:T(1,128)} %param.36) | copy-start | bytes 100
  25.8 39.8 %copy-start.4 = (s32[14,1,256]{2,1,0:T(1,128)S(1)}, s32[14,1,256]{2,1,0:T(1,128)}, u32[]{:S(2)}) copy-start(s32[14,1,256]{2,1,0:T(1,128)} %constant.270.clone.1) | copy-start | bytes 43012
  25.8 80.3 %all-gather.5.cloned.1.call-start = ((), (), s32[]{:S(2)}) async-start(), calls=%async_computation.3 | async-start | bytes 2621440 | tf_op jit(solution)/shard_map/all_gather | solution.py:307
  26.1 40.1 %collective-permute-start = (bf16[136,512]{1,0:T(8,128)(2,1)S(1)}, bf16[136,512]{1,0:T(8,128)(2,1)S(1)}, u32[]{:S(2)}, u32[]{:S(2)}) collective-permute-start(bf16[136,512]{1,0:T(8,128)(2,1)S(1)} %get-tuple-element.38), channel_id=1, source_target_pairs={{0,1},{1,2},{2,3},{3,0},{4,5},{5,6},{6,7},{7,4},{8,9},{9,10},{10,1... | collective-permute-start | bytes 417800 | tf_op jit(solution)/shard_map/ppermute | solution.py:228
  29.3 36.9 %collective-permute-start.1 = (bf16[136,512]{1,0:T(8,128)(2,1)S(1)}, bf16[136,512]{1,0:T(8,128)(2,1)S(1)}, u32[]{:S(2)}, u32[]{:S(2)}) collective-permute-start(bf16[136,512]{1,0:T(8,128)(2,1)S(1)} %get-tuple-element.39), channel_id=1, source_target_pairs={{0,2},{1,3},{2,0},{3,1},{4,6},{5,7},{6,4},{7,5},{8,10},{9,11},{10,... | collective-permute-start | bytes 417800 | tf_op jit(solution)/shard_map/ppermute | solution.py:228
  29.6 36.6 %collective-permute-start.2 = (bf16[136,512]{1,0:T(8,128)(2,1)S(1)}, bf16[136,512]{1,0:T(8,128)(2,1)S(1)}, u32[]{:S(2)}, u32[]{:S(2)}) collective-permute-start(bf16[136,512]{1,0:T(8,128)(2,1)S(1)} %get-tuple-element.40), channel_id=1, source_target_pairs={{0,3},{1,0},{2,1},{3,2},{4,7},{5,4},{6,5},{7,6},{8,11},{9,8},{10,9... | collective-permute-start | bytes 417800 | tf_op jit(solution)/shard_map/ppermute | solution.py:228
  60.7 6.3 %copy-start = (bf16[8,6,64,256]{3,2,1,0:T(8,128)(2,1)}, bf16[8,6,64,256]{3,2,1,0:T(8,128)(2,1)S(1)}, u32[]{:S(2)}) copy-start(bf16[8,6,64,256]{3,2,1,0:T(8,128)(2,1)S(1)} %all-to-all-done.1) | copy-start | bytes 4718596
  60.7 6.4 %collective-permute-start.3 = (bf16[8,6,64,256]{3,2,1,0:T(8,128)(2,1)S(1)}, bf16[8,6,64,256]{3,2,1,0:T(8,128)(2,1)}, u32[]{:S(2)}, u32[]{:S(2)}) collective-permute-start(bf16[8,6,64,256]{3,2,1,0:T(8,128)(2,1)S(1)} %all-to-all-done.1), channel_id=1, source_target_pairs={{0,1},{1,0},{2,3},{3,2},{4,5},{5,4},{6,7},{7,6},{8,9},{9,8},{10,11... | collective-permute-start | bytes 4718600 | tf_op jit(solution)/shard_map/ppermute | solution.py:293
  91.3 7.1 %collective-permute-start.4 = (bf16[128,512]{1,0:T(8,128)(2,1)S(1)}, bf16[128,512]{1,0:T(8,128)(2,1)S(1)}, u32[]{:S(2)}, u32[]{:S(2)}) collective-permute-start(bf16[128,512]{1,0:T(8,128)(2,1)S(1)} %get-tuple-element.47), channel_id=1, source_target_pairs={{0,1},{1,2},{2,3},{3,0},{4,5},{5,6},{6,7},{7,4},{8,9},{9,10},{10,1... | collective-permute-start | bytes 393224 | tf_op jit(solution)/shard_map/ppermute | solution.py:331
  92.6 9.0 %collective-permute-start.6 = (bf16[128,512]{1,0:T(8,128)(2,1)S(1)}, bf16[128,512]{1,0:T(8,128)(2,1)S(1)}, u32[]{:S(2)}, u32[]{:S(2)}) collective-permute-start(bf16[128,512]{1,0:T(8,128)(2,1)S(1)} %get-tuple-element.46), channel_id=1, source_target_pairs={{0,3},{1,0},{2,1},{3,2},{4,7},{5,4},{6,5},{7,6},{8,11},{9,8},{10,9... | collective-permute-start | bytes 393224 | tf_op jit(solution)/shard_map/ppermute | solution.py:331
  92.6 11.0 %collective-permute-start.5 = (bf16[128,512]{1,0:T(8,128)(2,1)S(1)}, bf16[128,512]{1,0:T(8,128)(2,1)S(1)}, u32[]{:S(2)}, u32[]{:S(2)}) collective-permute-start(bf16[128,512]{1,0:T(8,128)(2,1)S(1)} %get-tuple-element.45), channel_id=1, source_target_pairs={{0,2},{1,3},{2,0},{3,1},{4,6},{5,7},{6,4},{7,5},{8,10},{9,11},{10,... | collective-permute-start | bytes 393224 | tf_op jit(solution)/shard_map/ppermute | solution.py:331
  109.0 4.1 %collective-permute-start.7 = (bf16[128,512]{1,0:T(8,128)(2,1)S(1)}, bf16[128,512]{1,0:T(8,128)(2,1)S(1)}, u32[]{:S(2)}, u32[]{:S(2)}) collective-permute-start(bf16[128,512]{1,0:T(8,128)(2,1)S(1)} %get-tuple-element.44), channel_id=1, source_target_pairs={{0,1},{1,2},{2,3},{3,0},{4,5},{5,6},{6,7},{7,4},{8,9},{9,10},{10,1... | collective-permute-start | bytes 393224 | tf_op jit(solution)/shard_map/ppermute | solution.py:242
  110.5 6.7 %collective-permute-start.8 = (bf16[128,512]{1,0:T(8,128)(2,1)S(1)}, bf16[128,512]{1,0:T(8,128)(2,1)S(1)}, u32[]{:S(2)}, u32[]{:S(2)}) collective-permute-start(bf16[128,512]{1,0:T(8,128)(2,1)S(1)} %get-tuple-element.43), channel_id=1, source_target_pairs={{0,2},{1,3},{2,0},{3,1},{4,6},{5,7},{6,4},{7,5},{8,10},{9,11},{10,... | collective-permute-start | bytes 393224 | tf_op jit(solution)/shard_map/ppermute | solution.py:242
  111.3 6.6 %collective-permute-start.9 = (bf16[128,512]{1,0:T(8,128)(2,1)S(1)}, bf16[128,512]{1,0:T(8,128)(2,1)S(1)}, u32[]{:S(2)}, u32[]{:S(2)}) collective-permute-start(bf16[128,512]{1,0:T(8,128)(2,1)S(1)} %get-tuple-element.42), channel_id=1, source_target_pairs={{0,3},{1,0},{2,1},{3,2},{4,7},{5,4},{6,5},{7,6},{8,11},{9,8},{10,9... | collective-permute-start | bytes 393224 | tf_op jit(solution)/shard_map/ppermute | solution.py:242
Sparse Core Ops, SparseCore 0:
  8.9 66.7 all-gather.2
  77.3 26.7 all-gather.4

commit v16 on v15

--- a/solution.py
+++ b/solution.py
@@ -38,8 +38,8 @@
     return jnp.concatenate([context_mask, causal], axis=1)
 
 
-ROW_BLOCK = 64
-KEY_CHUNK = 256
+ROW_BLOCK = 256
+KEY_CHUNK = 512
 
 
 def pick(table, index):

time: 128 us -> 125 us (0.977)
  Pallas kernels: 23.1 us -> 14.4 us
  waiting for transfers between devices: 43.1 us -> 48.9 us
    pallas_call x1, Pallas kernels: 23.1 us -> 14.4 us  [sparse_attention(): pl.pallas_call(functools.partial(attention_kernel, slot_base=slot_base, m...]
    all_gather x1, waiting for transfers between devices: 0.02 us -> 6.53 us  [shards(): lax.all_gather(jnp.concatenate([ple_gate_weight, ple_proj_weight.T], axis...]
  transfers between devices with their start and end apart: 14 -> 14, of which waited for: 7 -> 9; matrix products, arithmetic and copies ran while one was open for 16% -> 17% of each run, Pallas kernels for 18% -> 12%
where the time goes in v16:
time: 125 us; the launch traced here: 124 us
  waiting for transfers between devices  48.9 us (39%)
  starting transfers between devices  20.6 us (16%)
  Pallas kernels  14.4 us (12%)
  between operations  13.9 us (11%)
  matrix products  11.3 us (9%)
  local copies, waits for them, and re-layouts  7.63 us (6%)
  other arithmetic  6.81 us (5%)
    all_to_all x1, waiting for transfers between devices, shards(): lax.all_to_all(outgoing, 'req', split_axis=0, concat_axis=0, tiled=True)  28.8 us
    pallas_call x1, Pallas kernels, sparse_attention(): pl.pallas_call(functools.partial(attention_kernel, slot_base=slot_base, m...  14.4 us
    all_gather x1, waiting for transfers between devices, shards(): lax.all_gather(jnp.concatenate([ple_gate_weight, ple_proj_weight.T], axis...  6.53 us
    all_to_all x1, starting transfers between devices, shards(): lax.all_to_all(request_table, 'req', split_axis=0, concat_axis=0, tiled=T...  6.38 us
    dot_general x3, matrix products, shards(): jnp.dot(piece, lax.dynamic_slice_in_dim(full_weight, source * width, widt...  6.32 us
    ppermute x3, waiting for transfers between devices, columns_to_rows(): received.append(lax.ppermute(outgoing, axis_name, perm))  6.23 us
    ppermute x3, waiting for transfers between devices, shards(): piece = lax.ppermute(outgoing, 'tp', perm)  3.97 us
    all_to_all x1, starting transfers between devices, shards(): lax.all_to_all(outgoing, 'req', split_axis=0, concat_axis=0, tiled=True)  3.75 us
  transfers between devices with their start and end apart: 14, of which 9 were waited for; matrix products, arithmetic and copies ran while one was open for 17% of the time, Pallas kernels for 12%

profile of v16, /device:TPU:1, one launch (start us, length us, event | category | flops | bytes accessed | tf_op | source)
XLA Modules:
  0.0 123.6 jit_solution(8401871323492033253)
XLA Ops:
  6.5 0.7 all-gather.3.cloned.1.call-update
  7.3 0.2 convert_reduce_fusion.1
  7.5 0.2 select_reduce_fusion.2
  7.7 0.7 copy.38
  8.4 6.4 %all-to-all-start = ((s32[8,1,6]{2,1,0:T(1,128)}), s32[8,1,6]{2,1,0:T(1,128)S(1)}, u32[]{:S(2)}, u32[]{:S(2)}) async-start(s32[8,1,6]{2,1,0:T(1,128)} %copy.38), calls=%async_computation | async-start | bytes 8192 | tf_op jit(solution)/shard_map/all_to_all | solution.py:283
  14.7 2.6 %dynamic-slice_select_fusion = bf16[48,64,256]{2,1,0:T(8,128)(2,1)S(1)} fusion(bf16[48,64,512]{2,1,0:T(8,128)(2,1)} %param.26, s32[]{:T(128)S(6)} %select_n.244, bf16[48,64,512]{2,1,0:T(8,128)(2,1)} %param.25, pred[]{:T(512)S(6)} %eq.140), kind=kLoop, calls=%fused_computation.12 | loop fusion | flops 786432 | bytes 4718597 | tf_op jit(solution)/shard_map/jit(_where)/select_n | solution.py:290
  17.3 2.7 %all-to-all-done = s32[8,1,6]{2,1,0:T(1,128)S(1)} async-done(((s32[8,1,6]{2,1,0:T(1,128)}), s32[8,1,6]{2,1,0:T(1,128)S(1)}, u32[]{:S(2)}, u32[]{:S(2)}) %all-to-all-start) | async-done | bytes 224 | tf_op jit(solution)/shard_map/all_to_all | solution.py:283
  20.0 0.1 reshape.538
  20.1 1.9 %gather_fusion.1 = bf16[48,64,256]{2,1,0:T(8,128)(2,1)} fusion(bf16[48,64,256]{2,1,0:T(8,128)(2,1)S(1)} %dynamic-slice_select_fusion, s32[1024]{0:T(1024)S(1)} %pad_clamp_fusion), kind=kCustom, calls=%fused_computation.1 | custom fusion | bytes 3145920 | tf_op jit(solution)/shard_map/gather | solution.py:291
  22.0 3.7 %all-to-all-start.1 = ((bf16[8,6,64,256]{3,2,1,0:T(8,128)(2,1)}), bf16[8,6,64,256]{3,2,1,0:T(8,128)(2,1)S(1)}, u32[]{:S(2)}, u32[]{:S(2)}) async-start(bf16[8,6,64,256]{3,2,1,0:T(8,128)(2,1)} %bitcast.20), calls=%async_computation.1 | async-start | bytes 3145728 | tf_op jit(solution)/shard_map/all_to_all | solution.py:292
  25.8 0.0 all-gather.5.cloned.1.call-start
  26.0 0.1 fusion.12
  26.1 3.2 %collective-permute-start = (bf16[136,512]{1,0:T(8,128)(2,1)S(1)}, bf16[136,512]{1,0:T(8,128)(2,1)S(1)}, u32[]{:S(2)}, u32[]{:S(2)}) collective-permute-start(bf16[136,512]{1,0:T(8,128)(2,1)S(1)} %get-tuple-element.38), channel_id=1, source_target_pairs={{0,1},{1,2},{2,3},{3,0},{4,5},{5,6},{6,7},{7,4},{8,9},{9,10},{10,1... | collective-permute-start | bytes 417800 | tf_op jit(solution)/shard_map/ppermute | solution.py:228
  29.3 0.3 collective-permute-start.1
  29.6 0.2 collective-permute-start.2
  29.8 0.1 copy.40
  29.9 0.8 pad_maximum_fusion.1
  30.8 0.0 all-gather.5.cloned.1.call-update
  30.8 0.2 reduce-window_clone.1
  31.0 0.1 convert_reduce_fusion.2
  31.1 0.1 slice.54
  31.2 0.1 slice.55
  31.3 0.2 reduce-window_1_clone.1
  31.5 0.1 convert_reduce_fusion
  31.6 0.2 select_reduce_fusion.3
  31.8 0.1 select_reduce_fusion.1
  32.0 28.8 %all-to-all-done.1 = bf16[8,6,64,256]{3,2,1,0:T(8,128)(2,1)S(1)} async-done(((bf16[8,6,64,256]{3,2,1,0:T(8,128)(2,1)}), bf16[8,6,64,256]{3,2,1,0:T(8,128)(2,1)S(1)}, u32[]{:S(2)}, u32[]{:S(2)}) %all-to-all-start.1) | async-done | bytes 1572896 | tf_op jit(solution)/shard_map/all_to_all | solution.py:292
  60.7 3.1 %collective-permute-start.3 = (bf16[8,6,64,256]{3,2,1,0:T(8,128)(2,1)S(1)}, bf16[8,6,64,256]{3,2,1,0:T(8,128)(2,1)}, u32[]{:S(2)}, u32[]{:S(2)}) collective-permute-start(bf16[8,6,64,256]{3,2,1,0:T(8,128)(2,1)S(1)} %all-to-all-done.1), channel_id=1, source_target_pairs={{0,1},{1,0},{2,3},{3,2},{4,5},{5,4},{6,7},{7,6},{8,9},{9,8},{10,11... | collective-permute-start | bytes 4718600 | tf_op jit(solution)/shard_map/ppermute | solution.py:293
  63.8 0.1 copy.33
  63.9 0.1 copy.34
  64.0 0.1 copy.35
  64.1 0.1 copy.36
  64.2 0.1 stack.47
  64.3 0.1 reshape.520
  64.4 0.6 pad_add_fusion.2.scalars_ref
  65.1 0.9 copy.39.rown_ref
  65.9 0.6 pad_add_fusion.kinfo_ref
  66.6 0.1 pad_maximum_fusion
  66.6 0.6 gather_fusion
  67.2 0.1 convert_bitcast_fusion
  67.4 0.1 copy.43
  67.5 14.4 %shard_map.163 = bf16[512,512]{1,0:T(8,128)(2,1)} custom-call(s32[60]{0:T(128)} %pad_add_fusion.2.scalars_ref, bf16[512,512]{1,0:T(8,128)(2,1)} %q_ref.1, bf16[48,64,256]{2,1,0:T(8,128)(2,1)} %bitcast.88, bf16[48,64,256]{2,1,0:T(8,128)(2,1)} %bitcast.22.partner_ref, bf16[512,512]{1,0:T(8,128)(2,1)} %fresh_k_ref.1, bf16[512,512]{1,0:T(8,128)(2,1)} %fresh_v_ref.1, ...), custom_call_target="tpu_custom_call" | custom-call | tf_op jit(solution)/shard_map/pallas_call | solution.py:187
  81.9 1.1 dynamic-slice_bitcast_fusion.2
  83.0 1.1 collective-permute-start.4
  84.1 0.6 collective-permute-start.5
  84.7 2.4 %fusion.5 = f32[128,2048]{1,0:T(8,128)S(1)} fusion(bf16[2048,2048]{1,0:T(8,128)(2,1)} %all-gather.3.cloned.1.call-done, s32[]{:T(128)S(6)} %select_n.251, bf16[4,128,512]{2,1,0:T(8,128)(2,1)} %bitcast.93, s32[]{:T(128)S(6)} %select_n.223), kind=kOutput, calls=%fused_computation.10 | convolution fusion | flops 268435456 | bytes 3276808 | tf_op jit(solution)/shard_map/dot_general | solution.py:323
  87.1 2.5 %collective-permute-done.4 = bf16[128,512]{1,0:T(8,128)(2,1)S(1)} collective-permute-done((bf16[128,512]{1,0:T(8,128)(2,1)S(1)}, bf16[128,512]{1,0:T(8,128)(2,1)S(1)}, u32[]{:S(2)}, u32[]{:S(2)}) %collective-permute-start.4) | collective-permute-done | bytes 131104 | tf_op jit(solution)/shard_map/ppermute | solution.py:331
  89.5 2.0 %convolution_add_fusion.1 = f32[128,2048]{1,0:T(8,128)S(1)} fusion(f32[128,2048]{1,0:T(8,128)S(1)} %fusion.5, bf16[128,512]{1,0:T(8,128)(2,1)S(1)} %collective-permute-done.4, bf16[2048,2048]{1,0:T(8,128)(2,1)} %all-gather.3.cloned.1.call-done, s32[]{:T(128)S(6)} %select_n.253), kind=kOutput, calls=%fused_computation.5 | convolution fusion | flops 268697600 | bytes 4325380 | tf_op jit(solution)/shard_map/dot_general | solution.py:333
  91.6 1.2 collective-permute-done.6
  92.7 2.1 %fusion.1 = f32[128,2048]{1,0:T(8,128)S(1)} fusion(bf16[128,512]{1,0:T(8,128)(2,1)S(1)} %collective-permute-done.6, bf16[2048,2048]{1,0:T(8,128)(2,1)} %all-gather.3.cloned.1.call-done, s32[]{:T(128)S(6)} %select_n.257), kind=kOutput, calls=%fused_computation.6 | convolution fusion | flops 268435456 | bytes 3276804 | tf_op jit(solution)/shard_map/dot_general | solution.py:333
  94.8 0.4 collective-permute-done.5
  95.2 2.2 %multiply_reduce_fusion.1 = (f32[128]{0:T(128)S(1)}, f32[128,2048]{1,0:T(8,128)S(1)}) fusion(f32[128,2048]{1,0:T(8,128)S(1)} %fusion.1, f32[128,2048]{1,0:T(8,128)S(1)} %convolution_add_fusion.1, bf16[128,512]{1,0:T(8,128)(2,1)S(1)} %collective-permute-done.5, bf16[2048,2048]{1,0:T(8,128)(2,1)} %all-gather.3.cloned.1.call-done, s32[]{:T(128)S(6)} %select_n.255), kind=kOutput, calls=%fused_computation.25 | convolution fusion | flops 269483904 | bytes 5374468 | tf_op jit(solution)/shard_map/dot_general | solution.py:333
  97.4 0.2 add_convert_fusion.1
  97.6 6.5 %all-gather.5.cloned.1.call-done = bf16[2048,512]{0,1:T(8,128)(2,1)} async-done(((bf16[512,512]{0,1:T(8,128)(2,1)}), bf16[2048,512]{0,1:T(8,128)(2,1)}) %all-gather.5.cloned.1.call-update) | async-done | bytes 2097168 | tf_op jit(solution)/shard_map/all_gather | solution.py:307
  104.2 2.6 %multiply_reduce_fusion = (f32[128]{0:T(128)S(1)}, f32[128,2048]{1,0:T(8,128)S(1)}) fusion(bf16[2048,512]{0,1:T(8,128)(2,1)} %all-gather.5.cloned.1.call-done, bf16[128,2048]{1,0:T(8,128)(2,1)S(1)} %add_convert_fusion.1, bf16[512,256]{1,0:T(8,128)(2,1)} %param.29, s32[]{:T(128)S(6)} %select_n.258), kind=kOutput, calls=%fused_computation.23 | convolution fusion | flops 269320064 | bytes 3736068 | tf_op jit(solution)/shard_map/dot_general | solution.py:351
  106.8 0.2 add_convert_fusion
  107.1 1.4 %collective-permute-start.7 = (bf16[128,512]{1,0:T(8,128)(2,1)S(1)}, bf16[128,512]{1,0:T(8,128)(2,1)S(1)}, u32[]{:S(2)}, u32[]{:S(2)}) collective-permute-start(bf16[128,512]{1,0:T(8,128)(2,1)S(1)} %get-tuple-element.44), channel_id=1, source_target_pairs={{0,1},{1,2},{2,3},{3,0},{4,5},{5,6},{6,7},{7,4},{8,9},{9,10},{10,1... | collective-permute-start | bytes 393224 | tf_op jit(solution)/shard_map/ppermute | solution.py:242
  108.5 0.3 collective-permute-start.8
  108.8 0.3 collective-permute-start.9
  109.1 1.9 %collective-permute-done.7 = bf16[128,512]{1,0:T(8,128)(2,1)S(1)} collective-permute-done((bf16[128,512]{1,0:T(8,128)(2,1)S(1)}, bf16[128,512]{1,0:T(8,128)(2,1)S(1)}, u32[]{:S(2)}, u32[]{:S(2)}) %collective-permute-start.7) | collective-permute-done | bytes 131104 | tf_op jit(solution)/shard_map/ppermute | solution.py:242
  111.0 3.5 %collective-permute-done.8 = bf16[128,512]{1,0:T(8,128)(2,1)S(1)} collective-permute-done((bf16[128,512]{1,0:T(8,128)(2,1)S(1)}, bf16[128,512]{1,0:T(8,128)(2,1)S(1)}, u32[]{:S(2)}, u32[]{:S(2)}) %collective-permute-start.8) | collective-permute-done | bytes 131104 | tf_op jit(solution)/shard_map/ppermute | solution.py:242
  114.5 0.8 collective-permute-done.9
  115.3 0.1 pad_maximum_fusion.2
  115.4 1.4 %gather_fusion.2 = bf16[4,128,512]{2,1,0:T(8,128)(2,1)} fusion(bf16[4,128,512]{2,1,0:T(8,128)(2,1)S(1)} %pad_maximum_fusion.2, s32[1024]{0:T(1024)S(1)} %pad_clamp_fusion.1), kind=kCustom, calls=%fused_computation.2 | custom fusion | bytes 1048592 | tf_op jit(solution)/shard_map/gather | solution.py:244
  (59 shorter events, 0.4 us)
Async XLA Ops:
  6.5 0.7 copy-start.11
  6.5 0.9 copy-start.9
  6.5 78.1 %all-gather.3.cloned.1.call-start = ((), (), s32[]{:S(2)}) async-start(), calls=%async_computation.2 | async-start | bytes 10485760 | tf_op jit(solution)/shard_map/all_gather | solution.py:306
  8.4 11.6 %all-to-all-start = ((s32[8,1,6]{2,1,0:T(1,128)}), s32[8,1,6]{2,1,0:T(1,128)S(1)}, u32[]{:S(2)}, u32[]{:S(2)}) async-start(s32[8,1,6]{2,1,0:T(1,128)} %copy.38), calls=%async_computation | async-start | bytes 8192 | tf_op jit(solution)/shard_map/all_to_all | solution.py:283
  22.0 3.9 %copy-start.6 = (bf16[512]{0:T(512)(128)(2,1)S(1)}, bf16[512]{0:T(512)(128)(2,1)}, u32[]{:S(2)}) copy-start(bf16[512]{0:T(512)(128)(2,1)} %param.28) | copy-start | bytes 3076
  22.0 3.9 %copy-start.7 = (bf16[512]{0:T(512)(128)(2,1)S(1)}, bf16[512]{0:T(512)(128)(2,1)}, u32[]{:S(2)}) copy-start(bf16[512]{0:T(512)(128)(2,1)} %param.32) | copy-start | bytes 3076
  22.0 4.1 %copy-start.1 = (bf16[512,512]{1,0:T(8,128)(2,1)S(1)}, bf16[512,512]{1,0:T(8,128)(2,1)}, u32[]{:S(2)}) copy-start(bf16[512,512]{1,0:T(8,128)(2,1)} %param.21) | copy-start | bytes 1572868
  22.0 7.8 %copy-start.2 = (bf16[512,256]{1,0:T(8,128)(2,1)S(1)}, bf16[512,256]{1,0:T(8,128)(2,1)}, u32[]{:S(2)}) copy-start(bf16[512,256]{1,0:T(8,128)(2,1)} %param.30) | copy-start | bytes 786436
  22.0 8.0 %copy-start.3 = (bf16[256,512]{1,0:T(8,128)(2,1)S(1)}, bf16[256,512]{1,0:T(8,128)(2,1)}, u32[]{:S(2)}) copy-start(bf16[256,512]{1,0:T(8,128)(2,1)} %param.31) | copy-start | bytes 786436
  22.0 38.7 %all-to-all-start.1 = ((bf16[8,6,64,256]{3,2,1,0:T(8,128)(2,1)}), bf16[8,6,64,256]{3,2,1,0:T(8,128)(2,1)S(1)}, u32[]{:S(2)}, u32[]{:S(2)}) async-start(bf16[8,6,64,256]{3,2,1,0:T(8,128)(2,1)} %bitcast.20), calls=%async_computation.1 | async-start | bytes 3145728 | tf_op jit(solution)/shard_map/all_to_all | solution.py:292
  25.7 5.1 %copy-start.10 = (s32[1,8]{1,0:T(1,128)S(1)}, s32[1,8]{1,0:T(1,128)}, u32[]{:S(2)}) copy-start(s32[1,8]{1,0:T(1,128)} %param.37) | copy-start | bytes 100
  25.8 5.5 %copy-start.5 = (s32[1,8]{1,0:T(1,128)S(1)}, s32[1,8]{1,0:T(1,128)}, u32[]{:S(2)}) copy-start(s32[1,8]{1,0:T(1,128)} %param.35) | copy-start | bytes 100
  25.8 5.7 %copy-start.8 = (s32[1,8]{1,0:T(1,128)S(1)}, s32[1,8]{1,0:T(1,128)}, u32[]{:S(2)}) copy-start(s32[1,8]{1,0:T(1,128)} %param.36) | copy-start | bytes 100
  25.8 40.2 %copy-start.4 = (s32[7,1,512]{2,1,0:T(1,128)S(1)}, s32[7,1,512]{2,1,0:T(1,128)}, u32[]{:S(2)}) copy-start(s32[7,1,512]{2,1,0:T(1,128)} %constant.272.clone.1) | copy-start | bytes 43012
  25.8 78.4 %all-gather.5.cloned.1.call-start = ((), (), s32[]{:S(2)}) async-start(), calls=%async_computation.3 | async-start | bytes 2621440 | tf_op jit(solution)/shard_map/all_gather | solution.py:307
  26.1 40.5 %collective-permute-start = (bf16[136,512]{1,0:T(8,128)(2,1)S(1)}, bf16[136,512]{1,0:T(8,128)(2,1)S(1)}, u32[]{:S(2)}, u32[]{:S(2)}) collective-permute-start(bf16[136,512]{1,0:T(8,128)(2,1)S(1)} %get-tuple-element.38), channel_id=1, source_target_pairs={{0,1},{1,2},{2,3},{3,0},{4,5},{5,6},{6,7},{7,4},{8,9},{9,10},{10,1... | collective-permute-start | bytes 417800 | tf_op jit(solution)/shard_map/ppermute | solution.py:228
  29.3 37.2 %collective-permute-start.1 = (bf16[136,512]{1,0:T(8,128)(2,1)S(1)}, bf16[136,512]{1,0:T(8,128)(2,1)S(1)}, u32[]{:S(2)}, u32[]{:S(2)}) collective-permute-start(bf16[136,512]{1,0:T(8,128)(2,1)S(1)} %get-tuple-element.39), channel_id=1, source_target_pairs={{0,2},{1,3},{2,0},{3,1},{4,6},{5,7},{6,4},{7,5},{8,10},{9,11},{10,... | collective-permute-start | bytes 417800 | tf_op jit(solution)/shard_map/ppermute | solution.py:228
  29.6 37.0 %collective-permute-start.2 = (bf16[136,512]{1,0:T(8,128)(2,1)S(1)}, bf16[136,512]{1,0:T(8,128)(2,1)S(1)}, u32[]{:S(2)}, u32[]{:S(2)}) collective-permute-start(bf16[136,512]{1,0:T(8,128)(2,1)S(1)} %get-tuple-element.40), channel_id=1, source_target_pairs={{0,3},{1,0},{2,1},{3,2},{4,7},{5,4},{6,5},{7,6},{8,11},{9,8},{10,9... | collective-permute-start | bytes 417800 | tf_op jit(solution)/shard_map/ppermute | solution.py:228
  60.7 6.6 %copy-start = (bf16[8,6,64,256]{3,2,1,0:T(8,128)(2,1)}, bf16[8,6,64,256]{3,2,1,0:T(8,128)(2,1)S(1)}, u32[]{:S(2)}) copy-start(bf16[8,6,64,256]{3,2,1,0:T(8,128)(2,1)S(1)} %all-to-all-done.1) | copy-start | bytes 4718596
  60.7 6.8 %collective-permute-start.3 = (bf16[8,6,64,256]{3,2,1,0:T(8,128)(2,1)S(1)}, bf16[8,6,64,256]{3,2,1,0:T(8,128)(2,1)}, u32[]{:S(2)}, u32[]{:S(2)}) collective-permute-start(bf16[8,6,64,256]{3,2,1,0:T(8,128)(2,1)S(1)} %all-to-all-done.1), channel_id=1, source_target_pairs={{0,1},{1,0},{2,3},{3,2},{4,5},{5,4},{6,7},{7,6},{8,9},{9,8},{10,11... | collective-permute-start | bytes 4718600 | tf_op jit(solution)/shard_map/ppermute | solution.py:293
  83.0 6.6 %collective-permute-start.4 = (bf16[128,512]{1,0:T(8,128)(2,1)S(1)}, bf16[128,512]{1,0:T(8,128)(2,1)S(1)}, u32[]{:S(2)}, u32[]{:S(2)}) collective-permute-start(bf16[128,512]{1,0:T(8,128)(2,1)S(1)} %get-tuple-element.47), channel_id=1, source_target_pairs={{0,1},{1,2},{2,3},{3,0},{4,5},{5,6},{6,7},{7,4},{8,9},{9,10},{10,1... | collective-permute-start | bytes 393224 | tf_op jit(solution)/shard_map/ppermute | solution.py:331
  84.1 8.6 %collective-permute-start.6 = (bf16[128,512]{1,0:T(8,128)(2,1)S(1)}, bf16[128,512]{1,0:T(8,128)(2,1)S(1)}, u32[]{:S(2)}, u32[]{:S(2)}) collective-permute-start(bf16[128,512]{1,0:T(8,128)(2,1)S(1)} %get-tuple-element.46), channel_id=1, source_target_pairs={{0,3},{1,0},{2,1},{3,2},{4,7},{5,4},{6,5},{7,6},{8,11},{9,8},{10,9... | collective-permute-start | bytes 393224 | tf_op jit(solution)/shard_map/ppermute | solution.py:331
  84.1 11.1 %collective-permute-start.5 = (bf16[128,512]{1,0:T(8,128)(2,1)S(1)}, bf16[128,512]{1,0:T(8,128)(2,1)S(1)}, u32[]{:S(2)}, u32[]{:S(2)}) collective-permute-start(bf16[128,512]{1,0:T(8,128)(2,1)S(1)} %get-tuple-element.45), channel_id=1, source_target_pairs={{0,2},{1,3},{2,0},{3,1},{4,6},{5,7},{6,4},{7,5},{8,10},{9,11},{10,... | collective-permute-start | bytes 393224 | tf_op jit(solution)/shard_map/ppermute | solution.py:331
  107.1 3.9 %collective-permute-start.7 = (bf16[128,512]{1,0:T(8,128)(2,1)S(1)}, bf16[128,512]{1,0:T(8,128)(2,1)S(1)}, u32[]{:S(2)}, u32[]{:S(2)}) collective-permute-start(bf16[128,512]{1,0:T(8,128)(2,1)S(1)} %get-tuple-element.44), channel_id=1, source_target_pairs={{0,1},{1,2},{2,3},{3,0},{4,5},{5,6},{6,7},{7,4},{8,9},{9,10},{10,1... | collective-permute-start | bytes 393224 | tf_op jit(solution)/shard_map/ppermute | solution.py:242
  108.5 6.1 %collective-permute-start.8 = (bf16[128,512]{1,0:T(8,128)(2,1)S(1)}, bf16[128,512]{1,0:T(8,128)(2,1)S(1)}, u32[]{:S(2)}, u32[]{:S(2)}) collective-permute-start(bf16[128,512]{1,0:T(8,128)(2,1)S(1)} %get-tuple-element.43), channel_id=1, source_target_pairs={{0,2},{1,3},{2,0},{3,1},{4,6},{5,7},{6,4},{7,5},{8,10},{9,11},{10,... | collective-permute-start | bytes 393224 | tf_op jit(solution)/shard_map/ppermute | solution.py:242
  108.8 6.6 %collective-permute-start.9 = (bf16[128,512]{1,0:T(8,128)(2,1)S(1)}, bf16[128,512]{1,0:T(8,128)(2,1)S(1)}, u32[]{:S(2)}, u32[]{:S(2)}) collective-permute-start(bf16[128,512]{1,0:T(8,128)(2,1)S(1)} %get-tuple-element.42), channel_id=1, source_target_pairs={{0,3},{1,0},{2,1},{3,2},{4,7},{5,4},{6,5},{7,6},{8,11},{9,8},{10,9... | collective-permute-start | bytes 393224 | tf_op jit(solution)/shard_map/ppermute | solution.py:242
Sparse Core Ops, SparseCore 0:
  8.9 66.7 all-gather.2
  77.3 26.8 all-gather.4

commit v17 on v16

--- a/solution.py
+++ b/solution.py
@@ -303,12 +303,13 @@
         page_counts[0], last_fill[0], row_counts[0], page_total,
     )
     tp_size = lax.axis_size("tp")
-    full_weight = lax.all_gather(out_weight, "tp", axis=0, tiled=True)
-    ple_joined = lax.all_gather(
-        jnp.concatenate([ple_gate_weight, ple_proj_weight.T], axis=1), "tp", axis=0, tiled=True
-    )
-    full_gate_weight = ple_joined[:, : ple_gate_weight.shape[1]]
-    full_proj_weight_t = ple_joined[:, ple_gate_weight.shape[1] :]
+    joined = jnp.concatenate([out_weight, ple_gate_weight, ple_proj_weight.T], axis=1)
+    full_joined = lax.all_gather(joined, "tp", axis=0, tiled=True)
+    gate_from = out_weight.shape[1]
+    proj_from = gate_from + ple_gate_weight.shape[1]
+    full_weight = full_joined[:, :gate_from]
+    full_gate_weight = full_joined[:, gate_from:proj_from]
+    full_proj_weight_t = full_joined[:, proj_from:]
     hidden_parts = hidden.reshape(tp_size, -1, hidden.shape[1])
     gain_rows = jnp.zeros((8, hidden.shape[1]), hidden.dtype).at[0].set(attn_gain).at[1].set(ple_gain)
     with_gains = jnp.concatenate(

time: 125 us -> 128 us (1.024)
  local copies, waits for them, and re-layouts: 7.63 us -> 17.6 us
  waiting for transfers between devices: 48.9 us -> 39.3 us
  other arithmetic: 6.81 us -> 9.82 us
    slice x0 -> x1, local copies, waits for them, and re-layouts: none -> 8.38 us  [shards(): full_weight = full_joined[:, :gate_from]]
    all_gather x2 -> x1, waiting for transfers between devices: 6.54 us -> 0.49 us  [shards(): full_joined = lax.all_gather(joined, 'tp', axis=0, tiled=True)]
    ppermute x3, waiting for transfers between devices: 3.97 us -> 0.01 us  [shards(): piece = lax.ppermute(outgoing, 'tp', perm)]
    concatenate x1, other arithmetic: 0.83 us -> 3.41 us  [shards(): jnp.concatenate([out_weight, ple_gate_weight, ple_proj_weight.T], axis=1)]
  transfers between devices with their start and end apart: 14 -> 13, of which waited for: 9 -> 6; matrix products, arithmetic and copies ran while one was open for 17% -> 21% of each run, Pallas kernels for 12% -> 11%
where the time goes in v17:
time: 128 us; the launch traced here: 127 us
  waiting for transfers between devices  39.3 us (31%)
  starting transfers between devices  21.2 us (17%)
  local copies, waits for them, and re-layouts  17.6 us (14%)
  Pallas kernels  14.4 us (11%)
  between operations  13.9 us (11%)
  matrix products  11 us (9%)
  other arithmetic  9.82 us (8%)
    all_to_all x1, waiting for transfers between devices, shards(): lax.all_to_all(outgoing, 'req', split_axis=0, concat_axis=0, tiled=True)  29.9 us
    pallas_call x1, Pallas kernels, sparse_attention(): pl.pallas_call(functools.partial(attention_kernel, slot_base=slot_base, m...  14.4 us
    slice x1, local copies, waits for them, and re-layouts, shards(): full_weight = full_joined[:, :gate_from]  8.38 us
    ppermute x3, waiting for transfers between devices, columns_to_rows(): received.append(lax.ppermute(outgoing, axis_name, perm))  6.56 us
    all_to_all x1, starting transfers between devices, shards(): lax.all_to_all(request_table, 'req', split_axis=0, concat_axis=0, tiled=T...  6.38 us
    dot_general x3, matrix products, shards(): jnp.dot(piece, lax.dynamic_slice_in_dim(full_weight, source * width, widt...  6.31 us
    ppermute x3, starting transfers between devices, rows_to_columns(): received.append(lax.ppermute(outgoing, axis_name, perm))  3.73 us
    all_to_all x1, starting transfers between devices, shards(): lax.all_to_all(outgoing, 'req', split_axis=0, concat_axis=0, tiled=True)  3.72 us
  transfers between devices with their start and end apart: 13, of which 6 were waited for; matrix products, arithmetic and copies ran while one was open for 21% of the time, Pallas kernels for 11%

profile of v17, /device:TPU:1, one launch (start us, length us, event | category | flops | bytes accessed | tf_op | source)
XLA Modules:
  0.0 127.2 jit_solution(10489171930774017362)
XLA Ops:
  6.5 1.1 copy.40
  7.6 3.4 %pad_maximum_fusion = bf16[512,2560]{1,0:T(8,128)(2,1)} fusion(bf16[512,256]{1,0:T(8,128)(2,1)S(1)} %copy.40, bf16[512,256]{1,0:T(8,128)(2,1)} %param.30, bf16[512,2048]{1,0:T(8,128)(2,1)} %param.27), kind=kLoop, calls=%fused_computation.3 | loop fusion | flops 7864320 | bytes 5242880 | tf_op jit(solution)/shard_map/concatenate | solution.py:306
  11.0 0.0 all-gather.2.cloned.1.call-update
  11.1 0.6 copy-done.9
  11.7 0.2 convert_reduce_fusion.1
  11.9 0.2 select_reduce_fusion.2
  12.1 0.7 copy.38
  12.8 6.4 %all-to-all-start = ((s32[8,1,6]{2,1,0:T(1,128)}), s32[8,1,6]{2,1,0:T(1,128)S(1)}, u32[]{:S(2)}, u32[]{:S(2)}) async-start(s32[8,1,6]{2,1,0:T(1,128)} %copy.38), calls=%async_computation | async-start | bytes 8192 | tf_op jit(solution)/shard_map/all_to_all | solution.py:283
  19.2 3.0 %dynamic-slice_select_fusion = bf16[48,64,256]{2,1,0:T(8,128)(2,1)S(1)} fusion(bf16[48,64,512]{2,1,0:T(8,128)(2,1)} %param.26, s32[]{:T(128)S(6)} %select_n.244, bf16[48,64,512]{2,1,0:T(8,128)(2,1)} %param.25, pred[]{:T(512)S(6)} %eq.140), kind=kLoop, calls=%fused_computation.13 | loop fusion | flops 786432 | bytes 4718597 | tf_op jit(solution)/shard_map/jit(_where)/select_n | solution.py:290
  22.2 2.2 %all-to-all-done = s32[8,1,6]{2,1,0:T(1,128)S(1)} async-done(((s32[8,1,6]{2,1,0:T(1,128)}), s32[8,1,6]{2,1,0:T(1,128)S(1)}, u32[]{:S(2)}, u32[]{:S(2)}) %all-to-all-start) | async-done | bytes 224 | tf_op jit(solution)/shard_map/all_to_all | solution.py:283
  24.4 0.1 reshape.538
  24.5 0.0 copy-start.5
  24.5 0.0 copy-start.1
  24.5 1.9 %gather_fusion.1 = bf16[48,64,256]{2,1,0:T(8,128)(2,1)} fusion(bf16[48,64,256]{2,1,0:T(8,128)(2,1)S(1)} %dynamic-slice_select_fusion, s32[1024]{0:T(1024)S(1)} %pad_clamp_fusion), kind=kCustom, calls=%fused_computation.1 | custom fusion | bytes 3145920 | tf_op jit(solution)/shard_map/gather | solution.py:291
  26.4 3.7 %all-to-all-start.1 = ((bf16[8,6,64,256]{3,2,1,0:T(8,128)(2,1)}), bf16[8,6,64,256]{3,2,1,0:T(8,128)(2,1)S(1)}, u32[]{:S(2)}, u32[]{:S(2)}) async-start(bf16[8,6,64,256]{3,2,1,0:T(8,128)(2,1)} %bitcast.20), calls=%async_computation.1 | async-start | bytes 3145728 | tf_op jit(solution)/shard_map/all_to_all | solution.py:292
  30.3 0.1 fusion.12
  30.4 3.3 %collective-permute-start = (bf16[136,512]{1,0:T(8,128)(2,1)S(1)}, bf16[136,512]{1,0:T(8,128)(2,1)S(1)}, u32[]{:S(2)}, u32[]{:S(2)}) collective-permute-start(bf16[136,512]{1,0:T(8,128)(2,1)S(1)} %get-tuple-element.38), channel_id=1, source_target_pairs={{0,1},{1,2},{2,3},{3,0},{4,5},{5,6},{6,7},{7,4},{8,9},{9,10},{10,1... | collective-permute-start | bytes 417800 | tf_op jit(solution)/shard_map/ppermute | solution.py:228
  33.7 0.3 collective-permute-start.1
  33.9 0.2 collective-permute-start.2
  34.1 0.2 reduce-window_clone.1
  34.3 0.1 convert_reduce_fusion.2
  34.4 0.1 slice.57
  34.5 0.1 slice.58
  34.6 0.2 reduce-window_1_clone.1
  34.8 0.1 convert_reduce_fusion
  34.9 0.2 select_reduce_fusion.3
  35.2 29.9 %all-to-all-done.1 = bf16[8,6,64,256]{3,2,1,0:T(8,128)(2,1)S(1)} async-done(((bf16[8,6,64,256]{3,2,1,0:T(8,128)(2,1)}), bf16[8,6,64,256]{3,2,1,0:T(8,128)(2,1)S(1)}, u32[]{:S(2)}, u32[]{:S(2)}) %all-to-all-start.1) | async-done | bytes 1572896 | tf_op jit(solution)/shard_map/all_to_all | solution.py:292
  65.1 3.1 %collective-permute-start.3 = (bf16[8,6,64,256]{3,2,1,0:T(8,128)(2,1)S(1)}, bf16[8,6,64,256]{3,2,1,0:T(8,128)(2,1)}, u32[]{:S(2)}, u32[]{:S(2)}) collective-permute-start(bf16[8,6,64,256]{3,2,1,0:T(8,128)(2,1)S(1)} %all-to-all-done.1), channel_id=1, source_target_pairs={{0,1},{1,0},{2,3},{3,2},{4,5},{5,4},{6,7},{7,6},{8,9},{9,8},{10,11... | collective-permute-start | bytes 4718600 | tf_op jit(solution)/shard_map/ppermute | solution.py:293
  68.2 0.1 copy.33
  68.3 0.1 copy.34
  68.4 0.1 copy.35
  68.5 0.1 copy.36
  68.6 0.1 stack.47
  68.7 0.1 reshape.520
  68.8 0.1 select_reduce_fusion.1
  69.0 0.6 pad_add_fusion.2.scalars_ref
  69.6 0.9 copy.39.rown_ref
  70.5 0.6 pad_add_fusion.kinfo_ref
  71.1 0.0 collective-permute-done
  71.1 0.0 collective-permute-done.1
  71.1 0.1 pad_maximum_fusion.1
  71.2 0.6 gather_fusion
  71.8 0.1 convert_bitcast_fusion
  71.9 0.1 copy.43
  72.1 14.4 %shard_map.163 = bf16[512,512]{1,0:T(8,128)(2,1)} custom-call(s32[60]{0:T(128)} %pad_add_fusion.2.scalars_ref, bf16[512,512]{1,0:T(8,128)(2,1)} %q_ref.1, bf16[48,64,256]{2,1,0:T(8,128)(2,1)} %bitcast.88, bf16[48,64,256]{2,1,0:T(8,128)(2,1)} %bitcast.22.partner_ref, bf16[512,512]{1,0:T(8,128)(2,1)} %fresh_k_ref.1, bf16[512,512]{1,0:T(8,128)(2,1)} %fresh_v_ref.1, ...), custom_call_target="tpu_custom_call" | custom-call | tf_op jit(solution)/shard_map/pallas_call | solution.py:187
  86.5 1.1 dynamic-slice_bitcast_fusion.2
  87.6 1.2 collective-permute-start.4
  88.8 0.6 collective-permute-start.5
  89.4 0.5 all-gather.2.cloned.1.call-done
  89.9 8.4 %slice.71 = bf16[2048,2048]{1,0:T(8,128)(2,1)} slice(bf16[2048,2560]{1,0:T(8,128)(2,1)} %all-gather.2.cloned.1.call-done), slice={[0:2048], [0:2048]} | slice | bytes 16777216 | tf_op jit(solution)/shard_map/slice | solution.py:310
  98.3 2.1 %fusion.5 = f32[128,2048]{1,0:T(8,128)S(1)} fusion(bf16[2048,2048]{1,0:T(8,128)(2,1)} %slice.71, s32[]{:T(128)S(6)} %select_n.251, bf16[4,128,512]{2,1,0:T(8,128)(2,1)} %bitcast.93, s32[]{:T(128)S(6)} %select_n.223), kind=kOutput, calls=%fused_computation.11 | convolution fusion | flops 268435456 | bytes 3276808 | tf_op jit(solution)/shard_map/dot_general | solution.py:324
  100.4 2.0 %convolution_add_fusion.1 = f32[128,2048]{1,0:T(8,128)S(1)} fusion(f32[128,2048]{1,0:T(8,128)S(1)} %fusion.5, bf16[128,512]{1,0:T(8,128)(2,1)S(1)} %collective-permute-done.4, bf16[2048,2048]{1,0:T(8,128)(2,1)} %slice.71, s32[]{:T(128)S(6)} %select_n.253), kind=kOutput, calls=%fused_computation.6 | convolution fusion | flops 268697600 | bytes 4325380 | tf_op jit(solution)/shard_map/dot_general | solution.py:334
  102.5 2.0 %fusion.1 = f32[128,2048]{1,0:T(8,128)S(1)} fusion(bf16[128,512]{1,0:T(8,128)(2,1)S(1)} %collective-permute-done.6, bf16[2048,2048]{1,0:T(8,128)(2,1)} %slice.71, s32[]{:T(128)S(6)} %select_n.257), kind=kOutput, calls=%fused_computation.7 | convolution fusion | flops 268435456 | bytes 3276804 | tf_op jit(solution)/shard_map/dot_general | solution.py:334
  104.5 2.2 %multiply_reduce_fusion.1 = (f32[128]{0:T(128)S(1)}, f32[128,2048]{1,0:T(8,128)S(1)}) fusion(f32[128,2048]{1,0:T(8,128)S(1)} %fusion.1, f32[128,2048]{1,0:T(8,128)S(1)} %convolution_add_fusion.1, bf16[128,512]{1,0:T(8,128)(2,1)S(1)} %collective-permute-done.5, bf16[2048,2048]{1,0:T(8,128)(2,1)} %slice.71, s32[]{:T(128)S(6)} %select_n.255), kind=kOutput, calls=%fused_computation.26 | convolution fusion | flops 269483904 | bytes 5374468 | tf_op jit(solution)/shard_map/dot_general | solution.py:334
  106.8 0.2 add_convert_fusion.1
  107.0 2.6 %multiply_reduce_fusion = (f32[128]{0:T(128)S(1)}, f32[128,2048]{1,0:T(8,128)S(1)}) fusion(bf16[2048,2560]{1,0:T(8,128)(2,1)} %all-gather.2.cloned.1.call-done, bf16[128,2048]{1,0:T(8,128)(2,1)S(1)} %add_convert_fusion.1, bf16[512,256]{1,0:T(8,128)(2,1)} %param.29, s32[]{:T(128)S(6)} %select_n.258), kind=kOutput, calls=%fused_computation.24 | convolution fusion | flops 269320064 | bytes 3736068 | tf_op jit(solution)/shard_map/dot_general | solution.py:352
  109.6 0.2 add_convert_fusion
  109.9 1.1 collective-permute-start.7
  111.0 1.3 %collective-permute-start.8 = (bf16[128,512]{1,0:T(8,128)(2,1)S(1)}, bf16[128,512]{1,0:T(8,128)(2,1)S(1)}, u32[]{:S(2)}, u32[]{:S(2)}) collective-permute-start(bf16[128,512]{1,0:T(8,128)(2,1)S(1)} %get-tuple-element.43), channel_id=1, source_target_pairs={{0,2},{1,3},{2,0},{3,1},{4,6},{5,7},{6,4},{7,5},{8,10},{9,11},{10,... | collective-permute-start | bytes 393224 | tf_op jit(solution)/shard_map/ppermute | solution.py:242
  112.3 1.4 %collective-permute-done.7 = bf16[128,512]{1,0:T(8,128)(2,1)S(1)} collective-permute-done((bf16[128,512]{1,0:T(8,128)(2,1)S(1)}, bf16[128,512]{1,0:T(8,128)(2,1)S(1)}, u32[]{:S(2)}, u32[]{:S(2)}) %collective-permute-start.7) | collective-permute-done | bytes 131104 | tf_op jit(solution)/shard_map/ppermute | solution.py:242
  113.7 4.5 %collective-permute-done.8 = bf16[128,512]{1,0:T(8,128)(2,1)S(1)} collective-permute-done((bf16[128,512]{1,0:T(8,128)(2,1)S(1)}, bf16[128,512]{1,0:T(8,128)(2,1)S(1)}, u32[]{:S(2)}, u32[]{:S(2)}) %collective-permute-start.8) | collective-permute-done | bytes 131104 | tf_op jit(solution)/shard_map/ppermute | solution.py:242
  118.3 0.6 collective-permute-done.9
  118.9 0.1 pad_maximum_fusion.2
  119.0 1.4 %gather_fusion.2 = bf16[4,128,512]{2,1,0:T(8,128)(2,1)} fusion(bf16[4,128,512]{2,1,0:T(8,128)(2,1)S(1)} %pad_maximum_fusion.2, s32[1024]{0:T(1024)S(1)} %pad_clamp_fusion.1), kind=kCustom, calls=%fused_computation.2 | custom fusion | bytes 1048592 | tf_op jit(solution)/shard_map/gather | solution.py:244
  (53 shorter events, 0.3 us)
Async XLA Ops:
  6.5 83.3 %all-gather.2.cloned.1.call-start = ((), (), s32[]{:S(2)}) async-start(), calls=%async_computation.2 | async-start | bytes 13107200 | tf_op jit(solution)/shard_map/all_gather | solution.py:307
  11.0 0.7 copy-start.9
  11.0 0.8 copy-start.7
  12.8 11.6 %all-to-all-start = ((s32[8,1,6]{2,1,0:T(1,128)}), s32[8,1,6]{2,1,0:T(1,128)S(1)}, u32[]{:S(2)}, u32[]{:S(2)}) async-start(s32[8,1,6]{2,1,0:T(1,128)} %copy.38), calls=%async_computation | async-start | bytes 8192 | tf_op jit(solution)/shard_map/all_to_all | solution.py:283
  24.5 5.7 %copy-start.4 = (bf16[512]{0:T(512)(128)(2,1)S(1)}, bf16[512]{0:T(512)(128)(2,1)}, u32[]{:S(2)}) copy-start(bf16[512]{0:T(512)(128)(2,1)} %param.28) | copy-start | bytes 3076
  24.5 5.7 %copy-start.5 = (bf16[512]{0:T(512)(128)(2,1)S(1)}, bf16[512]{0:T(512)(128)(2,1)}, u32[]{:S(2)}) copy-start(bf16[512]{0:T(512)(128)(2,1)} %param.32) | copy-start | bytes 3076
  24.5 5.8 %copy-start.1 = (bf16[512,512]{1,0:T(8,128)(2,1)S(1)}, bf16[512,512]{1,0:T(8,128)(2,1)}, u32[]{:S(2)}) copy-start(bf16[512,512]{1,0:T(8,128)(2,1)} %param.21) | copy-start | bytes 1572868
  26.4 7.7 %copy-start.8 = (s32[1,8]{1,0:T(1,128)S(1)}, s32[1,8]{1,0:T(1,128)}, u32[]{:S(2)}) copy-start(s32[1,8]{1,0:T(1,128)} %param.37) | copy-start | bytes 100
  26.4 8.2 %copy-start.3 = (s32[1,8]{1,0:T(1,128)S(1)}, s32[1,8]{1,0:T(1,128)}, u32[]{:S(2)}) copy-start(s32[1,8]{1,0:T(1,128)} %param.35) | copy-start | bytes 100
  26.4 8.4 %copy-start.6 = (s32[1,8]{1,0:T(1,128)S(1)}, s32[1,8]{1,0:T(1,128)}, u32[]{:S(2)}) copy-start(s32[1,8]{1,0:T(1,128)} %param.36) | copy-start | bytes 100
  26.4 44.1 %copy-start.2 = (s32[7,1,512]{2,1,0:T(1,128)S(1)}, s32[7,1,512]{2,1,0:T(1,128)}, u32[]{:S(2)}) copy-start(s32[7,1,512]{2,1,0:T(1,128)} %constant.272.clone.1) | copy-start | bytes 43012
  26.4 38.7 %all-to-all-start.1 = ((bf16[8,6,64,256]{3,2,1,0:T(8,128)(2,1)}), bf16[8,6,64,256]{3,2,1,0:T(8,128)(2,1)S(1)}, u32[]{:S(2)}, u32[]{:S(2)}) async-start(bf16[8,6,64,256]{3,2,1,0:T(8,128)(2,1)} %bitcast.20), calls=%async_computation.1 | async-start | bytes 3145728 | tf_op jit(solution)/shard_map/all_to_all | solution.py:292
  30.4 40.7 %collective-permute-start = (bf16[136,512]{1,0:T(8,128)(2,1)S(1)}, bf16[136,512]{1,0:T(8,128)(2,1)S(1)}, u32[]{:S(2)}, u32[]{:S(2)}) collective-permute-start(bf16[136,512]{1,0:T(8,128)(2,1)S(1)} %get-tuple-element.38), channel_id=1, source_target_pairs={{0,1},{1,2},{2,3},{3,0},{4,5},{5,6},{6,7},{7,4},{8,9},{9,10},{10,1... | collective-permute-start | bytes 417800 | tf_op jit(solution)/shard_map/ppermute | solution.py:228
  33.7 37.5 %collective-permute-start.1 = (bf16[136,512]{1,0:T(8,128)(2,1)S(1)}, bf16[136,512]{1,0:T(8,128)(2,1)S(1)}, u32[]{:S(2)}, u32[]{:S(2)}) collective-permute-start(bf16[136,512]{1,0:T(8,128)(2,1)S(1)} %get-tuple-element.39), channel_id=1, source_target_pairs={{0,2},{1,3},{2,0},{3,1},{4,6},{5,7},{6,4},{7,5},{8,10},{9,11},{10,... | collective-permute-start | bytes 417800 | tf_op jit(solution)/shard_map/ppermute | solution.py:228
  33.9 37.2 %collective-permute-start.2 = (bf16[136,512]{1,0:T(8,128)(2,1)S(1)}, bf16[136,512]{1,0:T(8,128)(2,1)S(1)}, u32[]{:S(2)}, u32[]{:S(2)}) collective-permute-start(bf16[136,512]{1,0:T(8,128)(2,1)S(1)} %get-tuple-element.40), channel_id=1, source_target_pairs={{0,3},{1,0},{2,1},{3,2},{4,7},{5,4},{6,5},{7,6},{8,11},{9,8},{10,9... | collective-permute-start | bytes 417800 | tf_op jit(solution)/shard_map/ppermute | solution.py:228
  65.1 6.9 %copy-start = (bf16[8,6,64,256]{3,2,1,0:T(8,128)(2,1)}, bf16[8,6,64,256]{3,2,1,0:T(8,128)(2,1)S(1)}, u32[]{:S(2)}) copy-start(bf16[8,6,64,256]{3,2,1,0:T(8,128)(2,1)S(1)} %all-to-all-done.1) | copy-start | bytes 4718596
  65.1 6.9 %collective-permute-start.3 = (bf16[8,6,64,256]{3,2,1,0:T(8,128)(2,1)S(1)}, bf16[8,6,64,256]{3,2,1,0:T(8,128)(2,1)}, u32[]{:S(2)}, u32[]{:S(2)}) collective-permute-start(bf16[8,6,64,256]{3,2,1,0:T(8,128)(2,1)S(1)} %all-to-all-done.1), channel_id=1, source_target_pairs={{0,1},{1,0},{2,3},{3,2},{4,5},{5,4},{6,7},{7,6},{8,9},{9,8},{10,11... | collective-permute-start | bytes 4718600 | tf_op jit(solution)/shard_map/ppermute | solution.py:293
  87.6 12.8 %collective-permute-start.4 = (bf16[128,512]{1,0:T(8,128)(2,1)S(1)}, bf16[128,512]{1,0:T(8,128)(2,1)S(1)}, u32[]{:S(2)}, u32[]{:S(2)}) collective-permute-start(bf16[128,512]{1,0:T(8,128)(2,1)S(1)} %get-tuple-element.47), channel_id=1, source_target_pairs={{0,1},{1,2},{2,3},{3,0},{4,5},{5,6},{6,7},{7,4},{8,9},{9,10},{10,1... | collective-permute-start | bytes 393224 | tf_op jit(solution)/shard_map/ppermute | solution.py:332
  88.8 13.7 %collective-permute-start.6 = (bf16[128,512]{1,0:T(8,128)(2,1)S(1)}, bf16[128,512]{1,0:T(8,128)(2,1)S(1)}, u32[]{:S(2)}, u32[]{:S(2)}) collective-permute-start(bf16[128,512]{1,0:T(8,128)(2,1)S(1)} %get-tuple-element.46), channel_id=1, source_target_pairs={{0,3},{1,0},{2,1},{3,2},{4,7},{5,4},{6,5},{7,6},{8,11},{9,8},{10,9... | collective-permute-start | bytes 393224 | tf_op jit(solution)/shard_map/ppermute | solution.py:332
  88.8 15.7 %collective-permute-start.5 = (bf16[128,512]{1,0:T(8,128)(2,1)S(1)}, bf16[128,512]{1,0:T(8,128)(2,1)S(1)}, u32[]{:S(2)}, u32[]{:S(2)}) collective-permute-start(bf16[128,512]{1,0:T(8,128)(2,1)S(1)} %get-tuple-element.45), channel_id=1, source_target_pairs={{0,2},{1,3},{2,0},{3,1},{4,6},{5,7},{6,4},{7,5},{8,10},{9,11},{10,... | collective-permute-start | bytes 393224 | tf_op jit(solution)/shard_map/ppermute | solution.py:332
  109.9 3.9 %collective-permute-start.7 = (bf16[128,512]{1,0:T(8,128)(2,1)S(1)}, bf16[128,512]{1,0:T(8,128)(2,1)S(1)}, u32[]{:S(2)}, u32[]{:S(2)}) collective-permute-start(bf16[128,512]{1,0:T(8,128)(2,1)S(1)} %get-tuple-element.44), channel_id=1, source_target_pairs={{0,1},{1,2},{2,3},{3,0},{4,5},{5,6},{6,7},{7,4},{8,9},{9,10},{10,1... | collective-permute-start | bytes 393224 | tf_op jit(solution)/shard_map/ppermute | solution.py:242
  111.0 7.3 %collective-permute-start.8 = (bf16[128,512]{1,0:T(8,128)(2,1)S(1)}, bf16[128,512]{1,0:T(8,128)(2,1)S(1)}, u32[]{:S(2)}, u32[]{:S(2)}) collective-permute-start(bf16[128,512]{1,0:T(8,128)(2,1)S(1)} %get-tuple-element.43), channel_id=1, source_target_pairs={{0,2},{1,3},{2,0},{3,1},{4,6},{5,7},{6,4},{7,5},{8,10},{9,11},{10,... | collective-permute-start | bytes 393224 | tf_op jit(solution)/shard_map/ppermute | solution.py:242
  112.3 6.6 %collective-permute-start.9 = (bf16[128,512]{1,0:T(8,128)(2,1)S(1)}, bf16[128,512]{1,0:T(8,128)(2,1)S(1)}, u32[]{:S(2)}, u32[]{:S(2)}) collective-permute-start(bf16[128,512]{1,0:T(8,128)(2,1)S(1)} %get-tuple-element.42), channel_id=1, source_target_pairs={{0,3},{1,0},{2,1},{3,2},{4,7},{5,4},{6,5},{7,6},{8,11},{9,8},{10,9... | collective-permute-start | bytes 393224 | tf_op jit(solution)/shard_map/ppermute | solution.py:242
Sparse Core Ops, SparseCore 0:
  11.2 78.6 all-gather.1

commit v18 on v16

--- a/solution.py
+++ b/solution.py
@@ -344,7 +344,18 @@
         * full_attn_gain.astype(jnp.float32)[None, :]
     )
     mixed_state = (row_hidden.astype(jnp.float32) + normed).astype(jnp.bfloat16)
-    gate = jnp.dot(mixed_state, full_gate_weight, preferred_element_type=jnp.float32)
+    gate = jnp.dot(
+        lax.dynamic_slice_in_dim(mixed_state, tp_index * width, width, 1),
+        ple_gate_weight,
+        preferred_element_type=jnp.float32,
+    )
+    for shift in range(1, tp_size):
+        source = (tp_index - shift) % tp_size
+        gate = gate + jnp.dot(
+            lax.dynamic_slice_in_dim(mixed_state, source * width, width, 1),
+            lax.dynamic_slice_in_dim(full_gate_weight, source * width, width, 0),
+            preferred_element_type=jnp.float32,
+        )
     activated = (jax.nn.gelu(gate, approximate=True) * row_ple.astype(jnp.float32)).astype(
         jnp.bfloat16
     )

time: 125 us -> 128 us (1.024)
  the two profiles are of different devices: /device:TPU:1 before, /device:TPU:13 now
where the time goes in v18:
time: 128 us; the launch traced here: 127 us
  waiting for transfers between devices  48.6 us (38%)
  starting transfers between devices  19.3 us (15%)
  Pallas kernels  14.4 us (11%)
  between operations  13.9 us (11%)
  local copies, waits for them, and re-layouts  11.8 us (9%)
  matrix products  11.2 us (9%)
  other arithmetic  7.91 us (6%)
    all_to_all x1, waiting for transfers between devices, shards(): lax.all_to_all(outgoing, 'req', split_axis=0, concat_axis=0, tiled=True)  29.1 us
    pallas_call x1, Pallas kernels, sparse_attention(): pl.pallas_call(functools.partial(attention_kernel, slot_base=slot_base, m...  14.4 us
    all_gather x1, waiting for transfers between devices, shards(): full_weight = lax.all_gather(out_weight, 'tp', axis=0, tiled=True)  11.6 us
    ppermute x3, waiting for transfers between devices, columns_to_rows(): received.append(lax.ppermute(outgoing, axis_name, perm))  6.56 us
    dot_general x3, matrix products, shards(): jnp.dot(piece, lax.dynamic_slice_in_dim(full_weight, source * width, widt...  6.34 us
    all_to_all x1, starting transfers between devices, shards(): lax.all_to_all(outgoing, 'req', split_axis=0, concat_axis=0, tiled=True)  5.71 us
    all_to_all x1, starting transfers between devices, shards(): lax.all_to_all(request_table, 'req', split_axis=0, concat_axis=0, tiled=T...  5.66 us
    ppermute x3, starting transfers between devices, rows_to_columns(): received.append(lax.ppermute(outgoing, axis_name, perm))  4.01 us
  transfers between devices with their start and end apart: 14, of which 6 were waited for; matrix products, arithmetic and copies ran while one was open for 16% of the time, Pallas kernels for 11%

profile of v18, /device:TPU:13, one launch (start us, length us, event | category | flops | bytes accessed | tf_op | source)
XLA Modules:
  0.0 127.0 jit_solution(17160872819927427503)
XLA Ops:
  6.5 1.1 copy.40
  7.7 1.8 %pad_maximum_fusion.1 = bf16[512,512]{0,1:T(8,128)(2,1)} fusion(bf16[512,256]{0,1:T(8,128)(2,1)} %bitcast.95, bf16[512,256]{0,1:T(8,128)(2,1)S(1)} %copy.40), kind=kLoop, calls=%fused_computation.28 | loop fusion | flops 1048576 | bytes 1048576 | tf_op jit(solution)/shard_map/concatenate | solution.py:308
  9.5 0.7 all-gather.3.cloned.1.call-update
  10.2 0.2 convert_reduce_fusion.1
  10.4 0.2 select_reduce_fusion.2
  10.6 0.7 copy.38
  11.3 5.7 %all-to-all-start = ((s32[8,1,6]{2,1,0:T(1,128)}), s32[8,1,6]{2,1,0:T(1,128)S(1)}, u32[]{:S(2)}, u32[]{:S(2)}) async-start(s32[8,1,6]{2,1,0:T(1,128)} %copy.38), calls=%async_computation | async-start | bytes 8192 | tf_op jit(solution)/shard_map/all_to_all | solution.py:283
  17.0 2.7 %dynamic-slice_select_fusion = bf16[48,64,256]{2,1,0:T(8,128)(2,1)S(1)} fusion(bf16[48,64,512]{2,1,0:T(8,128)(2,1)} %param.26, s32[]{:T(128)S(6)} %select_n.257, bf16[48,64,512]{2,1,0:T(8,128)(2,1)} %param.25, pred[]{:T(512)S(6)} %eq.143), kind=kLoop, calls=%fused_computation.12 | loop fusion | flops 786432 | bytes 4718597 | tf_op jit(solution)/shard_map/jit(_where)/select_n | solution.py:290
  19.7 0.5 all-to-all-done
  20.2 0.1 reshape.538
  20.3 1.9 %gather_fusion.1 = bf16[48,64,256]{2,1,0:T(8,128)(2,1)} fusion(bf16[48,64,256]{2,1,0:T(8,128)(2,1)S(1)} %dynamic-slice_select_fusion, s32[1024]{0:T(1024)S(1)} %pad_clamp_fusion), kind=kCustom, calls=%fused_computation.1 | custom fusion | bytes 3145920 | tf_op jit(solution)/shard_map/gather | solution.py:291
  22.2 5.7 %all-to-all-start.1 = ((bf16[8,6,64,256]{3,2,1,0:T(8,128)(2,1)}), bf16[8,6,64,256]{3,2,1,0:T(8,128)(2,1)S(1)}, u32[]{:S(2)}, u32[]{:S(2)}) async-start(bf16[8,6,64,256]{3,2,1,0:T(8,128)(2,1)} %bitcast.20), calls=%async_computation.1 | async-start | bytes 3145728 | tf_op jit(solution)/shard_map/all_to_all | solution.py:292
  28.1 0.1 fusion.13
  28.1 3.5 %collective-permute-start = (bf16[136,512]{1,0:T(8,128)(2,1)S(1)}, bf16[136,512]{1,0:T(8,128)(2,1)S(1)}, u32[]{:S(2)}, u32[]{:S(2)}) collective-permute-start(bf16[136,512]{1,0:T(8,128)(2,1)S(1)} %get-tuple-element.38), channel_id=1, source_target_pairs={{0,1},{1,2},{2,3},{3,0},{4,5},{5,6},{6,7},{7,4},{8,9},{9,10},{10,1... | collective-permute-start | bytes 417800 | tf_op jit(solution)/shard_map/ppermute | solution.py:228
  31.7 0.3 collective-permute-start.1
  31.9 0.2 collective-permute-start.2
  32.2 0.2 reduce-window_clone.1
  32.3 0.1 convert_reduce_fusion.2
  32.4 0.1 slice.54
  32.5 0.1 slice.55
  32.6 0.2 reduce-window_1_clone.1
  32.9 0.1 convert_reduce_fusion
  33.0 0.2 select_reduce_fusion.3
  33.2 29.1 %all-to-all-done.1 = bf16[8,6,64,256]{3,2,1,0:T(8,128)(2,1)S(1)} async-done(((bf16[8,6,64,256]{3,2,1,0:T(8,128)(2,1)}), bf16[8,6,64,256]{3,2,1,0:T(8,128)(2,1)S(1)}, u32[]{:S(2)}, u32[]{:S(2)}) %all-to-all-start.1) | async-done | bytes 1572896 | tf_op jit(solution)/shard_map/all_to_all | solution.py:292
  62.4 0.5 collective-permute-start.3
  62.9 0.1 copy.33
  63.0 0.1 copy.34
  63.1 0.1 copy.35
  63.1 0.1 copy.36
  63.2 0.1 stack.47
  63.3 0.1 reshape.520
  63.4 0.1 select_reduce_fusion.1
  63.6 0.6 pad_add_fusion.2.scalars_ref
  64.3 0.9 copy.39.rown_ref
  65.1 0.6 pad_add_fusion.kinfo_ref
  65.8 0.1 pad_maximum_fusion
  65.8 0.6 gather_fusion
  66.4 0.1 convert_bitcast_fusion
  66.6 0.1 copy.43
  66.7 2.3 %slice.68 = bf16[2048,256]{0,1:T(8,128)(2,1)} slice(bf16[2048,512]{0,1:T(8,128)(2,1)} %all-gather.5.cloned.1.call-done), slice={[0:2048], [0:256]} | slice | bytes 2097152 | tf_op jit(solution)/shard_map/slice | solution.py:310
  69.0 14.4 %shard_map.163 = bf16[512,512]{1,0:T(8,128)(2,1)} custom-call(s32[60]{0:T(128)} %pad_add_fusion.2.scalars_ref, bf16[512,512]{1,0:T(8,128)(2,1)} %q_ref.1, bf16[48,64,256]{2,1,0:T(8,128)(2,1)} %bitcast.88, bf16[48,64,256]{2,1,0:T(8,128)(2,1)} %bitcast.22.partner_ref, bf16[512,512]{1,0:T(8,128)(2,1)} %fresh_k_ref.1, bf16[512,512]{1,0:T(8,128)(2,1)} %fresh_v_ref.1, ...), custom_call_target="tpu_custom_call" | custom-call | tf_op jit(solution)/shard_map/pallas_call | solution.py:187
  83.4 1.1 dynamic-slice_bitcast_fusion.2
  84.5 1.2 collective-permute-start.4
  85.6 0.6 collective-permute-start.5
  86.2 11.6 %all-gather.3.cloned.1.call-done = bf16[2048,2048]{1,0:T(8,128)(2,1)} async-done(((bf16[512,2048]{1,0:T(8,128)(2,1)}), bf16[2048,2048]{1,0:T(8,128)(2,1)}) %all-gather.3.cloned.1.call-update) | async-done | bytes 8388624 | tf_op jit(solution)/shard_map/all_gather | solution.py:306
  97.8 2.1 %fusion.5 = f32[128,2048]{1,0:T(8,128)S(1)} fusion(bf16[2048,2048]{1,0:T(8,128)(2,1)} %all-gather.3.cloned.1.call-done, s32[]{:T(128)S(6)} %select_n.264, bf16[4,128,512]{2,1,0:T(8,128)(2,1)} %bitcast.93, s32[]{:T(128)S(6)} %select_n.236), kind=kOutput, calls=%fused_computation.10 | convolution fusion | flops 268435456 | bytes 3276808 | tf_op jit(solution)/shard_map/dot_general | solution.py:323
  100.0 2.1 %convolution_add_fusion.1 = f32[128,2048]{1,0:T(8,128)S(1)} fusion(f32[128,2048]{1,0:T(8,128)S(1)} %fusion.5, bf16[128,512]{1,0:T(8,128)(2,1)S(1)} %collective-permute-done.4, bf16[2048,2048]{1,0:T(8,128)(2,1)} %all-gather.3.cloned.1.call-done, s32[]{:T(128)S(6)} %select_n.266), kind=kOutput, calls=%fused_computation.5 | convolution fusion | flops 268697600 | bytes 4325380 | tf_op jit(solution)/shard_map/dot_general | solution.py:333
  102.1 2.0 %fusion.1 = f32[128,2048]{1,0:T(8,128)S(1)} fusion(bf16[128,512]{1,0:T(8,128)(2,1)S(1)} %collective-permute-done.6, bf16[2048,2048]{1,0:T(8,128)(2,1)} %all-gather.3.cloned.1.call-done, s32[]{:T(128)S(6)} %select_n.270), kind=kOutput, calls=%fused_computation.6 | convolution fusion | flops 268435456 | bytes 3276804 | tf_op jit(solution)/shard_map/dot_general | solution.py:333
  104.1 2.2 %multiply_reduce_fusion.1 = (f32[128]{0:T(128)S(1)}, f32[128,2048]{1,0:T(8,128)S(1)}) fusion(f32[128,2048]{1,0:T(8,128)S(1)} %fusion.1, f32[128,2048]{1,0:T(8,128)S(1)} %convolution_add_fusion.1, bf16[128,512]{1,0:T(8,128)(2,1)S(1)} %collective-permute-done.5, bf16[2048,2048]{1,0:T(8,128)(2,1)} %all-gather.3.cloned.1.call-done, s32[]{:T(128)S(6)} %select_n.268), kind=kOutput, calls=%fused_computation.26 | convolution fusion | flops 269483904 | bytes 5374468 | tf_op jit(solution)/shard_map/dot_general | solution.py:333
  106.4 0.2 add_convert_fusion.1
  106.6 0.7 copy-done.2
  107.3 0.2 fusion.42
  107.5 0.2 copy-done.1
  107.7 0.2 convolution_add_fusion.4
  107.9 0.2 convolution_add_fusion.3
  108.1 2.1 %multiply_reduce_fusion = (f32[128]{0:T(128)S(1)}, f32[128,2048]{1,0:T(8,128)S(1)}) fusion(bf16[2048,512]{0,1:T(8,128)(2,1)} %all-gather.5.cloned.1.call-done, f32[128,256]{1,0:T(8,128)S(1)} %convolution_add_fusion.3, bf16[2048,256]{0,1:T(8,128)(2,1)} %slice.68, s32[]{:T(128)S(6)} %select_n.270, bf16[128,2048]{1,0:T(8,128)(2,1)S(1)} %add_convert_fusion.1, ...), kind=kOutput, calls=%fused_computation.24 | convolution fusion | flops 168689536 | bytes 2689024 | tf_op jit(solution)/shard_map/dot_general | solution.py:362
  110.2 0.2 add_convert_fusion
  110.5 0.1 collective-permute-start.7
  110.6 1.6 %collective-permute-start.8 = (bf16[128,512]{1,0:T(8,128)(2,1)S(1)}, bf16[128,512]{1,0:T(8,128)(2,1)S(1)}, u32[]{:S(2)}, u32[]{:S(2)}) collective-permute-start(bf16[128,512]{1,0:T(8,128)(2,1)S(1)} %get-tuple-element.43), channel_id=1, source_target_pairs={{0,2},{1,3},{2,0},{3,1},{4,6},{5,7},{6,4},{7,5},{8,10},{9,11},{10,... | collective-permute-start | bytes 393224 | tf_op jit(solution)/shard_map/ppermute | solution.py:242
  112.2 1.1 collective-permute-done.7
  113.3 4.7 %collective-permute-done.8 = bf16[128,512]{1,0:T(8,128)(2,1)S(1)} collective-permute-done((bf16[128,512]{1,0:T(8,128)(2,1)S(1)}, bf16[128,512]{1,0:T(8,128)(2,1)S(1)}, u32[]{:S(2)}, u32[]{:S(2)}) %collective-permute-start.8) | collective-permute-done | bytes 131104 | tf_op jit(solution)/shard_map/ppermute | solution.py:242
  117.9 0.8 collective-permute-done.9
  118.7 0.1 pad_maximum_fusion.2
  118.8 1.4 %gather_fusion.2 = bf16[4,128,512]{2,1,0:T(8,128)(2,1)} fusion(bf16[4,128,512]{2,1,0:T(8,128)(2,1)S(1)} %pad_maximum_fusion.2, s32[1024]{0:T(1024)S(1)} %pad_clamp_fusion.1), kind=kCustom, calls=%fused_computation.2 | custom fusion | bytes 1048592 | tf_op jit(solution)/shard_map/gather | solution.py:244
  (63 shorter events, 0.4 us)
Async XLA Ops:
  6.5 3.7 %copy-start.11 = (s32[48,1]{0,1:T(1,128)S(1)}, s32[48,1]{0,1:T(1,128)}, u32[]{:S(2)}) copy-start(s32[48,1]{0,1:T(1,128)} %param.33) | copy-start | bytes 580
  6.5 3.9 %copy-start.9 = (s32[48,1]{0,1:T(1,128)S(1)}, s32[48,1]{0,1:T(1,128)}, u32[]{:S(2)}) copy-start(s32[48,1]{0,1:T(1,128)} %param.34) | copy-start | bytes 580
  6.5 60.2 %all-gather.5.cloned.1.call-start = ((), (), s32[]{:S(2)}) async-start(), calls=%async_computation.3 | async-start | bytes 2621440 | tf_op jit(solution)/shard_map/all_gather | solution.py:307
  9.5 88.4 %all-gather.3.cloned.1.call-start = ((), (), s32[]{:S(2)}) async-start(), calls=%async_computation.2 | async-start | bytes 10485760 | tf_op jit(solution)/shard_map/all_gather | solution.py:306
  11.3 8.9 %all-to-all-start = ((s32[8,1,6]{2,1,0:T(1,128)}), s32[8,1,6]{2,1,0:T(1,128)S(1)}, u32[]{:S(2)}, u32[]{:S(2)}) async-start(s32[8,1,6]{2,1,0:T(1,128)} %copy.38), calls=%async_computation | async-start | bytes 8192 | tf_op jit(solution)/shard_map/all_to_all | solution.py:283
  22.2 5.8 %copy-start.6 = (bf16[512]{0:T(512)(128)(2,1)S(1)}, bf16[512]{0:T(512)(128)(2,1)}, u32[]{:S(2)}) copy-start(bf16[512]{0:T(512)(128)(2,1)} %param.28) | copy-start | bytes 3076
  22.2 5.8 %copy-start.7 = (bf16[512]{0:T(512)(128)(2,1)S(1)}, bf16[512]{0:T(512)(128)(2,1)}, u32[]{:S(2)}) copy-start(bf16[512]{0:T(512)(128)(2,1)} %param.32) | copy-start | bytes 3076
  22.2 5.9 %copy-start.3 = (bf16[512,512]{1,0:T(8,128)(2,1)S(1)}, bf16[512,512]{1,0:T(8,128)(2,1)}, u32[]{:S(2)}) copy-start(bf16[512,512]{1,0:T(8,128)(2,1)} %param.21) | copy-start | bytes 1572868
  22.2 10.0 %copy-start.10 = (s32[1,8]{1,0:T(1,128)S(1)}, s32[1,8]{1,0:T(1,128)}, u32[]{:S(2)}) copy-start(s32[1,8]{1,0:T(1,128)} %param.37) | copy-start | bytes 100
  22.2 10.4 %copy-start.5 = (s32[1,8]{1,0:T(1,128)S(1)}, s32[1,8]{1,0:T(1,128)}, u32[]{:S(2)}) copy-start(s32[1,8]{1,0:T(1,128)} %param.35) | copy-start | bytes 100
  22.2 10.6 %copy-start.8 = (s32[1,8]{1,0:T(1,128)S(1)}, s32[1,8]{1,0:T(1,128)}, u32[]{:S(2)}) copy-start(s32[1,8]{1,0:T(1,128)} %param.36) | copy-start | bytes 100
  22.2 42.9 %copy-start.4 = (s32[7,1,512]{2,1,0:T(1,128)S(1)}, s32[7,1,512]{2,1,0:T(1,128)}, u32[]{:S(2)}) copy-start(s32[7,1,512]{2,1,0:T(1,128)} %constant.278.clone.1) | copy-start | bytes 43012
  22.2 40.1 %all-to-all-start.1 = ((bf16[8,6,64,256]{3,2,1,0:T(8,128)(2,1)}), bf16[8,6,64,256]{3,2,1,0:T(8,128)(2,1)S(1)}, u32[]{:S(2)}, u32[]{:S(2)}) async-start(bf16[8,6,64,256]{3,2,1,0:T(8,128)(2,1)} %bitcast.20), calls=%async_computation.1 | async-start | bytes 3145728 | tf_op jit(solution)/shard_map/all_to_all | solution.py:292
  28.1 37.6 %collective-permute-start = (bf16[136,512]{1,0:T(8,128)(2,1)S(1)}, bf16[136,512]{1,0:T(8,128)(2,1)S(1)}, u32[]{:S(2)}, u32[]{:S(2)}) collective-permute-start(bf16[136,512]{1,0:T(8,128)(2,1)S(1)} %get-tuple-element.38), channel_id=1, source_target_pairs={{0,1},{1,2},{2,3},{3,0},{4,5},{5,6},{6,7},{7,4},{8,9},{9,10},{10,1... | collective-permute-start | bytes 417800 | tf_op jit(solution)/shard_map/ppermute | solution.py:228
  31.7 34.1 %collective-permute-start.1 = (bf16[136,512]{1,0:T(8,128)(2,1)S(1)}, bf16[136,512]{1,0:T(8,128)(2,1)S(1)}, u32[]{:S(2)}, u32[]{:S(2)}) collective-permute-start(bf16[136,512]{1,0:T(8,128)(2,1)S(1)} %get-tuple-element.39), channel_id=1, source_target_pairs={{0,2},{1,3},{2,0},{3,1},{4,6},{5,7},{6,4},{7,5},{8,10},{9,11},{10,... | collective-permute-start | bytes 417800 | tf_op jit(solution)/shard_map/ppermute | solution.py:228
  31.9 33.8 %collective-permute-start.2 = (bf16[136,512]{1,0:T(8,128)(2,1)S(1)}, bf16[136,512]{1,0:T(8,128)(2,1)S(1)}, u32[]{:S(2)}, u32[]{:S(2)}) collective-permute-start(bf16[136,512]{1,0:T(8,128)(2,1)S(1)} %get-tuple-element.40), channel_id=1, source_target_pairs={{0,3},{1,0},{2,1},{3,2},{4,7},{5,4},{6,5},{7,6},{8,11},{9,8},{10,9... | collective-permute-start | bytes 417800 | tf_op jit(solution)/shard_map/ppermute | solution.py:228
  62.4 4.2 %copy-start = (bf16[8,6,64,256]{3,2,1,0:T(8,128)(2,1)}, bf16[8,6,64,256]{3,2,1,0:T(8,128)(2,1)S(1)}, u32[]{:S(2)}) copy-start(bf16[8,6,64,256]{3,2,1,0:T(8,128)(2,1)S(1)} %all-to-all-done.1) | copy-start | bytes 4718596
  62.4 6.6 %collective-permute-start.3 = (bf16[8,6,64,256]{3,2,1,0:T(8,128)(2,1)S(1)}, bf16[8,6,64,256]{3,2,1,0:T(8,128)(2,1)}, u32[]{:S(2)}, u32[]{:S(2)}) collective-permute-start(bf16[8,6,64,256]{3,2,1,0:T(8,128)(2,1)S(1)} %all-to-all-done.1), channel_id=1, source_target_pairs={{0,1},{1,0},{2,3},{3,2},{4,5},{5,4},{6,7},{7,6},{8,9},{9,8},{10,11... | collective-permute-start | bytes 4718600 | tf_op jit(solution)/shard_map/ppermute | solution.py:293
  84.5 15.5 %collective-permute-start.4 = (bf16[128,512]{1,0:T(8,128)(2,1)S(1)}, bf16[128,512]{1,0:T(8,128)(2,1)S(1)}, u32[]{:S(2)}, u32[]{:S(2)}) collective-permute-start(bf16[128,512]{1,0:T(8,128)(2,1)S(1)} %get-tuple-element.47), channel_id=1, source_target_pairs={{0,1},{1,2},{2,3},{3,0},{4,5},{5,6},{6,7},{7,4},{8,9},{9,10},{10,1... | collective-permute-start | bytes 393224 | tf_op jit(solution)/shard_map/ppermute | solution.py:331
  85.6 16.4 %collective-permute-start.6 = (bf16[128,512]{1,0:T(8,128)(2,1)S(1)}, bf16[128,512]{1,0:T(8,128)(2,1)S(1)}, u32[]{:S(2)}, u32[]{:S(2)}) collective-permute-start(bf16[128,512]{1,0:T(8,128)(2,1)S(1)} %get-tuple-element.46), channel_id=1, source_target_pairs={{0,3},{1,0},{2,1},{3,2},{4,7},{5,4},{6,5},{7,6},{8,11},{9,8},{10,9... | collective-permute-start | bytes 393224 | tf_op jit(solution)/shard_map/ppermute | solution.py:331
  85.6 18.5 %collective-permute-start.5 = (bf16[128,512]{1,0:T(8,128)(2,1)S(1)}, bf16[128,512]{1,0:T(8,128)(2,1)S(1)}, u32[]{:S(2)}, u32[]{:S(2)}) collective-permute-start(bf16[128,512]{1,0:T(8,128)(2,1)S(1)} %get-tuple-element.45), channel_id=1, source_target_pairs={{0,2},{1,3},{2,0},{3,1},{4,6},{5,7},{6,4},{7,5},{8,10},{9,11},{10,... | collective-permute-start | bytes 393224 | tf_op jit(solution)/shard_map/ppermute | solution.py:331
  106.4 1.0 copy-start.2
  106.4 1.3 %copy-start.1 = (bf16[2048,256]{0,1:T(8,128)(2,1)S(1)}, bf16[2048,256]{0,1:T(8,128)(2,1)}, u32[]{:S(2)}) copy-start(bf16[2048,256]{0,1:T(8,128)(2,1)} %slice.68) | copy-start | bytes 3145732
  110.5 2.7 %collective-permute-start.7 = (bf16[128,512]{1,0:T(8,128)(2,1)S(1)}, bf16[128,512]{1,0:T(8,128)(2,1)S(1)}, u32[]{:S(2)}, u32[]{:S(2)}) collective-permute-start(bf16[128,512]{1,0:T(8,128)(2,1)S(1)} %get-tuple-element.44), channel_id=1, source_target_pairs={{0,1},{1,2},{2,3},{3,0},{4,5},{5,6},{6,7},{7,4},{8,9},{9,10},{10,1... | collective-permute-start | bytes 393224 | tf_op jit(solution)/shard_map/ppermute | solution.py:242
  110.6 7.3 %collective-permute-start.8 = (bf16[128,512]{1,0:T(8,128)(2,1)S(1)}, bf16[128,512]{1,0:T(8,128)(2,1)S(1)}, u32[]{:S(2)}, u32[]{:S(2)}) collective-permute-start(bf16[128,512]{1,0:T(8,128)(2,1)S(1)} %get-tuple-element.43), channel_id=1, source_target_pairs={{0,2},{1,3},{2,0},{3,1},{4,6},{5,7},{6,4},{7,5},{8,10},{9,11},{10,... | collective-permute-start | bytes 393224 | tf_op jit(solution)/shard_map/ppermute | solution.py:242
  112.2 6.6 %collective-permute-start.9 = (bf16[128,512]{1,0:T(8,128)(2,1)S(1)}, bf16[128,512]{1,0:T(8,128)(2,1)S(1)}, u32[]{:S(2)}, u32[]{:S(2)}) collective-permute-start(bf16[128,512]{1,0:T(8,128)(2,1)S(1)} %get-tuple-element.42), channel_id=1, source_target_pairs={{0,3},{1,0},{2,1},{3,2},{4,7},{5,4},{6,5},{7,6},{8,11},{9,8},{10,9... | collective-permute-start | bytes 393224 | tf_op jit(solution)/shard_map/ppermute | solution.py:242
Sparse Core Ops, SparseCore 0:
  9.6 24.0 all-gather.4
  35.3 62.5 all-gather.2

commit v19 on v16

--- a/solution.py
+++ b/solution.py
@@ -54,14 +54,15 @@
     partner_ref,
     fresh_k_ref,
     fresh_v_ref,
-    kinfo_ref,
-    rown_ref,
     o_ref,
     s_scr,
     acc_scr,
     *,
     slot_base,
     meta_base,
+    request_base,
+    requests,
+    ctx_total,
 ):
     block = pl.program_id(0)
     ctx_lo = scalars_ref[block * 5]
@@ -75,8 +76,12 @@
     per_chunk = KEY_CHUNK // page_len
     q = q_ref[...]
     stacked = jnp.concatenate([q[:, h * HD:(h + 1) * HD] for h in range(heads)], axis=0)
-    row_owner = rown_ref[...]
     row_index = block * ROW_BLOCK + lax.broadcasted_iota(jnp.int32, (ROW_BLOCK, 1), 0)
+    row_owner = jnp.full((ROW_BLOCK, 1), -1, jnp.int32)
+    for s in range(requests):
+        lo = scalars_ref[request_base + 4 * s + 2]
+        hi = lo + scalars_ref[request_base + 4 * s + 3]
+        row_owner = jnp.where((row_index >= lo) & (row_index < hi), s, row_owner)
     scale = 1.0 / math.sqrt(HD)
 
     def chunk_of(t):
@@ -104,8 +109,19 @@
         s = lax.dot_general(
             stacked, keys, (((1,), (1,)), ((), ())), preferred_element_type=jnp.float32
         ) * scale
-        info = kinfo_ref[c]
-        seen = (info[0:1] == row_owner) & (info[1:2] <= row_index)
+        key_index = c * KEY_CHUNK + lax.broadcasted_iota(jnp.int32, (1, KEY_CHUNK), 1)
+        key_owner = jnp.full((1, KEY_CHUNK), -1, jnp.int32)
+        for r in range(requests):
+            ctx_lo_s = scalars_ref[request_base + 4 * r]
+            ctx_hi_s = ctx_lo_s + scalars_ref[request_base + 4 * r + 1]
+            new_lo_s = ctx_total + scalars_ref[request_base + 4 * r + 2]
+            new_hi_s = new_lo_s + scalars_ref[request_base + 4 * r + 3]
+            inside = ((key_index >= ctx_lo_s) & (key_index < ctx_hi_s)) | (
+                (key_index >= new_lo_s) & (key_index < new_hi_s)
+            )
+            key_owner = jnp.where(inside, r, key_owner)
+        key_pos = jnp.where(key_index >= ctx_total, key_index - ctx_total, -1)
+        seen = (key_owner == row_owner) & (key_pos <= row_index)
         s = jnp.where(seen[None], s.reshape(heads, ROW_BLOCK, KEY_CHUNK), -1e30).reshape(
             heads * ROW_BLOCK, KEY_CHUNK
         )
@@ -178,14 +194,27 @@
     meta = jnp.stack([half, kv_head]).astype(jnp.int32)
     slot_base = ranges.size
     meta_base = slot_base + slots.shape[0]
-    scalars = jnp.concatenate([ranges.reshape(-1), slots.astype(jnp.int32), meta])
+    request_base = meta_base + meta.shape[0]
+    per_request = jnp.stack(
+        [page_starts * page_len, context_len, row_starts, row_counts], axis=1
+    ).astype(jnp.int32)
+    scalars = jnp.concatenate(
+        [ranges.reshape(-1), slots.astype(jnp.int32), meta, per_request.reshape(-1)]
+    )
     key_info = jnp.stack(
         [key_owner.reshape(chunks, KEY_CHUNK), key_pos.reshape(chunks, KEY_CHUNK)], axis=1
     )
     whole = lambda b, s: (0, 0, 0)
     by_head = lambda b, s: (0, s[meta_base + 1])
     return pl.pallas_call(
-        functools.partial(attention_kernel, slot_base=slot_base, meta_base=meta_base),
+        functools.partial(
+            attention_kernel,
+            slot_base=slot_base,
+            meta_base=meta_base,
+            request_base=request_base,
+            requests=row_counts.shape[0],
+            ctx_total=ctx_total,
+        ),
         grid_spec=pltpu.PrefetchScalarGridSpec(
             num_scalar_prefetch=1,
             grid=(blocks,),
@@ -195,8 +224,6 @@
                 pl.BlockSpec(partner_pages.shape, whole),
                 pl.BlockSpec((row_total, HD), by_head),
                 pl.BlockSpec((row_total, HD), by_head),
-                pl.BlockSpec((chunks, 2, KEY_CHUNK), whole),
-                pl.BlockSpec((ROW_BLOCK, 1), lambda b, s: (b, 0)),
             ],
             out_specs=pl.BlockSpec((ROW_BLOCK, heads * HD), lambda b, s: (b, 0)),
             scratch_shapes=[
@@ -212,8 +239,6 @@
         partner_pages,
         new_keys,
         new_values,
-        key_info,
-        row_owner.reshape(row_total, 1),
     )
 
 

time: 125 us -> 125 us (level); the launches traced: 124 us -> 125 us
  waiting for transfers between devices: 48.9 us -> 50.7 us
  Pallas kernels: 14.4 us -> 16.1 us
  other arithmetic: 6.81 us -> 5.32 us
    ppermute x3, waiting for transfers between devices: 3.97 us -> 5.62 us  [shards(): piece = lax.ppermute(outgoing, 'tp', perm)]
    pallas_call x1, Pallas kernels: 14.4 us -> 16.1 us  [sparse_attention(): pl.pallas_call(functools.partial(attention_kernel, slot_base=slot_base, m...]
  transfers between devices with their start and end apart: 14 -> 14, of which waited for: 9 -> 10; matrix products, arithmetic and copies ran while one was open for 17% -> 16% of each run, Pallas kernels for 12% -> 13%
where the time goes in v19:
time: 125 us
  waiting for transfers between devices  50.7 us (41%)
  starting transfers between devices  20.3 us (16%)
  Pallas kernels  16.1 us (13%)
  between operations  13.9 us (11%)
  matrix products  11.1 us (9%)
  local copies, waits for them, and re-layouts  7.56 us (6%)
  other arithmetic  5.32 us (4%)
    all_to_all x1, waiting for transfers between devices, shards(): lax.all_to_all(outgoing, 'req', split_axis=0, concat_axis=0, tiled=True)  29.4 us
    pallas_call x1, Pallas kernels, sparse_attention(): pl.pallas_call(functools.partial(attention_kernel, slot_base=slot_base, m...  16.1 us
    ppermute x3, waiting for transfers between devices, columns_to_rows(): received.append(lax.ppermute(outgoing, axis_name, perm))  6.56 us
    all_to_all x1, starting transfers between devices, shards(): lax.all_to_all(request_table, 'req', split_axis=0, concat_axis=0, tiled=T...  6.38 us
    dot_general x3, matrix products, shards(): jnp.dot(piece, lax.dynamic_slice_in_dim(full_weight, source * width, widt...  6.32 us
    ppermute x3, waiting for transfers between devices, shards(): piece = lax.ppermute(outgoing, 'tp', perm)  5.62 us
    all_gather x1, waiting for transfers between devices, shards(): lax.all_gather(jnp.concatenate([ple_gate_weight, ple_proj_weight.T], axis...  5.32 us
    all_to_all x1, starting transfers between devices, shards(): lax.all_to_all(outgoing, 'req', split_axis=0, concat_axis=0, tiled=True)  3.75 us
  transfers between devices with their start and end apart: 14, of which 10 were waited for; matrix products, arithmetic and copies ran while one was open for 16% of the time, Pallas kernels for 13%

profile of v19, /device:TPU:1, one launch (start us, length us, event | category | flops | bytes accessed | tf_op | source)
XLA Modules:
  0.0 125.0 jit_solution(316898632340452315)
XLA Ops:
  6.5 0.7 all-gather.3.cloned.1.call-update
  7.3 0.2 convert_reduce_fusion
  7.5 0.2 select_reduce_fusion
  7.7 0.7 copy.40
  8.4 6.4 %all-to-all-start = ((s32[8,1,6]{2,1,0:T(1,128)}), s32[8,1,6]{2,1,0:T(1,128)S(1)}, u32[]{:S(2)}, u32[]{:S(2)}) async-start(s32[8,1,6]{2,1,0:T(1,128)} %copy.40), calls=%async_computation | async-start | bytes 8192 | tf_op jit(solution)/shard_map/all_to_all | solution.py:308
  14.7 2.6 %dynamic-slice_select_fusion = bf16[48,64,256]{2,1,0:T(8,128)(2,1)S(1)} fusion(bf16[48,64,512]{2,1,0:T(8,128)(2,1)} %param.26, s32[]{:T(128)S(6)} %select_n.216, bf16[48,64,512]{2,1,0:T(8,128)(2,1)} %param.25, pred[]{:T(512)S(6)} %eq.118), kind=kLoop, calls=%fused_computation.12 | loop fusion | flops 786432 | bytes 4718597 | tf_op jit(solution)/shard_map/jit(_where)/select_n | solution.py:315
  17.3 2.7 %all-to-all-done = s32[8,1,6]{2,1,0:T(1,128)S(1)} async-done(((s32[8,1,6]{2,1,0:T(1,128)}), s32[8,1,6]{2,1,0:T(1,128)S(1)}, u32[]{:S(2)}, u32[]{:S(2)}) %all-to-all-start) | async-done | bytes 224 | tf_op jit(solution)/shard_map/all_to_all | solution.py:308
  20.0 0.1 reshape.576
  20.1 1.9 %gather_fusion.1 = bf16[48,64,256]{2,1,0:T(8,128)(2,1)} fusion(bf16[48,64,256]{2,1,0:T(8,128)(2,1)S(1)} %dynamic-slice_select_fusion, s32[1024]{0:T(1024)S(1)} %pad_clamp_fusion), kind=kCustom, calls=%fused_computation.1 | custom fusion | bytes 3145920 | tf_op jit(solution)/shard_map/gather | solution.py:316
  22.0 0.0 copy-start.3
  22.0 3.7 %all-to-all-start.1 = ((bf16[8,6,64,256]{3,2,1,0:T(8,128)(2,1)}), bf16[8,6,64,256]{3,2,1,0:T(8,128)(2,1)S(1)}, u32[]{:S(2)}, u32[]{:S(2)}) async-start(bf16[8,6,64,256]{3,2,1,0:T(8,128)(2,1)} %bitcast.25), calls=%async_computation.1 | async-start | bytes 3145728 | tf_op jit(solution)/shard_map/all_to_all | solution.py:317
  25.7 0.0 copy-start.5
  25.8 0.0 all-gather.5.cloned.1.call-start
  26.0 0.1 fusion.12
  26.1 3.2 %collective-permute-start = (bf16[136,512]{1,0:T(8,128)(2,1)S(1)}, bf16[136,512]{1,0:T(8,128)(2,1)S(1)}, u32[]{:S(2)}, u32[]{:S(2)}) collective-permute-start(bf16[136,512]{1,0:T(8,128)(2,1)S(1)} %get-tuple-element.36), channel_id=1, source_target_pairs={{0,1},{1,2},{2,3},{3,0},{4,5},{5,6},{6,7},{7,4},{8,9},{9,10},{10,1... | collective-permute-start | bytes 417800 | tf_op jit(solution)/shard_map/ppermute | solution.py:253
  29.3 0.3 collective-permute-start.1
  29.6 0.2 collective-permute-start.2
  29.8 0.1 copy.41
  29.9 0.8 pad_maximum_fusion.1
  30.8 0.0 all-gather.5.cloned.1.call-update
  30.8 0.2 reduce-window.6
  31.0 0.2 reduce-window.9
  31.2 0.1 convert_reduce_fusion.1
  31.3 29.4 %all-to-all-done.1 = bf16[8,6,64,256]{3,2,1,0:T(8,128)(2,1)S(1)} async-done(((bf16[8,6,64,256]{3,2,1,0:T(8,128)(2,1)}), bf16[8,6,64,256]{3,2,1,0:T(8,128)(2,1)S(1)}, u32[]{:S(2)}, u32[]{:S(2)}) %all-to-all-start.1) | async-done | bytes 1572896 | tf_op jit(solution)/shard_map/all_to_all | solution.py:317
  60.7 3.1 %collective-permute-start.3 = (bf16[8,6,64,256]{3,2,1,0:T(8,128)(2,1)S(1)}, bf16[8,6,64,256]{3,2,1,0:T(8,128)(2,1)}, u32[]{:S(2)}, u32[]{:S(2)}) collective-permute-start(bf16[8,6,64,256]{3,2,1,0:T(8,128)(2,1)S(1)} %all-to-all-done.1), channel_id=1, source_target_pairs={{0,1},{1,0},{2,3},{3,2},{4,5},{5,4},{6,7},{7,6},{8,9},{9,8},{10,11... | collective-permute-start | bytes 4718600 | tf_op jit(solution)/shard_map/ppermute | solution.py:318
  63.8 0.1 slice.54
  63.9 0.1 slice.55
  64.0 0.2 select_reduce_fusion.1
  64.4 0.1 copy.34
  64.5 0.1 copy.35
  64.5 0.1 copy.36
  64.6 0.1 copy.37
  64.7 0.1 stack.50
  64.8 0.1 reshape.557
  64.9 0.1 copy.38
  65.0 0.1 reshape.558
  65.1 0.6 concatenate.14.scalars_ref
  65.7 0.1 pad_maximum_fusion
  65.8 0.6 gather_fusion
  66.4 0.1 convert_bitcast_fusion
  66.5 0.1 copy.44
  66.6 0.3 collective-permute-done.3
  67.0 16.1 %shard_map.163 = bf16[512,512]{1,0:T(8,128)(2,1)} custom-call(s32[92]{0:T(128)} %concatenate.14.scalars_ref, bf16[512,512]{1,0:T(8,128)(2,1)} %q_ref.1, bf16[48,64,256]{2,1,0:T(8,128)(2,1)} %bitcast.100, bf16[48,64,256]{2,1,0:T(8,128)(2,1)} %bitcast.27.partner_ref, bf16[512,512]{1,0:T(8,128)(2,1)} %fresh_k_ref.1, bf16[512,512]{1,0:T(8,128)(2,1)} %fresh_v_ref.1), custom_call_target="tpu_custom_call" | custom-call | tf_op jit(solution)/shard_map/pallas_call | solution.py:209
  83.0 1.1 dynamic-slice_bitcast_fusion.2
  84.1 1.5 %collective-permute-start.4 = (bf16[128,512]{1,0:T(8,128)(2,1)S(1)}, bf16[128,512]{1,0:T(8,128)(2,1)S(1)}, u32[]{:S(2)}, u32[]{:S(2)}) collective-permute-start(bf16[128,512]{1,0:T(8,128)(2,1)S(1)} %get-tuple-element.45), channel_id=1, source_target_pairs={{0,1},{1,2},{2,3},{3,0},{4,5},{5,6},{6,7},{7,4},{8,9},{9,10},{10,1... | collective-permute-start | bytes 393224 | tf_op jit(solution)/shard_map/ppermute | solution.py:356
  85.6 0.3 collective-permute-start.5
  85.9 2.1 %fusion.5 = f32[128,2048]{1,0:T(8,128)S(1)} fusion(bf16[2048,2048]{1,0:T(8,128)(2,1)} %all-gather.3.cloned.1.call-done, s32[]{:T(128)S(6)} %select_n.218, bf16[4,128,512]{2,1,0:T(8,128)(2,1)} %bitcast.105, s32[]{:T(128)S(6)} %select_n.195), kind=kOutput, calls=%fused_computation.10 | convolution fusion | flops 268435456 | bytes 3276808 | tf_op jit(solution)/shard_map/dot_general | solution.py:348
  88.0 3.2 %collective-permute-done.4 = bf16[128,512]{1,0:T(8,128)(2,1)S(1)} collective-permute-done((bf16[128,512]{1,0:T(8,128)(2,1)S(1)}, bf16[128,512]{1,0:T(8,128)(2,1)S(1)}, u32[]{:S(2)}, u32[]{:S(2)}) %collective-permute-start.4) | collective-permute-done | bytes 131104 | tf_op jit(solution)/shard_map/ppermute | solution.py:356
  91.2 2.0 %convolution_add_fusion.1 = f32[128,2048]{1,0:T(8,128)S(1)} fusion(f32[128,2048]{1,0:T(8,128)S(1)} %fusion.5, bf16[128,512]{1,0:T(8,128)(2,1)S(1)} %collective-permute-done.4, bf16[2048,2048]{1,0:T(8,128)(2,1)} %all-gather.3.cloned.1.call-done, s32[]{:T(128)S(6)} %select_n.220), kind=kOutput, calls=%fused_computation.5 | convolution fusion | flops 268697600 | bytes 4325380 | tf_op jit(solution)/shard_map/dot_general | solution.py:358
  93.2 1.3 %collective-permute-done.6 = bf16[128,512]{1,0:T(8,128)(2,1)S(1)} collective-permute-done((bf16[128,512]{1,0:T(8,128)(2,1)S(1)}, bf16[128,512]{1,0:T(8,128)(2,1)S(1)}, u32[]{:S(2)}, u32[]{:S(2)}) %collective-permute-start.6) | collective-permute-done | bytes 131104 | tf_op jit(solution)/shard_map/ppermute | solution.py:356
  94.5 2.0 %fusion.1 = f32[128,2048]{1,0:T(8,128)S(1)} fusion(bf16[128,512]{1,0:T(8,128)(2,1)S(1)} %collective-permute-done.6, bf16[2048,2048]{1,0:T(8,128)(2,1)} %all-gather.3.cloned.1.call-done, s32[]{:T(128)S(6)} %select_n.224), kind=kOutput, calls=%fused_computation.6 | convolution fusion | flops 268435456 | bytes 3276804 | tf_op jit(solution)/shard_map/dot_general | solution.py:358
  96.6 1.2 collective-permute-done.5
  97.7 2.2 %multiply_reduce_fusion.1 = (f32[128]{0:T(128)S(1)}, f32[128,2048]{1,0:T(8,128)S(1)}) fusion(f32[128,2048]{1,0:T(8,128)S(1)} %fusion.1, f32[128,2048]{1,0:T(8,128)S(1)} %convolution_add_fusion.1, bf16[128,512]{1,0:T(8,128)(2,1)S(1)} %collective-permute-done.5, bf16[2048,2048]{1,0:T(8,128)(2,1)} %all-gather.3.cloned.1.call-done, s32[]{:T(128)S(6)} %select_n.222), kind=kOutput, calls=%fused_computation.25 | convolution fusion | flops 269483904 | bytes 5374468 | tf_op jit(solution)/shard_map/dot_general | solution.py:358
  100.0 0.2 add_convert_fusion.1
  100.2 5.3 %all-gather.5.cloned.1.call-done = bf16[2048,512]{0,1:T(8,128)(2,1)} async-done(((bf16[512,512]{0,1:T(8,128)(2,1)}), bf16[2048,512]{0,1:T(8,128)(2,1)}) %all-gather.5.cloned.1.call-update) | async-done | bytes 2097168 | tf_op jit(solution)/shard_map/all_gather | solution.py:332
  105.5 2.6 %multiply_reduce_fusion = (f32[128]{0:T(128)S(1)}, f32[128,2048]{1,0:T(8,128)S(1)}) fusion(bf16[2048,512]{0,1:T(8,128)(2,1)} %all-gather.5.cloned.1.call-done, bf16[128,2048]{1,0:T(8,128)(2,1)S(1)} %add_convert_fusion.1, bf16[512,256]{1,0:T(8,128)(2,1)} %param.29, s32[]{:T(128)S(6)} %select_n.225), kind=kOutput, calls=%fused_computation.23 | convolution fusion | flops 269320064 | bytes 3736068 | tf_op jit(solution)/shard_map/dot_general | solution.py:376
  108.1 0.2 add_convert_fusion
  108.4 0.2 collective-permute-start.7
  108.7 1.4 %collective-permute-start.8 = (bf16[128,512]{1,0:T(8,128)(2,1)S(1)}, bf16[128,512]{1,0:T(8,128)(2,1)S(1)}, u32[]{:S(2)}, u32[]{:S(2)}) collective-permute-start(bf16[128,512]{1,0:T(8,128)(2,1)S(1)} %get-tuple-element.41), channel_id=1, source_target_pairs={{0,2},{1,3},{2,0},{3,1},{4,6},{5,7},{6,4},{7,5},{8,10},{9,11},{10,... | collective-permute-start | bytes 393224 | tf_op jit(solution)/shard_map/ppermute | solution.py:267
  110.1 1.1 collective-permute-done.7
  111.2 4.7 %collective-permute-done.8 = bf16[128,512]{1,0:T(8,128)(2,1)S(1)} collective-permute-done((bf16[128,512]{1,0:T(8,128)(2,1)S(1)}, bf16[128,512]{1,0:T(8,128)(2,1)S(1)}, u32[]{:S(2)}, u32[]{:S(2)}) %collective-permute-start.8) | collective-permute-done | bytes 131104 | tf_op jit(solution)/shard_map/ppermute | solution.py:267
  115.9 0.8 collective-permute-done.9
  116.7 0.1 pad_maximum_fusion.2
  116.7 1.4 %gather_fusion.2 = bf16[4,128,512]{2,1,0:T(8,128)(2,1)} fusion(bf16[4,128,512]{2,1,0:T(8,128)(2,1)S(1)} %pad_maximum_fusion.2, s32[1024]{0:T(1024)S(1)} %pad_clamp_fusion.1), kind=kCustom, calls=%fused_computation.2 | custom fusion | bytes 1048592 | tf_op jit(solution)/shard_map/gather | solution.py:269
  (52 shorter events, 0.3 us)
Async XLA Ops:
  6.5 0.7 copy-start.10
  6.5 0.9 copy-start.9
  6.5 79.3 %all-gather.3.cloned.1.call-start = ((), (), s32[]{:S(2)}) async-start(), calls=%async_computation.2 | async-start | bytes 10485760 | tf_op jit(solution)/shard_map/all_gather | solution.py:331
  8.4 11.6 %all-to-all-start = ((s32[8,1,6]{2,1,0:T(1,128)}), s32[8,1,6]{2,1,0:T(1,128)S(1)}, u32[]{:S(2)}, u32[]{:S(2)}) async-start(s32[8,1,6]{2,1,0:T(1,128)} %copy.40), calls=%async_computation | async-start | bytes 8192 | tf_op jit(solution)/shard_map/all_to_all | solution.py:308
  22.0 3.9 %copy-start.6 = (bf16[512]{0:T(512)(128)(2,1)S(1)}, bf16[512]{0:T(512)(128)(2,1)}, u32[]{:S(2)}) copy-start(bf16[512]{0:T(512)(128)(2,1)} %param.28) | copy-start | bytes 3076
  22.0 3.9 %copy-start.7 = (bf16[512]{0:T(512)(128)(2,1)S(1)}, bf16[512]{0:T(512)(128)(2,1)}, u32[]{:S(2)}) copy-start(bf16[512]{0:T(512)(128)(2,1)} %param.32) | copy-start | bytes 3076
  22.0 4.0 %copy-start.1 = (bf16[512,512]{1,0:T(8,128)(2,1)S(1)}, bf16[512,512]{1,0:T(8,128)(2,1)}, u32[]{:S(2)}) copy-start(bf16[512,512]{1,0:T(8,128)(2,1)} %param.21) | copy-start | bytes 1572868
  22.0 7.8 %copy-start.2 = (bf16[512,256]{1,0:T(8,128)(2,1)S(1)}, bf16[512,256]{1,0:T(8,128)(2,1)}, u32[]{:S(2)}) copy-start(bf16[512,256]{1,0:T(8,128)(2,1)} %param.30) | copy-start | bytes 786436
  22.0 8.0 %copy-start.3 = (bf16[256,512]{1,0:T(8,128)(2,1)S(1)}, bf16[256,512]{1,0:T(8,128)(2,1)}, u32[]{:S(2)}) copy-start(bf16[256,512]{1,0:T(8,128)(2,1)} %param.31) | copy-start | bytes 786436
  22.0 38.7 %all-to-all-start.1 = ((bf16[8,6,64,256]{3,2,1,0:T(8,128)(2,1)}), bf16[8,6,64,256]{3,2,1,0:T(8,128)(2,1)S(1)}, u32[]{:S(2)}, u32[]{:S(2)}) async-start(bf16[8,6,64,256]{3,2,1,0:T(8,128)(2,1)} %bitcast.25), calls=%async_computation.1 | async-start | bytes 3145728 | tf_op jit(solution)/shard_map/all_to_all | solution.py:317
  25.7 5.1 %copy-start.5 = (s32[1,8]{1,0:T(1,128)S(1)}, s32[1,8]{1,0:T(1,128)}, u32[]{:S(2)}) copy-start(s32[1,8]{1,0:T(1,128)} %param.37) | copy-start | bytes 100
  25.7 5.2 %copy-start.4 = (s32[1,8]{1,0:T(1,128)S(1)}, s32[1,8]{1,0:T(1,128)}, u32[]{:S(2)}) copy-start(s32[1,8]{1,0:T(1,128)} %param.35) | copy-start | bytes 100
  25.8 5.5 %copy-start.8 = (s32[1,8]{1,0:T(1,128)S(1)}, s32[1,8]{1,0:T(1,128)}, u32[]{:S(2)}) copy-start(s32[1,8]{1,0:T(1,128)} %param.36) | copy-start | bytes 100
  25.8 79.7 %all-gather.5.cloned.1.call-start = ((), (), s32[]{:S(2)}) async-start(), calls=%async_computation.3 | async-start | bytes 2621440 | tf_op jit(solution)/shard_map/all_gather | solution.py:332
  26.1 39.6 %collective-permute-start = (bf16[136,512]{1,0:T(8,128)(2,1)S(1)}, bf16[136,512]{1,0:T(8,128)(2,1)S(1)}, u32[]{:S(2)}, u32[]{:S(2)}) collective-permute-start(bf16[136,512]{1,0:T(8,128)(2,1)S(1)} %get-tuple-element.36), channel_id=1, source_target_pairs={{0,1},{1,2},{2,3},{3,0},{4,5},{5,6},{6,7},{7,4},{8,9},{9,10},{10,1... | collective-permute-start | bytes 417800 | tf_op jit(solution)/shard_map/ppermute | solution.py:253
  29.3 36.4 %collective-permute-start.1 = (bf16[136,512]{1,0:T(8,128)(2,1)S(1)}, bf16[136,512]{1,0:T(8,128)(2,1)S(1)}, u32[]{:S(2)}, u32[]{:S(2)}) collective-permute-start(bf16[136,512]{1,0:T(8,128)(2,1)S(1)} %get-tuple-element.37), channel_id=1, source_target_pairs={{0,2},{1,3},{2,0},{3,1},{4,6},{5,7},{6,4},{7,5},{8,10},{9,11},{10,... | collective-permute-start | bytes 417800 | tf_op jit(solution)/shard_map/ppermute | solution.py:253
  29.6 36.2 %collective-permute-start.2 = (bf16[136,512]{1,0:T(8,128)(2,1)S(1)}, bf16[136,512]{1,0:T(8,128)(2,1)S(1)}, u32[]{:S(2)}, u32[]{:S(2)}) collective-permute-start(bf16[136,512]{1,0:T(8,128)(2,1)S(1)} %get-tuple-element.38), channel_id=1, source_target_pairs={{0,3},{1,0},{2,1},{3,2},{4,7},{5,4},{6,5},{7,6},{8,11},{9,8},{10,9... | collective-permute-start | bytes 417800 | tf_op jit(solution)/shard_map/ppermute | solution.py:253
  60.7 5.9 %copy-start = (bf16[8,6,64,256]{3,2,1,0:T(8,128)(2,1)}, bf16[8,6,64,256]{3,2,1,0:T(8,128)(2,1)S(1)}, u32[]{:S(2)}) copy-start(bf16[8,6,64,256]{3,2,1,0:T(8,128)(2,1)S(1)} %all-to-all-done.1) | copy-start | bytes 4718596
  60.7 6.2 %collective-permute-start.3 = (bf16[8,6,64,256]{3,2,1,0:T(8,128)(2,1)S(1)}, bf16[8,6,64,256]{3,2,1,0:T(8,128)(2,1)}, u32[]{:S(2)}, u32[]{:S(2)}) collective-permute-start(bf16[8,6,64,256]{3,2,1,0:T(8,128)(2,1)S(1)} %all-to-all-done.1), channel_id=1, source_target_pairs={{0,1},{1,0},{2,3},{3,2},{4,5},{5,4},{6,7},{7,6},{8,9},{9,8},{10,11... | collective-permute-start | bytes 4718600 | tf_op jit(solution)/shard_map/ppermute | solution.py:318
  84.1 7.1 %collective-permute-start.4 = (bf16[128,512]{1,0:T(8,128)(2,1)S(1)}, bf16[128,512]{1,0:T(8,128)(2,1)S(1)}, u32[]{:S(2)}, u32[]{:S(2)}) collective-permute-start(bf16[128,512]{1,0:T(8,128)(2,1)S(1)} %get-tuple-element.45), channel_id=1, source_target_pairs={{0,1},{1,2},{2,3},{3,0},{4,5},{5,6},{6,7},{7,4},{8,9},{9,10},{10,1... | collective-permute-start | bytes 393224 | tf_op jit(solution)/shard_map/ppermute | solution.py:356
  85.6 8.9 %collective-permute-start.6 = (bf16[128,512]{1,0:T(8,128)(2,1)S(1)}, bf16[128,512]{1,0:T(8,128)(2,1)S(1)}, u32[]{:S(2)}, u32[]{:S(2)}) collective-permute-start(bf16[128,512]{1,0:T(8,128)(2,1)S(1)} %get-tuple-element.44), channel_id=1, source_target_pairs={{0,3},{1,0},{2,1},{3,2},{4,7},{5,4},{6,5},{7,6},{8,11},{9,8},{10,9... | collective-permute-start | bytes 393224 | tf_op jit(solution)/shard_map/ppermute | solution.py:356
  85.6 12.1 %collective-permute-start.5 = (bf16[128,512]{1,0:T(8,128)(2,1)S(1)}, bf16[128,512]{1,0:T(8,128)(2,1)S(1)}, u32[]{:S(2)}, u32[]{:S(2)}) collective-permute-start(bf16[128,512]{1,0:T(8,128)(2,1)S(1)} %get-tuple-element.43), channel_id=1, source_target_pairs={{0,2},{1,3},{2,0},{3,1},{4,6},{5,7},{6,4},{7,5},{8,10},{9,11},{10,... | collective-permute-start | bytes 393224 | tf_op jit(solution)/shard_map/ppermute | solution.py:356
  108.4 2.8 %collective-permute-start.7 = (bf16[128,512]{1,0:T(8,128)(2,1)S(1)}, bf16[128,512]{1,0:T(8,128)(2,1)S(1)}, u32[]{:S(2)}, u32[]{:S(2)}) collective-permute-start(bf16[128,512]{1,0:T(8,128)(2,1)S(1)} %get-tuple-element.42), channel_id=1, source_target_pairs={{0,1},{1,2},{2,3},{3,0},{4,5},{5,6},{6,7},{7,4},{8,9},{9,10},{10,1... | collective-permute-start | bytes 393224 | tf_op jit(solution)/shard_map/ppermute | solution.py:267
  108.7 7.2 %collective-permute-start.8 = (bf16[128,512]{1,0:T(8,128)(2,1)S(1)}, bf16[128,512]{1,0:T(8,128)(2,1)S(1)}, u32[]{:S(2)}, u32[]{:S(2)}) collective-permute-start(bf16[128,512]{1,0:T(8,128)(2,1)S(1)} %get-tuple-element.41), channel_id=1, source_target_pairs={{0,2},{1,3},{2,0},{3,1},{4,6},{5,7},{6,4},{7,5},{8,10},{9,11},{10,... | collective-permute-start | bytes 393224 | tf_op jit(solution)/shard_map/ppermute | solution.py:267
  110.1 6.6 %collective-permute-start.9 = (bf16[128,512]{1,0:T(8,128)(2,1)S(1)}, bf16[128,512]{1,0:T(8,128)(2,1)S(1)}, u32[]{:S(2)}, u32[]{:S(2)}) collective-permute-start(bf16[128,512]{1,0:T(8,128)(2,1)S(1)} %get-tuple-element.40), channel_id=1, source_target_pairs={{0,3},{1,0},{2,1},{3,2},{4,7},{5,4},{6,5},{7,6},{8,11},{9,8},{10,9... | collective-permute-start | bytes 393224 | tf_op jit(solution)/shard_map/ppermute | solution.py:267
Sparse Core Ops, SparseCore 0:
  8.9 66.7 all-gather.2
  77.3 28.1 all-gather.4

commit v20 on v16

--- a/solution.py
+++ b/solution.py
@@ -320,11 +320,7 @@
     full_ple_gain = row_hidden_gains[hidden_parts.shape[1] + 1]
     parts = attention.reshape(tp_size, -1, attention.shape[1])
     width = attention.shape[1]
-    projected = jnp.dot(
-        parts[tp_index],
-        lax.dynamic_slice_in_dim(full_weight, tp_index * width, width, 0),
-        preferred_element_type=jnp.float32,
-    )
+    projected = jnp.dot(parts[tp_index], out_weight, preferred_element_type=jnp.float32)
     for shift in range(1, tp_size):
         outgoing = lax.dynamic_index_in_dim(parts, (tp_index + shift) % tp_size, 0, keepdims=False)
         perm = [(i, (i + shift) % tp_size) for i in range(tp_size)]

time: 125 us -> 126 us (level)
  local copies, waits for them, and re-layouts: 7.63 us -> 9.42 us
  Pallas kernels: 14.4 us -> 15.7 us
  waiting for transfers between devices: 48.9 us -> 47.6 us
    all_gather x1, waiting for transfers between devices: 6.53 us -> 2.51 us  [shards(): lax.all_gather(jnp.concatenate([ple_gate_weight, ple_proj_weight.T], axis...]
    ppermute x3, waiting for transfers between devices: 3.97 us -> 6.32 us  [shards(): piece = lax.ppermute(outgoing, 'tp', perm)]
    pallas_call x1, Pallas kernels: 14.4 us -> 15.7 us  [sparse_attention(): pl.pallas_call(functools.partial(attention_kernel, slot_base=slot_base, m...]
  transfers between devices with their start and end apart: 14 -> 14, of which waited for: 9 -> 8; matrix products, arithmetic and copies ran while one was open for 17% -> 18% of each run, Pallas kernels for 12% -> 13%
where the time goes in v20:
time: 126 us; the launch traced here: 125 us
  waiting for transfers between devices  47.6 us (38%)
  starting transfers between devices  20.5 us (16%)
  Pallas kernels  15.7 us (12%)
  between operations  13.9 us (11%)
  matrix products  10.4 us (8%)
  local copies, waits for them, and re-layouts  9.42 us (7%)
  other arithmetic  7.59 us (6%)
    all_to_all x1, waiting for transfers between devices, shards(): lax.all_to_all(outgoing, 'req', split_axis=0, concat_axis=0, tiled=True)  28.8 us
    pallas_call x1, Pallas kernels, sparse_attention(): pl.pallas_call(functools.partial(attention_kernel, slot_base=slot_base, m...  15.7 us
    ppermute x3, waiting for transfers between devices, columns_to_rows(): received.append(lax.ppermute(outgoing, axis_name, perm))  6.56 us
    all_to_all x1, starting transfers between devices, shards(): lax.all_to_all(request_table, 'req', split_axis=0, concat_axis=0, tiled=T...  6.38 us
    dot_general x3, matrix products, shards(): jnp.dot(piece, lax.dynamic_slice_in_dim(full_weight, source * width, widt...  6.38 us
    ppermute x3, waiting for transfers between devices, shards(): piece = lax.ppermute(outgoing, 'tp', perm)  6.32 us
    all_to_all x1, starting transfers between devices, shards(): lax.all_to_all(outgoing, 'req', split_axis=0, concat_axis=0, tiled=True)  3.75 us
    ppermute x3, starting transfers between devices, rows_to_columns(): received.append(lax.ppermute(outgoing, axis_name, perm))  3.7 us
  transfers between devices with their start and end apart: 14, of which 8 were waited for; matrix products, arithmetic and copies ran while one was open for 18% of the time, Pallas kernels for 13%

profile of v20, /device:TPU:1, one launch (start us, length us, event | category | flops | bytes accessed | tf_op | source)
XLA Modules:
  0.0 125.1 jit_solution(4421147462392002924)
XLA Ops:
  6.5 0.7 all-gather.3.cloned.1.call-update
  7.3 0.2 convert_reduce_fusion.1
  7.5 0.2 select_reduce_fusion.2
  7.7 0.7 copy.38
  8.4 6.4 %all-to-all-start = ((s32[8,1,6]{2,1,0:T(1,128)}), s32[8,1,6]{2,1,0:T(1,128)S(1)}, u32[]{:S(2)}, u32[]{:S(2)}) async-start(s32[8,1,6]{2,1,0:T(1,128)} %copy.38), calls=%async_computation | async-start | bytes 8192 | tf_op jit(solution)/shard_map/all_to_all | solution.py:283
  14.7 2.5 %dynamic-slice_select_fusion = bf16[48,64,256]{2,1,0:T(8,128)(2,1)S(1)} fusion(bf16[48,64,512]{2,1,0:T(8,128)(2,1)} %param.26, s32[]{:T(128)S(6)} %select_n.243, bf16[48,64,512]{2,1,0:T(8,128)(2,1)} %param.25, pred[]{:T(512)S(6)} %eq.140), kind=kLoop, calls=%fused_computation.10 | loop fusion | flops 786432 | bytes 4718597 | tf_op jit(solution)/shard_map/jit(_where)/select_n | solution.py:290
  17.2 2.8 %all-to-all-done = s32[8,1,6]{2,1,0:T(1,128)S(1)} async-done(((s32[8,1,6]{2,1,0:T(1,128)}), s32[8,1,6]{2,1,0:T(1,128)S(1)}, u32[]{:S(2)}, u32[]{:S(2)}) %all-to-all-start) | async-done | bytes 224 | tf_op jit(solution)/shard_map/all_to_all | solution.py:283
  20.0 0.1 reshape.538
  20.1 1.9 %gather_fusion.1 = bf16[48,64,256]{2,1,0:T(8,128)(2,1)} fusion(bf16[48,64,256]{2,1,0:T(8,128)(2,1)S(1)} %dynamic-slice_select_fusion, s32[1024]{0:T(1024)S(1)} %pad_clamp_fusion), kind=kCustom, calls=%fused_computation.1 | custom fusion | bytes 3145920 | tf_op jit(solution)/shard_map/gather | solution.py:291
  22.0 3.7 %all-to-all-start.1 = ((bf16[8,6,64,256]{3,2,1,0:T(8,128)(2,1)}), bf16[8,6,64,256]{3,2,1,0:T(8,128)(2,1)S(1)}, u32[]{:S(2)}, u32[]{:S(2)}) async-start(bf16[8,6,64,256]{3,2,1,0:T(8,128)(2,1)} %bitcast.20), calls=%async_computation.1 | async-start | bytes 3145728 | tf_op jit(solution)/shard_map/all_to_all | solution.py:292
  25.8 0.0 all-gather.5.cloned.1.call-start
  26.0 0.1 fusion.10
  26.1 3.2 %collective-permute-start = (bf16[136,512]{1,0:T(8,128)(2,1)S(1)}, bf16[136,512]{1,0:T(8,128)(2,1)S(1)}, u32[]{:S(2)}, u32[]{:S(2)}) collective-permute-start(bf16[136,512]{1,0:T(8,128)(2,1)S(1)} %get-tuple-element.38), channel_id=1, source_target_pairs={{0,1},{1,2},{2,3},{3,0},{4,5},{5,6},{6,7},{7,4},{8,9},{9,10},{10,1... | collective-permute-start | bytes 417800 | tf_op jit(solution)/shard_map/ppermute | solution.py:228
  29.3 0.3 collective-permute-start.1
  29.6 0.2 collective-permute-start.2
  29.8 0.1 copy.40
  29.9 0.8 pad_maximum_fusion.1
  30.8 0.0 all-gather.5.cloned.1.call-update
  30.8 0.2 reduce-window_clone.1
  31.0 0.1 convert_reduce_fusion.2
  31.1 0.1 slice.54
  31.2 0.1 slice.55
  31.3 0.2 reduce-window_1_clone.1
  31.5 0.1 convert_reduce_fusion
  31.6 0.2 select_reduce_fusion.3
  31.8 0.1 select_reduce_fusion.1
  32.0 28.8 %all-to-all-done.1 = bf16[8,6,64,256]{3,2,1,0:T(8,128)(2,1)S(1)} async-done(((bf16[8,6,64,256]{3,2,1,0:T(8,128)(2,1)}), bf16[8,6,64,256]{3,2,1,0:T(8,128)(2,1)S(1)}, u32[]{:S(2)}, u32[]{:S(2)}) %all-to-all-start.1) | async-done | bytes 1572896 | tf_op jit(solution)/shard_map/all_to_all | solution.py:292
  60.7 3.1 %collective-permute-start.3 = (bf16[8,6,64,256]{3,2,1,0:T(8,128)(2,1)S(1)}, bf16[8,6,64,256]{3,2,1,0:T(8,128)(2,1)}, u32[]{:S(2)}, u32[]{:S(2)}) collective-permute-start(bf16[8,6,64,256]{3,2,1,0:T(8,128)(2,1)S(1)} %all-to-all-done.1), channel_id=1, source_target_pairs={{0,1},{1,0},{2,3},{3,2},{4,5},{5,4},{6,7},{7,6},{8,9},{9,8},{10,11... | collective-permute-start | bytes 4718600 | tf_op jit(solution)/shard_map/ppermute | solution.py:293
  63.8 0.1 copy.33
  63.9 0.1 copy.34
  64.0 0.1 copy.35
  64.1 0.1 copy.36
  64.2 0.1 stack.47
  64.3 0.1 reshape.520
  64.4 0.6 pad_add_fusion.2.scalars_ref
  65.0 0.9 copy.39.rown_ref
  65.9 0.6 pad_add_fusion.kinfo_ref
  66.6 0.6 copy-done.6
  67.2 1.0 pad_maximum_fusion
  68.2 0.6 gather_fusion
  68.8 0.1 convert_bitcast_fusion
  68.9 1.1 copy.43
  70.0 15.7 %shard_map.163 = bf16[512,512]{1,0:T(8,128)(2,1)} custom-call(s32[60]{0:T(128)} %pad_add_fusion.2.scalars_ref, bf16[512,512]{1,0:T(8,128)(2,1)} %q_ref.1, bf16[48,64,256]{2,1,0:T(8,128)(2,1)} %bitcast.89, bf16[48,64,256]{2,1,0:T(8,128)(2,1)} %bitcast.22.partner_ref, bf16[512,512]{1,0:T(8,128)(2,1)} %fresh_k_ref.1, bf16[512,512]{1,0:T(8,128)(2,1)} %fresh_v_ref.1, ...), custom_call_target="tpu_custom_call" | custom-call | tf_op jit(solution)/shard_map/pallas_call | solution.py:187
  85.8 1.1 dynamic-slice_bitcast_fusion.2
  86.8 1.2 collective-permute-start.4
  88.0 1.3 %fusion.33 = f32[128,2048]{1,0:T(8,128)S(1)} fusion(bf16[512,2048]{1,0:T(8,128)(2,1)S(1)} %copy-done, bf16[4,128,512]{2,1,0:T(8,128)(2,1)} %bitcast.94, s32[]{:T(128)S(6)} %select_n.222), kind=kOutput, calls=%fused_computation.48 | convolution fusion | flops 268435456 | bytes 3276804 | tf_op jit(solution)/shard_map/dot_general | solution.py:323
  89.4 0.1 collective-permute-start.6
  89.4 0.6 collective-permute-start.5
  90.0 3.4 %collective-permute-done.4 = bf16[128,512]{1,0:T(8,128)(2,1)S(1)} collective-permute-done((bf16[128,512]{1,0:T(8,128)(2,1)S(1)}, bf16[128,512]{1,0:T(8,128)(2,1)S(1)}, u32[]{:S(2)}, u32[]{:S(2)}) %collective-permute-start.4) | collective-permute-done | bytes 131104 | tf_op jit(solution)/shard_map/ppermute | solution.py:327
  93.4 2.0 %convolution_add_fusion.1 = f32[128,2048]{1,0:T(8,128)S(1)} fusion(f32[128,2048]{1,0:T(8,128)S(1)} %fusion.33, bf16[128,512]{1,0:T(8,128)(2,1)S(1)} %collective-permute-done.4, bf16[2048,2048]{1,0:T(8,128)(2,1)} %all-gather.3.cloned.1.call-done, s32[]{:T(128)S(6)} %select_n.251), kind=kOutput, calls=%fused_computation.5 | convolution fusion | flops 268697600 | bytes 4325380 | tf_op jit(solution)/shard_map/dot_general | solution.py:329
  95.4 3.0 %collective-permute-done.6 = bf16[128,512]{1,0:T(8,128)(2,1)S(1)} collective-permute-done((bf16[128,512]{1,0:T(8,128)(2,1)S(1)}, bf16[128,512]{1,0:T(8,128)(2,1)S(1)}, u32[]{:S(2)}, u32[]{:S(2)}) %collective-permute-start.6) | collective-permute-done | bytes 131104 | tf_op jit(solution)/shard_map/ppermute | solution.py:327
  98.4 2.0 %fusion.1 = f32[128,2048]{1,0:T(8,128)S(1)} fusion(bf16[128,512]{1,0:T(8,128)(2,1)S(1)} %collective-permute-done.6, bf16[2048,2048]{1,0:T(8,128)(2,1)} %all-gather.3.cloned.1.call-done, s32[]{:T(128)S(6)} %select_n.255), kind=kOutput, calls=%fused_computation.6 | convolution fusion | flops 268435456 | bytes 3276804 | tf_op jit(solution)/shard_map/dot_general | solution.py:329
  100.5 2.3 %multiply_reduce_fusion.1 = (f32[128]{0:T(128)S(1)}, f32[128,2048]{1,0:T(8,128)S(1)}) fusion(f32[128,2048]{1,0:T(8,128)S(1)} %fusion.1, f32[128,2048]{1,0:T(8,128)S(1)} %convolution_add_fusion.1, bf16[128,512]{1,0:T(8,128)(2,1)S(1)} %collective-permute-done.5, bf16[2048,2048]{1,0:T(8,128)(2,1)} %all-gather.3.cloned.1.call-done, s32[]{:T(128)S(6)} %select_n.253), kind=kOutput, calls=%fused_computation.23 | convolution fusion | flops 269483904 | bytes 5374468 | tf_op jit(solution)/shard_map/dot_general | solution.py:329
  102.8 0.2 add_convert_fusion.1
  103.0 2.5 %all-gather.5.cloned.1.call-done = bf16[2048,512]{0,1:T(8,128)(2,1)} async-done(((bf16[512,512]{0,1:T(8,128)(2,1)}), bf16[2048,512]{0,1:T(8,128)(2,1)}) %all-gather.5.cloned.1.call-update) | async-done | bytes 2097168 | tf_op jit(solution)/shard_map/all_gather | solution.py:307
  105.5 2.6 %multiply_reduce_fusion = (f32[128]{0:T(128)S(1)}, f32[128,2048]{1,0:T(8,128)S(1)}) fusion(bf16[2048,512]{0,1:T(8,128)(2,1)} %all-gather.5.cloned.1.call-done, bf16[128,2048]{1,0:T(8,128)(2,1)S(1)} %add_convert_fusion.1, bf16[512,256]{1,0:T(8,128)(2,1)} %param.29, s32[]{:T(128)S(6)} %select_n.256), kind=kOutput, calls=%fused_computation.21 | convolution fusion | flops 269320064 | bytes 3736068 | tf_op jit(solution)/shard_map/dot_general | solution.py:347
  108.1 0.2 add_convert_fusion
  108.4 0.7 collective-permute-start.7
  109.1 1.0 collective-permute-start.8
  110.1 1.7 %collective-permute-done.7 = bf16[128,512]{1,0:T(8,128)(2,1)S(1)} collective-permute-done((bf16[128,512]{1,0:T(8,128)(2,1)S(1)}, bf16[128,512]{1,0:T(8,128)(2,1)S(1)}, u32[]{:S(2)}, u32[]{:S(2)}) %collective-permute-start.7) | collective-permute-done | bytes 131104 | tf_op jit(solution)/shard_map/ppermute | solution.py:242
  111.8 4.1 %collective-permute-done.8 = bf16[128,512]{1,0:T(8,128)(2,1)S(1)} collective-permute-done((bf16[128,512]{1,0:T(8,128)(2,1)S(1)}, bf16[128,512]{1,0:T(8,128)(2,1)S(1)}, u32[]{:S(2)}, u32[]{:S(2)}) %collective-permute-start.8) | collective-permute-done | bytes 131104 | tf_op jit(solution)/shard_map/ppermute | solution.py:242
  115.9 0.8 collective-permute-done.9
  116.7 0.1 pad_maximum_fusion.2
  116.8 1.5 %gather_fusion.2 = bf16[4,128,512]{2,1,0:T(8,128)(2,1)} fusion(bf16[4,128,512]{2,1,0:T(8,128)(2,1)S(1)} %pad_maximum_fusion.2, s32[1024]{0:T(1024)} %copy-done.8), kind=kCustom, calls=%fused_computation.2 | custom fusion | bytes 1048592 | tf_op jit(solution)/shard_map/gather | solution.py:244
  (67 shorter events, 0.4 us)
Async XLA Ops:
  6.5 0.7 copy-start.15
  6.5 0.9 copy-start.13
  6.5 86.9 %all-gather.3.cloned.1.call-start = ((), (), s32[]{:S(2)}) async-start(), calls=%async_computation.2 | async-start | bytes 10485760 | tf_op jit(solution)/shard_map/all_gather | solution.py:306
  8.4 11.6 %all-to-all-start = ((s32[8,1,6]{2,1,0:T(1,128)}), s32[8,1,6]{2,1,0:T(1,128)S(1)}, u32[]{:S(2)}, u32[]{:S(2)}) async-start(s32[8,1,6]{2,1,0:T(1,128)} %copy.38), calls=%async_computation | async-start | bytes 8192 | tf_op jit(solution)/shard_map/all_to_all | solution.py:283
  22.0 3.9 %copy-start.10 = (bf16[512]{0:T(512)(128)(2,1)S(1)}, bf16[512]{0:T(512)(128)(2,1)}, u32[]{:S(2)}) copy-start(bf16[512]{0:T(512)(128)(2,1)} %param.28) | copy-start | bytes 3076
  22.0 3.9 %copy-start.11 = (bf16[512]{0:T(512)(128)(2,1)S(1)}, bf16[512]{0:T(512)(128)(2,1)}, u32[]{:S(2)}) copy-start(bf16[512]{0:T(512)(128)(2,1)} %param.32) | copy-start | bytes 3076
  22.0 4.1 %copy-start.3 = (bf16[512,512]{1,0:T(8,128)(2,1)S(1)}, bf16[512,512]{1,0:T(8,128)(2,1)}, u32[]{:S(2)}) copy-start(bf16[512,512]{1,0:T(8,128)(2,1)} %param.21) | copy-start | bytes 1572868
  22.0 7.8 %copy-start.4 = (bf16[512,256]{1,0:T(8,128)(2,1)S(1)}, bf16[512,256]{1,0:T(8,128)(2,1)}, u32[]{:S(2)}) copy-start(bf16[512,256]{1,0:T(8,128)(2,1)} %param.30) | copy-start | bytes 786436
  22.0 8.0 %copy-start.5 = (bf16[256,512]{1,0:T(8,128)(2,1)S(1)}, bf16[256,512]{1,0:T(8,128)(2,1)}, u32[]{:S(2)}) copy-start(bf16[256,512]{1,0:T(8,128)(2,1)} %param.31) | copy-start | bytes 786436
  22.0 38.7 %all-to-all-start.1 = ((bf16[8,6,64,256]{3,2,1,0:T(8,128)(2,1)}), bf16[8,6,64,256]{3,2,1,0:T(8,128)(2,1)S(1)}, u32[]{:S(2)}, u32[]{:S(2)}) async-start(bf16[8,6,64,256]{3,2,1,0:T(8,128)(2,1)} %bitcast.20), calls=%async_computation.1 | async-start | bytes 3145728 | tf_op jit(solution)/shard_map/all_to_all | solution.py:292
  25.7 5.1 %copy-start.14 = (s32[1,8]{1,0:T(1,128)S(1)}, s32[1,8]{1,0:T(1,128)}, u32[]{:S(2)}) copy-start(s32[1,8]{1,0:T(1,128)} %param.37) | copy-start | bytes 100
  25.7 5.5 %copy-start.9 = (s32[1,8]{1,0:T(1,128)S(1)}, s32[1,8]{1,0:T(1,128)}, u32[]{:S(2)}) copy-start(s32[1,8]{1,0:T(1,128)} %param.35) | copy-start | bytes 100
  25.8 5.7 %copy-start.12 = (s32[1,8]{1,0:T(1,128)S(1)}, s32[1,8]{1,0:T(1,128)}, u32[]{:S(2)}) copy-start(s32[1,8]{1,0:T(1,128)} %param.36) | copy-start | bytes 100
  25.8 40.2 %copy-start.7 = (s32[7,1,512]{2,1,0:T(1,128)S(1)}, s32[7,1,512]{2,1,0:T(1,128)}, u32[]{:S(2)}) copy-start(s32[7,1,512]{2,1,0:T(1,128)} %constant.272.clone.1) | copy-start | bytes 43012
  25.8 79.7 %all-gather.5.cloned.1.call-start = ((), (), s32[]{:S(2)}) async-start(), calls=%async_computation.3 | async-start | bytes 2621440 | tf_op jit(solution)/shard_map/all_gather | solution.py:307
  26.1 40.5 %collective-permute-start = (bf16[136,512]{1,0:T(8,128)(2,1)S(1)}, bf16[136,512]{1,0:T(8,128)(2,1)S(1)}, u32[]{:S(2)}, u32[]{:S(2)}) collective-permute-start(bf16[136,512]{1,0:T(8,128)(2,1)S(1)} %get-tuple-element.38), channel_id=1, source_target_pairs={{0,1},{1,2},{2,3},{3,0},{4,5},{5,6},{6,7},{7,4},{8,9},{9,10},{10,1... | collective-permute-start | bytes 417800 | tf_op jit(solution)/shard_map/ppermute | solution.py:228
  29.3 37.2 %collective-permute-start.1 = (bf16[136,512]{1,0:T(8,128)(2,1)S(1)}, bf16[136,512]{1,0:T(8,128)(2,1)S(1)}, u32[]{:S(2)}, u32[]{:S(2)}) collective-permute-start(bf16[136,512]{1,0:T(8,128)(2,1)S(1)} %get-tuple-element.39), channel_id=1, source_target_pairs={{0,2},{1,3},{2,0},{3,1},{4,6},{5,7},{6,4},{7,5},{8,10},{9,11},{10,... | collective-permute-start | bytes 417800 | tf_op jit(solution)/shard_map/ppermute | solution.py:228
  29.6 37.0 %collective-permute-start.2 = (bf16[136,512]{1,0:T(8,128)(2,1)S(1)}, bf16[136,512]{1,0:T(8,128)(2,1)S(1)}, u32[]{:S(2)}, u32[]{:S(2)}) collective-permute-start(bf16[136,512]{1,0:T(8,128)(2,1)S(1)} %get-tuple-element.40), channel_id=1, source_target_pairs={{0,3},{1,0},{2,1},{3,2},{4,7},{5,4},{6,5},{7,6},{8,11},{9,8},{10,9... | collective-permute-start | bytes 417800 | tf_op jit(solution)/shard_map/ppermute | solution.py:228
  60.7 8.2 %copy-start.1 = (bf16[8,6,64,256]{3,2,1,0:T(8,128)(2,1)}, bf16[8,6,64,256]{3,2,1,0:T(8,128)(2,1)S(1)}, u32[]{:S(2)}) copy-start(bf16[8,6,64,256]{3,2,1,0:T(8,128)(2,1)S(1)} %all-to-all-done.1) | copy-start | bytes 4718596
  60.7 9.3 %collective-permute-start.3 = (bf16[8,6,64,256]{3,2,1,0:T(8,128)(2,1)S(1)}, bf16[8,6,64,256]{3,2,1,0:T(8,128)(2,1)}, u32[]{:S(2)}, u32[]{:S(2)}) collective-permute-start(bf16[8,6,64,256]{3,2,1,0:T(8,128)(2,1)S(1)} %all-to-all-done.1), channel_id=1, source_target_pairs={{0,1},{1,0},{2,3},{3,2},{4,5},{5,4},{6,7},{7,6},{8,9},{9,8},{10,11... | collective-permute-start | bytes 4718600 | tf_op jit(solution)/shard_map/ppermute | solution.py:293
  64.4 22.4 %copy-start.8 = (s32[1024]{0:T(1024)}, s32[1024]{0:T(1024)S(1)}, u32[]{:S(2)}) copy-start(s32[1024]{0:T(1024)S(1)} %pad_clamp_fusion.1) | copy-start | bytes 12292
  66.6 0.7 copy-start.6
  70.0 18.0 %copy-start = (bf16[512,2048]{1,0:T(8,128)(2,1)S(1)}, bf16[512,2048]{1,0:T(8,128)(2,1)}, u32[]{:S(2)}) copy-start(bf16[512,2048]{1,0:T(8,128)(2,1)} %param.27) | copy-start | bytes 6291460
  86.8 6.6 %collective-permute-start.4 = (bf16[128,512]{1,0:T(8,128)(2,1)S(1)}, bf16[128,512]{1,0:T(8,128)(2,1)S(1)}, u32[]{:S(2)}, u32[]{:S(2)}) collective-permute-start(bf16[128,512]{1,0:T(8,128)(2,1)S(1)} %get-tuple-element.47), channel_id=1, source_target_pairs={{0,1},{1,2},{2,3},{3,0},{4,5},{5,6},{6,7},{7,4},{8,9},{9,10},{10,1... | collective-permute-start | bytes 393224 | tf_op jit(solution)/shard_map/ppermute | solution.py:327
  89.4 9.0 %collective-permute-start.6 = (bf16[128,512]{1,0:T(8,128)(2,1)S(1)}, bf16[128,512]{1,0:T(8,128)(2,1)S(1)}, u32[]{:S(2)}, u32[]{:S(2)}) collective-permute-start(bf16[128,512]{1,0:T(8,128)(2,1)S(1)} %get-tuple-element.46), channel_id=1, source_target_pairs={{0,3},{1,0},{2,1},{3,2},{4,7},{5,4},{6,5},{7,6},{8,11},{9,8},{10,9... | collective-permute-start | bytes 393224 | tf_op jit(solution)/shard_map/ppermute | solution.py:327
  89.4 11.0 %collective-permute-start.5 = (bf16[128,512]{1,0:T(8,128)(2,1)S(1)}, bf16[128,512]{1,0:T(8,128)(2,1)S(1)}, u32[]{:S(2)}, u32[]{:S(2)}) collective-permute-start(bf16[128,512]{1,0:T(8,128)(2,1)S(1)} %get-tuple-element.45), channel_id=1, source_target_pairs={{0,2},{1,3},{2,0},{3,1},{4,6},{5,7},{6,4},{7,5},{8,10},{9,11},{10,... | collective-permute-start | bytes 393224 | tf_op jit(solution)/shard_map/ppermute | solution.py:327
  100.4 2.3 %copy-start.2 = (f32[4,16,8,512]{3,2,0,1:T(8,128)S(1)}, f32[4,16,8,512]{3,2,0,1:T(8,128)}, u32[]{:S(2)}) copy-start(f32[4,16,8,512]{3,2,0,1:T(8,128)} %copy.43) | copy-start | bytes 3145732
  108.4 3.4 %collective-permute-start.7 = (bf16[128,512]{1,0:T(8,128)(2,1)S(1)}, bf16[128,512]{1,0:T(8,128)(2,1)S(1)}, u32[]{:S(2)}, u32[]{:S(2)}) collective-permute-start(bf16[128,512]{1,0:T(8,128)(2,1)S(1)} %get-tuple-element.44), channel_id=1, source_target_pairs={{0,1},{1,2},{2,3},{3,0},{4,5},{5,6},{6,7},{7,4},{8,9},{9,10},{10,1... | collective-permute-start | bytes 393224 | tf_op jit(solution)/shard_map/ppermute | solution.py:242
  109.1 6.8 %collective-permute-start.8 = (bf16[128,512]{1,0:T(8,128)(2,1)S(1)}, bf16[128,512]{1,0:T(8,128)(2,1)S(1)}, u32[]{:S(2)}, u32[]{:S(2)}) collective-permute-start(bf16[128,512]{1,0:T(8,128)(2,1)S(1)} %get-tuple-element.43), channel_id=1, source_target_pairs={{0,2},{1,3},{2,0},{3,1},{4,6},{5,7},{6,4},{7,5},{8,10},{9,11},{10,... | collective-permute-start | bytes 393224 | tf_op jit(solution)/shard_map/ppermute | solution.py:242
  110.1 6.6 %collective-permute-start.9 = (bf16[128,512]{1,0:T(8,128)(2,1)S(1)}, bf16[128,512]{1,0:T(8,128)(2,1)S(1)}, u32[]{:S(2)}, u32[]{:S(2)}) collective-permute-start(bf16[128,512]{1,0:T(8,128)(2,1)S(1)} %get-tuple-element.42), channel_id=1, source_target_pairs={{0,3},{1,0},{2,1},{3,2},{4,7},{5,4},{6,5},{7,6},{8,11},{9,8},{10,9... | collective-permute-start | bytes 393224 | tf_op jit(solution)/shard_map/ppermute | solution.py:242
Sparse Core Ops, SparseCore 0:
  8.9 66.7 all-gather.2
  77.3 28.1 all-gather.4

commit v21 on v16

--- a/solution.py
+++ b/solution.py
@@ -55,13 +55,14 @@
     fresh_k_ref,
     fresh_v_ref,
     kinfo_ref,
-    rown_ref,
     o_ref,
     s_scr,
     acc_scr,
     *,
     slot_base,
     meta_base,
+    request_base,
+    requests,
 ):
     block = pl.program_id(0)
     ctx_lo = scalars_ref[block * 5]
@@ -75,8 +76,12 @@
     per_chunk = KEY_CHUNK // page_len
     q = q_ref[...]
     stacked = jnp.concatenate([q[:, h * HD:(h + 1) * HD] for h in range(heads)], axis=0)
-    row_owner = rown_ref[...]
     row_index = block * ROW_BLOCK + lax.broadcasted_iota(jnp.int32, (ROW_BLOCK, 1), 0)
+    row_owner = jnp.full((ROW_BLOCK, 1), -1, jnp.int32)
+    for r in range(requests):
+        lo = scalars_ref[request_base + 2 * r]
+        hi = lo + scalars_ref[request_base + 2 * r + 1]
+        row_owner = jnp.where((row_index >= lo) & (row_index < hi), r, row_owner)
     scale = 1.0 / math.sqrt(HD)
 
     def chunk_of(t):
@@ -178,14 +183,24 @@
     meta = jnp.stack([half, kv_head]).astype(jnp.int32)
     slot_base = ranges.size
     meta_base = slot_base + slots.shape[0]
-    scalars = jnp.concatenate([ranges.reshape(-1), slots.astype(jnp.int32), meta])
+    request_base = meta_base + meta.shape[0]
+    per_request = jnp.stack([row_starts, row_counts], axis=1).astype(jnp.int32)
+    scalars = jnp.concatenate(
+        [ranges.reshape(-1), slots.astype(jnp.int32), meta, per_request.reshape(-1)]
+    )
     key_info = jnp.stack(
         [key_owner.reshape(chunks, KEY_CHUNK), key_pos.reshape(chunks, KEY_CHUNK)], axis=1
     )
     whole = lambda b, s: (0, 0, 0)
     by_head = lambda b, s: (0, s[meta_base + 1])
     return pl.pallas_call(
-        functools.partial(attention_kernel, slot_base=slot_base, meta_base=meta_base),
+        functools.partial(
+            attention_kernel,
+            slot_base=slot_base,
+            meta_base=meta_base,
+            request_base=request_base,
+            requests=row_counts.shape[0],
+        ),
         grid_spec=pltpu.PrefetchScalarGridSpec(
             num_scalar_prefetch=1,
             grid=(blocks,),
@@ -196,7 +211,6 @@
                 pl.BlockSpec((row_total, HD), by_head),
                 pl.BlockSpec((row_total, HD), by_head),
                 pl.BlockSpec((chunks, 2, KEY_CHUNK), whole),
-                pl.BlockSpec((ROW_BLOCK, 1), lambda b, s: (b, 0)),
             ],
             out_specs=pl.BlockSpec((ROW_BLOCK, heads * HD), lambda b, s: (b, 0)),
             scratch_shapes=[
@@ -213,7 +227,6 @@
         new_keys,
         new_values,
         key_info,
-        row_owner.reshape(row_total, 1),
     )
 
 

time: 125 us -> 125 us (level)
  no operation moved by 1% of the time
where the time goes in v21:
time: 125 us; the launch traced here: 124 us
  waiting for transfers between devices  49.3 us (39%)
  starting transfers between devices  20.6 us (16%)
  Pallas kernels  14.6 us (12%)
  between operations  14 us (11%)
  matrix products  11.4 us (9%)
  local copies, waits for them, and re-layouts  7.54 us (6%)
  other arithmetic  6.1 us (5%)
    all_to_all x1, waiting for transfers between devices, shards(): lax.all_to_all(outgoing, 'req', split_axis=0, concat_axis=0, tiled=True)  29.1 us
    pallas_call x1, Pallas kernels, sparse_attention(): pl.pallas_call(functools.partial(attention_kernel, slot_base=slot_base, m...  14.6 us
    all_gather x1, waiting for transfers between devices, shards(): lax.all_gather(jnp.concatenate([ple_gate_weight, ple_proj_weight.T], axis...  6.58 us
    all_to_all x1, starting transfers between devices, shards(): lax.all_to_all(request_table, 'req', split_axis=0, concat_axis=0, tiled=T...  6.38 us
    dot_general x3, matrix products, shards(): jnp.dot(piece, lax.dynamic_slice_in_dim(full_weight, source * width, widt...  6.36 us
    ppermute x3, waiting for transfers between devices, columns_to_rows(): received.append(lax.ppermute(outgoing, axis_name, perm))  6.22 us
    ppermute x3, waiting for transfers between devices, shards(): piece = lax.ppermute(outgoing, 'tp', perm)  3.86 us
    all_to_all x1, starting transfers between devices, shards(): lax.all_to_all(outgoing, 'req', split_axis=0, concat_axis=0, tiled=True)  3.75 us
  transfers between devices with their start and end apart: 14, of which 9 were waited for; matrix products, arithmetic and copies ran while one was open for 17% of the time, Pallas kernels for 12%

profile of v21, /device:TPU:1, one launch (start us, length us, event | category | flops | bytes accessed | tf_op | source)
XLA Modules:
  0.0 123.6 jit_solution(4808751818653630973)
XLA Ops:
  6.5 0.7 all-gather.3.cloned.1.call-update
  7.3 0.2 convert_reduce_fusion.1
  7.5 0.2 select_reduce_fusion.2
  7.7 0.7 copy.40
  8.4 6.4 %all-to-all-start = ((s32[8,1,6]{2,1,0:T(1,128)}), s32[8,1,6]{2,1,0:T(1,128)S(1)}, u32[]{:S(2)}, u32[]{:S(2)}) async-start(s32[8,1,6]{2,1,0:T(1,128)} %copy.40), calls=%async_computation | async-start | bytes 8192 | tf_op jit(solution)/shard_map/all_to_all | solution.py:296
  14.7 2.5 %dynamic-slice_select_fusion = bf16[48,64,256]{2,1,0:T(8,128)(2,1)S(1)} fusion(bf16[48,64,512]{2,1,0:T(8,128)(2,1)} %param.26, s32[]{:T(128)S(6)} %select_n.244, bf16[48,64,512]{2,1,0:T(8,128)(2,1)} %param.25, pred[]{:T(512)S(6)} %eq.140), kind=kLoop, calls=%fused_computation.12 | loop fusion | flops 786432 | bytes 4718597 | tf_op jit(solution)/shard_map/jit(_where)/select_n | solution.py:303
  17.2 2.8 %all-to-all-done = s32[8,1,6]{2,1,0:T(1,128)S(1)} async-done(((s32[8,1,6]{2,1,0:T(1,128)}), s32[8,1,6]{2,1,0:T(1,128)S(1)}, u32[]{:S(2)}, u32[]{:S(2)}) %all-to-all-start) | async-done | bytes 224 | tf_op jit(solution)/shard_map/all_to_all | solution.py:296
  20.0 0.1 reshape.549
  20.1 1.9 %gather_fusion.1 = bf16[48,64,256]{2,1,0:T(8,128)(2,1)} fusion(bf16[48,64,256]{2,1,0:T(8,128)(2,1)S(1)} %dynamic-slice_select_fusion, s32[1024]{0:T(1024)S(1)} %pad_clamp_fusion), kind=kCustom, calls=%fused_computation.1 | custom fusion | bytes 3145920 | tf_op jit(solution)/shard_map/gather | solution.py:304
  22.0 3.7 %all-to-all-start.1 = ((bf16[8,6,64,256]{3,2,1,0:T(8,128)(2,1)}), bf16[8,6,64,256]{3,2,1,0:T(8,128)(2,1)S(1)}, u32[]{:S(2)}, u32[]{:S(2)}) async-start(bf16[8,6,64,256]{3,2,1,0:T(8,128)(2,1)} %bitcast.22), calls=%async_computation.1 | async-start | bytes 3145728 | tf_op jit(solution)/shard_map/all_to_all | solution.py:305
  25.8 0.0 all-gather.5.cloned.1.call-start
  26.0 0.1 fusion.12
  26.1 3.2 %collective-permute-start = (bf16[136,512]{1,0:T(8,128)(2,1)S(1)}, bf16[136,512]{1,0:T(8,128)(2,1)S(1)}, u32[]{:S(2)}, u32[]{:S(2)}) collective-permute-start(bf16[136,512]{1,0:T(8,128)(2,1)S(1)} %get-tuple-element.38), channel_id=1, source_target_pairs={{0,1},{1,2},{2,3},{3,0},{4,5},{5,6},{6,7},{7,4},{8,9},{9,10},{10,1... | collective-permute-start | bytes 417800 | tf_op jit(solution)/shard_map/ppermute | solution.py:241
  29.3 0.3 collective-permute-start.1
  29.6 0.2 collective-permute-start.2
  29.8 0.1 copy.41
  29.9 0.8 pad_maximum_fusion.1
  30.8 0.2 reduce-window.6
  31.0 0.2 reduce-window_1_clone.1
  31.2 0.1 convert_reduce_fusion.2
  31.3 0.1 convert_reduce_fusion
  31.4 0.1 select_reduce_fusion.1
  31.6 29.1 %all-to-all-done.1 = bf16[8,6,64,256]{3,2,1,0:T(8,128)(2,1)S(1)} async-done(((bf16[8,6,64,256]{3,2,1,0:T(8,128)(2,1)}), bf16[8,6,64,256]{3,2,1,0:T(8,128)(2,1)S(1)}, u32[]{:S(2)}, u32[]{:S(2)}) %all-to-all-start.1) | async-done | bytes 1572896 | tf_op jit(solution)/shard_map/all_to_all | solution.py:305
  60.7 3.1 %collective-permute-start.3 = (bf16[8,6,64,256]{3,2,1,0:T(8,128)(2,1)S(1)}, bf16[8,6,64,256]{3,2,1,0:T(8,128)(2,1)}, u32[]{:S(2)}, u32[]{:S(2)}) collective-permute-start(bf16[8,6,64,256]{3,2,1,0:T(8,128)(2,1)S(1)} %all-to-all-done.1), channel_id=1, source_target_pairs={{0,1},{1,0},{2,3},{3,2},{4,5},{5,4},{6,7},{7,6},{8,9},{9,8},{10,11... | collective-permute-start | bytes 4718600 | tf_op jit(solution)/shard_map/ppermute | solution.py:306
  63.8 0.1 slice.54
  63.9 0.1 slice.55
  64.0 0.2 select_reduce_fusion.3
  64.4 0.1 copy.34
  64.5 0.1 copy.35
  64.5 0.1 copy.36
  64.6 0.1 copy.37
  64.7 0.1 stack.51
  64.8 0.1 reshape.530
  64.9 0.1 copy.38
  65.0 0.1 reshape.531
  65.1 0.6 concatenate.18.scalars_ref
  65.7 0.6 pad_add_fusion.kinfo_ref
  66.4 0.1 pad_maximum_fusion
  66.5 0.6 gather_fusion
  67.0 0.1 convert_bitcast_fusion
  67.2 0.1 copy.44
  67.3 14.6 %shard_map.163 = bf16[512,512]{1,0:T(8,128)(2,1)} custom-call(s32[76]{0:T(128)} %concatenate.18.scalars_ref, bf16[512,512]{1,0:T(8,128)(2,1)} %q_ref.1, bf16[48,64,256]{2,1,0:T(8,128)(2,1)} %bitcast.93, bf16[48,64,256]{2,1,0:T(8,128)(2,1)} %bitcast.24.partner_ref, bf16[512,512]{1,0:T(8,128)(2,1)} %fresh_k_ref.1, bf16[512,512]{1,0:T(8,128)(2,1)} %fresh_v_ref.1, ...), custom_call_target="tpu_custom_call" | custom-call | tf_op jit(solution)/shard_map/pallas_call | solution.py:196
  81.9 1.1 dynamic-slice_bitcast_fusion.2
  83.0 1.1 collective-permute-start.4
  84.1 0.6 collective-permute-start.5
  84.6 2.4 %fusion.5 = f32[128,2048]{1,0:T(8,128)S(1)} fusion(bf16[2048,2048]{1,0:T(8,128)(2,1)} %all-gather.3.cloned.1.call-done, s32[]{:T(128)S(6)} %select_n.251, bf16[4,128,512]{2,1,0:T(8,128)(2,1)} %bitcast.98, s32[]{:T(128)S(6)} %select_n.223), kind=kOutput, calls=%fused_computation.10 | convolution fusion | flops 268435456 | bytes 3276808 | tf_op jit(solution)/shard_map/dot_general | solution.py:336
  87.1 2.4 %collective-permute-done.4 = bf16[128,512]{1,0:T(8,128)(2,1)S(1)} collective-permute-done((bf16[128,512]{1,0:T(8,128)(2,1)S(1)}, bf16[128,512]{1,0:T(8,128)(2,1)S(1)}, u32[]{:S(2)}, u32[]{:S(2)}) %collective-permute-start.4) | collective-permute-done | bytes 131104 | tf_op jit(solution)/shard_map/ppermute | solution.py:344
  89.5 2.1 %convolution_add_fusion.1 = f32[128,2048]{1,0:T(8,128)S(1)} fusion(f32[128,2048]{1,0:T(8,128)S(1)} %fusion.5, bf16[128,512]{1,0:T(8,128)(2,1)S(1)} %collective-permute-done.4, bf16[2048,2048]{1,0:T(8,128)(2,1)} %all-gather.3.cloned.1.call-done, s32[]{:T(128)S(6)} %select_n.253), kind=kOutput, calls=%fused_computation.5 | convolution fusion | flops 268697600 | bytes 4325380 | tf_op jit(solution)/shard_map/dot_general | solution.py:346
  91.5 1.2 collective-permute-done.6
  92.7 2.1 %fusion.1 = f32[128,2048]{1,0:T(8,128)S(1)} fusion(bf16[128,512]{1,0:T(8,128)(2,1)S(1)} %collective-permute-done.6, bf16[2048,2048]{1,0:T(8,128)(2,1)} %all-gather.3.cloned.1.call-done, s32[]{:T(128)S(6)} %select_n.257), kind=kOutput, calls=%fused_computation.6 | convolution fusion | flops 268435456 | bytes 3276804 | tf_op jit(solution)/shard_map/dot_general | solution.py:346
  94.8 0.3 collective-permute-done.5
  95.1 2.2 %multiply_reduce_fusion.1 = (f32[128]{0:T(128)S(1)}, f32[128,2048]{1,0:T(8,128)S(1)}) fusion(f32[128,2048]{1,0:T(8,128)S(1)} %fusion.1, f32[128,2048]{1,0:T(8,128)S(1)} %convolution_add_fusion.1, bf16[128,512]{1,0:T(8,128)(2,1)S(1)} %collective-permute-done.5, bf16[2048,2048]{1,0:T(8,128)(2,1)} %all-gather.3.cloned.1.call-done, s32[]{:T(128)S(6)} %select_n.255), kind=kOutput, calls=%fused_computation.25 | convolution fusion | flops 269483904 | bytes 5374468 | tf_op jit(solution)/shard_map/dot_general | solution.py:346
  97.3 0.2 add_convert_fusion.1
  97.5 6.6 %all-gather.5.cloned.1.call-done = bf16[2048,512]{0,1:T(8,128)(2,1)} async-done(((bf16[512,512]{0,1:T(8,128)(2,1)}), bf16[2048,512]{0,1:T(8,128)(2,1)}) %all-gather.5.cloned.1.call-update) | async-done | bytes 2097168 | tf_op jit(solution)/shard_map/all_gather | solution.py:320
  104.1 2.6 %multiply_reduce_fusion = (f32[128]{0:T(128)S(1)}, f32[128,2048]{1,0:T(8,128)S(1)}) fusion(bf16[2048,512]{0,1:T(8,128)(2,1)} %all-gather.5.cloned.1.call-done, bf16[128,2048]{1,0:T(8,128)(2,1)S(1)} %add_convert_fusion.1, bf16[512,256]{1,0:T(8,128)(2,1)} %param.29, s32[]{:T(128)S(6)} %select_n.258), kind=kOutput, calls=%fused_computation.23 | convolution fusion | flops 269320064 | bytes 3736068 | tf_op jit(solution)/shard_map/dot_general | solution.py:364
  106.8 0.2 add_convert_fusion
  107.1 1.4 %collective-permute-start.7 = (bf16[128,512]{1,0:T(8,128)(2,1)S(1)}, bf16[128,512]{1,0:T(8,128)(2,1)S(1)}, u32[]{:S(2)}, u32[]{:S(2)}) collective-permute-start(bf16[128,512]{1,0:T(8,128)(2,1)S(1)} %get-tuple-element.44), channel_id=1, source_target_pairs={{0,1},{1,2},{2,3},{3,0},{4,5},{5,6},{6,7},{7,4},{8,9},{9,10},{10,1... | collective-permute-start | bytes 393224 | tf_op jit(solution)/shard_map/ppermute | solution.py:255
  108.4 0.3 collective-permute-start.8
  108.7 0.3 collective-permute-start.9
  109.1 1.9 %collective-permute-done.7 = bf16[128,512]{1,0:T(8,128)(2,1)S(1)} collective-permute-done((bf16[128,512]{1,0:T(8,128)(2,1)S(1)}, bf16[128,512]{1,0:T(8,128)(2,1)S(1)}, u32[]{:S(2)}, u32[]{:S(2)}) %collective-permute-start.7) | collective-permute-done | bytes 131104 | tf_op jit(solution)/shard_map/ppermute | solution.py:255
  111.0 3.5 %collective-permute-done.8 = bf16[128,512]{1,0:T(8,128)(2,1)S(1)} collective-permute-done((bf16[128,512]{1,0:T(8,128)(2,1)S(1)}, bf16[128,512]{1,0:T(8,128)(2,1)S(1)}, u32[]{:S(2)}, u32[]{:S(2)}) %collective-permute-start.8) | collective-permute-done | bytes 131104 | tf_op jit(solution)/shard_map/ppermute | solution.py:255
  114.5 0.8 collective-permute-done.9
  115.3 0.1 pad_maximum_fusion.2
  115.4 1.4 %gather_fusion.2 = bf16[4,128,512]{2,1,0:T(8,128)(2,1)} fusion(bf16[4,128,512]{2,1,0:T(8,128)(2,1)S(1)} %pad_maximum_fusion.2, s32[1024]{0:T(1024)S(1)} %pad_clamp_fusion.1), kind=kCustom, calls=%fused_computation.2 | custom fusion | bytes 1048592 | tf_op jit(solution)/shard_map/gather | solution.py:257
  (62 shorter events, 0.4 us)
Async XLA Ops:
  6.5 0.7 copy-start.11
  6.5 0.9 copy-start.10
  6.5 78.1 %all-gather.3.cloned.1.call-start = ((), (), s32[]{:S(2)}) async-start(), calls=%async_computation.2 | async-start | bytes 10485760 | tf_op jit(solution)/shard_map/all_gather | solution.py:319
  8.4 11.6 %all-to-all-start = ((s32[8,1,6]{2,1,0:T(1,128)}), s32[8,1,6]{2,1,0:T(1,128)S(1)}, u32[]{:S(2)}, u32[]{:S(2)}) async-start(s32[8,1,6]{2,1,0:T(1,128)} %copy.40), calls=%async_computation | async-start | bytes 8192 | tf_op jit(solution)/shard_map/all_to_all | solution.py:296
  22.0 3.9 %copy-start.6 = (bf16[512]{0:T(512)(128)(2,1)S(1)}, bf16[512]{0:T(512)(128)(2,1)}, u32[]{:S(2)}) copy-start(bf16[512]{0:T(512)(128)(2,1)} %param.28) | copy-start | bytes 3076
  22.0 3.9 %copy-start.7 = (bf16[512]{0:T(512)(128)(2,1)S(1)}, bf16[512]{0:T(512)(128)(2,1)}, u32[]{:S(2)}) copy-start(bf16[512]{0:T(512)(128)(2,1)} %param.32) | copy-start | bytes 3076
  22.0 4.1 %copy-start.1 = (bf16[512,512]{1,0:T(8,128)(2,1)S(1)}, bf16[512,512]{1,0:T(8,128)(2,1)}, u32[]{:S(2)}) copy-start(bf16[512,512]{1,0:T(8,128)(2,1)} %param.21) | copy-start | bytes 1572868
  22.0 7.8 %copy-start.2 = (bf16[512,256]{1,0:T(8,128)(2,1)S(1)}, bf16[512,256]{1,0:T(8,128)(2,1)}, u32[]{:S(2)}) copy-start(bf16[512,256]{1,0:T(8,128)(2,1)} %param.30) | copy-start | bytes 786436
  22.0 8.0 %copy-start.3 = (bf16[256,512]{1,0:T(8,128)(2,1)S(1)}, bf16[256,512]{1,0:T(8,128)(2,1)}, u32[]{:S(2)}) copy-start(bf16[256,512]{1,0:T(8,128)(2,1)} %param.31) | copy-start | bytes 786436
  22.0 38.7 %all-to-all-start.1 = ((bf16[8,6,64,256]{3,2,1,0:T(8,128)(2,1)}), bf16[8,6,64,256]{3,2,1,0:T(8,128)(2,1)S(1)}, u32[]{:S(2)}, u32[]{:S(2)}) async-start(bf16[8,6,64,256]{3,2,1,0:T(8,128)(2,1)} %bitcast.22), calls=%async_computation.1 | async-start | bytes 3145728 | tf_op jit(solution)/shard_map/all_to_all | solution.py:305
  25.7 5.1 %copy-start.9 = (s32[1,8]{1,0:T(1,128)S(1)}, s32[1,8]{1,0:T(1,128)}, u32[]{:S(2)}) copy-start(s32[1,8]{1,0:T(1,128)} %param.37) | copy-start | bytes 100
  25.8 5.2 %copy-start.5 = (s32[1,8]{1,0:T(1,128)S(1)}, s32[1,8]{1,0:T(1,128)}, u32[]{:S(2)}) copy-start(s32[1,8]{1,0:T(1,128)} %param.35) | copy-start | bytes 100
  25.8 5.5 %copy-start.8 = (s32[1,8]{1,0:T(1,128)S(1)}, s32[1,8]{1,0:T(1,128)}, u32[]{:S(2)}) copy-start(s32[1,8]{1,0:T(1,128)} %param.36) | copy-start | bytes 100
  25.8 40.0 %copy-start.4 = (s32[7,1,512]{2,1,0:T(1,128)S(1)}, s32[7,1,512]{2,1,0:T(1,128)}, u32[]{:S(2)}) copy-start(s32[7,1,512]{2,1,0:T(1,128)} %constant.272.clone.1) | copy-start | bytes 43012
  25.8 78.3 %all-gather.5.cloned.1.call-start = ((), (), s32[]{:S(2)}) async-start(), calls=%async_computation.3 | async-start | bytes 2621440 | tf_op jit(solution)/shard_map/all_gather | solution.py:320
  26.1 40.3 %collective-permute-start = (bf16[136,512]{1,0:T(8,128)(2,1)S(1)}, bf16[136,512]{1,0:T(8,128)(2,1)S(1)}, u32[]{:S(2)}, u32[]{:S(2)}) collective-permute-start(bf16[136,512]{1,0:T(8,128)(2,1)S(1)} %get-tuple-element.38), channel_id=1, source_target_pairs={{0,1},{1,2},{2,3},{3,0},{4,5},{5,6},{6,7},{7,4},{8,9},{9,10},{10,1... | collective-permute-start | bytes 417800 | tf_op jit(solution)/shard_map/ppermute | solution.py:241
  29.3 37.1 %collective-permute-start.1 = (bf16[136,512]{1,0:T(8,128)(2,1)S(1)}, bf16[136,512]{1,0:T(8,128)(2,1)S(1)}, u32[]{:S(2)}, u32[]{:S(2)}) collective-permute-start(bf16[136,512]{1,0:T(8,128)(2,1)S(1)} %get-tuple-element.39), channel_id=1, source_target_pairs={{0,2},{1,3},{2,0},{3,1},{4,6},{5,7},{6,4},{7,5},{8,10},{9,11},{10,... | collective-permute-start | bytes 417800 | tf_op jit(solution)/shard_map/ppermute | solution.py:241
  29.6 36.8 %collective-permute-start.2 = (bf16[136,512]{1,0:T(8,128)(2,1)S(1)}, bf16[136,512]{1,0:T(8,128)(2,1)S(1)}, u32[]{:S(2)}, u32[]{:S(2)}) collective-permute-start(bf16[136,512]{1,0:T(8,128)(2,1)S(1)} %get-tuple-element.40), channel_id=1, source_target_pairs={{0,3},{1,0},{2,1},{3,2},{4,7},{5,4},{6,5},{7,6},{8,11},{9,8},{10,9... | collective-permute-start | bytes 417800 | tf_op jit(solution)/shard_map/ppermute | solution.py:241
  60.7 6.5 %copy-start = (bf16[8,6,64,256]{3,2,1,0:T(8,128)(2,1)}, bf16[8,6,64,256]{3,2,1,0:T(8,128)(2,1)S(1)}, u32[]{:S(2)}) copy-start(bf16[8,6,64,256]{3,2,1,0:T(8,128)(2,1)S(1)} %all-to-all-done.1) | copy-start | bytes 4718596
  60.7 6.6 %collective-permute-start.3 = (bf16[8,6,64,256]{3,2,1,0:T(8,128)(2,1)S(1)}, bf16[8,6,64,256]{3,2,1,0:T(8,128)(2,1)}, u32[]{:S(2)}, u32[]{:S(2)}) collective-permute-start(bf16[8,6,64,256]{3,2,1,0:T(8,128)(2,1)S(1)} %all-to-all-done.1), channel_id=1, source_target_pairs={{0,1},{1,0},{2,3},{3,2},{4,5},{5,4},{6,7},{7,6},{8,9},{9,8},{10,11... | collective-permute-start | bytes 4718600 | tf_op jit(solution)/shard_map/ppermute | solution.py:306
  83.0 6.5 %collective-permute-start.4 = (bf16[128,512]{1,0:T(8,128)(2,1)S(1)}, bf16[128,512]{1,0:T(8,128)(2,1)S(1)}, u32[]{:S(2)}, u32[]{:S(2)}) collective-permute-start(bf16[128,512]{1,0:T(8,128)(2,1)S(1)} %get-tuple-element.47), channel_id=1, source_target_pairs={{0,1},{1,2},{2,3},{3,0},{4,5},{5,6},{6,7},{7,4},{8,9},{9,10},{10,1... | collective-permute-start | bytes 393224 | tf_op jit(solution)/shard_map/ppermute | solution.py:344
  84.1 8.7 %collective-permute-start.6 = (bf16[128,512]{1,0:T(8,128)(2,1)S(1)}, bf16[128,512]{1,0:T(8,128)(2,1)S(1)}, u32[]{:S(2)}, u32[]{:S(2)}) collective-permute-start(bf16[128,512]{1,0:T(8,128)(2,1)S(1)} %get-tuple-element.46), channel_id=1, source_target_pairs={{0,3},{1,0},{2,1},{3,2},{4,7},{5,4},{6,5},{7,6},{8,11},{9,8},{10,9... | collective-permute-start | bytes 393224 | tf_op jit(solution)/shard_map/ppermute | solution.py:344
  84.1 11.0 %collective-permute-start.5 = (bf16[128,512]{1,0:T(8,128)(2,1)S(1)}, bf16[128,512]{1,0:T(8,128)(2,1)S(1)}, u32[]{:S(2)}, u32[]{:S(2)}) collective-permute-start(bf16[128,512]{1,0:T(8,128)(2,1)S(1)} %get-tuple-element.45), channel_id=1, source_target_pairs={{0,2},{1,3},{2,0},{3,1},{4,6},{5,7},{6,4},{7,5},{8,10},{9,11},{10,... | collective-permute-start | bytes 393224 | tf_op jit(solution)/shard_map/ppermute | solution.py:344
  107.1 3.9 %collective-permute-start.7 = (bf16[128,512]{1,0:T(8,128)(2,1)S(1)}, bf16[128,512]{1,0:T(8,128)(2,1)S(1)}, u32[]{:S(2)}, u32[]{:S(2)}) collective-permute-start(bf16[128,512]{1,0:T(8,128)(2,1)S(1)} %get-tuple-element.44), channel_id=1, source_target_pairs={{0,1},{1,2},{2,3},{3,0},{4,5},{5,6},{6,7},{7,4},{8,9},{9,10},{10,1... | collective-permute-start | bytes 393224 | tf_op jit(solution)/shard_map/ppermute | solution.py:255
  108.4 6.1 %collective-permute-start.8 = (bf16[128,512]{1,0:T(8,128)(2,1)S(1)}, bf16[128,512]{1,0:T(8,128)(2,1)S(1)}, u32[]{:S(2)}, u32[]{:S(2)}) collective-permute-start(bf16[128,512]{1,0:T(8,128)(2,1)S(1)} %get-tuple-element.43), channel_id=1, source_target_pairs={{0,2},{1,3},{2,0},{3,1},{4,6},{5,7},{6,4},{7,5},{8,10},{9,11},{10,... | collective-permute-start | bytes 393224 | tf_op jit(solution)/shard_map/ppermute | solution.py:255
  108.7 6.6 %collective-permute-start.9 = (bf16[128,512]{1,0:T(8,128)(2,1)S(1)}, bf16[128,512]{1,0:T(8,128)(2,1)S(1)}, u32[]{:S(2)}, u32[]{:S(2)}) collective-permute-start(bf16[128,512]{1,0:T(8,128)(2,1)S(1)} %get-tuple-element.42), channel_id=1, source_target_pairs={{0,3},{1,0},{2,1},{3,2},{4,7},{5,4},{6,5},{7,6},{8,11},{9,8},{10,9... | collective-permute-start | bytes 393224 | tf_op jit(solution)/shard_map/ppermute | solution.py:255
Sparse Core Ops, SparseCore 0:
  8.9 66.7 all-gather.2
  77.3 26.7 all-gather.4

commit v22 on v16

--- a/solution.py
+++ b/solution.py
@@ -38,7 +38,7 @@
     return jnp.concatenate([context_mask, causal], axis=1)
 
 
-ROW_BLOCK = 256
+ROW_BLOCK = 128
 KEY_CHUNK = 512
 
 

time: 125 us -> 125 us (level)
  no operation moved by 1% of the time
where the time goes in v22:
time: 125 us; the launch traced here: 124 us
  waiting for transfers between devices  49.4 us (40%)
  starting transfers between devices  20.4 us (16%)
  Pallas kernels  15.1 us (12%)
  between operations  13.9 us (11%)
  matrix products  11.1 us (9%)
  local copies, waits for them, and re-layouts  7.33 us (6%)
  other arithmetic  6.81 us (5%)
    all_to_all x1, waiting for transfers between devices, shards(): lax.all_to_all(outgoing, 'req', split_axis=0, concat_axis=0, tiled=True)  28.8 us
    pallas_call x1, Pallas kernels, sparse_attention(): pl.pallas_call(functools.partial(attention_kernel, slot_base=slot_base, m...  15.1 us
    ppermute x3, waiting for transfers between devices, columns_to_rows(): received.append(lax.ppermute(outgoing, axis_name, perm))  6.42 us
    all_to_all x1, starting transfers between devices, shards(): lax.all_to_all(request_table, 'req', split_axis=0, concat_axis=0, tiled=T...  6.38 us
    dot_general x3, matrix products, shards(): jnp.dot(piece, lax.dynamic_slice_in_dim(full_weight, source * width, widt...  6.29 us
    all_gather x1, waiting for transfers between devices, shards(): lax.all_gather(jnp.concatenate([ple_gate_weight, ple_proj_weight.T], axis...  6.26 us
    ppermute x3, waiting for transfers between devices, shards(): piece = lax.ppermute(outgoing, 'tp', perm)  4.58 us
    all_to_all x1, starting transfers between devices, shards(): lax.all_to_all(outgoing, 'req', split_axis=0, concat_axis=0, tiled=True)  3.75 us
  transfers between devices with their start and end apart: 14, of which 9 were waited for; matrix products, arithmetic and copies ran while one was open for 17% of the time, Pallas kernels for 12%

profile of v22, /device:TPU:1, one launch (start us, length us, event | category | flops | bytes accessed | tf_op | source)
XLA Modules:
  0.0 124.0 jit_solution(4729141172498800459)
XLA Ops:
  6.5 0.7 all-gather.3.cloned.1.call-update
  7.3 0.2 convert_reduce_fusion.1
  7.5 0.2 select_reduce_fusion.2
  7.7 0.7 copy.32
  8.4 6.4 %all-to-all-start = ((s32[8,1,6]{2,1,0:T(1,128)}), s32[8,1,6]{2,1,0:T(1,128)S(1)}, u32[]{:S(2)}, u32[]{:S(2)}) async-start(s32[8,1,6]{2,1,0:T(1,128)} %copy.32), calls=%async_computation | async-start | bytes 8192 | tf_op jit(solution)/shard_map/all_to_all | solution.py:283
  14.7 2.6 %dynamic-slice_select_fusion = bf16[48,64,256]{2,1,0:T(8,128)(2,1)S(1)} fusion(bf16[48,64,512]{2,1,0:T(8,128)(2,1)} %param.26, s32[]{:T(128)S(6)} %select_n.244, bf16[48,64,512]{2,1,0:T(8,128)(2,1)} %param.25, pred[]{:T(512)S(6)} %eq.140), kind=kLoop, calls=%fused_computation.12 | loop fusion | flops 786432 | bytes 4718597 | tf_op jit(solution)/shard_map/jit(_where)/select_n | solution.py:290
  17.3 2.7 %all-to-all-done = s32[8,1,6]{2,1,0:T(1,128)S(1)} async-done(((s32[8,1,6]{2,1,0:T(1,128)}), s32[8,1,6]{2,1,0:T(1,128)S(1)}, u32[]{:S(2)}, u32[]{:S(2)}) %all-to-all-start) | async-done | bytes 224 | tf_op jit(solution)/shard_map/all_to_all | solution.py:283
  20.0 0.1 reshape.538
  20.1 1.9 %gather_fusion.1 = bf16[48,64,256]{2,1,0:T(8,128)(2,1)} fusion(bf16[48,64,256]{2,1,0:T(8,128)(2,1)S(1)} %dynamic-slice_select_fusion, s32[1024]{0:T(1024)S(1)} %pad_clamp_fusion), kind=kCustom, calls=%fused_computation.1 | custom fusion | bytes 3145920 | tf_op jit(solution)/shard_map/gather | solution.py:291
  22.0 0.0 copy-start.3
  22.0 3.7 %all-to-all-start.1 = ((bf16[8,6,64,256]{3,2,1,0:T(8,128)(2,1)}), bf16[8,6,64,256]{3,2,1,0:T(8,128)(2,1)S(1)}, u32[]{:S(2)}, u32[]{:S(2)}) async-start(bf16[8,6,64,256]{3,2,1,0:T(8,128)(2,1)} %bitcast.20), calls=%async_computation.1 | async-start | bytes 3145728 | tf_op jit(solution)/shard_map/all_to_all | solution.py:292
  25.8 0.0 copy-start.5
  25.8 0.0 copy-start.8
  25.8 0.0 copy-start.4
  25.8 0.0 all-gather.5.cloned.1.call-start
  26.0 0.1 fusion.12
  26.1 3.2 %collective-permute-start = (bf16[136,512]{1,0:T(8,128)(2,1)S(1)}, bf16[136,512]{1,0:T(8,128)(2,1)S(1)}, u32[]{:S(2)}, u32[]{:S(2)}) collective-permute-start(bf16[136,512]{1,0:T(8,128)(2,1)S(1)} %get-tuple-element.38), channel_id=1, source_target_pairs={{0,1},{1,2},{2,3},{3,0},{4,5},{5,6},{6,7},{7,4},{8,9},{9,10},{10,1... | collective-permute-start | bytes 417800 | tf_op jit(solution)/shard_map/ppermute | solution.py:228
  29.3 0.3 collective-permute-start.1
  29.6 0.2 collective-permute-start.2
  29.8 0.1 copy.34
  29.9 0.8 pad_maximum_fusion.1
  30.8 0.0 all-gather.5.cloned.1.call-update
  30.8 0.2 reduce-window_clone.1
  31.0 0.1 convert_reduce_fusion.2
  31.1 0.1 slice.54
  31.2 0.1 slice.55
  31.3 0.2 reduce-window_1_clone.1
  31.5 0.1 convert_reduce_fusion
  31.6 0.2 select_reduce_fusion.3
  31.8 0.1 select_reduce_fusion.1
  32.0 28.8 %all-to-all-done.1 = bf16[8,6,64,256]{3,2,1,0:T(8,128)(2,1)S(1)} async-done(((bf16[8,6,64,256]{3,2,1,0:T(8,128)(2,1)}), bf16[8,6,64,256]{3,2,1,0:T(8,128)(2,1)S(1)}, u32[]{:S(2)}, u32[]{:S(2)}) %all-to-all-start.1) | async-done | bytes 1572896 | tf_op jit(solution)/shard_map/all_to_all | solution.py:292
  60.7 3.1 %collective-permute-start.3 = (bf16[8,6,64,256]{3,2,1,0:T(8,128)(2,1)S(1)}, bf16[8,6,64,256]{3,2,1,0:T(8,128)(2,1)}, u32[]{:S(2)}, u32[]{:S(2)}) collective-permute-start(bf16[8,6,64,256]{3,2,1,0:T(8,128)(2,1)S(1)} %all-to-all-done.1), channel_id=1, source_target_pairs={{0,1},{1,0},{2,3},{3,2},{4,5},{5,4},{6,7},{7,6},{8,9},{9,8},{10,11... | collective-permute-start | bytes 4718600 | tf_op jit(solution)/shard_map/ppermute | solution.py:293
  63.9 0.1 copy.30
  64.0 0.1 reshape.520
  64.1 0.6 pad_add_fusion.2.scalars_ref
  64.7 0.9 copy.33.rown_ref
  65.6 0.6 pad_add_fusion.kinfo_ref
  66.2 0.1 pad_maximum_fusion
  66.3 0.6 gather_fusion
  66.9 0.1 convert_bitcast_fusion
  67.0 0.1 copy.37
  67.2 15.1 %shard_map.163 = bf16[512,512]{1,0:T(8,128)(2,1)} custom-call(s32[70]{0:T(128)} %pad_add_fusion.2.scalars_ref, bf16[512,512]{1,0:T(8,128)(2,1)} %q_ref.1, bf16[48,64,256]{2,1,0:T(8,128)(2,1)} %bitcast.88, bf16[48,64,256]{2,1,0:T(8,128)(2,1)} %bitcast.22.partner_ref, bf16[512,512]{1,0:T(8,128)(2,1)} %fresh_k_ref.1, bf16[512,512]{1,0:T(8,128)(2,1)} %fresh_v_ref.1, ...), custom_call_target="tpu_custom_call" | custom-call | tf_op jit(solution)/shard_map/pallas_call | solution.py:187
  82.2 1.1 dynamic-slice_bitcast_fusion.2
  83.3 1.2 collective-permute-start.4
  84.5 0.4 collective-permute-start.5
  85.0 2.2 %fusion.5 = f32[128,2048]{1,0:T(8,128)S(1)} fusion(bf16[2048,2048]{1,0:T(8,128)(2,1)} %all-gather.3.cloned.1.call-done, s32[]{:T(128)S(6)} %select_n.251, bf16[4,128,512]{2,1,0:T(8,128)(2,1)} %bitcast.93, s32[]{:T(128)S(6)} %select_n.223), kind=kOutput, calls=%fused_computation.10 | convolution fusion | flops 268435456 | bytes 3276808 | tf_op jit(solution)/shard_map/dot_general | solution.py:323
  87.2 3.0 %collective-permute-done.4 = bf16[128,512]{1,0:T(8,128)(2,1)S(1)} collective-permute-done((bf16[128,512]{1,0:T(8,128)(2,1)S(1)}, bf16[128,512]{1,0:T(8,128)(2,1)S(1)}, u32[]{:S(2)}, u32[]{:S(2)}) %collective-permute-start.4) | collective-permute-done | bytes 131104 | tf_op jit(solution)/shard_map/ppermute | solution.py:331
  90.2 2.0 %convolution_add_fusion.1 = f32[128,2048]{1,0:T(8,128)S(1)} fusion(f32[128,2048]{1,0:T(8,128)S(1)} %fusion.5, bf16[128,512]{1,0:T(8,128)(2,1)S(1)} %collective-permute-done.4, bf16[2048,2048]{1,0:T(8,128)(2,1)} %all-gather.3.cloned.1.call-done, s32[]{:T(128)S(6)} %select_n.253), kind=kOutput, calls=%fused_computation.5 | convolution fusion | flops 268697600 | bytes 4325380 | tf_op jit(solution)/shard_map/dot_general | solution.py:333
  92.3 0.7 collective-permute-done.6
  93.0 2.0 %fusion.1 = f32[128,2048]{1,0:T(8,128)S(1)} fusion(bf16[128,512]{1,0:T(8,128)(2,1)S(1)} %collective-permute-done.6, bf16[2048,2048]{1,0:T(8,128)(2,1)} %all-gather.3.cloned.1.call-done, s32[]{:T(128)S(6)} %select_n.257), kind=kOutput, calls=%fused_computation.6 | convolution fusion | flops 268435456 | bytes 3276804 | tf_op jit(solution)/shard_map/dot_general | solution.py:333
  95.1 0.8 collective-permute-done.5
  95.8 2.2 %multiply_reduce_fusion.1 = (f32[128]{0:T(128)S(1)}, f32[128,2048]{1,0:T(8,128)S(1)}) fusion(f32[128,2048]{1,0:T(8,128)S(1)} %fusion.1, f32[128,2048]{1,0:T(8,128)S(1)} %convolution_add_fusion.1, bf16[128,512]{1,0:T(8,128)(2,1)S(1)} %collective-permute-done.5, bf16[2048,2048]{1,0:T(8,128)(2,1)} %all-gather.3.cloned.1.call-done, s32[]{:T(128)S(6)} %select_n.255), kind=kOutput, calls=%fused_computation.25 | convolution fusion | flops 269483904 | bytes 5374468 | tf_op jit(solution)/shard_map/dot_general | solution.py:333
  98.1 0.2 add_convert_fusion.1
  98.3 6.3 %all-gather.5.cloned.1.call-done = bf16[2048,512]{0,1:T(8,128)(2,1)} async-done(((bf16[512,512]{0,1:T(8,128)(2,1)}), bf16[2048,512]{0,1:T(8,128)(2,1)}) %all-gather.5.cloned.1.call-update) | async-done | bytes 2097168 | tf_op jit(solution)/shard_map/all_gather | solution.py:307
  104.6 2.6 %multiply_reduce_fusion = (f32[128]{0:T(128)S(1)}, f32[128,2048]{1,0:T(8,128)S(1)}) fusion(bf16[2048,512]{0,1:T(8,128)(2,1)} %all-gather.5.cloned.1.call-done, bf16[128,2048]{1,0:T(8,128)(2,1)S(1)} %add_convert_fusion.1, bf16[512,256]{1,0:T(8,128)(2,1)} %param.29, s32[]{:T(128)S(6)} %select_n.258), kind=kOutput, calls=%fused_computation.23 | convolution fusion | flops 269320064 | bytes 3736068 | tf_op jit(solution)/shard_map/dot_general | solution.py:351
  107.2 0.2 add_convert_fusion
  107.5 1.2 collective-permute-start.7
  108.7 0.5 collective-permute-start.8
  109.2 0.1 collective-permute-start.9
  109.3 1.9 %collective-permute-done.7 = bf16[128,512]{1,0:T(8,128)(2,1)S(1)} collective-permute-done((bf16[128,512]{1,0:T(8,128)(2,1)S(1)}, bf16[128,512]{1,0:T(8,128)(2,1)S(1)}, u32[]{:S(2)}, u32[]{:S(2)}) %collective-permute-start.7) | collective-permute-done | bytes 131104 | tf_op jit(solution)/shard_map/ppermute | solution.py:242
  111.2 3.7 %collective-permute-done.8 = bf16[128,512]{1,0:T(8,128)(2,1)S(1)} collective-permute-done((bf16[128,512]{1,0:T(8,128)(2,1)S(1)}, bf16[128,512]{1,0:T(8,128)(2,1)S(1)}, u32[]{:S(2)}, u32[]{:S(2)}) %collective-permute-start.8) | collective-permute-done | bytes 131104 | tf_op jit(solution)/shard_map/ppermute | solution.py:242
  114.9 0.8 collective-permute-done.9
  115.7 0.1 pad_maximum_fusion.2
  115.8 1.4 %gather_fusion.2 = bf16[4,128,512]{2,1,0:T(8,128)(2,1)} fusion(bf16[4,128,512]{2,1,0:T(8,128)(2,1)S(1)} %pad_maximum_fusion.2, s32[1024]{0:T(1024)S(1)} %pad_clamp_fusion.1), kind=kCustom, calls=%fused_computation.2 | custom fusion | bytes 1048592 | tf_op jit(solution)/shard_map/gather | solution.py:244
  (56 shorter events, 0.4 us)
Async XLA Ops:
  6.5 0.7 copy-start.11
  6.5 0.9 copy-start.9
  6.5 78.4 %all-gather.3.cloned.1.call-start = ((), (), s32[]{:S(2)}) async-start(), calls=%async_computation.2 | async-start | bytes 10485760 | tf_op jit(solution)/shard_map/all_gather | solution.py:306
  8.4 11.6 %all-to-all-start = ((s32[8,1,6]{2,1,0:T(1,128)}), s32[8,1,6]{2,1,0:T(1,128)S(1)}, u32[]{:S(2)}, u32[]{:S(2)}) async-start(s32[8,1,6]{2,1,0:T(1,128)} %copy.32), calls=%async_computation | async-start | bytes 8192 | tf_op jit(solution)/shard_map/all_to_all | solution.py:283
  22.0 3.9 %copy-start.6 = (bf16[512]{0:T(512)(128)(2,1)S(1)}, bf16[512]{0:T(512)(128)(2,1)}, u32[]{:S(2)}) copy-start(bf16[512]{0:T(512)(128)(2,1)} %param.28) | copy-start | bytes 3076
  22.0 3.9 %copy-start.7 = (bf16[512]{0:T(512)(128)(2,1)S(1)}, bf16[512]{0:T(512)(128)(2,1)}, u32[]{:S(2)}) copy-start(bf16[512]{0:T(512)(128)(2,1)} %param.32) | copy-start | bytes 3076
  22.0 4.1 %copy-start.1 = (bf16[512,512]{1,0:T(8,128)(2,1)S(1)}, bf16[512,512]{1,0:T(8,128)(2,1)}, u32[]{:S(2)}) copy-start(bf16[512,512]{1,0:T(8,128)(2,1)} %param.21) | copy-start | bytes 1572868
  22.0 7.8 %copy-start.2 = (bf16[512,256]{1,0:T(8,128)(2,1)S(1)}, bf16[512,256]{1,0:T(8,128)(2,1)}, u32[]{:S(2)}) copy-start(bf16[512,256]{1,0:T(8,128)(2,1)} %param.30) | copy-start | bytes 786436
  22.0 8.0 %copy-start.3 = (bf16[256,512]{1,0:T(8,128)(2,1)S(1)}, bf16[256,512]{1,0:T(8,128)(2,1)}, u32[]{:S(2)}) copy-start(bf16[256,512]{1,0:T(8,128)(2,1)} %param.31) | copy-start | bytes 786436
  22.0 38.7 %all-to-all-start.1 = ((bf16[8,6,64,256]{3,2,1,0:T(8,128)(2,1)}), bf16[8,6,64,256]{3,2,1,0:T(8,128)(2,1)S(1)}, u32[]{:S(2)}, u32[]{:S(2)}) async-start(bf16[8,6,64,256]{3,2,1,0:T(8,128)(2,1)} %bitcast.20), calls=%async_computation.1 | async-start | bytes 3145728 | tf_op jit(solution)/shard_map/all_to_all | solution.py:292
  25.7 5.1 %copy-start.10 = (s32[1,8]{1,0:T(1,128)S(1)}, s32[1,8]{1,0:T(1,128)}, u32[]{:S(2)}) copy-start(s32[1,8]{1,0:T(1,128)} %param.37) | copy-start | bytes 100
  25.8 5.5 %copy-start.5 = (s32[1,8]{1,0:T(1,128)S(1)}, s32[1,8]{1,0:T(1,128)}, u32[]{:S(2)}) copy-start(s32[1,8]{1,0:T(1,128)} %param.35) | copy-start | bytes 100
  25.8 5.7 %copy-start.8 = (s32[1,8]{1,0:T(1,128)S(1)}, s32[1,8]{1,0:T(1,128)}, u32[]{:S(2)}) copy-start(s32[1,8]{1,0:T(1,128)} %param.36) | copy-start | bytes 100
  25.8 39.8 %copy-start.4 = (s32[7,1,512]{2,1,0:T(1,128)S(1)}, s32[7,1,512]{2,1,0:T(1,128)}, u32[]{:S(2)}) copy-start(s32[7,1,512]{2,1,0:T(1,128)} %constant.273.clone.1) | copy-start | bytes 43012
  25.8 78.8 %all-gather.5.cloned.1.call-start = ((), (), s32[]{:S(2)}) async-start(), calls=%async_computation.3 | async-start | bytes 2621440 | tf_op jit(solution)/shard_map/all_gather | solution.py:307
  26.1 40.1 %collective-permute-start = (bf16[136,512]{1,0:T(8,128)(2,1)S(1)}, bf16[136,512]{1,0:T(8,128)(2,1)S(1)}, u32[]{:S(2)}, u32[]{:S(2)}) collective-permute-start(bf16[136,512]{1,0:T(8,128)(2,1)S(1)} %get-tuple-element.38), channel_id=1, source_target_pairs={{0,1},{1,2},{2,3},{3,0},{4,5},{5,6},{6,7},{7,4},{8,9},{9,10},{10,1... | collective-permute-start | bytes 417800 | tf_op jit(solution)/shard_map/ppermute | solution.py:228
  29.3 36.9 %collective-permute-start.1 = (bf16[136,512]{1,0:T(8,128)(2,1)S(1)}, bf16[136,512]{1,0:T(8,128)(2,1)S(1)}, u32[]{:S(2)}, u32[]{:S(2)}) collective-permute-start(bf16[136,512]{1,0:T(8,128)(2,1)S(1)} %get-tuple-element.39), channel_id=1, source_target_pairs={{0,2},{1,3},{2,0},{3,1},{4,6},{5,7},{6,4},{7,5},{8,10},{9,11},{10,... | collective-permute-start | bytes 417800 | tf_op jit(solution)/shard_map/ppermute | solution.py:228
  29.6 36.7 %collective-permute-start.2 = (bf16[136,512]{1,0:T(8,128)(2,1)S(1)}, bf16[136,512]{1,0:T(8,128)(2,1)S(1)}, u32[]{:S(2)}, u32[]{:S(2)}) collective-permute-start(bf16[136,512]{1,0:T(8,128)(2,1)S(1)} %get-tuple-element.40), channel_id=1, source_target_pairs={{0,3},{1,0},{2,1},{3,2},{4,7},{5,4},{6,5},{7,6},{8,11},{9,8},{10,9... | collective-permute-start | bytes 417800 | tf_op jit(solution)/shard_map/ppermute | solution.py:228
  60.7 6.3 %copy-start = (bf16[8,6,64,256]{3,2,1,0:T(8,128)(2,1)}, bf16[8,6,64,256]{3,2,1,0:T(8,128)(2,1)S(1)}, u32[]{:S(2)}) copy-start(bf16[8,6,64,256]{3,2,1,0:T(8,128)(2,1)S(1)} %all-to-all-done.1) | copy-start | bytes 4718596
  60.7 6.4 %collective-permute-start.3 = (bf16[8,6,64,256]{3,2,1,0:T(8,128)(2,1)S(1)}, bf16[8,6,64,256]{3,2,1,0:T(8,128)(2,1)}, u32[]{:S(2)}, u32[]{:S(2)}) collective-permute-start(bf16[8,6,64,256]{3,2,1,0:T(8,128)(2,1)S(1)} %all-to-all-done.1), channel_id=1, source_target_pairs={{0,1},{1,0},{2,3},{3,2},{4,5},{5,4},{6,7},{7,6},{8,9},{9,8},{10,11... | collective-permute-start | bytes 4718600 | tf_op jit(solution)/shard_map/ppermute | solution.py:293
  83.3 6.9 %collective-permute-start.4 = (bf16[128,512]{1,0:T(8,128)(2,1)S(1)}, bf16[128,512]{1,0:T(8,128)(2,1)S(1)}, u32[]{:S(2)}, u32[]{:S(2)}) collective-permute-start(bf16[128,512]{1,0:T(8,128)(2,1)S(1)} %get-tuple-element.47), channel_id=1, source_target_pairs={{0,1},{1,2},{2,3},{3,0},{4,5},{5,6},{6,7},{7,4},{8,9},{9,10},{10,1... | collective-permute-start | bytes 393224 | tf_op jit(solution)/shard_map/ppermute | solution.py:331
  84.5 8.5 %collective-permute-start.6 = (bf16[128,512]{1,0:T(8,128)(2,1)S(1)}, bf16[128,512]{1,0:T(8,128)(2,1)S(1)}, u32[]{:S(2)}, u32[]{:S(2)}) collective-permute-start(bf16[128,512]{1,0:T(8,128)(2,1)S(1)} %get-tuple-element.46), channel_id=1, source_target_pairs={{0,3},{1,0},{2,1},{3,2},{4,7},{5,4},{6,5},{7,6},{8,11},{9,8},{10,9... | collective-permute-start | bytes 393224 | tf_op jit(solution)/shard_map/ppermute | solution.py:331
  84.5 11.3 %collective-permute-start.5 = (bf16[128,512]{1,0:T(8,128)(2,1)S(1)}, bf16[128,512]{1,0:T(8,128)(2,1)S(1)}, u32[]{:S(2)}, u32[]{:S(2)}) collective-permute-start(bf16[128,512]{1,0:T(8,128)(2,1)S(1)} %get-tuple-element.45), channel_id=1, source_target_pairs={{0,2},{1,3},{2,0},{3,1},{4,6},{5,7},{6,4},{7,5},{8,10},{9,11},{10,... | collective-permute-start | bytes 393224 | tf_op jit(solution)/shard_map/ppermute | solution.py:331
  107.5 3.7 %collective-permute-start.7 = (bf16[128,512]{1,0:T(8,128)(2,1)S(1)}, bf16[128,512]{1,0:T(8,128)(2,1)S(1)}, u32[]{:S(2)}, u32[]{:S(2)}) collective-permute-start(bf16[128,512]{1,0:T(8,128)(2,1)S(1)} %get-tuple-element.44), channel_id=1, source_target_pairs={{0,1},{1,2},{2,3},{3,0},{4,5},{5,6},{6,7},{7,4},{8,9},{9,10},{10,1... | collective-permute-start | bytes 393224 | tf_op jit(solution)/shard_map/ppermute | solution.py:242
  108.7 6.3 %collective-permute-start.8 = (bf16[128,512]{1,0:T(8,128)(2,1)S(1)}, bf16[128,512]{1,0:T(8,128)(2,1)S(1)}, u32[]{:S(2)}, u32[]{:S(2)}) collective-permute-start(bf16[128,512]{1,0:T(8,128)(2,1)S(1)} %get-tuple-element.43), channel_id=1, source_target_pairs={{0,2},{1,3},{2,0},{3,1},{4,6},{5,7},{6,4},{7,5},{8,10},{9,11},{10,... | collective-permute-start | bytes 393224 | tf_op jit(solution)/shard_map/ppermute | solution.py:242
  109.2 6.6 %collective-permute-start.9 = (bf16[128,512]{1,0:T(8,128)(2,1)S(1)}, bf16[128,512]{1,0:T(8,128)(2,1)S(1)}, u32[]{:S(2)}, u32[]{:S(2)}) collective-permute-start(bf16[128,512]{1,0:T(8,128)(2,1)S(1)} %get-tuple-element.42), channel_id=1, source_target_pairs={{0,3},{1,0},{2,1},{3,2},{4,7},{5,4},{6,5},{7,6},{8,11},{9,8},{10,9... | collective-permute-start | bytes 393224 | tf_op jit(solution)/shard_map/ppermute | solution.py:242
Sparse Core Ops, SparseCore 0:
  8.9 66.7 all-gather.2
  77.3 27.2 all-gather.4
